TPU v7x, 128 devices: a whole 4x4x4 slice. The times are simulated.
128 devices in a mesh: kv: 4 (over x), tok: 32 (over z, y, core).
Axes of the slice: x: 4, y: 4, z: 4, core: 2. Of those that a mesh axis runs over, the one named last changes fastest.
Arguments:
- dec_tokens: bfloat16 [512, 5120], P('tok', 'kv'), may hold values from -60 to 60
- pre_tokens: bfloat16 [8192, 5120], P('tok', 'kv'), may hold values from -60 to 60
- w_query: bfloat16 [5120, 2560], P(None, 'kv'), may hold values from -0.078125 to 0.078125
- w_keyval: bfloat16 [5120, 2, 512], P(None, None, 'kv'), may hold values from -0.078125 to 0.078125
- b_query: float32 [2560], P('kv'), may hold values from -3 to 3
- b_keyval: float32 [2, 512], P(None, 'kv'), may hold values from -3 to 3
- dec_pool: bfloat16 [2, 393216, 512], P(None, 'tok', 'kv'), may hold values from -72 to 72
- owner_slots: int32 [512], P('tok'), may hold values from 0 to 511, each once
- dec_lengths: int32 [512], P('tok'), may hold values from 1 to 4096, as said below
- pre_cache: bfloat16 [2, 32768, 512], P(None, 'tok', 'kv'), may hold values from -72 to 72
- pre_offsets: int32 [16], replicated, may hold values from 1536 to 2048
Outputs:
- dec_attn: bfloat16 [512, 2560], P('tok', 'kv')
- pre_attn: bfloat16 [8192, 2560], P('tok', 'kv')
- new_pool: bfloat16 [2, 393216, 512], P(None, 'tok', 'kv')
- pre_keyval: bfloat16 [2, 8192, 512], P(None, 'tok', 'kv')
Inputs may be any that keep to these rules, and one draw needn't show every extreme that they name: `dec_lengths`: in the 16 slots of each owner, one length is 512 or more and the others are below 512, so an owner's lengths plus one each sum to at most 12288.
All inputs are finite; a program needn't handle non-finite values.
Results may differ from a plain program's by a relative error of at most 0.0065.
The roundings to bfloat16 on the way count: a program that leaves them out, or rounds other values in their place, can miss the bound.
Values may be sent and summed in bfloat16 or wider, within the bound.
No kernel may reach another device: no remote copies, remote signals or barrier semaphores. Data moves between devices by JAX's collectives and lax.ppermute only.
A program may use at most 128 MiB of HBM per device.

v0:
```python
import jax
import jax.numpy as jnp
from jax import lax
from jax.sharding import PartitionSpec as P

HD = 128


THETA = 1000000.0


def swapped(value, axis, distance):
    return lax.ppermute(value, axis, [(i, i ^ 1 << distance) for i in range(lax.axis_size(axis))])


def rotate(values, positions):
    halfway = values.shape[-1] // 2
    spread = jnp.arange(halfway, dtype=jnp.float32) * (2.0 / values.shape[-1])
    rates = jnp.power(jnp.float32(THETA), -spread)
    angles = positions.astype(jnp.float32)[:, None] * rates[None, :]
    cosine = jnp.cos(angles)[:, None, :]
    sine = jnp.sin(angles)[:, None, :]
    former = values[..., :halfway]
    latter = values[..., halfway:]
    return jnp.concatenate(
        [former * cosine - latter * sine, latter * cosine + former * sine], axis=-1
    )


def head_scores(queries, key_rows, allowed):
    amount = queries.shape[0]
    q_heads = queries.shape[1] // HD
    shaped = queries.reshape(amount, q_heads, HD)
    product = jnp.einsum("ngd,md->ngm", shaped, key_rows, preferred_element_type=jnp.float32)
    scores = product * HD ** (-0.5)
    return jnp.where(allowed[:, None, :], scores, -jnp.inf)


def head_mix(scores, peaks, value_rows):
    powers = jnp.exp(scores - peaks[..., None])
    totals = jnp.sum(powers, axis=-1)
    weights = powers.astype(jnp.bfloat16)
    product = jnp.einsum("ngm,md->ngd", weights, value_rows, preferred_element_type=jnp.float32)
    return (totals, product)


def serve_owner(queries, keyval, lengths, cache_pool):
    amount = queries.shape[0]
    q_heads = queries.shape[1] // HD
    kv_heads = cache_pool.shape[2] // HD
    finish = jnp.cumsum(lengths + 1)
    starts = finish - lengths - 1
    turned = rotate(queries.astype(jnp.float32).reshape(amount, q_heads, HD), lengths)
    turned = turned.astype(jnp.bfloat16).reshape(amount, q_heads * HD)
    new_keys = rotate(keyval[:, 0].astype(jnp.float32).reshape(amount, kv_heads, HD), lengths)
    new_keys = new_keys.astype(jnp.bfloat16).reshape(amount, kv_heads * HD)
    appended = jnp.stack([new_keys, keyval[:, 1]], axis=0)
    cache_pool = cache_pool.at[:, starts + lengths].set(appended)
    spots = jnp.arange(cache_pool.shape[1], dtype=jnp.int32)
    allowed = (spots[None, :] >= starts[:, None]) & (spots[None, :] <= (starts + lengths)[:, None])
    scores = head_scores(turned, cache_pool[0], allowed)
    totals, mixed = head_mix(scores, jnp.max(scores, axis=-1), cache_pool[1])
    result = (mixed / totals[..., None]).astype(jnp.bfloat16).reshape(amount, q_heads * HD)
    return (result, cache_pool)


def body(
    dec_tokens,
    pre_tokens,
    w_query,
    w_keyval,
    b_query,
    b_keyval,
    dec_pool,
    owner_slots,
    dec_lengths,
    pre_cache,
    pre_offsets,
):
    dec_count = dec_tokens.shape[0]
    pre_count = pre_tokens.shape[0]
    q_width = w_query.shape[1]
    kv_width = w_keyval.shape[2]
    kv_weight = w_keyval.reshape(w_keyval.shape[0], 2 * kv_width)
    stacked = jnp.concatenate([dec_tokens, pre_tokens], axis=0)
    columns = lax.all_gather(stacked, "kv", axis=1, tiled=True)
    all_query = jnp.dot(columns, w_query, preferred_element_type=jnp.float32)
    all_keyval = jnp.dot(columns, kv_weight, preferred_element_type=jnp.float32)
    all_query = all_query + b_query
    all_keyval = all_keyval + b_keyval.reshape(2 * kv_width)
    dec_query = all_query[:dec_count].astype(jnp.bfloat16)
    dec_keyval = all_keyval[:dec_count].astype(jnp.bfloat16).reshape(dec_count, 2, kv_width)
    every_query, every_keyval = (
        lax.all_gather(dec_query, "tok", axis=0, tiled=True),
        lax.all_gather(dec_keyval, "tok", axis=0, tiled=True),
    )
    served, new_pool = serve_owner(
        jnp.take(every_query, owner_slots, axis=0),
        jnp.take(every_keyval, owner_slots, axis=0),
        dec_lengths,
        dec_pool,
    )
    every_result = lax.all_gather(served, "tok", axis=0, tiled=True)
    every_owner = lax.all_gather(owner_slots, "tok", axis=0, tiled=True)
    inverse = (
        jnp.zeros(every_owner.shape, jnp.int32)
        .at[every_owner]
        .set(jnp.arange(every_owner.shape[0], dtype=jnp.int32))
    )
    wanted = lax.axis_index("tok") * dec_count + jnp.arange(dec_count, dtype=jnp.int32)
    dec_attn = jnp.take(every_result, jnp.take(inverse, wanted), axis=0)
    tok_place = lax.axis_index("tok")
    half_id = tok_place % 2
    offset = pre_offsets[tok_place // 2]
    local_pos = jnp.arange(pre_count, dtype=jnp.int32)
    positions = offset + half_id * pre_count + local_pos
    q_heads = q_width // HD
    kv_heads = kv_width // HD
    turned = rotate(all_query[dec_count:].reshape(pre_count, q_heads, HD), positions)
    turned = turned.astype(jnp.bfloat16).reshape(pre_count, q_width)
    pre_kv = all_keyval[dec_count:].reshape(pre_count, 2, kv_width)
    new_keys = rotate(pre_kv[:, 0].reshape(pre_count, kv_heads, HD), positions)
    new_keys = new_keys.astype(jnp.bfloat16).reshape(pre_count, kv_width)
    appended = jnp.stack([new_keys, pre_kv[:, 1].astype(jnp.bfloat16)], axis=0)
    shard = pre_cache.shape[1]
    other_cache, other_new = swapped((pre_cache, appended), "tok", 0)
    is_lower = half_id == 0
    history = jnp.where(
        is_lower,
        jnp.concatenate([pre_cache, other_cache], axis=1),
        jnp.concatenate([other_cache, pre_cache], axis=1),
    )
    block_rows = jnp.where(
        is_lower,
        jnp.concatenate([appended, other_new], axis=1),
        jnp.concatenate([other_new, appended], axis=1),
    )
    key_rows = jnp.concatenate([history, block_rows], axis=1)
    key_slots = jnp.arange(key_rows.shape[1], dtype=jnp.int32)
    key_pos = jnp.where(key_slots < 2 * shard, key_slots, offset + key_slots - 2 * shard)
    usable = (key_slots < offset) | (key_slots >= 2 * shard)
    allowed = usable[None, :] & (key_pos[None, :] <= positions[:, None])
    scores = head_scores(turned, key_rows[0], allowed)
    totals, mixed = head_mix(scores, jnp.max(scores, axis=-1), key_rows[1])
    pre_attn = (mixed / totals[..., None]).astype(jnp.bfloat16).reshape(pre_count, q_width)
    return (dec_attn, pre_attn, new_pool, appended)


def solution(mesh):
    in_specs = (
        P("tok", "kv"),
        P("tok", "kv"),
        P(None, "kv"),
        P(None, None, "kv"),
        P("kv"),
        P(None, "kv"),
        P(None, "tok", "kv"),
        P("tok"),
        P("tok"),
        P(None, "tok", "kv"),
        P(),
    )
    out_specs = (P("tok", "kv"), P("tok", "kv"), P(None, "tok", "kv"), P(None, "tok", "kv"))
    return jax.shard_map(body, mesh=mesh, in_specs=in_specs, out_specs=out_specs, check_vma=False)
```

profile of v0, /device:TPU:1, one launch (start us, length us, event | category | flops | bytes accessed | tf_op | source)
XLA Modules:
  0.0 184.4 jit_solution(5696479850076960690)
XLA Ops:
  7.2 0.0 copy-start.9
  7.2 0.0 copy-start.3
  7.2 0.0 copy-start.1
  7.2 0.0 copy-start.8
  7.2 0.0 all-gather.2.cloned.1.call-start
  7.3 6.5 %copy.145 = bf16[2,12288,128]{2,1,0:T(8,128)(2,1)} copy(bf16[2,12288,128]{2,1,0:T(8,128)(2,1)} %param.19) | data formatting | bytes 12582912
  13.8 0.0 copy-done.1
  13.8 0.9 pad_maximum_fusion
  14.7 0.0 all-gather.2.cloned.1.call-update
  14.7 1.5 collective-permute-start
  16.2 0.6 dynamic_slice.3
  17.5 0.7 add_select_fusion
  18.1 0.7 fusion.58
  18.9 0.1 copy.88
  19.0 0.1 reduce
  19.1 0.6 dynamic-slice
  20.4 0.2 dynamic-update-slice
  20.6 15.3 %all-reduce = s32[512]{0:T(512)S(1)} all-reduce(s32[512]{0:T(512)S(1)} %dynamic-update-slice), channel_id=1, replica_groups=mesh['kv'=4,'tok'=32] {'tok'}, use_global_device_ids=true, to_apply=%add | all-reduce | flops 512 | bytes 4096
  35.9 2.4 %scatter_custom_fusion.1 = s32[512]{0:T(512)S(1)} fusion(s32[512]{0:T(512)S(1)} %compare_select_fusion, s32[512]{0:T(512)S(1)} %iota.58, s32[]{:T(128)} %constant.56.clone.1), kind=kCustom, calls=%fused_computation.115 | custom fusion | bytes 2052 | tf_op jit(solution)/shard_map/scatter | solution.py:108
  38.4 0.7 gather_fusion.1
  39.1 0.1 multiply_cosine_fusion.3
  39.2 0.5 multiply_cosine_fusion.1
  39.7 0.2 fusion.33
  40.0 0.5 compare_and_fusion
  40.5 0.0 collective-permute-done
  40.5 1.2 maximum_select_fusion
  41.7 12.7 %all-gather.2.cloned.1.call-done = bf16[272,5120]{1,0:T(8,128)(2,1)} async-done(((bf16[272,1280]{1,0:T(8,128)(2,1)}), bf16[272,5120]{1,0:T(8,128)(2,1)}) %all-gather.2.cloned.1.call-update) | async-done | bytes 2785296 | tf_op jit(solution)/shard_map/all_gather | solution.py:86
  54.4 3.5 %fusion.15 = f32[272,256]{1,0:T(8,128)S(1)} fusion(bf16[272,5120]{1,0:T(8,128)(2,1)} %all-gather.2.cloned.1.call-done, bf16[640,8,2,128]{3,2,1,0:T(2,128)(2,1)} %bitcast.74, f32[256]{0:T(256)S(1)} %bitcast.75), kind=kOutput, calls=%fused_computation.29 | convolution fusion | flops 713101312 | bytes 5686272 | tf_op jit(solution)/shard_map/dot_general | solution.py:88
  57.9 0.1 reshape.478
  58.0 0.3 fusion.81
  58.4 0.1 slice.106
  58.5 0.0 copy-done.5
  58.6 6.0 %convolution_add_fusion = f32[272,640]{1,0:T(8,128)S(1)} fusion(bf16[272,5120]{1,0:T(8,128)(2,1)} %all-gather.2.cloned.1.call-done, bf16[5120,640]{1,0:T(8,128)(2,1)} %param.15, f32[640]{0:T(1024)S(1)} %copy-done.5), kind=kOutput, calls=%fused_computation.28 | convolution fusion | flops 1782753280 | bytes 10037760 | tf_op jit(solution)/shard_map/dot_general | solution.py:87
  64.7 0.6 fusion.54
  65.2 0.8 pad_maximum_fusion.2
  66.0 0.8 collective-permute-start.1
  66.8 0.2 copy.93
  67.1 0.2 copy.105
  67.4 0.2 copy.106
  67.6 24.9 %all_gather.17 = bf16[512,2,128]{2,1,0:T(2,128)(2,1)S(1)} all-gather(bf16[16,2,128]{2,1,0:T(2,128)(2,1)S(1)} %reshape.475), channel_id=1, replica_groups=mesh['kv'=4,'tok'=32] {'tok'}, dimensions={0}, use_global_device_ids=true | all-gather | bytes 270336 | tf_op jit(solution)/shard_map/all_gather | solution.py:95
  92.6 0.6 gather_fusion
  93.2 0.1 copy_select_fusion
  93.2 0.1 fusion.68
  93.4 24.4 %all_gather.16 = bf16[512,640]{1,0:T(8,128)(2,1)S(1)} all-gather(bf16[16,640]{1,0:T(8,128)(2,1)S(1)} %slice.145), channel_id=1, replica_groups=mesh['kv'=4,'tok'=32] {'tok'}, dimensions={0}, use_global_device_ids=true | all-gather | bytes 675840 | tf_op jit(solution)/shard_map/all_gather | solution.py:94
  117.8 0.6 gather_fusion.2
  118.4 0.1 select_convert_fusion
  118.5 0.1 fusion.82
  118.5 0.1 maximum_bitcast_fusion
  118.6 2.3 %scatter_fusion = bf16[2,12288,128]{2,1,0:T(8,128)(2,1)} fusion(bf16[2,12288,128]{2,1,0:T(8,128)(2,1)} %copy.145, s32[16]{0:T(128)S(1)} %get-tuple-element.35, bf16[16,2,128]{2,0,1:T(8,128)(2,1)S(1)} %maximum_bitcast_fusion), kind=kCustom, calls=%fused_computation.4 | custom fusion | bytes 24640 | tf_op jit(solution)/shard_map/scatter | solution.py:58
  121.0 0.0 slice-start.1
  121.0 3.4 %fusion.84 = (f32[16,5]{0,1:T(8,128)S(1)}, f32[16,5,12288]{2,0,1:T(8,128)S(1)}) fusion(bf16[2,12288,128]{2,1,0:T(8,128)(2,1)} %scatter_fusion, bf16[16,5,64]{2,0,1:T(8,128)(2,1)S(1)} %get-tuple-element.46, bf16[16,5,64]{2,0,1:T(8,128)(2,1)S(1)} %get-tuple-element.45, pred[16,12288]{1,0:T(8,128)(4,1)S(1)} %fusion.33), kind=kOutput, calls=%fused_computation.132 | convolution fusion | flops 254648240 | bytes 7295296 | tf_op jit(solution)/shard_map/ngd,md->ngm/dot_general | solution.py:34
  124.4 0.8 fusion.7
  125.2 0.0 slice-done
  125.2 0.9 fusion.24
  126.1 24.8 %all_gather.18 = bf16[512,640]{1,0:T(8,128)(2,1)} all-gather(bf16[16,640]{1,0:T(8,128)(2,1)S(1)} %bitcast.73), channel_id=1, replica_groups=mesh['kv'=4,'tok'=32] {'tok'}, dimensions={0}, use_global_device_ids=true | all-gather | bytes 675840 | tf_op jit(solution)/shard_map/all_gather | solution.py:103
  150.9 1.8 gather_fusion.3
  152.7 0.2 subtract_convert_fusion
  152.8 0.7 broadcast_select_fusion
  153.5 0.0 collective-permute-done.1
  153.5 1.1 maximum_select_fusion.1
  154.7 6.6 %fusion.1 = (f32[256,5]{0,1:T(8,128)S(1)}, f32[256,5,2560]{2,0,1:T(8,128)}) fusion(pred[256,2560]{1,0:T(8,128)(4,1)S(1)} %compare_and_fusion, bf16[2,2048,128]{2,1,0:T(8,128)(2,1)S(1)} %copy-done, bf16[2,512,128]{2,1,0:T(8,128)(2,1)S(1)} %maximum_select_fusion.1, bf16[256,5,64]{2,0,1:T(8,128)(2,1)S(1)} %get-tuple-element.38, ...), kind=kOutput, calls=%fused_computation.10 | convolution fusion | flops 850656000 | bytes 15406080 | tf_op jit(solution)/shard_map/ngd,md->ngm/dot_general | solution.py:34
  161.3 8.4 %fusion.2 = f32[256,5]{0,1:T(8,128)S(1)} fusion(f32[256,5,2560]{2,0,1:T(8,128)} %get-tuple-element.63, f32[256,5]{0,1:T(8,128)S(1)} %get-tuple-element.62, pred[256,2560]{1,0:T(8,128)(4,1)S(1)} %compare_and_fusion), kind=kLoop, calls=%fused_computation.11 | loop fusion | flops 13105920 | bytes 13772800 | tf_op jit(solution)/shard_map/reduce_sum | solution.py:41
  169.7 7.0 %fusion.30 = bf16[256,5,128]{0,2,1:T(8,128)(2,1)S(1)} fusion(f32[256,5,2560]{2,0,1:T(8,128)} %get-tuple-element.63, f32[256,5]{0,1:T(8,128)S(1)} %get-tuple-element.62, pred[256,2560]{1,0:T(8,128)(4,1)S(1)} %compare_and_fusion, bf16[2,512,128]{2,1,0:T(8,128)(2,1)S(1)} %maximum_select_fusion.1, bf16[2,2048,128]{2,1,0:T(8,128)(2,1)S(1)} %copy-done, ...), kind=kOutput, calls=%fused_computation.35 | convolution fusion | flops 853606400 | bytes 15411200 | tf_op jit(solution)/shard_map/ngm,md->ngd/dot_general | solution.py:43
  176.6 0.9 copy.100
  (44 shorter events, 0.3 us)
Async XLA Ops:
  7.2 12.0 %copy-start.9 = (u32[128]{0:T(128)S(1)}, u32[128]{0:T(128)}, u32[]{:S(2)}) copy-start(u32[128]{0:T(128)} %constant.101) | copy-start | bytes 1540
  7.2 6.6 %copy-start.3 = (bf16[16,1280]{1,0:T(8,128)(2,1)S(1)}, bf16[16,1280]{1,0:T(8,128)(2,1)}, u32[]{:S(2)}) copy-start(bf16[16,1280]{1,0:T(8,128)(2,1)} %param.13) | copy-start | bytes 122884
  7.2 6.6 %copy-start.1 = (bf16[256,1280]{1,0:T(8,128)(2,1)S(1)}, bf16[256,1280]{1,0:T(8,128)(2,1)}, u32[]{:S(2)}) copy-start(bf16[256,1280]{1,0:T(8,128)(2,1)} %param.14) | copy-start | bytes 1966084
  7.2 11.6 %copy-start.8 = (s32[16]{0:T(128)S(1)}, s32[16]{0:T(128)}, u32[]{:S(2)}) copy-start(s32[16]{0:T(128)} %param.20) | copy-start | bytes 196
  7.2 11.6 %copy-start.4 = (s32[16]{0:T(128)S(1)}, s32[16]{0:T(128)}, u32[]{:S(2)}) copy-start(s32[16]{0:T(128)} %param.21) | copy-start | bytes 196
  7.2 7.5 %copy-start.2 = (bf16[2,1024,128]{2,1,0:T(8,128)(2,1)S(1)}, bf16[2,1024,128]{2,1,0:T(8,128)(2,1)}, u32[]{:S(2)}) copy-start(bf16[2,1024,128]{2,1,0:T(8,128)(2,1)} %param.22) | copy-start | bytes 1572868
  7.2 9.0 %copy-start.7 = (s32[16]{0:T(128)S(1)}, s32[16]{0:T(128)}, u32[]{:S(2)}) copy-start(s32[16]{0:T(128)} %param.23) | copy-start | bytes 196
  7.2 47.1 %all-gather.2.cloned.1.call-start = ((), (), s32[]{:S(2)}) async-start(), calls=%async_computation | async-start | bytes 3481600 | tf_op jit(solution)/shard_map/all_gather | solution.py:86
  13.8 40.6 %copy-start.6 = (f32[2,128]{1,0:T(2,128)S(1)}, f32[2,128]{1,0:T(2,128)}, u32[]{:S(2)}) copy-start(f32[2,128]{1,0:T(2,128)} %param.18) | copy-start | bytes 3076
  14.7 25.7 %collective-permute-start = (bf16[2,1024,128]{2,1,0:T(8,128)(2,1)S(1)}, bf16[2,1024,128]{2,1,0:T(8,128)(2,1)S(1)}, u32[]{:S(2)}, u32[]{:S(2)}) collective-permute-start(bf16[2,1024,128]{2,1,0:T(8,128)(2,1)S(1)} %copy-done.2), channel_id=1, source_target_pairs={{0,1},{1,0},{2,3},{3,2},{4,5},{5,4},{6,7},{7,6},{8,9},{9,8},{10,11... | collective-permute-start | bytes 1572872 | tf_op jit(solution)/shard_map/ppermute | solution.py:13
  54.4 4.2 %copy-start.5 = (f32[640]{0:T(1024)S(1)}, f32[640]{0:T(1024)}, u32[]{:S(2)}) copy-start(f32[640]{0:T(1024)} %param.17) | copy-start | bytes 7684
  66.0 87.5 %collective-permute-start.1 = (bf16[2,256,128]{2,1,0:T(8,128)(2,1)}, bf16[2,256,128]{2,1,0:T(8,128)(2,1)}, u32[]{:S(2)}, u32[]{:S(2)}) collective-permute-start(bf16[2,256,128]{2,1,0:T(8,128)(2,1)} %pad_maximum_fusion.2), channel_id=1, source_target_pairs={{0,1},{1,0},{2,3},{3,2},{4,5},{5,4},{6,7},{7,6},{8,9},{9,8},{10,11... | collective-permute-start | bytes 393224 | tf_op jit(solution)/shard_map/ppermute | solution.py:13
  120.9 4.2 %slice-start = ((s8[6291456]{0:T(1024)(128)(4,1)}), s8[4194304]{0:T(1024)(128)(4,1)S(1)}, s32[]{:S(2)}) async-start(s8[6291456]{0:T(1024)(128)(4,1)} %bitcast.67), calls=%async_computation.1 | async-start | bytes 8388608
  121.0 4.2 %slice-start.1 = ((s8[6291456]{0:T(1024)(128)(4,1)}), s8[2097152]{0:T(1024)(128)(4,1)S(1)}, s32[]{:S(2)}) async-start(s8[6291456]{0:T(1024)(128)(4,1)} %bitcast.67), calls=%async_computation.2 | async-start | bytes 4194304
  125.2 29.5 %copy-start = (bf16[2,2048,128]{2,1,0:T(8,128)(2,1)S(1)}, bf16[2,2048,128]{2,1,0:T(8,128)(2,1)}, u32[]{:S(2)}) copy-start(bf16[2,2048,128]{2,1,0:T(8,128)(2,1)} %maximum_select_fusion) | copy-start | bytes 3145732
Sparse Core Ops, SparseCore 0:
  14.8 39.4 all-gather.1
where the time goes:
time: 185 us; the launch traced here: 184 us
  blocking collectives  89.4 us (48%)
  matrix products  27.3 us (15%)
  local copies, waits for them, and re-layouts  18.9 us (10%)
  other arithmetic  17.9 us (10%)
  between operations  15.8 us (9%)
  waiting for transfers between devices  12.7 us (7%)
  starting transfers between devices  2.34 us (1%)
    all_gather x1, blocking collectives, body(): lax.all_gather(dec_keyval, 'tok', axis=0, tiled=True)  24.9 us
    all_gather x1, blocking collectives, body(): every_result = lax.all_gather(served, 'tok', axis=0, tiled=True)  24.8 us
    all_gather x1, blocking collectives, body(): lax.all_gather(dec_query, 'tok', axis=0, tiled=True)  24.4 us
    unnamed x1, blocking collectives  15.3 us
    all_gather x1, waiting for transfers between devices, body(): columns = lax.all_gather(stacked, 'kv', axis=1, tiled=True)  12.7 us
    dot_general x2, matrix products, head_scores(): jnp.einsum('ngd,md->ngm', shaped, key_rows, preferred_element_type=jnp.fl...  9.99 us
    reduce_sum x2, other arithmetic, head_mix(): totals = jnp.sum(powers, axis=-1)  9.2 us
    unnamed x31, local copies, waits for them, and re-layouts  8.76 us
  transfers between devices with their start and end apart: 3, of which 1 were waited for; matrix products, arithmetic and copies ran while one was open for 11% of the time, Pallas kernels for 0%

commit v1 on v0

--- a/solution.py
+++ b/solution.py
@@ -64,6 +64,27 @@
     return (result, cache_pool)
 
 
+def fan(value, axis):
+    count = lax.axis_size(axis)
+    parts = [value]
+    for shift in range(1, count):
+        parts.append(lax.ppermute(value, axis, [(i, (i + shift) % count) for i in range(count)]))
+    return parts
+
+
+def project(rows, weight, bias):
+    parts = fan(rows, "kv")
+    place = lax.axis_index("kv")
+    width = rows.shape[1]
+    total = None
+    for shift, part in enumerate(parts):
+        source = (place - shift) % len(parts)
+        block = lax.dynamic_slice_in_dim(weight, source * width, width, axis=0)
+        piece = jnp.dot(part, block, preferred_element_type=jnp.float32)
+        total = piece if total is None else total + piece
+    return total + bias
+
+
 def body(
     dec_tokens,
     pre_tokens,
@@ -82,43 +103,40 @@
     q_width = w_query.shape[1]
     kv_width = w_keyval.shape[2]
     kv_weight = w_keyval.reshape(w_keyval.shape[0], 2 * kv_width)
-    stacked = jnp.concatenate([dec_tokens, pre_tokens], axis=0)
-    columns = lax.all_gather(stacked, "kv", axis=1, tiled=True)
-    all_query = jnp.dot(columns, w_query, preferred_element_type=jnp.float32)
-    all_keyval = jnp.dot(columns, kv_weight, preferred_element_type=jnp.float32)
-    all_query = all_query + b_query
-    all_keyval = all_keyval + b_keyval.reshape(2 * kv_width)
-    dec_query = all_query[:dec_count].astype(jnp.bfloat16)
-    dec_keyval = all_keyval[:dec_count].astype(jnp.bfloat16).reshape(dec_count, 2, kv_width)
-    every_query, every_keyval = (
-        lax.all_gather(dec_query, "tok", axis=0, tiled=True),
-        lax.all_gather(dec_keyval, "tok", axis=0, tiled=True),
-    )
-    served, new_pool = serve_owner(
-        jnp.take(every_query, owner_slots, axis=0),
-        jnp.take(every_keyval, owner_slots, axis=0),
-        dec_lengths,
-        dec_pool,
-    )
-    every_result = lax.all_gather(served, "tok", axis=0, tiled=True)
-    every_owner = lax.all_gather(owner_slots, "tok", axis=0, tiled=True)
-    inverse = (
-        jnp.zeros(every_owner.shape, jnp.int32)
-        .at[every_owner]
-        .set(jnp.arange(every_owner.shape[0], dtype=jnp.int32))
-    )
-    wanted = lax.axis_index("tok") * dec_count + jnp.arange(dec_count, dtype=jnp.int32)
-    dec_attn = jnp.take(every_result, jnp.take(inverse, wanted), axis=0)
+    weight = jnp.concatenate([w_query, kv_weight], axis=1)
+    bias = jnp.concatenate([b_query, b_keyval.reshape(2 * kv_width)])
+    dec_all = project(dec_tokens, weight, bias).astype(jnp.bfloat16)
+    tok_count = lax.axis_size("tok")
     tok_place = lax.axis_index("tok")
+    ids = jnp.stack([owner_slots // dec_count, owner_slots % dec_count], axis=1).astype(jnp.bfloat16)
+    send_width = -(-(q_width + 2 * kv_width + 2) // 128) * 128
+    pad = jnp.zeros((dec_count, send_width - q_width - 2 * kv_width - 2), jnp.bfloat16)
+    sent = jnp.concatenate([dec_all, ids, pad], axis=1)
+    got = jnp.concatenate(fan(sent, "tok"), axis=0)
+    source = owner_slots // dec_count
+    rows = ((tok_place - source) % tok_count) * dec_count + owner_slots % dec_count
+    chosen = jnp.take(got, rows, axis=0)
+    dec_query = chosen[:, :q_width]
+    dec_keyval = chosen[:, q_width:q_width + 2 * kv_width].reshape(dec_count, 2, kv_width)
+    served, new_pool = serve_owner(dec_query, dec_keyval, dec_lengths, dec_pool)
+    back = jnp.concatenate(fan(served, "tok"), axis=0)
+    got_ids = got[:, q_width + 2 * kv_width:q_width + 2 * kv_width + 2].astype(jnp.int32)
+    requests = got_ids[:, 0] * dec_count + got_ids[:, 1]
+    wanted = tok_place * dec_count + jnp.arange(dec_count, dtype=jnp.int32)
+    where = jnp.argmax(requests[None, :] == wanted[:, None], axis=1)
+    dec_attn = jnp.take(back, where, axis=0)
+    pre_all = project(pre_tokens, weight, bias)
+    all_query = pre_all[:, :q_width]
+    all_keyval = pre_all[:, q_width:]
     half_id = tok_place % 2
     offset = pre_offsets[tok_place // 2]
     local_pos = jnp.arange(pre_count, dtype=jnp.int32)
     positions = offset + half_id * pre_count + local_pos
     q_heads = q_width // HD
     kv_heads = kv_width // HD
-    turned = rotate(all_query[dec_count:].reshape(pre_count, q_heads, HD), positions)
+    turned = rotate(all_query.reshape(pre_count, q_heads, HD), positions)
     turned = turned.astype(jnp.bfloat16).reshape(pre_count, q_width)
-    pre_kv = all_keyval[dec_count:].reshape(pre_count, 2, kv_width)
+    pre_kv = all_keyval.reshape(pre_count, 2, kv_width)
     new_keys = rotate(pre_kv[:, 0].reshape(pre_count, kv_heads, HD), positions)
     new_keys = new_keys.astype(jnp.bfloat16).reshape(pre_count, kv_width)
     appended = jnp.stack([new_keys, pre_kv[:, 1].astype(jnp.bfloat16)], axis=0)

time: 185 us -> 490 us (2.65); the launches traced: 184 us -> 481 us
  waiting for transfers between devices: 12.7 us -> 203 us
  starting transfers between devices: 2.34 us -> 178 us
  blocking collectives: 89.4 us -> 0 us
  local copies, waits for them, and re-layouts: 18.9 us -> 41.8 us
  between operations: 15.8 us -> 2.1 us
  matrix products: 27.3 us -> 37.5 us
    ppermute x0 -> x68, waiting for transfers between devices: none -> 203 us  [fan(): lax.ppermute(value, axis, [(i, (i + shift) % count) for i in range(count)])]
    ppermute x0 -> x68, starting transfers between devices: none -> 177 us  [fan(): lax.ppermute(value, axis, [(i, (i + shift) % count) for i in range(count)])]
    all_gather x3 -> x0, blocking collectives: 74.2 us -> none  [the longest x1 24.9 us: body(): lax.all_gather(dec_keyval, 'tok', axis=0, tiled=True)]
    unnamed x31 -> x92, local copies, waits for them, and re-layouts: 8.76 us -> 33.4 us
    unnamed x1 -> x0, blocking collectives: 15.3 us -> none
    all_gather x1 -> x0, waiting for transfers between devices: 12.7 us -> none  [body(): columns = lax.all_gather(stacked, 'kv', axis=1, tiled=True)]
    dot_general x2 -> x8, matrix products: 9.51 us -> 19.8 us  [project(): piece = jnp.dot(part, block, preferred_element_type=jnp.float32)]
  transfers between devices with their start and end apart: 3 -> 70, of which waited for: 1 -> 62; matrix products, arithmetic and copies ran while one was open for 11% -> 13% of each run, Pallas kernels for 0% -> 0%
where the time goes in v1:
time: 490 us; the launch traced here: 481 us
  waiting for transfers between devices  203 us (41%)
  starting transfers between devices  178 us (36%)
  local copies, waits for them, and re-layouts  41.8 us (9%)
  matrix products  37.5 us (8%)
  other arithmetic  18.8 us (4%)
    ppermute x68, waiting for transfers between devices, fan(): lax.ppermute(value, axis, [(i, (i + shift) % count) for i in range(count)])  203 us
    ppermute x68, starting transfers between devices, fan(): lax.ppermute(value, axis, [(i, (i + shift) % count) for i in range(count)])  177 us
    unnamed x92, local copies, waits for them, and re-layouts  33.4 us
    dot_general x8, matrix products, project(): piece = jnp.dot(part, block, preferred_element_type=jnp.float32)  19.8 us
    dot_general x2, matrix products, head_scores(): jnp.einsum('ngd,md->ngm', shaped, key_rows, preferred_element_type=jnp.fl...  9.85 us
  transfers between devices with their start and end apart: 70, of which 62 were waited for; matrix products, arithmetic and copies ran while one was open for 13% of the time, Pallas kernels for 0%

profile of v1, /device:TPU:1, one launch (start us, length us, event | category | flops | bytes accessed | tf_op | source)
XLA Modules:
  0.0 481.4 jit_solution(8037972605733571696)
XLA Ops:
  0.7 6.4 %copy.147 = bf16[2,12288,128]{2,1,0:T(8,128)(2,1)} copy(bf16[2,12288,128]{2,1,0:T(8,128)(2,1)} %param.17) | data formatting | bytes 12582912
  7.1 10.6 %collective-permute-start.2 = (bf16[16,1280]{1,0:T(8,128)(2,1)S(1)}, bf16[16,1280]{1,0:T(8,128)(2,1)S(1)}, u32[]{:S(2)}, u32[]{:S(2)}) collective-permute-start(bf16[16,1280]{1,0:T(8,128)(2,1)S(1)} %copy-done.2), channel_id=1, source_target_pairs={{0,96},{32,0},{64,32},{96,64},{1,97},{33,1},{65,33},{97,65},{2,98}... | collective-permute-start | bytes 122888 | tf_op jit(solution)/shard_map/ppermute | solution.py:71
  17.7 2.9 collective-permute-start.1
  20.9 9.0 %collective-permute-start.67 = (bf16[256,1280]{1,0:T(8,128)(2,1)}, bf16[256,1280]{1,0:T(8,128)(2,1)}, u32[]{:S(2)}, u32[]{:S(2)}) collective-permute-start(bf16[256,1280]{1,0:T(8,128)(2,1)} %param.12), channel_id=1, source_target_pairs={{0,96},{32,0},{64,32},{96,64},{1,97},{33,1},{65,33},{97,65},{2,98}... | collective-permute-start | bytes 1966088 | tf_op jit(solution)/shard_map/ppermute | solution.py:71
  29.8 2.9 collective-permute-start.66
  34.6 6.5 %constant_dynamic-update-slice_fusion = bf16[5120,896]{1,0:T(8,128)(2,1)} fusion(bf16[5120,640]{1,0:T(8,128)(2,1)} %param.13), kind=kLoop, calls=%fused_computation.82 | loop fusion | bytes 13107200
  45.1 3.6 fusion.22
  63.2 4.9 %collective-permute-done.4 = bf16[16,1024]{1,0:T(8,128)(2,1)S(1)} collective-permute-done((bf16[16,1024]{1,0:T(8,128)(2,1)S(1)}, bf16[16,1024]{1,0:T(8,128)(2,1)S(1)}, u32[]{:S(2)}, u32[]{:S(2)}) %collective-permute-start.4) | collective-permute-done | bytes 32800 | tf_op jit(solution)/shard_map/ppermute | solution.py:71
  69.8 5.7 %collective-permute-done.5 = bf16[16,1024]{1,0:T(8,128)(2,1)S(1)} collective-permute-done((bf16[16,1024]{1,0:T(8,128)(2,1)S(1)}, bf16[16,1024]{1,0:T(8,128)(2,1)S(1)}, u32[]{:S(2)}, u32[]{:S(2)}) %collective-permute-start.5) | collective-permute-done | bytes 32800 | tf_op jit(solution)/shard_map/ppermute | solution.py:71
  76.3 5.5 %collective-permute-done.6 = bf16[16,1024]{1,0:T(8,128)(2,1)S(1)} collective-permute-done((bf16[16,1024]{1,0:T(8,128)(2,1)S(1)}, bf16[16,1024]{1,0:T(8,128)(2,1)S(1)}, u32[]{:S(2)}, u32[]{:S(2)}) %collective-permute-start.6) | collective-permute-done | bytes 32800 | tf_op jit(solution)/shard_map/ppermute | solution.py:71
  82.3 7.6 %collective-permute-done.7 = bf16[16,1024]{1,0:T(8,128)(2,1)S(1)} collective-permute-done((bf16[16,1024]{1,0:T(8,128)(2,1)S(1)}, bf16[16,1024]{1,0:T(8,128)(2,1)S(1)}, u32[]{:S(2)}, u32[]{:S(2)}) %collective-permute-start.7) | collective-permute-done | bytes 32800 | tf_op jit(solution)/shard_map/ppermute | solution.py:71
  89.9 4.9 %collective-permute-done.8 = bf16[16,1024]{1,0:T(8,128)(2,1)S(1)} collective-permute-done((bf16[16,1024]{1,0:T(8,128)(2,1)S(1)}, bf16[16,1024]{1,0:T(8,128)(2,1)S(1)}, u32[]{:S(2)}, u32[]{:S(2)}) %collective-permute-start.8) | collective-permute-done | bytes 32800 | tf_op jit(solution)/shard_map/ppermute | solution.py:71
  94.8 6.6 %collective-permute-done.9 = bf16[16,1024]{1,0:T(8,128)(2,1)S(1)} collective-permute-done((bf16[16,1024]{1,0:T(8,128)(2,1)S(1)}, bf16[16,1024]{1,0:T(8,128)(2,1)S(1)}, u32[]{:S(2)}, u32[]{:S(2)}) %collective-permute-start.9) | collective-permute-done | bytes 32800 | tf_op jit(solution)/shard_map/ppermute | solution.py:71
  101.4 4.0 collective-permute-done.10
  105.4 5.7 %collective-permute-done.11 = bf16[16,1024]{1,0:T(8,128)(2,1)S(1)} collective-permute-done((bf16[16,1024]{1,0:T(8,128)(2,1)S(1)}, bf16[16,1024]{1,0:T(8,128)(2,1)S(1)}, u32[]{:S(2)}, u32[]{:S(2)}) %collective-permute-start.11) | collective-permute-done | bytes 32800 | tf_op jit(solution)/shard_map/ppermute | solution.py:71
  111.1 6.4 %collective-permute-done.12 = bf16[16,1024]{1,0:T(8,128)(2,1)S(1)} collective-permute-done((bf16[16,1024]{1,0:T(8,128)(2,1)S(1)}, bf16[16,1024]{1,0:T(8,128)(2,1)S(1)}, u32[]{:S(2)}, u32[]{:S(2)}) %collective-permute-start.12) | collective-permute-done | bytes 32800 | tf_op jit(solution)/shard_map/ppermute | solution.py:71
  117.4 8.1 %collective-permute-done.13 = bf16[16,1024]{1,0:T(8,128)(2,1)S(1)} collective-permute-done((bf16[16,1024]{1,0:T(8,128)(2,1)S(1)}, bf16[16,1024]{1,0:T(8,128)(2,1)S(1)}, u32[]{:S(2)}, u32[]{:S(2)}) %collective-permute-start.13) | collective-permute-done | bytes 32800 | tf_op jit(solution)/shard_map/ppermute | solution.py:71
  128.0 4.3 collective-permute-done.14
  133.1 7.6 %collective-permute-done.15 = bf16[16,1024]{1,0:T(8,128)(2,1)S(1)} collective-permute-done((bf16[16,1024]{1,0:T(8,128)(2,1)S(1)}, bf16[16,1024]{1,0:T(8,128)(2,1)S(1)}, u32[]{:S(2)}, u32[]{:S(2)}) %collective-permute-start.15) | collective-permute-done | bytes 32800 | tf_op jit(solution)/shard_map/ppermute | solution.py:71
  140.8 5.2 %collective-permute-done.16 = bf16[16,1024]{1,0:T(8,128)(2,1)S(1)} collective-permute-done((bf16[16,1024]{1,0:T(8,128)(2,1)S(1)}, bf16[16,1024]{1,0:T(8,128)(2,1)S(1)}, u32[]{:S(2)}, u32[]{:S(2)}) %collective-permute-start.16) | collective-permute-done | bytes 32800 | tf_op jit(solution)/shard_map/ppermute | solution.py:71
  148.1 4.8 collective-permute-done.17
  152.9 3.0 collective-permute-start.18
  157.1 4.7 collective-permute-start.19
  164.9 3.4 collective-permute-done.20
  168.3 5.4 %collective-permute-start.21 = (bf16[16,1024]{1,0:T(8,128)(2,1)S(1)}, bf16[16,1024]{1,0:T(8,128)(2,1)S(1)}, u32[]{:S(2)}, u32[]{:S(2)}) collective-permute-start(bf16[16,1024]{1,0:T(8,128)(2,1)S(1)} %get-tuple-element.23), channel_id=1, source_target_pairs={{0,19},{1,20},{2,21},{3,22},{4,23},{5,24},{6,25},{7,26},{8,27},{9,... | collective-permute-start | bytes 98312 | tf_op jit(solution)/shard_map/ppermute | solution.py:71
  177.3 3.1 collective-permute-done.22
  180.4 7.1 %collective-permute-start.23 = (bf16[16,1024]{1,0:T(8,128)(2,1)S(1)}, bf16[16,1024]{1,0:T(8,128)(2,1)S(1)}, u32[]{:S(2)}, u32[]{:S(2)}) collective-permute-start(bf16[16,1024]{1,0:T(8,128)(2,1)S(1)} %get-tuple-element.23), channel_id=1, source_target_pairs={{0,21},{1,22},{2,23},{3,24},{4,25},{5,26},{6,27},{7,28},{8,29},{9,... | collective-permute-start | bytes 98312 | tf_op jit(solution)/shard_map/ppermute | solution.py:71
  193.1 8.4 %collective-permute-start.25 = (bf16[16,1024]{1,0:T(8,128)(2,1)S(1)}, bf16[16,1024]{1,0:T(8,128)(2,1)S(1)}, u32[]{:S(2)}, u32[]{:S(2)}) collective-permute-start(bf16[16,1024]{1,0:T(8,128)(2,1)S(1)} %get-tuple-element.23), channel_id=1, source_target_pairs={{0,23},{1,24},{2,25},{3,26},{4,27},{5,28},{6,29},{7,30},{8,31},{9,... | collective-permute-start | bytes 98312 | tf_op jit(solution)/shard_map/ppermute | solution.py:71
  202.5 2.8 collective-permute-done.26
  208.7 3.2 collective-permute-start.28
  213.8 7.5 %collective-permute-start.29 = (bf16[16,1024]{1,0:T(8,128)(2,1)S(1)}, bf16[16,1024]{1,0:T(8,128)(2,1)S(1)}, u32[]{:S(2)}, u32[]{:S(2)}) collective-permute-start(bf16[16,1024]{1,0:T(8,128)(2,1)S(1)} %get-tuple-element.23), channel_id=1, source_target_pairs={{0,27},{1,28},{2,29},{3,30},{4,31},{5,0},{6,1},{7,2},{8,3},{9,4},{... | collective-permute-start | bytes 98312 | tf_op jit(solution)/shard_map/ppermute | solution.py:71
  222.3 3.9 collective-permute-start.30
  227.3 11.1 %collective-permute-start.31 = (bf16[16,1024]{1,0:T(8,128)(2,1)S(1)}, bf16[16,1024]{1,0:T(8,128)(2,1)S(1)}, u32[]{:S(2)}, u32[]{:S(2)}) collective-permute-start(bf16[16,1024]{1,0:T(8,128)(2,1)S(1)} %get-tuple-element.23), channel_id=1, source_target_pairs={{0,29},{1,30},{2,31},{3,0},{4,1},{5,2},{6,3},{7,4},{8,5},{9,6},{10... | collective-permute-start | bytes 98312 | tf_op jit(solution)/shard_map/ppermute | solution.py:71
  239.4 2.8 collective-permute-done.32
  242.1 4.9 %collective-permute-start.33 = (bf16[16,1024]{1,0:T(8,128)(2,1)S(1)}, bf16[16,1024]{1,0:T(8,128)(2,1)S(1)}, u32[]{:S(2)}, u32[]{:S(2)}) collective-permute-start(bf16[16,1024]{1,0:T(8,128)(2,1)S(1)} %get-tuple-element.23), channel_id=1, source_target_pairs={{0,31},{1,0},{2,1},{3,2},{4,3},{5,4},{6,5},{7,6},{8,7},{9,8},{10,9... | collective-permute-start | bytes 98312 | tf_op jit(solution)/shard_map/ppermute | solution.py:71
  251.2 3.4 fusion.136
  260.0 5.9 %collective-permute-done.35 = bf16[16,640]{1,0:T(8,128)(2,1)S(1)} collective-permute-done((bf16[16,640]{1,0:T(8,128)(2,1)S(1)}, bf16[16,640]{1,0:T(8,128)(2,1)S(1)}, u32[]{:S(2)}, u32[]{:S(2)}) %collective-permute-start.35) | collective-permute-done | bytes 20512 | tf_op jit(solution)/shard_map/ppermute | solution.py:71
  266.5 6.6 %collective-permute-done.36 = bf16[16,640]{1,0:T(8,128)(2,1)S(1)} collective-permute-done((bf16[16,640]{1,0:T(8,128)(2,1)S(1)}, bf16[16,640]{1,0:T(8,128)(2,1)S(1)}, u32[]{:S(2)}, u32[]{:S(2)}) %collective-permute-start.36) | collective-permute-done | bytes 20512 | tf_op jit(solution)/shard_map/ppermute | solution.py:71
  273.8 5.6 %collective-permute-done.37 = bf16[16,640]{1,0:T(8,128)(2,1)S(1)} collective-permute-done((bf16[16,640]{1,0:T(8,128)(2,1)S(1)}, bf16[16,640]{1,0:T(8,128)(2,1)S(1)}, u32[]{:S(2)}, u32[]{:S(2)}) %collective-permute-start.37) | collective-permute-done | bytes 20512 | tf_op jit(solution)/shard_map/ppermute | solution.py:71
  280.9 6.9 %collective-permute-done.38 = bf16[16,640]{1,0:T(8,128)(2,1)S(1)} collective-permute-done((bf16[16,640]{1,0:T(8,128)(2,1)S(1)}, bf16[16,640]{1,0:T(8,128)(2,1)S(1)}, u32[]{:S(2)}, u32[]{:S(2)}) %collective-permute-start.38) | collective-permute-done | bytes 20512 | tf_op jit(solution)/shard_map/ppermute | solution.py:71
  288.4 4.1 collective-permute-done.39
  293.1 5.9 %collective-permute-done.40 = bf16[16,640]{1,0:T(8,128)(2,1)S(1)} collective-permute-done((bf16[16,640]{1,0:T(8,128)(2,1)S(1)}, bf16[16,640]{1,0:T(8,128)(2,1)S(1)}, u32[]{:S(2)}, u32[]{:S(2)}) %collective-permute-start.40) | collective-permute-done | bytes 20512 | tf_op jit(solution)/shard_map/ppermute | solution.py:71
  299.6 3.2 collective-permute-done.41
  303.4 5.0 %collective-permute-done.42 = bf16[16,640]{1,0:T(8,128)(2,1)S(1)} collective-permute-done((bf16[16,640]{1,0:T(8,128)(2,1)S(1)}, bf16[16,640]{1,0:T(8,128)(2,1)S(1)}, u32[]{:S(2)}, u32[]{:S(2)}) %collective-permute-start.42) | collective-permute-done | bytes 20512 | tf_op jit(solution)/shard_map/ppermute | solution.py:71
  309.0 5.6 %collective-permute-done.43 = bf16[16,640]{1,0:T(8,128)(2,1)S(1)} collective-permute-done((bf16[16,640]{1,0:T(8,128)(2,1)S(1)}, bf16[16,640]{1,0:T(8,128)(2,1)S(1)}, u32[]{:S(2)}, u32[]{:S(2)}) %collective-permute-start.43) | collective-permute-done | bytes 20512 | tf_op jit(solution)/shard_map/ppermute | solution.py:71
  315.2 7.4 %collective-permute-done.44 = bf16[16,640]{1,0:T(8,128)(2,1)S(1)} collective-permute-done((bf16[16,640]{1,0:T(8,128)(2,1)S(1)}, bf16[16,640]{1,0:T(8,128)(2,1)S(1)}, u32[]{:S(2)}, u32[]{:S(2)}) %collective-permute-start.44) | collective-permute-done | bytes 20512 | tf_op jit(solution)/shard_map/ppermute | solution.py:71
  325.6 3.5 collective-permute-done.45
  330.6 6.8 %collective-permute-done.46 = bf16[16,640]{1,0:T(8,128)(2,1)S(1)} collective-permute-done((bf16[16,640]{1,0:T(8,128)(2,1)S(1)}, bf16[16,640]{1,0:T(8,128)(2,1)S(1)}, u32[]{:S(2)}, u32[]{:S(2)}) %collective-permute-start.46) | collective-permute-done | bytes 20512 | tf_op jit(solution)/shard_map/ppermute | solution.py:71
  338.0 4.4 collective-permute-done.47
  345.1 4.1 collective-permute-done.48
  349.2 3.0 collective-permute-start.49
  353.3 4.6 collective-permute-start.50
  361.5 2.7 collective-permute-done.51
  364.2 5.3 %collective-permute-start.52 = (bf16[16,640]{1,0:T(8,128)(2,1)S(1)}, bf16[16,640]{1,0:T(8,128)(2,1)S(1)}, u32[]{:S(2)}, u32[]{:S(2)}) collective-permute-start(bf16[16,640]{1,0:T(8,128)(2,1)S(1)} %bitcast.103), channel_id=1, source_target_pairs={{0,19},{1,20},{2,21},{3,22},{4,23},{5,24},{6,25},{7,26},{8,27},{9,... | collective-permute-start | bytes 61448 | tf_op jit(solution)/shard_map/ppermute | solution.py:71
  376.0 7.1 %collective-permute-start.54 = (bf16[16,640]{1,0:T(8,128)(2,1)S(1)}, bf16[16,640]{1,0:T(8,128)(2,1)S(1)}, u32[]{:S(2)}, u32[]{:S(2)}) collective-permute-start(bf16[16,640]{1,0:T(8,128)(2,1)S(1)} %bitcast.105), channel_id=1, source_target_pairs={{0,21},{1,22},{2,23},{3,24},{4,25},{5,26},{6,27},{7,28},{8,29},{9,... | collective-permute-start | bytes 61448 | tf_op jit(solution)/shard_map/ppermute | solution.py:71
  388.3 8.5 %collective-permute-start.56 = (bf16[16,640]{1,0:T(8,128)(2,1)S(1)}, bf16[16,640]{1,0:T(8,128)(2,1)S(1)}, u32[]{:S(2)}, u32[]{:S(2)}) collective-permute-start(bf16[16,640]{1,0:T(8,128)(2,1)S(1)} %bitcast.107), channel_id=1, source_target_pairs={{0,23},{1,24},{2,25},{3,26},{4,27},{5,28},{6,29},{7,30},{8,31},{9,... | collective-permute-start | bytes 61448 | tf_op jit(solution)/shard_map/ppermute | solution.py:71
  403.6 3.2 collective-permute-start.59
  408.5 7.5 %collective-permute-start.60 = (bf16[16,640]{1,0:T(8,128)(2,1)S(1)}, bf16[16,640]{1,0:T(8,128)(2,1)S(1)}, u32[]{:S(2)}, u32[]{:S(2)}) collective-permute-start(bf16[16,640]{1,0:T(8,128)(2,1)S(1)} %bitcast.111), channel_id=1, source_target_pairs={{0,27},{1,28},{2,29},{3,30},{4,31},{5,0},{6,1},{7,2},{8,3},{9,4},{... | collective-permute-start | bytes 61448 | tf_op jit(solution)/shard_map/ppermute | solution.py:71
  416.9 3.6 collective-permute-start.61
  421.4 11.1 %collective-permute-start.62 = (bf16[16,640]{1,0:T(8,128)(2,1)S(1)}, bf16[16,640]{1,0:T(8,128)(2,1)S(1)}, u32[]{:S(2)}, u32[]{:S(2)}) collective-permute-start(bf16[16,640]{1,0:T(8,128)(2,1)S(1)} %bitcast.113), channel_id=1, source_target_pairs={{0,29},{1,30},{2,31},{3,0},{4,1},{5,2},{6,3},{7,4},{8,5},{9,6},{10... | collective-permute-start | bytes 61448 | tf_op jit(solution)/shard_map/ppermute | solution.py:71
  436.1 5.0 %collective-permute-start.64 = (bf16[16,640]{1,0:T(8,128)(2,1)S(1)}, bf16[16,640]{1,0:T(8,128)(2,1)S(1)}, u32[]{:S(2)}, u32[]{:S(2)}) collective-permute-start(bf16[16,640]{1,0:T(8,128)(2,1)S(1)} %bitcast.115), channel_id=1, source_target_pairs={{0,31},{1,0},{2,1},{3,2},{4,3},{5,4},{6,5},{7,6},{8,7},{9,8},{10,9... | collective-permute-start | bytes 61448 | tf_op jit(solution)/shard_map/ppermute | solution.py:71
  458.5 6.5 %fusion.1 = (f32[256,5]{0,1:T(8,128)S(1)}, f32[256,5,2560]{2,0,1:T(8,128)}) fusion(pred[256,2560]{1,0:T(8,128)(4,1)S(1)} %compare_and_fusion, bf16[2,2048,128]{2,1,0:T(8,128)(2,1)S(1)} %maximum_select_fusion, bf16[2,512,128]{2,1,0:T(8,128)(2,1)S(1)} %maximum_select_fusion.1, bf16[256,5,64]{2,0,1:T(8,128)(2,1)S(1)} %get-tuple-element.27, ...), kind=kOutput, calls=%fused_computation.7 | convolution fusion | flops 850656000 | bytes 15406080 | tf_op jit(solution)/shard_map/ngd,md->ngm/dot_general | solution.py:34
  464.9 8.4 %fusion.2 = f32[256,5]{0,1:T(8,128)S(1)} fusion(f32[256,5,2560]{2,0,1:T(8,128)} %get-tuple-element.52, f32[256,5]{0,1:T(8,128)S(1)} %get-tuple-element.51, pred[256,2560]{1,0:T(8,128)(4,1)S(1)} %compare_and_fusion), kind=kLoop, calls=%fused_computation.8 | loop fusion | flops 13105920 | bytes 13772800 | tf_op jit(solution)/shard_map/reduce_sum | solution.py:41
  473.4 7.0 %fusion.73 = bf16[256,5,128]{0,2,1:T(8,128)(2,1)S(1)} fusion(f32[256,5,2560]{2,0,1:T(8,128)} %get-tuple-element.52, f32[256,5]{0,1:T(8,128)S(1)} %get-tuple-element.51, pred[256,2560]{1,0:T(8,128)(4,1)S(1)} %compare_and_fusion, bf16[2,512,128]{2,1,0:T(8,128)(2,1)S(1)} %maximum_select_fusion.1, bf16[2,2048,128]{2,1,0:T(8,128)(2,1)S(1)} %maximum_select_fusion, ...), kind=kOutput, calls=%fused_computation.55 | convolution fusion | flops 853606400 | bytes 15411200 | tf_op jit(solution)/shard_map/ngm,md->ngd/dot_general | solution.py:43
  (243 shorter events, 123.0 us)
Async XLA Ops:
  7.1 45.1 %collective-permute-start.2 = (bf16[16,1280]{1,0:T(8,128)(2,1)S(1)}, bf16[16,1280]{1,0:T(8,128)(2,1)S(1)}, u32[]{:S(2)}, u32[]{:S(2)}) collective-permute-start(bf16[16,1280]{1,0:T(8,128)(2,1)S(1)} %copy-done.2), channel_id=1, source_target_pairs={{0,96},{32,0},{64,32},{96,64},{1,97},{33,1},{65,33},{97,65},{2,98}... | collective-permute-start | bytes 122888 | tf_op jit(solution)/shard_map/ppermute | solution.py:71
  17.7 36.9 %collective-permute-start.1 = (bf16[16,1280]{1,0:T(8,128)(2,1)S(1)}, bf16[16,1280]{1,0:T(8,128)(2,1)S(1)}, u32[]{:S(2)}, u32[]{:S(2)}) collective-permute-start(bf16[16,1280]{1,0:T(8,128)(2,1)S(1)} %copy-done.2), channel_id=1, source_target_pairs={{0,64},{32,96},{64,0},{96,32},{1,65},{33,97},{65,1},{97,33},{2,66}... | collective-permute-start | bytes 122888 | tf_op jit(solution)/shard_map/ppermute | solution.py:71
  20.6 37.1 %collective-permute-start = (bf16[16,1280]{1,0:T(8,128)(2,1)S(1)}, bf16[16,1280]{1,0:T(8,128)(2,1)S(1)}, u32[]{:S(2)}, u32[]{:S(2)}) collective-permute-start(bf16[16,1280]{1,0:T(8,128)(2,1)S(1)} %copy-done.2), channel_id=1, source_target_pairs={{0,32},{32,64},{64,96},{96,0},{1,33},{33,65},{65,97},{97,1},{2,34}... | collective-permute-start | bytes 122888 | tf_op jit(solution)/shard_map/ppermute | solution.py:71
  20.9 424.4 %collective-permute-start.67 = (bf16[256,1280]{1,0:T(8,128)(2,1)}, bf16[256,1280]{1,0:T(8,128)(2,1)}, u32[]{:S(2)}, u32[]{:S(2)}) collective-permute-start(bf16[256,1280]{1,0:T(8,128)(2,1)} %param.12), channel_id=1, source_target_pairs={{0,96},{32,0},{64,32},{96,64},{1,97},{33,1},{65,33},{97,65},{2,98}... | collective-permute-start | bytes 1966088 | tf_op jit(solution)/shard_map/ppermute | solution.py:71
  29.8 418.1 %collective-permute-start.66 = (bf16[256,1280]{1,0:T(8,128)(2,1)}, bf16[256,1280]{1,0:T(8,128)(2,1)}, u32[]{:S(2)}, u32[]{:S(2)}) collective-permute-start(bf16[256,1280]{1,0:T(8,128)(2,1)} %param.12), channel_id=1, source_target_pairs={{0,64},{32,96},{64,0},{96,32},{1,65},{33,97},{65,1},{97,33},{2,66}... | collective-permute-start | bytes 1966088 | tf_op jit(solution)/shard_map/ppermute | solution.py:71
  52.2 398.4 %collective-permute-start.65 = (bf16[256,1280]{1,0:T(8,128)(2,1)}, bf16[256,1280]{1,0:T(8,128)(2,1)}, u32[]{:S(2)}, u32[]{:S(2)}) collective-permute-start(bf16[256,1280]{1,0:T(8,128)(2,1)} %param.12), channel_id=1, source_target_pairs={{0,32},{32,64},{64,96},{96,0},{1,33},{33,65},{65,97},{97,1},{2,34}... | collective-permute-start | bytes 1966088 | tf_op jit(solution)/shard_map/ppermute | solution.py:71
  54.6 390.4 %collective-permute-start.68 = (bf16[2,1024,128]{2,1,0:T(8,128)(2,1)S(1)}, bf16[2,1024,128]{2,1,0:T(8,128)(2,1)S(1)}, u32[]{:S(2)}, u32[]{:S(2)}) collective-permute-start(bf16[2,1024,128]{2,1,0:T(8,128)(2,1)S(1)} %copy-done.1), channel_id=1, source_target_pairs={{0,1},{1,0},{2,3},{3,2},{4,5},{5,4},{6,7},{7,6},{8,9},{9,8},{10,11... | collective-permute-start | bytes 1572872 | tf_op jit(solution)/shard_map/ppermute | solution.py:13
  62.0 6.1 %collective-permute-start.4 = (bf16[16,1024]{1,0:T(8,128)(2,1)S(1)}, bf16[16,1024]{1,0:T(8,128)(2,1)S(1)}, u32[]{:S(2)}, u32[]{:S(2)}) collective-permute-start(bf16[16,1024]{1,0:T(8,128)(2,1)S(1)} %get-tuple-element.23), channel_id=1, source_target_pairs={{0,2},{1,3},{2,4},{3,5},{4,6},{5,7},{6,8},{7,9},{8,10},{9,11},{10,... | collective-permute-start | bytes 98312 | tf_op jit(solution)/shard_map/ppermute | solution.py:71
  68.1 7.4 %collective-permute-start.5 = (bf16[16,1024]{1,0:T(8,128)(2,1)S(1)}, bf16[16,1024]{1,0:T(8,128)(2,1)S(1)}, u32[]{:S(2)}, u32[]{:S(2)}) collective-permute-start(bf16[16,1024]{1,0:T(8,128)(2,1)S(1)} %get-tuple-element.23), channel_id=1, source_target_pairs={{0,3},{1,4},{2,5},{3,6},{4,7},{5,8},{6,9},{7,10},{8,11},{9,12},{10... | collective-permute-start | bytes 98312 | tf_op jit(solution)/shard_map/ppermute | solution.py:71
  75.4 6.4 %collective-permute-start.6 = (bf16[16,1024]{1,0:T(8,128)(2,1)S(1)}, bf16[16,1024]{1,0:T(8,128)(2,1)S(1)}, u32[]{:S(2)}, u32[]{:S(2)}) collective-permute-start(bf16[16,1024]{1,0:T(8,128)(2,1)S(1)} %get-tuple-element.23), channel_id=1, source_target_pairs={{0,4},{1,5},{2,6},{3,7},{4,8},{5,9},{6,10},{7,11},{8,12},{9,13},{1... | collective-permute-start | bytes 98312 | tf_op jit(solution)/shard_map/ppermute | solution.py:71
  81.8 8.1 %collective-permute-start.7 = (bf16[16,1024]{1,0:T(8,128)(2,1)S(1)}, bf16[16,1024]{1,0:T(8,128)(2,1)S(1)}, u32[]{:S(2)}, u32[]{:S(2)}) collective-permute-start(bf16[16,1024]{1,0:T(8,128)(2,1)S(1)} %get-tuple-element.23), channel_id=1, source_target_pairs={{0,5},{1,6},{2,7},{3,8},{4,9},{5,10},{6,11},{7,12},{8,13},{9,14},{... | collective-permute-start | bytes 98312 | tf_op jit(solution)/shard_map/ppermute | solution.py:71
  89.9 4.9 %collective-permute-start.8 = (bf16[16,1024]{1,0:T(8,128)(2,1)S(1)}, bf16[16,1024]{1,0:T(8,128)(2,1)S(1)}, u32[]{:S(2)}, u32[]{:S(2)}) collective-permute-start(bf16[16,1024]{1,0:T(8,128)(2,1)S(1)} %get-tuple-element.23), channel_id=1, source_target_pairs={{0,6},{1,7},{2,8},{3,9},{4,10},{5,11},{6,12},{7,13},{8,14},{9,15},... | collective-permute-start | bytes 98312 | tf_op jit(solution)/shard_map/ppermute | solution.py:71
  94.8 6.6 %collective-permute-start.9 = (bf16[16,1024]{1,0:T(8,128)(2,1)S(1)}, bf16[16,1024]{1,0:T(8,128)(2,1)S(1)}, u32[]{:S(2)}, u32[]{:S(2)}) collective-permute-start(bf16[16,1024]{1,0:T(8,128)(2,1)S(1)} %get-tuple-element.23), channel_id=1, source_target_pairs={{0,7},{1,8},{2,9},{3,10},{4,11},{5,12},{6,13},{7,14},{8,15},{9,16}... | collective-permute-start | bytes 98312 | tf_op jit(solution)/shard_map/ppermute | solution.py:71
  101.4 4.0 collective-permute-start.10
  105.4 5.7 %collective-permute-start.11 = (bf16[16,1024]{1,0:T(8,128)(2,1)S(1)}, bf16[16,1024]{1,0:T(8,128)(2,1)S(1)}, u32[]{:S(2)}, u32[]{:S(2)}) collective-permute-start(bf16[16,1024]{1,0:T(8,128)(2,1)S(1)} %get-tuple-element.23), channel_id=1, source_target_pairs={{0,9},{1,10},{2,11},{3,12},{4,13},{5,14},{6,15},{7,16},{8,17},{9,1... | collective-permute-start | bytes 98312 | tf_op jit(solution)/shard_map/ppermute | solution.py:71
  111.1 6.4 %collective-permute-start.12 = (bf16[16,1024]{1,0:T(8,128)(2,1)S(1)}, bf16[16,1024]{1,0:T(8,128)(2,1)S(1)}, u32[]{:S(2)}, u32[]{:S(2)}) collective-permute-start(bf16[16,1024]{1,0:T(8,128)(2,1)S(1)} %get-tuple-element.23), channel_id=1, source_target_pairs={{0,10},{1,11},{2,12},{3,13},{4,14},{5,15},{6,16},{7,17},{8,18},{9,... | collective-permute-start | bytes 98312 | tf_op jit(solution)/shard_map/ppermute | solution.py:71
  117.4 8.1 %collective-permute-start.13 = (bf16[16,1024]{1,0:T(8,128)(2,1)S(1)}, bf16[16,1024]{1,0:T(8,128)(2,1)S(1)}, u32[]{:S(2)}, u32[]{:S(2)}) collective-permute-start(bf16[16,1024]{1,0:T(8,128)(2,1)S(1)} %get-tuple-element.23), channel_id=1, source_target_pairs={{0,11},{1,12},{2,13},{3,14},{4,15},{5,16},{6,17},{7,18},{8,19},{9,... | collective-permute-start | bytes 98312 | tf_op jit(solution)/shard_map/ppermute | solution.py:71
  125.5 6.7 %collective-permute-start.14 = (bf16[16,1024]{1,0:T(8,128)(2,1)S(1)}, bf16[16,1024]{1,0:T(8,128)(2,1)S(1)}, u32[]{:S(2)}, u32[]{:S(2)}) collective-permute-start(bf16[16,1024]{1,0:T(8,128)(2,1)S(1)} %get-tuple-element.23), channel_id=1, source_target_pairs={{0,12},{1,13},{2,14},{3,15},{4,16},{5,17},{6,18},{7,19},{8,20},{9,... | collective-permute-start | bytes 98312 | tf_op jit(solution)/shard_map/ppermute | solution.py:71
  132.2 8.4 %collective-permute-start.15 = (bf16[16,1024]{1,0:T(8,128)(2,1)S(1)}, bf16[16,1024]{1,0:T(8,128)(2,1)S(1)}, u32[]{:S(2)}, u32[]{:S(2)}) collective-permute-start(bf16[16,1024]{1,0:T(8,128)(2,1)S(1)} %get-tuple-element.23), channel_id=1, source_target_pairs={{0,13},{1,14},{2,15},{3,16},{4,17},{5,18},{6,19},{7,20},{8,21},{9,... | collective-permute-start | bytes 98312 | tf_op jit(solution)/shard_map/ppermute | solution.py:71
  140.6 5.4 %collective-permute-start.16 = (bf16[16,1024]{1,0:T(8,128)(2,1)S(1)}, bf16[16,1024]{1,0:T(8,128)(2,1)S(1)}, u32[]{:S(2)}, u32[]{:S(2)}) collective-permute-start(bf16[16,1024]{1,0:T(8,128)(2,1)S(1)} %get-tuple-element.23), channel_id=1, source_target_pairs={{0,14},{1,15},{2,16},{3,17},{4,18},{5,19},{6,20},{7,21},{8,22},{9,... | collective-permute-start | bytes 98312 | tf_op jit(solution)/shard_map/ppermute | solution.py:71
  146.0 6.8 %collective-permute-start.17 = (bf16[16,1024]{1,0:T(8,128)(2,1)S(1)}, bf16[16,1024]{1,0:T(8,128)(2,1)S(1)}, u32[]{:S(2)}, u32[]{:S(2)}) collective-permute-start(bf16[16,1024]{1,0:T(8,128)(2,1)S(1)} %get-tuple-element.23), channel_id=1, source_target_pairs={{0,15},{1,16},{2,17},{3,18},{4,19},{5,20},{6,21},{7,22},{8,23},{9,... | collective-permute-start | bytes 98312 | tf_op jit(solution)/shard_map/ppermute | solution.py:71
  152.9 4.3 collective-permute-start.18
  157.1 6.3 %collective-permute-start.19 = (bf16[16,1024]{1,0:T(8,128)(2,1)S(1)}, bf16[16,1024]{1,0:T(8,128)(2,1)S(1)}, u32[]{:S(2)}, u32[]{:S(2)}) collective-permute-start(bf16[16,1024]{1,0:T(8,128)(2,1)S(1)} %get-tuple-element.23), channel_id=1, source_target_pairs={{0,17},{1,18},{2,19},{3,20},{4,21},{5,22},{6,23},{7,24},{8,25},{9,... | collective-permute-start | bytes 98312 | tf_op jit(solution)/shard_map/ppermute | solution.py:71
  163.4 4.9 %collective-permute-start.20 = (bf16[16,1024]{1,0:T(8,128)(2,1)S(1)}, bf16[16,1024]{1,0:T(8,128)(2,1)S(1)}, u32[]{:S(2)}, u32[]{:S(2)}) collective-permute-start(bf16[16,1024]{1,0:T(8,128)(2,1)S(1)} %get-tuple-element.23), channel_id=1, source_target_pairs={{0,18},{1,19},{2,20},{3,21},{4,22},{5,23},{6,24},{7,25},{8,26},{9,... | collective-permute-start | bytes 98312 | tf_op jit(solution)/shard_map/ppermute | solution.py:71
  168.3 6.9 %collective-permute-start.21 = (bf16[16,1024]{1,0:T(8,128)(2,1)S(1)}, bf16[16,1024]{1,0:T(8,128)(2,1)S(1)}, u32[]{:S(2)}, u32[]{:S(2)}) collective-permute-start(bf16[16,1024]{1,0:T(8,128)(2,1)S(1)} %get-tuple-element.23), channel_id=1, source_target_pairs={{0,19},{1,20},{2,21},{3,22},{4,23},{5,24},{6,25},{7,26},{8,27},{9,... | collective-permute-start | bytes 98312 | tf_op jit(solution)/shard_map/ppermute | solution.py:71
  175.2 5.2 %collective-permute-start.22 = (bf16[16,1024]{1,0:T(8,128)(2,1)S(1)}, bf16[16,1024]{1,0:T(8,128)(2,1)S(1)}, u32[]{:S(2)}, u32[]{:S(2)}) collective-permute-start(bf16[16,1024]{1,0:T(8,128)(2,1)S(1)} %get-tuple-element.23), channel_id=1, source_target_pairs={{0,20},{1,21},{2,22},{3,23},{4,24},{5,25},{6,26},{7,27},{8,28},{9,... | collective-permute-start | bytes 98312 | tf_op jit(solution)/shard_map/ppermute | solution.py:71
  180.4 9.0 %collective-permute-start.23 = (bf16[16,1024]{1,0:T(8,128)(2,1)S(1)}, bf16[16,1024]{1,0:T(8,128)(2,1)S(1)}, u32[]{:S(2)}, u32[]{:S(2)}) collective-permute-start(bf16[16,1024]{1,0:T(8,128)(2,1)S(1)} %get-tuple-element.23), channel_id=1, source_target_pairs={{0,21},{1,22},{2,23},{3,24},{4,25},{5,26},{6,27},{7,28},{8,29},{9,... | collective-permute-start | bytes 98312 | tf_op jit(solution)/shard_map/ppermute | solution.py:71
  189.4 3.7 collective-permute-start.24
  193.1 9.4 %collective-permute-start.25 = (bf16[16,1024]{1,0:T(8,128)(2,1)S(1)}, bf16[16,1024]{1,0:T(8,128)(2,1)S(1)}, u32[]{:S(2)}, u32[]{:S(2)}) collective-permute-start(bf16[16,1024]{1,0:T(8,128)(2,1)S(1)} %get-tuple-element.23), channel_id=1, source_target_pairs={{0,23},{1,24},{2,25},{3,26},{4,27},{5,28},{6,29},{7,30},{8,31},{9,... | collective-permute-start | bytes 98312 | tf_op jit(solution)/shard_map/ppermute | solution.py:71
  202.5 2.8 collective-permute-start.26
  205.2 3.5 collective-permute-start.27
  208.7 5.0 %collective-permute-start.28 = (bf16[16,1024]{1,0:T(8,128)(2,1)S(1)}, bf16[16,1024]{1,0:T(8,128)(2,1)S(1)}, u32[]{:S(2)}, u32[]{:S(2)}) collective-permute-start(bf16[16,1024]{1,0:T(8,128)(2,1)S(1)} %get-tuple-element.23), channel_id=1, source_target_pairs={{0,26},{1,27},{2,28},{3,29},{4,30},{5,31},{6,0},{7,1},{8,2},{9,3},... | collective-permute-start | bytes 98312 | tf_op jit(solution)/shard_map/ppermute | solution.py:71
  213.8 8.6 %collective-permute-start.29 = (bf16[16,1024]{1,0:T(8,128)(2,1)S(1)}, bf16[16,1024]{1,0:T(8,128)(2,1)S(1)}, u32[]{:S(2)}, u32[]{:S(2)}) collective-permute-start(bf16[16,1024]{1,0:T(8,128)(2,1)S(1)} %get-tuple-element.23), channel_id=1, source_target_pairs={{0,27},{1,28},{2,29},{3,30},{4,31},{5,0},{6,1},{7,2},{8,3},{9,4},{... | collective-permute-start | bytes 98312 | tf_op jit(solution)/shard_map/ppermute | solution.py:71
  222.3 4.9 %collective-permute-start.30 = (bf16[16,1024]{1,0:T(8,128)(2,1)S(1)}, bf16[16,1024]{1,0:T(8,128)(2,1)S(1)}, u32[]{:S(2)}, u32[]{:S(2)}) collective-permute-start(bf16[16,1024]{1,0:T(8,128)(2,1)S(1)} %get-tuple-element.23), channel_id=1, source_target_pairs={{0,28},{1,29},{2,30},{3,31},{4,0},{5,1},{6,2},{7,3},{8,4},{9,5},{1... | collective-permute-start | bytes 98312 | tf_op jit(solution)/shard_map/ppermute | solution.py:71
  227.3 12.1 %collective-permute-start.31 = (bf16[16,1024]{1,0:T(8,128)(2,1)S(1)}, bf16[16,1024]{1,0:T(8,128)(2,1)S(1)}, u32[]{:S(2)}, u32[]{:S(2)}) collective-permute-start(bf16[16,1024]{1,0:T(8,128)(2,1)S(1)} %get-tuple-element.23), channel_id=1, source_target_pairs={{0,29},{1,30},{2,31},{3,0},{4,1},{5,2},{6,3},{7,4},{8,5},{9,6},{10... | collective-permute-start | bytes 98312 | tf_op jit(solution)/shard_map/ppermute | solution.py:71
  242.1 5.7 %collective-permute-start.33 = (bf16[16,1024]{1,0:T(8,128)(2,1)S(1)}, bf16[16,1024]{1,0:T(8,128)(2,1)S(1)}, u32[]{:S(2)}, u32[]{:S(2)}) collective-permute-start(bf16[16,1024]{1,0:T(8,128)(2,1)S(1)} %get-tuple-element.23), channel_id=1, source_target_pairs={{0,31},{1,0},{2,1},{3,2},{4,3},{5,4},{6,5},{7,6},{8,7},{9,8},{10,9... | collective-permute-start | bytes 98312 | tf_op jit(solution)/shard_map/ppermute | solution.py:71
  259.4 6.5 %collective-permute-start.35 = (bf16[16,640]{1,0:T(8,128)(2,1)S(1)}, bf16[16,640]{1,0:T(8,128)(2,1)S(1)}, u32[]{:S(2)}, u32[]{:S(2)}) collective-permute-start(bf16[16,640]{1,0:T(8,128)(2,1)S(1)} %bitcast.86), channel_id=1, source_target_pairs={{0,2},{1,3},{2,4},{3,5},{4,6},{5,7},{6,8},{7,9},{8,10},{9,11},{10,... | collective-permute-start | bytes 61448 | tf_op jit(solution)/shard_map/ppermute | solution.py:71
  265.9 7.2 %collective-permute-start.36 = (bf16[16,640]{1,0:T(8,128)(2,1)S(1)}, bf16[16,640]{1,0:T(8,128)(2,1)S(1)}, u32[]{:S(2)}, u32[]{:S(2)}) collective-permute-start(bf16[16,640]{1,0:T(8,128)(2,1)S(1)} %bitcast.87), channel_id=1, source_target_pairs={{0,3},{1,4},{2,5},{3,6},{4,7},{5,8},{6,9},{7,10},{8,11},{9,12},{10... | collective-permute-start | bytes 61448 | tf_op jit(solution)/shard_map/ppermute | solution.py:71
  273.2 6.2 %collective-permute-start.37 = (bf16[16,640]{1,0:T(8,128)(2,1)S(1)}, bf16[16,640]{1,0:T(8,128)(2,1)S(1)}, u32[]{:S(2)}, u32[]{:S(2)}) collective-permute-start(bf16[16,640]{1,0:T(8,128)(2,1)S(1)} %bitcast.88), channel_id=1, source_target_pairs={{0,4},{1,5},{2,6},{3,7},{4,8},{5,9},{6,10},{7,11},{8,12},{9,13},{1... | collective-permute-start | bytes 61448 | tf_op jit(solution)/shard_map/ppermute | solution.py:71
  279.4 8.4 %collective-permute-start.38 = (bf16[16,640]{1,0:T(8,128)(2,1)S(1)}, bf16[16,640]{1,0:T(8,128)(2,1)S(1)}, u32[]{:S(2)}, u32[]{:S(2)}) collective-permute-start(bf16[16,640]{1,0:T(8,128)(2,1)S(1)} %bitcast.89), channel_id=1, source_target_pairs={{0,5},{1,6},{2,7},{3,8},{4,9},{5,10},{6,11},{7,12},{8,13},{9,14},{... | collective-permute-start | bytes 61448 | tf_op jit(solution)/shard_map/ppermute | solution.py:71
  287.8 4.7 collective-permute-start.39
  292.5 6.5 %collective-permute-start.40 = (bf16[16,640]{1,0:T(8,128)(2,1)S(1)}, bf16[16,640]{1,0:T(8,128)(2,1)S(1)}, u32[]{:S(2)}, u32[]{:S(2)}) collective-permute-start(bf16[16,640]{1,0:T(8,128)(2,1)S(1)} %bitcast.91), channel_id=1, source_target_pairs={{0,7},{1,8},{2,9},{3,10},{4,11},{5,12},{6,13},{7,14},{8,15},{9,16}... | collective-permute-start | bytes 61448 | tf_op jit(solution)/shard_map/ppermute | solution.py:71
  299.0 3.8 collective-permute-start.41
  302.8 5.6 %collective-permute-start.42 = (bf16[16,640]{1,0:T(8,128)(2,1)S(1)}, bf16[16,640]{1,0:T(8,128)(2,1)S(1)}, u32[]{:S(2)}, u32[]{:S(2)}) collective-permute-start(bf16[16,640]{1,0:T(8,128)(2,1)S(1)} %bitcast.93), channel_id=1, source_target_pairs={{0,9},{1,10},{2,11},{3,12},{4,13},{5,14},{6,15},{7,16},{8,17},{9,1... | collective-permute-start | bytes 61448 | tf_op jit(solution)/shard_map/ppermute | solution.py:71
  308.4 6.2 %collective-permute-start.43 = (bf16[16,640]{1,0:T(8,128)(2,1)S(1)}, bf16[16,640]{1,0:T(8,128)(2,1)S(1)}, u32[]{:S(2)}, u32[]{:S(2)}) collective-permute-start(bf16[16,640]{1,0:T(8,128)(2,1)S(1)} %bitcast.94), channel_id=1, source_target_pairs={{0,10},{1,11},{2,12},{3,13},{4,14},{5,15},{6,16},{7,17},{8,18},{9,... | collective-permute-start | bytes 61448 | tf_op jit(solution)/shard_map/ppermute | solution.py:71
  314.6 8.0 %collective-permute-start.44 = (bf16[16,640]{1,0:T(8,128)(2,1)S(1)}, bf16[16,640]{1,0:T(8,128)(2,1)S(1)}, u32[]{:S(2)}, u32[]{:S(2)}) collective-permute-start(bf16[16,640]{1,0:T(8,128)(2,1)S(1)} %bitcast.95), channel_id=1, source_target_pairs={{0,11},{1,12},{2,13},{3,14},{4,15},{5,16},{6,17},{7,18},{8,19},{9,... | collective-permute-start | bytes 61448 | tf_op jit(solution)/shard_map/ppermute | solution.py:71
  322.6 6.5 %collective-permute-start.45 = (bf16[16,640]{1,0:T(8,128)(2,1)S(1)}, bf16[16,640]{1,0:T(8,128)(2,1)S(1)}, u32[]{:S(2)}, u32[]{:S(2)}) collective-permute-start(bf16[16,640]{1,0:T(8,128)(2,1)S(1)} %bitcast.96), channel_id=1, source_target_pairs={{0,12},{1,13},{2,14},{3,15},{4,16},{5,17},{6,18},{7,19},{8,20},{9,... | collective-permute-start | bytes 61448 | tf_op jit(solution)/shard_map/ppermute | solution.py:71
  329.1 8.3 %collective-permute-start.46 = (bf16[16,640]{1,0:T(8,128)(2,1)S(1)}, bf16[16,640]{1,0:T(8,128)(2,1)S(1)}, u32[]{:S(2)}, u32[]{:S(2)}) collective-permute-start(bf16[16,640]{1,0:T(8,128)(2,1)S(1)} %bitcast.97), channel_id=1, source_target_pairs={{0,13},{1,14},{2,15},{3,16},{4,17},{5,18},{6,19},{7,20},{8,21},{9,... | collective-permute-start | bytes 61448 | tf_op jit(solution)/shard_map/ppermute | solution.py:71
  337.4 5.0 %collective-permute-start.47 = (bf16[16,640]{1,0:T(8,128)(2,1)S(1)}, bf16[16,640]{1,0:T(8,128)(2,1)S(1)}, u32[]{:S(2)}, u32[]{:S(2)}) collective-permute-start(bf16[16,640]{1,0:T(8,128)(2,1)S(1)} %bitcast.98), channel_id=1, source_target_pairs={{0,14},{1,15},{2,16},{3,17},{4,18},{5,19},{6,20},{7,21},{8,22},{9,... | collective-permute-start | bytes 61448 | tf_op jit(solution)/shard_map/ppermute | solution.py:71
  342.4 6.8 %collective-permute-start.48 = (bf16[16,640]{1,0:T(8,128)(2,1)S(1)}, bf16[16,640]{1,0:T(8,128)(2,1)S(1)}, u32[]{:S(2)}, u32[]{:S(2)}) collective-permute-start(bf16[16,640]{1,0:T(8,128)(2,1)S(1)} %bitcast.99), channel_id=1, source_target_pairs={{0,15},{1,16},{2,17},{3,18},{4,19},{5,20},{6,21},{7,22},{8,23},{9,... | collective-permute-start | bytes 61448 | tf_op jit(solution)/shard_map/ppermute | solution.py:71
  349.2 4.1 collective-permute-start.49
  353.3 6.1 %collective-permute-start.50 = (bf16[16,640]{1,0:T(8,128)(2,1)S(1)}, bf16[16,640]{1,0:T(8,128)(2,1)S(1)}, u32[]{:S(2)}, u32[]{:S(2)}) collective-permute-start(bf16[16,640]{1,0:T(8,128)(2,1)S(1)} %bitcast.101), channel_id=1, source_target_pairs={{0,17},{1,18},{2,19},{3,20},{4,21},{5,22},{6,23},{7,24},{8,25},{9,... | collective-permute-start | bytes 61448 | tf_op jit(solution)/shard_map/ppermute | solution.py:71
  359.5 4.7 collective-permute-start.51
  364.2 6.8 %collective-permute-start.52 = (bf16[16,640]{1,0:T(8,128)(2,1)S(1)}, bf16[16,640]{1,0:T(8,128)(2,1)S(1)}, u32[]{:S(2)}, u32[]{:S(2)}) collective-permute-start(bf16[16,640]{1,0:T(8,128)(2,1)S(1)} %bitcast.103), channel_id=1, source_target_pairs={{0,19},{1,20},{2,21},{3,22},{4,23},{5,24},{6,25},{7,26},{8,27},{9,... | collective-permute-start | bytes 61448 | tf_op jit(solution)/shard_map/ppermute | solution.py:71
  371.0 5.0 %collective-permute-start.53 = (bf16[16,640]{1,0:T(8,128)(2,1)S(1)}, bf16[16,640]{1,0:T(8,128)(2,1)S(1)}, u32[]{:S(2)}, u32[]{:S(2)}) collective-permute-start(bf16[16,640]{1,0:T(8,128)(2,1)S(1)} %bitcast.104), channel_id=1, source_target_pairs={{0,20},{1,21},{2,22},{3,23},{4,24},{5,25},{6,26},{7,27},{8,28},{9,... | collective-permute-start | bytes 61448 | tf_op jit(solution)/shard_map/ppermute | solution.py:71
  376.0 8.7 %collective-permute-start.54 = (bf16[16,640]{1,0:T(8,128)(2,1)S(1)}, bf16[16,640]{1,0:T(8,128)(2,1)S(1)}, u32[]{:S(2)}, u32[]{:S(2)}) collective-permute-start(bf16[16,640]{1,0:T(8,128)(2,1)S(1)} %bitcast.105), channel_id=1, source_target_pairs={{0,21},{1,22},{2,23},{3,24},{4,25},{5,26},{6,27},{7,28},{8,29},{9,... | collective-permute-start | bytes 61448 | tf_op jit(solution)/shard_map/ppermute | solution.py:71
  384.7 3.5 collective-permute-start.55
  388.3 9.4 %collective-permute-start.56 = (bf16[16,640]{1,0:T(8,128)(2,1)S(1)}, bf16[16,640]{1,0:T(8,128)(2,1)S(1)}, u32[]{:S(2)}, u32[]{:S(2)}) collective-permute-start(bf16[16,640]{1,0:T(8,128)(2,1)S(1)} %bitcast.107), channel_id=1, source_target_pairs={{0,23},{1,24},{2,25},{3,26},{4,27},{5,28},{6,29},{7,30},{8,31},{9,... | collective-permute-start | bytes 61448 | tf_op jit(solution)/shard_map/ppermute | solution.py:71
  400.3 3.3 collective-permute-start.58
  403.6 4.8 %collective-permute-start.59 = (bf16[16,640]{1,0:T(8,128)(2,1)S(1)}, bf16[16,640]{1,0:T(8,128)(2,1)S(1)}, u32[]{:S(2)}, u32[]{:S(2)}) collective-permute-start(bf16[16,640]{1,0:T(8,128)(2,1)S(1)} %bitcast.110), channel_id=1, source_target_pairs={{0,26},{1,27},{2,28},{3,29},{4,30},{5,31},{6,0},{7,1},{8,2},{9,3},... | collective-permute-start | bytes 61448 | tf_op jit(solution)/shard_map/ppermute | solution.py:71
  408.5 8.5 %collective-permute-start.60 = (bf16[16,640]{1,0:T(8,128)(2,1)S(1)}, bf16[16,640]{1,0:T(8,128)(2,1)S(1)}, u32[]{:S(2)}, u32[]{:S(2)}) collective-permute-start(bf16[16,640]{1,0:T(8,128)(2,1)S(1)} %bitcast.111), channel_id=1, source_target_pairs={{0,27},{1,28},{2,29},{3,30},{4,31},{5,0},{6,1},{7,2},{8,3},{9,4},{... | collective-permute-start | bytes 61448 | tf_op jit(solution)/shard_map/ppermute | solution.py:71
  416.9 4.5 collective-permute-start.61
  421.4 12.0 %collective-permute-start.62 = (bf16[16,640]{1,0:T(8,128)(2,1)S(1)}, bf16[16,640]{1,0:T(8,128)(2,1)S(1)}, u32[]{:S(2)}, u32[]{:S(2)}) collective-permute-start(bf16[16,640]{1,0:T(8,128)(2,1)S(1)} %bitcast.113), channel_id=1, source_target_pairs={{0,29},{1,30},{2,31},{3,0},{4,1},{5,2},{6,3},{7,4},{8,5},{9,6},{10... | collective-permute-start | bytes 61448 | tf_op jit(solution)/shard_map/ppermute | solution.py:71
  436.1 5.9 %collective-permute-start.64 = (bf16[16,640]{1,0:T(8,128)(2,1)S(1)}, bf16[16,640]{1,0:T(8,128)(2,1)S(1)}, u32[]{:S(2)}, u32[]{:S(2)}) collective-permute-start(bf16[16,640]{1,0:T(8,128)(2,1)S(1)} %bitcast.115), channel_id=1, source_target_pairs={{0,31},{1,0},{2,1},{3,2},{4,3},{5,4},{6,5},{7,6},{8,7},{9,8},{10,9... | collective-permute-start | bytes 61448 | tf_op jit(solution)/shard_map/ppermute | solution.py:71
  (17 other events, 106.1 us)

commit v2 on v1

--- a/solution.py
+++ b/solution.py
@@ -64,25 +64,34 @@
     return (result, cache_pool)
 
 
-def fan(value, axis):
-    count = lax.axis_size(axis)
-    parts = [value]
-    for shift in range(1, count):
-        parts.append(lax.ppermute(value, axis, [(i, (i + shift) % count) for i in range(count)]))
-    return parts
+def tree_gather(value):
+    place = lax.axis_index("tok")
+    buffer = value
+    for stride, count in ((1, 2), (2, 4), (8, 4)):
+        parts = [buffer]
+        for shift in range(1, count):
+            pairs = []
+            for i in range(32):
+                digit = (i // stride) % count
+                target = i + (((digit + shift) % count) - digit) * stride
+                pairs.append((i, target))
+            parts.append(lax.ppermute(buffer, "tok", pairs))
+        buffer = jnp.concatenate(parts, axis=0)
+    return buffer
 
 
-def project(rows, weight, bias):
-    parts = fan(rows, "kv")
-    place = lax.axis_index("kv")
-    width = rows.shape[1]
-    total = None
-    for shift, part in enumerate(parts):
-        source = (place - shift) % len(parts)
-        block = lax.dynamic_slice_in_dim(weight, source * width, width, axis=0)
-        piece = jnp.dot(part, block, preferred_element_type=jnp.float32)
-        total = piece if total is None else total + piece
-    return total + bias
+def tree_row(place, source, rows):
+    core = (place % 2) ^ (source % 2)
+    y = ((place // 2) % 4 - (source // 2) % 4) % 4
+    z = (place // 8 - source // 8) % 4
+    return ((z * 4 + y) * 2 + core) * rows
+
+
+def project(rows, w_query, kv_weight, b_query, kv_bias):
+    cols = lax.all_gather(rows, "kv", axis=1, tiled=True)
+    query = jnp.dot(cols, w_query, preferred_element_type=jnp.float32) + b_query
+    keyval = jnp.dot(cols, kv_weight, preferred_element_type=jnp.float32) + kv_bias
+    return query, keyval
 
 
 def body(
@@ -103,31 +112,26 @@
     q_width = w_query.shape[1]
     kv_width = w_keyval.shape[2]
     kv_weight = w_keyval.reshape(w_keyval.shape[0], 2 * kv_width)
-    weight = jnp.concatenate([w_query, kv_weight], axis=1)
-    bias = jnp.concatenate([b_query, b_keyval.reshape(2 * kv_width)])
-    dec_all = project(dec_tokens, weight, bias).astype(jnp.bfloat16)
-    tok_count = lax.axis_size("tok")
+    kv_bias = b_keyval.reshape(2 * kv_width)
+    dec_q, dec_kv = project(dec_tokens, w_query, kv_weight, b_query, kv_bias)
     tok_place = lax.axis_index("tok")
     ids = jnp.stack([owner_slots // dec_count, owner_slots % dec_count], axis=1).astype(jnp.bfloat16)
-    send_width = -(-(q_width + 2 * kv_width + 2) // 128) * 128
-    pad = jnp.zeros((dec_count, send_width - q_width - 2 * kv_width - 2), jnp.bfloat16)
-    sent = jnp.concatenate([dec_all, ids, pad], axis=1)
-    got = jnp.concatenate(fan(sent, "tok"), axis=0)
-    source = owner_slots // dec_count
-    rows = ((tok_place - source) % tok_count) * dec_count + owner_slots % dec_count
+    used = q_width + 2 * kv_width + 2
+    pad = jnp.zeros((dec_count, -(-used // 128) * 128 - used), jnp.bfloat16)
+    sent = jnp.concatenate([dec_q.astype(jnp.bfloat16), dec_kv.astype(jnp.bfloat16), ids, pad], axis=1)
+    got = tree_gather(sent)
+    rows = tree_row(tok_place, owner_slots // dec_count, dec_count) + owner_slots % dec_count
     chosen = jnp.take(got, rows, axis=0)
     dec_query = chosen[:, :q_width]
     dec_keyval = chosen[:, q_width:q_width + 2 * kv_width].reshape(dec_count, 2, kv_width)
     served, new_pool = serve_owner(dec_query, dec_keyval, dec_lengths, dec_pool)
-    back = jnp.concatenate(fan(served, "tok"), axis=0)
-    got_ids = got[:, q_width + 2 * kv_width:q_width + 2 * kv_width + 2].astype(jnp.int32)
+    back = tree_gather(served)
+    got_ids = got[:, q_width + 2 * kv_width:used].astype(jnp.int32)
     requests = got_ids[:, 0] * dec_count + got_ids[:, 1]
     wanted = tok_place * dec_count + jnp.arange(dec_count, dtype=jnp.int32)
     where = jnp.argmax(requests[None, :] == wanted[:, None], axis=1)
     dec_attn = jnp.take(back, where, axis=0)
-    pre_all = project(pre_tokens, weight, bias)
-    all_query = pre_all[:, :q_width]
-    all_keyval = pre_all[:, q_width:]
+    all_query, all_keyval = project(pre_tokens, w_query, kv_weight, b_query, kv_bias)
     half_id = tok_place % 2
     offset = pre_offsets[tok_place // 2]
     local_pos = jnp.arange(pre_count, dtype=jnp.int32)

time: 490 us -> 155 us (0.32); the launches traced: 481 us -> 155 us
  waiting for transfers between devices: 203 us -> 10.5 us
  starting transfers between devices: 178 us -> 27.6 us
  between operations: 2.1 us -> 15.1 us
  blocking collectives: 0 us -> 9.84 us
  local copies, waits for them, and re-layouts: 41.8 us -> 32.2 us
  other arithmetic: 18.8 us -> 27.3 us
  matrix products: 37.5 us -> 32 us
    ppermute x68 -> x14, waiting for transfers between devices: 203 us -> 10.5 us  [tree_gather(): parts.append(lax.ppermute(buffer, 'tok', pairs))]
    ppermute x68 -> x14, starting transfers between devices: 177 us -> 22.4 us  [tree_gather(): parts.append(lax.ppermute(buffer, 'tok', pairs))]
    unnamed x92 -> x60, local copies, waits for them, and re-layouts: 33.4 us -> 18.3 us
    all_gather x0 -> x1, blocking collectives: none -> 9.84 us  [project(): cols = lax.all_gather(rows, 'kv', axis=1, tiled=True)]
    dot_general x8 -> x4, matrix products: 19.8 us -> 13.5 us  [the longest x2 10.1 us: project(): query = jnp.dot(cols, w_query, preferred_element_type=jnp.float32) + b_query]
  transfers between devices with their start and end apart: 70 -> 17, of which waited for: 62 -> 9; matrix products, arithmetic and copies ran while one was open for 13% -> 37% of each run, Pallas kernels for 0% -> 0%
where the time goes in v2:
time: 155 us
  local copies, waits for them, and re-layouts  32.2 us (21%)
  matrix products  32 us (21%)
  starting transfers between devices  27.6 us (18%)
  other arithmetic  27.3 us (18%)
  between operations  15.1 us (10%)
  waiting for transfers between devices  10.5 us (7%)
  blocking collectives  9.84 us (6%)
    ppermute x14, starting transfers between devices, tree_gather(): parts.append(lax.ppermute(buffer, 'tok', pairs))  22.4 us
    unnamed x60, local copies, waits for them, and re-layouts  18.3 us
    dot_general x2, matrix products, head_scores(): jnp.einsum('ngd,md->ngm', shaped, key_rows, preferred_element_type=jnp.fl...  10.7 us
    ppermute x14, waiting for transfers between devices, tree_gather(): parts.append(lax.ppermute(buffer, 'tok', pairs))  10.5 us
    dot_general x2, matrix products, project(): query = jnp.dot(cols, w_query, preferred_element_type=jnp.float32) + b_query  10.1 us
    all_gather x1, blocking collectives, project(): cols = lax.all_gather(rows, 'kv', axis=1, tiled=True)  9.84 us
    reduce_sum x2, other arithmetic, head_mix(): totals = jnp.sum(powers, axis=-1)  9.29 us
    dot_general x2, matrix products, head_mix(): jnp.einsum('ngm,md->ngd', weights, value_rows, preferred_element_type=jnp...  7.83 us
  transfers between devices with their start and end apart: 17, of which 9 were waited for; matrix products, arithmetic and copies ran while one was open for 37% of the time, Pallas kernels for 0%

profile of v2, /device:TPU:1, one launch (start us, length us, event | category | flops | bytes accessed | tf_op | source)
XLA Modules:
  0.0 154.6 jit_solution(9778527914307117133)
XLA Ops:
  7.3 6.7 %copy.126 = bf16[2,12288,128]{2,1,0:T(8,128)(2,1)} copy(bf16[2,12288,128]{2,1,0:T(8,128)(2,1)} %param.17) | data formatting | bytes 12582912
  14.0 1.5 collective-permute-start.14
  16.3 9.8 %all_gather.6 = bf16[16,5120]{1,0:T(8,128)(2,1)S(1)} all-gather(bf16[16,1280]{1,0:T(8,128)(2,1)S(1)} %copy-done.5), channel_id=1, replica_groups=mesh['kv'=4,'tok'=32] {'kv'}, dimensions={1}, use_global_device_ids=true | all-gather | bytes 204800 | tf_op jit(solution)/shard_map/all_gather | solution.py:91
  26.6 4.2 %fusion.21 = bf16[16,640]{1,0:T(8,128)(2,1)S(1)} fusion(bf16[16,5120]{1,0:T(8,128)(2,1)S(1)} %all_gather.6, bf16[5120,640]{1,0:T(8,128)(2,1)} %param.13, f32[640]{0:T(1024)S(1)} %copy-done.8), kind=kOutput, calls=%fused_computation.31 | convolution fusion | flops 104878080 | bytes 6740480 | tf_op jit(solution)/shard_map/dot_general | solution.py:92
  30.9 2.3 %collective-permute-start = (bf16[16,1024]{1,0:T(8,128)(2,1)S(1)}, bf16[16,1024]{1,0:T(8,128)(2,1)S(1)}, u32[]{:S(2)}, u32[]{:S(2)}) collective-permute-start(bf16[16,1024]{1,0:T(8,128)(2,1)S(1)} %concatenate.83), channel_id=1, source_target_pairs={{0,1},{1,0},{2,3},{3,2},{4,5},{5,4},{6,7},{7,6},{8,9},{9,8},{10,11... | collective-permute-start | bytes 98312 | tf_op jit(solution)/shard_map/ppermute | solution.py:78
  35.2 0.7 add_select_fusion
  35.8 0.7 fusion.68
  37.8 1.3 multiply_cosine_fusion.1
  39.3 1.2 compare_and_fusion
  40.5 0.6 constant_dynamic-update-slice_fusion.4
  41.2 1.4 collective-permute-start.1
  42.5 2.6 %collective-permute-start.2 = (bf16[32,1024]{1,0:T(8,128)(2,1)S(1)}, bf16[32,1024]{1,0:T(8,128)(2,1)S(1)}, u32[]{:S(2)}, u32[]{:S(2)}) collective-permute-start(bf16[32,1024]{1,0:T(8,128)(2,1)S(1)} %pad_maximum_fusion.2), channel_id=1, source_target_pairs={{0,4},{1,5},{2,6},{3,7},{4,0},{5,1},{6,2},{7,3},{8,12},{9,13},{10,... | collective-permute-start | bytes 196616 | tf_op jit(solution)/shard_map/ppermute | solution.py:78
  45.1 1.1 collective-permute-start.3
  46.2 0.6 constant_dynamic-update-slice_fusion.3
  46.8 0.6 constant_dynamic-update-slice_fusion.2
  47.5 1.2 collective-permute-done.2
  48.7 0.6 constant_dynamic-update-slice_fusion.1
  49.3 0.7 constant_dynamic-update-slice_fusion
  50.0 1.6 %collective-permute-start.4 = (bf16[128,1024]{1,0:T(8,128)(2,1)}, bf16[128,1024]{1,0:T(8,128)(2,1)}, u32[]{:S(2)}, u32[]{:S(2)}) collective-permute-start(bf16[128,1024]{1,0:T(8,128)(2,1)} %get-tuple-element.36), channel_id=1, source_target_pairs={{0,8},{1,9},{2,10},{3,11},{4,12},{5,13},{6,14},{7,15},{8,16},{9,17... | collective-permute-start | bytes 786440 | tf_op jit(solution)/shard_map/ppermute | solution.py:78
  51.6 0.8 multiply_cosine_fusion.3
  52.4 3.4 %collective-permute-start.5 = (bf16[128,1024]{1,0:T(8,128)(2,1)}, bf16[128,1024]{1,0:T(8,128)(2,1)}, u32[]{:S(2)}, u32[]{:S(2)}) collective-permute-start(bf16[128,1024]{1,0:T(8,128)(2,1)} %get-tuple-element.36), channel_id=1, source_target_pairs={{0,16},{1,17},{2,18},{3,19},{4,20},{5,21},{6,22},{7,23},{8,24},{9,... | collective-permute-start | bytes 786440 | tf_op jit(solution)/shard_map/ppermute | solution.py:78
  55.8 0.7 pad_clamp_fusion.1
  56.5 0.7 collective-permute-start.6
  57.8 2.1 %collective-permute-done.4 = bf16[128,1024]{1,0:T(8,128)(2,1)} collective-permute-done((bf16[128,1024]{1,0:T(8,128)(2,1)}, bf16[128,1024]{1,0:T(8,128)(2,1)}, u32[]{:S(2)}, u32[]{:S(2)}) %collective-permute-start.4) | collective-permute-done | bytes 262176 | tf_op jit(solution)/shard_map/ppermute | solution.py:78
  59.9 1.7 %constant_dynamic-update-slice_fusion.7 = bf16[512,1024]{1,0:T(8,128)(2,1)} fusion(bf16[512,1024]{1,0:T(8,128)(2,1)} %get-tuple-element.37, bf16[128,1024]{1,0:T(8,128)(2,1)} %collective-permute-done.4), kind=kLoop, calls=%fused_computation.83 | loop fusion | bytes 524288
  61.5 4.8 %collective-permute-done.5 = bf16[128,1024]{1,0:T(8,128)(2,1)} collective-permute-done((bf16[128,1024]{1,0:T(8,128)(2,1)}, bf16[128,1024]{1,0:T(8,128)(2,1)}, u32[]{:S(2)}, u32[]{:S(2)}) %collective-permute-start.5) | collective-permute-done | bytes 262176 | tf_op jit(solution)/shard_map/ppermute | solution.py:78
  66.4 1.7 %constant_dynamic-update-slice_fusion.6 = bf16[512,1024]{1,0:T(8,128)(2,1)} fusion(bf16[512,1024]{1,0:T(8,128)(2,1)} %constant_dynamic-update-slice_fusion.7, bf16[128,1024]{1,0:T(8,128)(2,1)} %collective-permute-done.5), kind=kLoop, calls=%fused_computation.82 | loop fusion | bytes 524288
  68.1 1.7 %constant_dynamic-update-slice_fusion.5 = bf16[512,1024]{1,0:T(8,128)(2,1)} fusion(bf16[512,1024]{1,0:T(8,128)(2,1)} %constant_dynamic-update-slice_fusion.6, bf16[128,1024]{1,0:T(8,128)(2,1)} %collective-permute-done.6), kind=kLoop, calls=%fused_computation.81 | loop fusion | bytes 524288 | tf_op jit(solution)/shard_map/concatenate | solution.py:79
  69.7 2.0 %gather_fusion = bf16[16,1024]{1,0:T(8,128)(2,1)S(1)} fusion(bf16[512,1024]{1,0:T(8,128)(2,1)} %constant_dynamic-update-slice_fusion.5, s32[1024]{0:T(1024)S(1)} %pad_clamp_fusion.1), kind=kCustom, calls=%fused_computation | custom fusion | bytes 65600 | tf_op jit(solution)/shard_map/jit(_take)/gather | solution.py:124
  71.7 0.7 broadcast_select_fusion
  72.4 0.6 slice_convert_fusion.1
  73.7 0.8 reshape.477
  74.4 0.7 fusion.97
  75.2 0.7 reshape.471
  75.9 0.8 fusion.78
  76.8 2.4 %scatter_fusion = bf16[2,12288,128]{2,1,0:T(8,128)(2,1)} fusion(bf16[2,12288,128]{2,1,0:T(8,128)(2,1)} %copy.126, s32[16]{0:T(128)} %get-tuple-element.22, bf16[16,2,128]{2,0,1:T(8,128)(2,1)S(1)} %maximum_bitcast_fusion), kind=kCustom, calls=%fused_computation.2 | custom fusion | bytes 24640 | tf_op jit(solution)/shard_map/scatter | solution.py:58
  79.2 1.0 subtract_convert_fusion.1
  80.3 3.5 %fusion.100 = (f32[16,5]{0,1:T(8,128)S(1)}, f32[16,5,12288]{2,0,1:T(8,128)S(1)}) fusion(bf16[2,12288,128]{2,1,0:T(8,128)(2,1)} %scatter_fusion, bf16[16,5,64]{2,0,1:T(8,128)(2,1)S(1)} %get-tuple-element.33, bf16[16,5,64]{2,0,1:T(8,128)(2,1)S(1)} %get-tuple-element.32, pred[16,12288]{1,0:T(8,128)(4,1)S(1)} %fusion.43), kind=kOutput, calls=%fused_computation.192 | convolution fusion | flops 254648240 | bytes 7295296 | tf_op jit(solution)/shard_map/ngd,md->ngm/dot_general | solution.py:34
  83.8 0.8 fusion.7
  84.6 0.9 fusion.34
  85.5 1.8 %collective-permute-start.7 = (bf16[16,640]{1,0:T(8,128)(2,1)S(1)}, bf16[16,640]{1,0:T(8,128)(2,1)S(1)}, u32[]{:S(2)}, u32[]{:S(2)}) collective-permute-start(bf16[16,640]{1,0:T(8,128)(2,1)S(1)} %bitcast.93), channel_id=1, source_target_pairs={{0,1},{1,0},{2,3},{3,2},{4,5},{5,4},{6,7},{7,6},{8,9},{9,8},{10,11... | collective-permute-start | bytes 61448 | tf_op jit(solution)/shard_map/ppermute | solution.py:78
  87.3 0.9 slice_convert_fusion
  88.5 0.7 iota_reduce_fusion
  89.8 0.6 constant_dynamic-update-slice_fusion.18
  90.6 2.6 %collective-permute-start.9 = (bf16[32,640]{1,0:T(8,128)(2,1)S(1)}, bf16[32,640]{1,0:T(8,128)(2,1)S(1)}, u32[]{:S(2)}, u32[]{:S(2)}) collective-permute-start(bf16[32,640]{1,0:T(8,128)(2,1)S(1)} %get-tuple-element.54), channel_id=1, source_target_pairs={{0,4},{1,5},{2,6},{3,7},{4,0},{5,1},{6,2},{7,3},{8,12},{9,13},{10,... | collective-permute-start | bytes 122888 | tf_op jit(solution)/shard_map/ppermute | solution.py:78
  93.2 0.8 collective-permute-start.10
  94.5 0.6 constant_dynamic-update-slice_fusion.17
  96.3 0.6 constant_dynamic-update-slice_fusion.15
  97.4 1.7 %collective-permute-start.12 = (bf16[128,640]{1,0:T(8,128)(2,1)S(1)}, bf16[128,640]{1,0:T(8,128)(2,1)S(1)}, u32[]{:S(2)}, u32[]{:S(2)}) collective-permute-start(bf16[128,640]{1,0:T(8,128)(2,1)S(1)} %get-tuple-element.42), channel_id=1, source_target_pairs={{0,16},{1,17},{2,18},{3,19},{4,20},{5,21},{6,22},{7,23},{8,24},{9,... | collective-permute-start | bytes 491528 | tf_op jit(solution)/shard_map/ppermute | solution.py:78
  99.1 1.7 %collective-permute-start.13 = (bf16[128,640]{1,0:T(8,128)(2,1)S(1)}, bf16[128,640]{1,0:T(8,128)(2,1)S(1)}, u32[]{:S(2)}, u32[]{:S(2)}) collective-permute-start(bf16[128,640]{1,0:T(8,128)(2,1)S(1)} %get-tuple-element.42), channel_id=1, source_target_pairs={{0,24},{1,25},{2,26},{3,27},{4,28},{5,29},{6,30},{7,31},{8,0},{9,1... | collective-permute-start | bytes 491528 | tf_op jit(solution)/shard_map/ppermute | solution.py:78
  100.8 2.8 %maximum_select_fusion = bf16[2,2048,128]{2,1,0:T(8,128)(2,1)} fusion(bf16[2,1024,128]{2,1,0:T(8,128)(2,1)} %collective-permute-done.14, bf16[2,1024,128]{2,1,0:T(8,128)(2,1)} %param.20, pred[]{:T(512)S(6)} %eq.32), kind=kLoop, calls=%fused_computation.37 | loop fusion | flops 4718592 | bytes 2097153 | tf_op jit(solution)/shard_map/jit(_where)/select_n | solution.py:150
  103.7 0.7 constant_dynamic-update-slice_fusion.22
  104.4 0.7 collective-permute-done.12
  105.1 0.7 constant_dynamic-update-slice_fusion.21
  106.2 0.7 constant_dynamic-update-slice_fusion.20
  106.8 1.8 %gather_fusion.1 = bf16[16,640]{1,0:T(8,128)(2,1)S(1)} fusion(bf16[512,640]{1,0:T(8,128)(2,1)} %constant_dynamic-update-slice_fusion.20, s32[1024]{0:T(1024)S(1)} %pad_clamp_fusion), kind=kCustom, calls=%fused_computation.1 | custom fusion | bytes 41024 | tf_op jit(solution)/shard_map/jit(_take)/gather | solution.py:133
  108.6 0.7 broadcast_select_fusion.1
  109.3 2.9 %fusion.18 = f32[256,256]{0,1:T(8,128)S(1)} fusion(bf16[256,5120]{1,0:T(8,128)(2,1)} %all-gather.2.cloned.1.call-done, bf16[640,8,2,128]{3,2,1,0:T(2,128)(2,1)S(1)} %bitcast.86, f32[256]{0:T(256)S(1)} %bitcast.96), kind=kOutput, calls=%fused_computation.29 | convolution fusion | flops 671154176 | bytes 5506048 | tf_op jit(solution)/shard_map/dot_general | solution.py:93
  113.3 3.7 %collective-permute-start.15 = (bf16[2,256,128]{2,1,0:T(8,128)(2,1)S(1)}, bf16[2,256,128]{2,1,0:T(8,128)(2,1)S(1)}, u32[]{:S(2)}, u32[]{:S(2)}) collective-permute-start(bf16[2,256,128]{2,1,0:T(8,128)(2,1)S(1)} %pad_maximum_fusion.1), channel_id=1, source_target_pairs={{0,1},{1,0},{2,3},{3,2},{4,5},{5,4},{6,7},{7,6},{8,9},{9,8},{10,11... | collective-permute-start | bytes 393224 | tf_op jit(solution)/shard_map/ppermute | solution.py:13
  117.0 5.9 %convolution_add_fusion = f32[256,640]{1,0:T(8,128)S(1)} fusion(bf16[256,5120]{1,0:T(8,128)(2,1)} %all-gather.2.cloned.1.call-done, bf16[5120,640]{1,0:T(8,128)(2,1)} %param.13, f32[640]{0:T(1024)S(1)} %copy-done.9), kind=kOutput, calls=%fused_computation.28 | convolution fusion | flops 1677885440 | bytes 9832960 | tf_op jit(solution)/shard_map/dot_general | solution.py:92
  124.2 7.2 %fusion.1 = (f32[256,5]{0,1:T(8,128)S(1)}, f32[256,5,2560]{2,0,1:T(8,128)}) fusion(pred[256,2560]{1,0:T(8,128)(4,1)S(1)} %compare_and_fusion, bf16[2,2048,128]{2,1,0:T(8,128)(2,1)} %maximum_select_fusion, bf16[2,512,128]{2,1,0:T(8,128)(2,1)S(1)} %maximum_select_fusion.1, bf16[256,5,64]{2,0,1:T(8,128)(2,1)S(1)} %get-tuple-element.25, ...), kind=kOutput, calls=%fused_computation.7 | convolution fusion | flops 850656000 | bytes 15406080 | tf_op jit(solution)/shard_map/ngd,md->ngm/dot_general | solution.py:34
  131.4 8.5 %fusion.2 = f32[256,5]{0,1:T(8,128)S(1)} fusion(f32[256,5,2560]{2,0,1:T(8,128)} %get-tuple-element.72, f32[256,5]{0,1:T(8,128)S(1)} %get-tuple-element.71, pred[256,2560]{1,0:T(8,128)(4,1)S(1)} %compare_and_fusion), kind=kLoop, calls=%fused_computation.8 | loop fusion | flops 13105920 | bytes 13772800 | tf_op jit(solution)/shard_map/reduce_sum | solution.py:41
  139.9 7.0 %fusion.40 = bf16[256,5,128]{0,2,1:T(8,128)(2,1)S(1)} fusion(f32[256,5,2560]{2,0,1:T(8,128)} %get-tuple-element.72, f32[256,5]{0,1:T(8,128)S(1)} %get-tuple-element.71, pred[256,2560]{1,0:T(8,128)(4,1)S(1)} %compare_and_fusion, bf16[2,512,128]{2,1,0:T(8,128)(2,1)S(1)} %maximum_select_fusion.1, bf16[2,2048,128]{2,1,0:T(8,128)(2,1)S(1)} %copy-done.1, ...), kind=kOutput, calls=%fused_computation.39 | convolution fusion | flops 853606400 | bytes 15411200 | tf_op jit(solution)/shard_map/ngm,md->ngd/dot_general | solution.py:43
  146.8 0.9 copy.58
  (102 shorter events, 11.6 us)
Async XLA Ops:
  7.2 8.3 %copy-start.16 = (s32[16]{0:T(128)S(1)}, s32[16]{0:T(128)}, u32[]{:S(2)}) copy-start(s32[16]{0:T(128)} %param.18) | copy-start | bytes 196
  7.2 9.1 %copy-start.5 = (bf16[16,1280]{1,0:T(8,128)(2,1)S(1)}, bf16[16,1280]{1,0:T(8,128)(2,1)}, u32[]{:S(2)}) copy-start(bf16[16,1280]{1,0:T(8,128)(2,1)} %param.11) | copy-start | bytes 122884
  7.2 18.9 %copy-start.12 = (f32[2,128]{1,0:T(2,128)S(1)}, f32[2,128]{1,0:T(2,128)}, u32[]{:S(2)}) copy-start(f32[2,128]{1,0:T(2,128)} %param.16) | copy-start | bytes 3076
  7.2 18.9 %copy-start = (bf16[5120,2,128]{2,1,0:T(2,128)(2,1)S(1)}, bf16[5120,2,128]{2,1,0:T(2,128)(2,1)}, u32[]{:S(2)}) copy-start(bf16[5120,2,128]{2,1,0:T(2,128)(2,1)} %param.14) | copy-start | bytes 7864324
  7.2 19.4 %copy-start.8 = (f32[640]{0:T(1024)S(1)}, f32[640]{0:T(1024)}, u32[]{:S(2)}) copy-start(f32[640]{0:T(1024)} %param.15) | copy-start | bytes 7684
  7.2 102.1 %all-gather.2.cloned.1.call-start = ((), (), s32[]{:S(2)}) async-start(), calls=%async_computation | async-start | bytes 3276800 | tf_op jit(solution)/shard_map/all_gather | solution.py:91
  14.0 86.8 %collective-permute-start.14 = (bf16[2,1024,128]{2,1,0:T(8,128)(2,1)}, bf16[2,1024,128]{2,1,0:T(8,128)(2,1)}, u32[]{:S(2)}, u32[]{:S(2)}) collective-permute-start(bf16[2,1024,128]{2,1,0:T(8,128)(2,1)} %param.20), channel_id=1, source_target_pairs={{0,1},{1,0},{2,3},{3,2},{4,5},{5,4},{6,7},{7,6},{8,9},{9,8},{10,11... | collective-permute-start | bytes 1572872 | tf_op jit(solution)/shard_map/ppermute | solution.py:13
  26.6 6.7 %copy-start.17 = (s32[16]{0:T(128)S(1)}, s32[16]{0:T(128)}, u32[]{:S(2)}) copy-start(s32[16]{0:T(128)} %param.21) | copy-start | bytes 196
  26.6 9.9 %copy-start.14 = (s32[16]{0:T(128)S(1)}, s32[16]{0:T(128)}, u32[]{:S(2)}) copy-start(s32[16]{0:T(128)} %param.19) | copy-start | bytes 196
  30.9 10.2 %collective-permute-start = (bf16[16,1024]{1,0:T(8,128)(2,1)S(1)}, bf16[16,1024]{1,0:T(8,128)(2,1)S(1)}, u32[]{:S(2)}, u32[]{:S(2)}) collective-permute-start(bf16[16,1024]{1,0:T(8,128)(2,1)S(1)} %concatenate.83), channel_id=1, source_target_pairs={{0,1},{1,0},{2,3},{3,2},{4,5},{5,4},{6,7},{7,6},{8,9},{9,8},{10,11... | collective-permute-start | bytes 98312 | tf_op jit(solution)/shard_map/ppermute | solution.py:78
  33.3 5.8 %copy-start.6 = (f32[64]{0:T(128)}, f32[64]{0:T(128)S(1)}, u32[]{:S(2)}) copy-start(f32[64]{0:T(128)S(1)} %negate_power_fusion) | copy-start | bytes 772
  34.6 4.5 %copy-start.10 = (f32[256]{0:T(256)}, f32[256]{0:T(256)S(1)}, u32[]{:S(2)}) copy-start(f32[256]{0:T(256)S(1)} %fusion.87) | copy-start | bytes 3076
  41.2 5.7 %collective-permute-start.1 = (bf16[32,1024]{1,0:T(8,128)(2,1)S(1)}, bf16[32,1024]{1,0:T(8,128)(2,1)S(1)}, u32[]{:S(2)}, u32[]{:S(2)}) collective-permute-start(bf16[32,1024]{1,0:T(8,128)(2,1)S(1)} %pad_maximum_fusion.2), channel_id=1, source_target_pairs={{0,2},{1,3},{2,4},{3,5},{4,6},{5,7},{6,0},{7,1},{8,10},{9,11},{10,... | collective-permute-start | bytes 196616 | tf_op jit(solution)/shard_map/ppermute | solution.py:78
  42.5 6.2 %collective-permute-start.2 = (bf16[32,1024]{1,0:T(8,128)(2,1)S(1)}, bf16[32,1024]{1,0:T(8,128)(2,1)S(1)}, u32[]{:S(2)}, u32[]{:S(2)}) collective-permute-start(bf16[32,1024]{1,0:T(8,128)(2,1)S(1)} %pad_maximum_fusion.2), channel_id=1, source_target_pairs={{0,4},{1,5},{2,6},{3,7},{4,0},{5,1},{6,2},{7,3},{8,12},{9,13},{10,... | collective-permute-start | bytes 196616 | tf_op jit(solution)/shard_map/ppermute | solution.py:78
  45.1 4.2 %collective-permute-start.3 = (bf16[32,1024]{1,0:T(8,128)(2,1)S(1)}, bf16[32,1024]{1,0:T(8,128)(2,1)S(1)}, u32[]{:S(2)}, u32[]{:S(2)}) collective-permute-start(bf16[32,1024]{1,0:T(8,128)(2,1)S(1)} %pad_maximum_fusion.2), channel_id=1, source_target_pairs={{0,6},{1,7},{2,0},{3,1},{4,2},{5,3},{6,4},{7,5},{8,14},{9,15},{10,... | collective-permute-start | bytes 196616 | tf_op jit(solution)/shard_map/ppermute | solution.py:78
  50.0 9.9 %collective-permute-start.4 = (bf16[128,1024]{1,0:T(8,128)(2,1)}, bf16[128,1024]{1,0:T(8,128)(2,1)}, u32[]{:S(2)}, u32[]{:S(2)}) collective-permute-start(bf16[128,1024]{1,0:T(8,128)(2,1)} %get-tuple-element.36), channel_id=1, source_target_pairs={{0,8},{1,9},{2,10},{3,11},{4,12},{5,13},{6,14},{7,15},{8,16},{9,17... | collective-permute-start | bytes 786440 | tf_op jit(solution)/shard_map/ppermute | solution.py:78
  52.4 14.0 %collective-permute-start.5 = (bf16[128,1024]{1,0:T(8,128)(2,1)}, bf16[128,1024]{1,0:T(8,128)(2,1)}, u32[]{:S(2)}, u32[]{:S(2)}) collective-permute-start(bf16[128,1024]{1,0:T(8,128)(2,1)} %get-tuple-element.36), channel_id=1, source_target_pairs={{0,16},{1,17},{2,18},{3,19},{4,20},{5,21},{6,22},{7,23},{8,24},{9,... | collective-permute-start | bytes 786440 | tf_op jit(solution)/shard_map/ppermute | solution.py:78
  56.5 11.6 %collective-permute-start.6 = (bf16[128,1024]{1,0:T(8,128)(2,1)}, bf16[128,1024]{1,0:T(8,128)(2,1)}, u32[]{:S(2)}, u32[]{:S(2)}) collective-permute-start(bf16[128,1024]{1,0:T(8,128)(2,1)} %get-tuple-element.36), channel_id=1, source_target_pairs={{0,24},{1,25},{2,26},{3,27},{4,28},{5,29},{6,30},{7,31},{8,0},{9,1... | collective-permute-start | bytes 786440 | tf_op jit(solution)/shard_map/ppermute | solution.py:78
  79.2 5.4 %slice-start = ((s8[6291456]{0:T(1024)(128)(4,1)}), s8[4194304]{0:T(1024)(128)(4,1)S(1)}, s32[]{:S(2)}) async-start(s8[6291456]{0:T(1024)(128)(4,1)} %bitcast.83), calls=%async_computation.1 | async-start | bytes 8388608
  80.3 4.3 %slice-start.1 = ((s8[6291456]{0:T(1024)(128)(4,1)}), s8[2097152]{0:T(1024)(128)(4,1)S(1)}, s32[]{:S(2)}) async-start(s8[6291456]{0:T(1024)(128)(4,1)} %bitcast.83), calls=%async_computation.2 | async-start | bytes 4194304
  84.6 3.9 %copy-start.15 = (s32[16]{0:T(128)S(1)}, s32[16]{0:T(128)}, u32[]{:S(2)}) copy-start(s32[16]{0:T(128)} %iota_add_fusion.1) | copy-start | bytes 196
  85.5 23.8 %copy-start.13 = (f32[2,128]{1,0:T(2,128)S(1)}, f32[2,128]{1,0:T(2,128)}, u32[]{:S(2)}) copy-start(f32[2,128]{1,0:T(2,128)} %param.16) | copy-start | bytes 3076
  85.5 4.3 %collective-permute-start.7 = (bf16[16,640]{1,0:T(8,128)(2,1)S(1)}, bf16[16,640]{1,0:T(8,128)(2,1)S(1)}, u32[]{:S(2)}, u32[]{:S(2)}) collective-permute-start(bf16[16,640]{1,0:T(8,128)(2,1)S(1)} %bitcast.93), channel_id=1, source_target_pairs={{0,1},{1,0},{2,3},{3,2},{4,5},{5,4},{6,7},{7,6},{8,9},{9,8},{10,11... | collective-permute-start | bytes 61448 | tf_op jit(solution)/shard_map/ppermute | solution.py:78
  90.4 4.1 %collective-permute-start.8 = (bf16[32,640]{1,0:T(8,128)(2,1)S(1)}, bf16[32,640]{1,0:T(8,128)(2,1)S(1)}, u32[]{:S(2)}, u32[]{:S(2)}) collective-permute-start(bf16[32,640]{1,0:T(8,128)(2,1)S(1)} %get-tuple-element.54), channel_id=1, source_target_pairs={{0,2},{1,3},{2,4},{3,5},{4,6},{5,7},{6,0},{7,1},{8,10},{9,11},{10,... | collective-permute-start | bytes 122888 | tf_op jit(solution)/shard_map/ppermute | solution.py:78
  90.6 4.8 %collective-permute-start.9 = (bf16[32,640]{1,0:T(8,128)(2,1)S(1)}, bf16[32,640]{1,0:T(8,128)(2,1)S(1)}, u32[]{:S(2)}, u32[]{:S(2)}) collective-permute-start(bf16[32,640]{1,0:T(8,128)(2,1)S(1)} %get-tuple-element.54), channel_id=1, source_target_pairs={{0,4},{1,5},{2,6},{3,7},{4,0},{5,1},{6,2},{7,3},{8,12},{9,13},{10,... | collective-permute-start | bytes 122888 | tf_op jit(solution)/shard_map/ppermute | solution.py:78
  93.2 3.1 %collective-permute-start.10 = (bf16[32,640]{1,0:T(8,128)(2,1)S(1)}, bf16[32,640]{1,0:T(8,128)(2,1)S(1)}, u32[]{:S(2)}, u32[]{:S(2)}) collective-permute-start(bf16[32,640]{1,0:T(8,128)(2,1)S(1)} %get-tuple-element.54), channel_id=1, source_target_pairs={{0,6},{1,7},{2,0},{3,1},{4,2},{5,3},{6,4},{7,5},{8,14},{9,15},{10,... | collective-permute-start | bytes 122888 | tf_op jit(solution)/shard_map/ppermute | solution.py:78
  96.9 6.8 %collective-permute-start.11 = (bf16[128,640]{1,0:T(8,128)(2,1)S(1)}, bf16[128,640]{1,0:T(8,128)(2,1)S(1)}, u32[]{:S(2)}, u32[]{:S(2)}) collective-permute-start(bf16[128,640]{1,0:T(8,128)(2,1)S(1)} %get-tuple-element.42), channel_id=1, source_target_pairs={{0,8},{1,9},{2,10},{3,11},{4,12},{5,13},{6,14},{7,15},{8,16},{9,17... | collective-permute-start | bytes 491528 | tf_op jit(solution)/shard_map/ppermute | solution.py:78
  97.4 7.7 %collective-permute-start.12 = (bf16[128,640]{1,0:T(8,128)(2,1)S(1)}, bf16[128,640]{1,0:T(8,128)(2,1)S(1)}, u32[]{:S(2)}, u32[]{:S(2)}) collective-permute-start(bf16[128,640]{1,0:T(8,128)(2,1)S(1)} %get-tuple-element.42), channel_id=1, source_target_pairs={{0,16},{1,17},{2,18},{3,19},{4,20},{5,21},{6,22},{7,23},{8,24},{9,... | collective-permute-start | bytes 491528 | tf_op jit(solution)/shard_map/ppermute | solution.py:78
  99.1 7.1 %collective-permute-start.13 = (bf16[128,640]{1,0:T(8,128)(2,1)S(1)}, bf16[128,640]{1,0:T(8,128)(2,1)S(1)}, u32[]{:S(2)}, u32[]{:S(2)}) collective-permute-start(bf16[128,640]{1,0:T(8,128)(2,1)S(1)} %get-tuple-element.42), channel_id=1, source_target_pairs={{0,24},{1,25},{2,26},{3,27},{4,28},{5,29},{6,30},{7,31},{8,0},{9,1... | collective-permute-start | bytes 491528 | tf_op jit(solution)/shard_map/ppermute | solution.py:78
  105.8 6.8 %copy-start.7 = (f32[64]{0:T(128)S(1)}, f32[64]{0:T(128)}, u32[]{:S(2)}) copy-start(f32[64]{0:T(128)} %copy-done.6) | copy-start | bytes 772
  105.8 6.8 %copy-start.11 = (f32[256]{0:T(256)S(1)}, f32[256]{0:T(256)}, u32[]{:S(2)}) copy-start(f32[256]{0:T(256)} %copy-done.10) | copy-start | bytes 3076
  109.3 7.7 %copy-start.9 = (f32[640]{0:T(1024)S(1)}, f32[640]{0:T(1024)}, u32[]{:S(2)}) copy-start(f32[640]{0:T(1024)} %param.15) | copy-start | bytes 7684
  113.3 9.6 %copy-start.4 = (bf16[2,256,128]{2,1,0:T(8,128)(2,1)}, bf16[2,256,128]{2,1,0:T(8,128)(2,1)S(1)}, u32[]{:S(2)}) copy-start(bf16[2,256,128]{2,1,0:T(8,128)(2,1)S(1)} %pad_maximum_fusion.1) | copy-start | bytes 393220
  113.3 10.7 %collective-permute-start.15 = (bf16[2,256,128]{2,1,0:T(8,128)(2,1)S(1)}, bf16[2,256,128]{2,1,0:T(8,128)(2,1)S(1)}, u32[]{:S(2)}, u32[]{:S(2)}) collective-permute-start(bf16[2,256,128]{2,1,0:T(8,128)(2,1)S(1)} %pad_maximum_fusion.1), channel_id=1, source_target_pairs={{0,1},{1,0},{2,3},{3,2},{4,5},{5,4},{6,7},{7,6},{8,9},{9,8},{10,11... | collective-permute-start | bytes 393224 | tf_op jit(solution)/shard_map/ppermute | solution.py:13
  122.9 0.9 copy-start.2
  122.9 1.0 copy-start.3
  131.4 8.5 %copy-start.1 = (bf16[2,2048,128]{2,1,0:T(8,128)(2,1)S(1)}, bf16[2,2048,128]{2,1,0:T(8,128)(2,1)}, u32[]{:S(2)}) copy-start(bf16[2,2048,128]{2,1,0:T(8,128)(2,1)} %maximum_select_fusion) | copy-start | bytes 3145732
Sparse Core Ops, SparseCore 0:
  14.1 38.1 all-gather.1

commit v3 on v2

--- a/solution.py
+++ b/solution.py
@@ -65,18 +65,17 @@
 
 
 def tree_gather(value):
-    place = lax.axis_index("tok")
     buffer = value
     for stride, count in ((1, 2), (2, 4), (8, 4)):
-        parts = [buffer]
-        for shift in range(1, count):
-            pairs = []
-            for i in range(32):
-                digit = (i // stride) % count
-                target = i + (((digit + shift) % count) - digit) * stride
-                pairs.append((i, target))
-            parts.append(lax.ppermute(buffer, "tok", pairs))
-        buffer = jnp.concatenate(parts, axis=0)
+      parts = [buffer]
+      for shift in range(1, count):
+          pairs = []
+          for i in range(32):
+              digit = (i // stride) % count
+              target = i + (((digit + shift) % count) - digit) * stride
+              pairs.append((i, target))
+          parts.append(lax.ppermute(buffer, "tok", pairs))
+      buffer = jnp.concatenate(parts, axis=0)
     return buffer
 
 
@@ -94,21 +93,8 @@
     return query, keyval
 
 
-def body(
-    dec_tokens,
-    pre_tokens,
-    w_query,
-    w_keyval,
-    b_query,
-    b_keyval,
-    dec_pool,
-    owner_slots,
-    dec_lengths,
-    pre_cache,
-    pre_offsets,
-):
+def body_inner(dec_tokens, pre_tokens, w_query, w_keyval, b_query, b_keyval, dec_pool, owner_slots, dec_lengths):
     dec_count = dec_tokens.shape[0]
-    pre_count = pre_tokens.shape[0]
     q_width = w_query.shape[1]
     kv_width = w_keyval.shape[2]
     kv_weight = w_keyval.reshape(w_keyval.shape[0], 2 * kv_width)
@@ -132,6 +118,14 @@
     where = jnp.argmax(requests[None, :] == wanted[:, None], axis=1)
     dec_attn = jnp.take(back, where, axis=0)
     all_query, all_keyval = project(pre_tokens, w_query, kv_weight, b_query, kv_bias)
+    return dec_attn, new_pool, all_query, all_keyval
+
+
+def prefill(all_query, all_keyval, pre_tokens, w_query, w_keyval, pre_cache, pre_offsets):
+    pre_count = pre_tokens.shape[0]
+    q_width = w_query.shape[1]
+    kv_width = w_keyval.shape[2]
+    tok_place = lax.axis_index("tok")
     half_id = tok_place % 2
     offset = pre_offsets[tok_place // 2]
     local_pos = jnp.arange(pre_count, dtype=jnp.int32)
@@ -165,6 +159,14 @@
     scores = head_scores(turned, key_rows[0], allowed)
     totals, mixed = head_mix(scores, jnp.max(scores, axis=-1), key_rows[1])
     pre_attn = (mixed / totals[..., None]).astype(jnp.bfloat16).reshape(pre_count, q_width)
+    return pre_attn, appended
+
+
+def body(dec_tokens, pre_tokens, w_query, w_keyval, b_query, b_keyval, dec_pool, owner_slots, dec_lengths, pre_cache, pre_offsets):
+    dec_attn, new_pool, all_query, all_keyval = body_inner(
+        dec_tokens, pre_tokens, w_query, w_keyval, b_query, b_keyval, dec_pool, owner_slots, dec_lengths
+    )
+    pre_attn, appended = prefill(all_query, all_keyval, pre_tokens, w_query, w_keyval, pre_cache, pre_offsets)
     return (dec_attn, pre_attn, new_pool, appended)
 
 

time: 155 us -> 155 us (level)
  no operation moved by 1% of the time
where the time goes in v3:
time: 155 us
  local copies, waits for them, and re-layouts  32.2 us (21%)
  matrix products  32 us (21%)
  starting transfers between devices  27.6 us (18%)
  other arithmetic  27.3 us (18%)
  between operations  15.1 us (10%)
  waiting for transfers between devices  10.5 us (7%)
  blocking collectives  9.84 us (6%)
    ppermute x14, starting transfers between devices, tree_gather(): parts.append(lax.ppermute(buffer, 'tok', pairs))  22.4 us
    unnamed x60, local copies, waits for them, and re-layouts  18.3 us
    dot_general x2, matrix products, head_scores(): jnp.einsum('ngd,md->ngm', shaped, key_rows, preferred_element_type=jnp.fl...  10.7 us
    ppermute x14, waiting for transfers between devices, tree_gather(): parts.append(lax.ppermute(buffer, 'tok', pairs))  10.5 us
    dot_general x2, matrix products, project(): query = jnp.dot(cols, w_query, preferred_element_type=jnp.float32) + b_query  10.1 us
    all_gather x1, blocking collectives, project(): cols = lax.all_gather(rows, 'kv', axis=1, tiled=True)  9.84 us
    reduce_sum x2, other arithmetic, head_mix(): totals = jnp.sum(powers, axis=-1)  9.29 us
    dot_general x2, matrix products, head_mix(): jnp.einsum('ngm,md->ngd', weights, value_rows, preferred_element_type=jnp...  7.83 us
  transfers between devices with their start and end apart: 17, of which 9 were waited for; matrix products, arithmetic and copies ran while one was open for 37% of the time, Pallas kernels for 0%

profile of v3, /device:TPU:1, one launch (start us, length us, event | category | flops | bytes accessed | tf_op | source)
XLA Modules:
  0.0 154.6 jit_solution(9778527914307117133)
XLA Ops:
  7.3 6.7 %copy.126 = bf16[2,12288,128]{2,1,0:T(8,128)(2,1)} copy(bf16[2,12288,128]{2,1,0:T(8,128)(2,1)} %param.17) | data formatting | bytes 12582912
  14.0 1.5 collective-permute-start.14
  16.3 9.8 %all_gather.6 = bf16[16,5120]{1,0:T(8,128)(2,1)S(1)} all-gather(bf16[16,1280]{1,0:T(8,128)(2,1)S(1)} %copy-done.5), channel_id=1, replica_groups=mesh['kv'=4,'tok'=32] {'kv'}, dimensions={1}, use_global_device_ids=true | all-gather | bytes 204800 | tf_op jit(solution)/shard_map/all_gather | solution.py:90
  26.6 4.2 %fusion.21 = bf16[16,640]{1,0:T(8,128)(2,1)S(1)} fusion(bf16[16,5120]{1,0:T(8,128)(2,1)S(1)} %all_gather.6, bf16[5120,640]{1,0:T(8,128)(2,1)} %param.13, f32[640]{0:T(1024)S(1)} %copy-done.8), kind=kOutput, calls=%fused_computation.31 | convolution fusion | flops 104878080 | bytes 6740480 | tf_op jit(solution)/shard_map/dot_general | solution.py:91
  30.9 2.3 %collective-permute-start = (bf16[16,1024]{1,0:T(8,128)(2,1)S(1)}, bf16[16,1024]{1,0:T(8,128)(2,1)S(1)}, u32[]{:S(2)}, u32[]{:S(2)}) collective-permute-start(bf16[16,1024]{1,0:T(8,128)(2,1)S(1)} %concatenate.83), channel_id=1, source_target_pairs={{0,1},{1,0},{2,3},{3,2},{4,5},{5,4},{6,7},{7,6},{8,9},{9,8},{10,11... | collective-permute-start | bytes 98312 | tf_op jit(solution)/shard_map/ppermute | solution.py:77
  35.2 0.7 add_select_fusion
  35.8 0.7 fusion.68
  37.8 1.3 multiply_cosine_fusion.1
  39.3 1.2 compare_and_fusion
  40.5 0.6 constant_dynamic-update-slice_fusion.4
  41.2 1.4 collective-permute-start.1
  42.5 2.6 %collective-permute-start.2 = (bf16[32,1024]{1,0:T(8,128)(2,1)S(1)}, bf16[32,1024]{1,0:T(8,128)(2,1)S(1)}, u32[]{:S(2)}, u32[]{:S(2)}) collective-permute-start(bf16[32,1024]{1,0:T(8,128)(2,1)S(1)} %pad_maximum_fusion.2), channel_id=1, source_target_pairs={{0,4},{1,5},{2,6},{3,7},{4,0},{5,1},{6,2},{7,3},{8,12},{9,13},{10,... | collective-permute-start | bytes 196616 | tf_op jit(solution)/shard_map/ppermute | solution.py:77
  45.1 1.1 collective-permute-start.3
  46.2 0.6 constant_dynamic-update-slice_fusion.3
  46.8 0.6 constant_dynamic-update-slice_fusion.2
  47.5 1.2 collective-permute-done.2
  48.7 0.6 constant_dynamic-update-slice_fusion.1
  49.3 0.7 constant_dynamic-update-slice_fusion
  50.0 1.6 %collective-permute-start.4 = (bf16[128,1024]{1,0:T(8,128)(2,1)}, bf16[128,1024]{1,0:T(8,128)(2,1)}, u32[]{:S(2)}, u32[]{:S(2)}) collective-permute-start(bf16[128,1024]{1,0:T(8,128)(2,1)} %get-tuple-element.36), channel_id=1, source_target_pairs={{0,8},{1,9},{2,10},{3,11},{4,12},{5,13},{6,14},{7,15},{8,16},{9,17... | collective-permute-start | bytes 786440 | tf_op jit(solution)/shard_map/ppermute | solution.py:77
  51.6 0.8 multiply_cosine_fusion.3
  52.4 3.4 %collective-permute-start.5 = (bf16[128,1024]{1,0:T(8,128)(2,1)}, bf16[128,1024]{1,0:T(8,128)(2,1)}, u32[]{:S(2)}, u32[]{:S(2)}) collective-permute-start(bf16[128,1024]{1,0:T(8,128)(2,1)} %get-tuple-element.36), channel_id=1, source_target_pairs={{0,16},{1,17},{2,18},{3,19},{4,20},{5,21},{6,22},{7,23},{8,24},{9,... | collective-permute-start | bytes 786440 | tf_op jit(solution)/shard_map/ppermute | solution.py:77
  55.8 0.7 pad_clamp_fusion.1
  56.5 0.7 collective-permute-start.6
  57.8 2.1 %collective-permute-done.4 = bf16[128,1024]{1,0:T(8,128)(2,1)} collective-permute-done((bf16[128,1024]{1,0:T(8,128)(2,1)}, bf16[128,1024]{1,0:T(8,128)(2,1)}, u32[]{:S(2)}, u32[]{:S(2)}) %collective-permute-start.4) | collective-permute-done | bytes 262176 | tf_op jit(solution)/shard_map/ppermute | solution.py:77
  59.9 1.7 %constant_dynamic-update-slice_fusion.7 = bf16[512,1024]{1,0:T(8,128)(2,1)} fusion(bf16[512,1024]{1,0:T(8,128)(2,1)} %get-tuple-element.37, bf16[128,1024]{1,0:T(8,128)(2,1)} %collective-permute-done.4), kind=kLoop, calls=%fused_computation.83 | loop fusion | bytes 524288
  61.5 4.8 %collective-permute-done.5 = bf16[128,1024]{1,0:T(8,128)(2,1)} collective-permute-done((bf16[128,1024]{1,0:T(8,128)(2,1)}, bf16[128,1024]{1,0:T(8,128)(2,1)}, u32[]{:S(2)}, u32[]{:S(2)}) %collective-permute-start.5) | collective-permute-done | bytes 262176 | tf_op jit(solution)/shard_map/ppermute | solution.py:77
  66.4 1.7 %constant_dynamic-update-slice_fusion.6 = bf16[512,1024]{1,0:T(8,128)(2,1)} fusion(bf16[512,1024]{1,0:T(8,128)(2,1)} %constant_dynamic-update-slice_fusion.7, bf16[128,1024]{1,0:T(8,128)(2,1)} %collective-permute-done.5), kind=kLoop, calls=%fused_computation.82 | loop fusion | bytes 524288
  68.1 1.7 %constant_dynamic-update-slice_fusion.5 = bf16[512,1024]{1,0:T(8,128)(2,1)} fusion(bf16[512,1024]{1,0:T(8,128)(2,1)} %constant_dynamic-update-slice_fusion.6, bf16[128,1024]{1,0:T(8,128)(2,1)} %collective-permute-done.6), kind=kLoop, calls=%fused_computation.81 | loop fusion | bytes 524288 | tf_op jit(solution)/shard_map/concatenate | solution.py:78
  69.7 2.0 %gather_fusion = bf16[16,1024]{1,0:T(8,128)(2,1)S(1)} fusion(bf16[512,1024]{1,0:T(8,128)(2,1)} %constant_dynamic-update-slice_fusion.5, s32[1024]{0:T(1024)S(1)} %pad_clamp_fusion.1), kind=kCustom, calls=%fused_computation | custom fusion | bytes 65600 | tf_op jit(solution)/shard_map/jit(_take)/gather | solution.py:110
  71.7 0.7 broadcast_select_fusion
  72.4 0.6 slice_convert_fusion.1
  73.7 0.8 reshape.477
  74.4 0.7 fusion.97
  75.2 0.7 reshape.471
  75.9 0.8 fusion.78
  76.8 2.4 %scatter_fusion = bf16[2,12288,128]{2,1,0:T(8,128)(2,1)} fusion(bf16[2,12288,128]{2,1,0:T(8,128)(2,1)} %copy.126, s32[16]{0:T(128)} %get-tuple-element.22, bf16[16,2,128]{2,0,1:T(8,128)(2,1)S(1)} %maximum_bitcast_fusion), kind=kCustom, calls=%fused_computation.2 | custom fusion | bytes 24640 | tf_op jit(solution)/shard_map/scatter | solution.py:58
  79.2 1.0 subtract_convert_fusion.1
  80.3 3.5 %fusion.100 = (f32[16,5]{0,1:T(8,128)S(1)}, f32[16,5,12288]{2,0,1:T(8,128)S(1)}) fusion(bf16[2,12288,128]{2,1,0:T(8,128)(2,1)} %scatter_fusion, bf16[16,5,64]{2,0,1:T(8,128)(2,1)S(1)} %get-tuple-element.33, bf16[16,5,64]{2,0,1:T(8,128)(2,1)S(1)} %get-tuple-element.32, pred[16,12288]{1,0:T(8,128)(4,1)S(1)} %fusion.43), kind=kOutput, calls=%fused_computation.192 | convolution fusion | flops 254648240 | bytes 7295296 | tf_op jit(solution)/shard_map/ngd,md->ngm/dot_general | solution.py:34
  83.8 0.8 fusion.7
  84.6 0.9 fusion.34
  85.5 1.8 %collective-permute-start.7 = (bf16[16,640]{1,0:T(8,128)(2,1)S(1)}, bf16[16,640]{1,0:T(8,128)(2,1)S(1)}, u32[]{:S(2)}, u32[]{:S(2)}) collective-permute-start(bf16[16,640]{1,0:T(8,128)(2,1)S(1)} %bitcast.93), channel_id=1, source_target_pairs={{0,1},{1,0},{2,3},{3,2},{4,5},{5,4},{6,7},{7,6},{8,9},{9,8},{10,11... | collective-permute-start | bytes 61448 | tf_op jit(solution)/shard_map/ppermute | solution.py:77
  87.3 0.9 slice_convert_fusion
  88.5 0.7 iota_reduce_fusion
  89.8 0.6 constant_dynamic-update-slice_fusion.18
  90.6 2.6 %collective-permute-start.9 = (bf16[32,640]{1,0:T(8,128)(2,1)S(1)}, bf16[32,640]{1,0:T(8,128)(2,1)S(1)}, u32[]{:S(2)}, u32[]{:S(2)}) collective-permute-start(bf16[32,640]{1,0:T(8,128)(2,1)S(1)} %get-tuple-element.54), channel_id=1, source_target_pairs={{0,4},{1,5},{2,6},{3,7},{4,0},{5,1},{6,2},{7,3},{8,12},{9,13},{10,... | collective-permute-start | bytes 122888 | tf_op jit(solution)/shard_map/ppermute | solution.py:77
  93.2 0.8 collective-permute-start.10
  94.5 0.6 constant_dynamic-update-slice_fusion.17
  96.3 0.6 constant_dynamic-update-slice_fusion.15
  97.4 1.7 %collective-permute-start.12 = (bf16[128,640]{1,0:T(8,128)(2,1)S(1)}, bf16[128,640]{1,0:T(8,128)(2,1)S(1)}, u32[]{:S(2)}, u32[]{:S(2)}) collective-permute-start(bf16[128,640]{1,0:T(8,128)(2,1)S(1)} %get-tuple-element.42), channel_id=1, source_target_pairs={{0,16},{1,17},{2,18},{3,19},{4,20},{5,21},{6,22},{7,23},{8,24},{9,... | collective-permute-start | bytes 491528 | tf_op jit(solution)/shard_map/ppermute | solution.py:77
  99.1 1.7 %collective-permute-start.13 = (bf16[128,640]{1,0:T(8,128)(2,1)S(1)}, bf16[128,640]{1,0:T(8,128)(2,1)S(1)}, u32[]{:S(2)}, u32[]{:S(2)}) collective-permute-start(bf16[128,640]{1,0:T(8,128)(2,1)S(1)} %get-tuple-element.42), channel_id=1, source_target_pairs={{0,24},{1,25},{2,26},{3,27},{4,28},{5,29},{6,30},{7,31},{8,0},{9,1... | collective-permute-start | bytes 491528 | tf_op jit(solution)/shard_map/ppermute | solution.py:77
  100.8 2.8 %maximum_select_fusion = bf16[2,2048,128]{2,1,0:T(8,128)(2,1)} fusion(bf16[2,1024,128]{2,1,0:T(8,128)(2,1)} %collective-permute-done.14, bf16[2,1024,128]{2,1,0:T(8,128)(2,1)} %param.20, pred[]{:T(512)S(6)} %eq.32), kind=kLoop, calls=%fused_computation.37 | loop fusion | flops 4718592 | bytes 2097153 | tf_op jit(solution)/shard_map/jit(_where)/select_n | solution.py:144
  103.7 0.7 constant_dynamic-update-slice_fusion.22
  104.4 0.7 collective-permute-done.12
  105.1 0.7 constant_dynamic-update-slice_fusion.21
  106.2 0.7 constant_dynamic-update-slice_fusion.20
  106.8 1.8 %gather_fusion.1 = bf16[16,640]{1,0:T(8,128)(2,1)S(1)} fusion(bf16[512,640]{1,0:T(8,128)(2,1)} %constant_dynamic-update-slice_fusion.20, s32[1024]{0:T(1024)S(1)} %pad_clamp_fusion), kind=kCustom, calls=%fused_computation.1 | custom fusion | bytes 41024 | tf_op jit(solution)/shard_map/jit(_take)/gather | solution.py:119
  108.6 0.7 broadcast_select_fusion.1
  109.3 2.9 %fusion.18 = f32[256,256]{0,1:T(8,128)S(1)} fusion(bf16[256,5120]{1,0:T(8,128)(2,1)} %all-gather.2.cloned.1.call-done, bf16[640,8,2,128]{3,2,1,0:T(2,128)(2,1)S(1)} %bitcast.86, f32[256]{0:T(256)S(1)} %bitcast.96), kind=kOutput, calls=%fused_computation.29 | convolution fusion | flops 671154176 | bytes 5506048 | tf_op jit(solution)/shard_map/dot_general | solution.py:92
  113.3 3.7 %collective-permute-start.15 = (bf16[2,256,128]{2,1,0:T(8,128)(2,1)S(1)}, bf16[2,256,128]{2,1,0:T(8,128)(2,1)S(1)}, u32[]{:S(2)}, u32[]{:S(2)}) collective-permute-start(bf16[2,256,128]{2,1,0:T(8,128)(2,1)S(1)} %pad_maximum_fusion.1), channel_id=1, source_target_pairs={{0,1},{1,0},{2,3},{3,2},{4,5},{5,4},{6,7},{7,6},{8,9},{9,8},{10,11... | collective-permute-start | bytes 393224 | tf_op jit(solution)/shard_map/ppermute | solution.py:13
  117.0 5.9 %convolution_add_fusion = f32[256,640]{1,0:T(8,128)S(1)} fusion(bf16[256,5120]{1,0:T(8,128)(2,1)} %all-gather.2.cloned.1.call-done, bf16[5120,640]{1,0:T(8,128)(2,1)} %param.13, f32[640]{0:T(1024)S(1)} %copy-done.9), kind=kOutput, calls=%fused_computation.28 | convolution fusion | flops 1677885440 | bytes 9832960 | tf_op jit(solution)/shard_map/dot_general | solution.py:91
  124.2 7.2 %fusion.1 = (f32[256,5]{0,1:T(8,128)S(1)}, f32[256,5,2560]{2,0,1:T(8,128)}) fusion(pred[256,2560]{1,0:T(8,128)(4,1)S(1)} %compare_and_fusion, bf16[2,2048,128]{2,1,0:T(8,128)(2,1)} %maximum_select_fusion, bf16[2,512,128]{2,1,0:T(8,128)(2,1)S(1)} %maximum_select_fusion.1, bf16[256,5,64]{2,0,1:T(8,128)(2,1)S(1)} %get-tuple-element.25, ...), kind=kOutput, calls=%fused_computation.7 | convolution fusion | flops 850656000 | bytes 15406080 | tf_op jit(solution)/shard_map/ngd,md->ngm/dot_general | solution.py:34
  131.4 8.5 %fusion.2 = f32[256,5]{0,1:T(8,128)S(1)} fusion(f32[256,5,2560]{2,0,1:T(8,128)} %get-tuple-element.72, f32[256,5]{0,1:T(8,128)S(1)} %get-tuple-element.71, pred[256,2560]{1,0:T(8,128)(4,1)S(1)} %compare_and_fusion), kind=kLoop, calls=%fused_computation.8 | loop fusion | flops 13105920 | bytes 13772800 | tf_op jit(solution)/shard_map/reduce_sum | solution.py:41
  139.9 7.0 %fusion.40 = bf16[256,5,128]{0,2,1:T(8,128)(2,1)S(1)} fusion(f32[256,5,2560]{2,0,1:T(8,128)} %get-tuple-element.72, f32[256,5]{0,1:T(8,128)S(1)} %get-tuple-element.71, pred[256,2560]{1,0:T(8,128)(4,1)S(1)} %compare_and_fusion, bf16[2,512,128]{2,1,0:T(8,128)(2,1)S(1)} %maximum_select_fusion.1, bf16[2,2048,128]{2,1,0:T(8,128)(2,1)S(1)} %copy-done.1, ...), kind=kOutput, calls=%fused_computation.39 | convolution fusion | flops 853606400 | bytes 15411200 | tf_op jit(solution)/shard_map/ngm,md->ngd/dot_general | solution.py:43
  146.8 0.9 copy.58
  (102 shorter events, 11.6 us)
Async XLA Ops:
  7.2 8.3 %copy-start.16 = (s32[16]{0:T(128)S(1)}, s32[16]{0:T(128)}, u32[]{:S(2)}) copy-start(s32[16]{0:T(128)} %param.18) | copy-start | bytes 196
  7.2 9.1 %copy-start.5 = (bf16[16,1280]{1,0:T(8,128)(2,1)S(1)}, bf16[16,1280]{1,0:T(8,128)(2,1)}, u32[]{:S(2)}) copy-start(bf16[16,1280]{1,0:T(8,128)(2,1)} %param.11) | copy-start | bytes 122884
  7.2 18.9 %copy-start.12 = (f32[2,128]{1,0:T(2,128)S(1)}, f32[2,128]{1,0:T(2,128)}, u32[]{:S(2)}) copy-start(f32[2,128]{1,0:T(2,128)} %param.16) | copy-start | bytes 3076
  7.2 18.9 %copy-start = (bf16[5120,2,128]{2,1,0:T(2,128)(2,1)S(1)}, bf16[5120,2,128]{2,1,0:T(2,128)(2,1)}, u32[]{:S(2)}) copy-start(bf16[5120,2,128]{2,1,0:T(2,128)(2,1)} %param.14) | copy-start | bytes 7864324
  7.2 19.4 %copy-start.8 = (f32[640]{0:T(1024)S(1)}, f32[640]{0:T(1024)}, u32[]{:S(2)}) copy-start(f32[640]{0:T(1024)} %param.15) | copy-start | bytes 7684
  7.2 102.1 %all-gather.2.cloned.1.call-start = ((), (), s32[]{:S(2)}) async-start(), calls=%async_computation | async-start | bytes 3276800 | tf_op jit(solution)/shard_map/all_gather | solution.py:90
  14.0 86.8 %collective-permute-start.14 = (bf16[2,1024,128]{2,1,0:T(8,128)(2,1)}, bf16[2,1024,128]{2,1,0:T(8,128)(2,1)}, u32[]{:S(2)}, u32[]{:S(2)}) collective-permute-start(bf16[2,1024,128]{2,1,0:T(8,128)(2,1)} %param.20), channel_id=1, source_target_pairs={{0,1},{1,0},{2,3},{3,2},{4,5},{5,4},{6,7},{7,6},{8,9},{9,8},{10,11... | collective-permute-start | bytes 1572872 | tf_op jit(solution)/shard_map/ppermute | solution.py:13
  26.6 6.7 %copy-start.17 = (s32[16]{0:T(128)S(1)}, s32[16]{0:T(128)}, u32[]{:S(2)}) copy-start(s32[16]{0:T(128)} %param.21) | copy-start | bytes 196
  26.6 9.9 %copy-start.14 = (s32[16]{0:T(128)S(1)}, s32[16]{0:T(128)}, u32[]{:S(2)}) copy-start(s32[16]{0:T(128)} %param.19) | copy-start | bytes 196
  30.9 10.2 %collective-permute-start = (bf16[16,1024]{1,0:T(8,128)(2,1)S(1)}, bf16[16,1024]{1,0:T(8,128)(2,1)S(1)}, u32[]{:S(2)}, u32[]{:S(2)}) collective-permute-start(bf16[16,1024]{1,0:T(8,128)(2,1)S(1)} %concatenate.83), channel_id=1, source_target_pairs={{0,1},{1,0},{2,3},{3,2},{4,5},{5,4},{6,7},{7,6},{8,9},{9,8},{10,11... | collective-permute-start | bytes 98312 | tf_op jit(solution)/shard_map/ppermute | solution.py:77
  33.3 5.8 %copy-start.6 = (f32[64]{0:T(128)}, f32[64]{0:T(128)S(1)}, u32[]{:S(2)}) copy-start(f32[64]{0:T(128)S(1)} %negate_power_fusion) | copy-start | bytes 772
  34.6 4.5 %copy-start.10 = (f32[256]{0:T(256)}, f32[256]{0:T(256)S(1)}, u32[]{:S(2)}) copy-start(f32[256]{0:T(256)S(1)} %fusion.87) | copy-start | bytes 3076
  41.2 5.7 %collective-permute-start.1 = (bf16[32,1024]{1,0:T(8,128)(2,1)S(1)}, bf16[32,1024]{1,0:T(8,128)(2,1)S(1)}, u32[]{:S(2)}, u32[]{:S(2)}) collective-permute-start(bf16[32,1024]{1,0:T(8,128)(2,1)S(1)} %pad_maximum_fusion.2), channel_id=1, source_target_pairs={{0,2},{1,3},{2,4},{3,5},{4,6},{5,7},{6,0},{7,1},{8,10},{9,11},{10,... | collective-permute-start | bytes 196616 | tf_op jit(solution)/shard_map/ppermute | solution.py:77
  42.5 6.2 %collective-permute-start.2 = (bf16[32,1024]{1,0:T(8,128)(2,1)S(1)}, bf16[32,1024]{1,0:T(8,128)(2,1)S(1)}, u32[]{:S(2)}, u32[]{:S(2)}) collective-permute-start(bf16[32,1024]{1,0:T(8,128)(2,1)S(1)} %pad_maximum_fusion.2), channel_id=1, source_target_pairs={{0,4},{1,5},{2,6},{3,7},{4,0},{5,1},{6,2},{7,3},{8,12},{9,13},{10,... | collective-permute-start | bytes 196616 | tf_op jit(solution)/shard_map/ppermute | solution.py:77
  45.1 4.2 %collective-permute-start.3 = (bf16[32,1024]{1,0:T(8,128)(2,1)S(1)}, bf16[32,1024]{1,0:T(8,128)(2,1)S(1)}, u32[]{:S(2)}, u32[]{:S(2)}) collective-permute-start(bf16[32,1024]{1,0:T(8,128)(2,1)S(1)} %pad_maximum_fusion.2), channel_id=1, source_target_pairs={{0,6},{1,7},{2,0},{3,1},{4,2},{5,3},{6,4},{7,5},{8,14},{9,15},{10,... | collective-permute-start | bytes 196616 | tf_op jit(solution)/shard_map/ppermute | solution.py:77
  50.0 9.9 %collective-permute-start.4 = (bf16[128,1024]{1,0:T(8,128)(2,1)}, bf16[128,1024]{1,0:T(8,128)(2,1)}, u32[]{:S(2)}, u32[]{:S(2)}) collective-permute-start(bf16[128,1024]{1,0:T(8,128)(2,1)} %get-tuple-element.36), channel_id=1, source_target_pairs={{0,8},{1,9},{2,10},{3,11},{4,12},{5,13},{6,14},{7,15},{8,16},{9,17... | collective-permute-start | bytes 786440 | tf_op jit(solution)/shard_map/ppermute | solution.py:77
  52.4 14.0 %collective-permute-start.5 = (bf16[128,1024]{1,0:T(8,128)(2,1)}, bf16[128,1024]{1,0:T(8,128)(2,1)}, u32[]{:S(2)}, u32[]{:S(2)}) collective-permute-start(bf16[128,1024]{1,0:T(8,128)(2,1)} %get-tuple-element.36), channel_id=1, source_target_pairs={{0,16},{1,17},{2,18},{3,19},{4,20},{5,21},{6,22},{7,23},{8,24},{9,... | collective-permute-start | bytes 786440 | tf_op jit(solution)/shard_map/ppermute | solution.py:77
  56.5 11.6 %collective-permute-start.6 = (bf16[128,1024]{1,0:T(8,128)(2,1)}, bf16[128,1024]{1,0:T(8,128)(2,1)}, u32[]{:S(2)}, u32[]{:S(2)}) collective-permute-start(bf16[128,1024]{1,0:T(8,128)(2,1)} %get-tuple-element.36), channel_id=1, source_target_pairs={{0,24},{1,25},{2,26},{3,27},{4,28},{5,29},{6,30},{7,31},{8,0},{9,1... | collective-permute-start | bytes 786440 | tf_op jit(solution)/shard_map/ppermute | solution.py:77
  79.2 5.4 %slice-start = ((s8[6291456]{0:T(1024)(128)(4,1)}), s8[4194304]{0:T(1024)(128)(4,1)S(1)}, s32[]{:S(2)}) async-start(s8[6291456]{0:T(1024)(128)(4,1)} %bitcast.83), calls=%async_computation.1 | async-start | bytes 8388608
  80.3 4.3 %slice-start.1 = ((s8[6291456]{0:T(1024)(128)(4,1)}), s8[2097152]{0:T(1024)(128)(4,1)S(1)}, s32[]{:S(2)}) async-start(s8[6291456]{0:T(1024)(128)(4,1)} %bitcast.83), calls=%async_computation.2 | async-start | bytes 4194304
  84.6 3.9 %copy-start.15 = (s32[16]{0:T(128)S(1)}, s32[16]{0:T(128)}, u32[]{:S(2)}) copy-start(s32[16]{0:T(128)} %iota_add_fusion.1) | copy-start | bytes 196
  85.5 23.8 %copy-start.13 = (f32[2,128]{1,0:T(2,128)S(1)}, f32[2,128]{1,0:T(2,128)}, u32[]{:S(2)}) copy-start(f32[2,128]{1,0:T(2,128)} %param.16) | copy-start | bytes 3076
  85.5 4.3 %collective-permute-start.7 = (bf16[16,640]{1,0:T(8,128)(2,1)S(1)}, bf16[16,640]{1,0:T(8,128)(2,1)S(1)}, u32[]{:S(2)}, u32[]{:S(2)}) collective-permute-start(bf16[16,640]{1,0:T(8,128)(2,1)S(1)} %bitcast.93), channel_id=1, source_target_pairs={{0,1},{1,0},{2,3},{3,2},{4,5},{5,4},{6,7},{7,6},{8,9},{9,8},{10,11... | collective-permute-start | bytes 61448 | tf_op jit(solution)/shard_map/ppermute | solution.py:77
  90.4 4.1 %collective-permute-start.8 = (bf16[32,640]{1,0:T(8,128)(2,1)S(1)}, bf16[32,640]{1,0:T(8,128)(2,1)S(1)}, u32[]{:S(2)}, u32[]{:S(2)}) collective-permute-start(bf16[32,640]{1,0:T(8,128)(2,1)S(1)} %get-tuple-element.54), channel_id=1, source_target_pairs={{0,2},{1,3},{2,4},{3,5},{4,6},{5,7},{6,0},{7,1},{8,10},{9,11},{10,... | collective-permute-start | bytes 122888 | tf_op jit(solution)/shard_map/ppermute | solution.py:77
  90.6 4.8 %collective-permute-start.9 = (bf16[32,640]{1,0:T(8,128)(2,1)S(1)}, bf16[32,640]{1,0:T(8,128)(2,1)S(1)}, u32[]{:S(2)}, u32[]{:S(2)}) collective-permute-start(bf16[32,640]{1,0:T(8,128)(2,1)S(1)} %get-tuple-element.54), channel_id=1, source_target_pairs={{0,4},{1,5},{2,6},{3,7},{4,0},{5,1},{6,2},{7,3},{8,12},{9,13},{10,... | collective-permute-start | bytes 122888 | tf_op jit(solution)/shard_map/ppermute | solution.py:77
  93.2 3.1 %collective-permute-start.10 = (bf16[32,640]{1,0:T(8,128)(2,1)S(1)}, bf16[32,640]{1,0:T(8,128)(2,1)S(1)}, u32[]{:S(2)}, u32[]{:S(2)}) collective-permute-start(bf16[32,640]{1,0:T(8,128)(2,1)S(1)} %get-tuple-element.54), channel_id=1, source_target_pairs={{0,6},{1,7},{2,0},{3,1},{4,2},{5,3},{6,4},{7,5},{8,14},{9,15},{10,... | collective-permute-start | bytes 122888 | tf_op jit(solution)/shard_map/ppermute | solution.py:77
  96.9 6.8 %collective-permute-start.11 = (bf16[128,640]{1,0:T(8,128)(2,1)S(1)}, bf16[128,640]{1,0:T(8,128)(2,1)S(1)}, u32[]{:S(2)}, u32[]{:S(2)}) collective-permute-start(bf16[128,640]{1,0:T(8,128)(2,1)S(1)} %get-tuple-element.42), channel_id=1, source_target_pairs={{0,8},{1,9},{2,10},{3,11},{4,12},{5,13},{6,14},{7,15},{8,16},{9,17... | collective-permute-start | bytes 491528 | tf_op jit(solution)/shard_map/ppermute | solution.py:77
  97.4 7.7 %collective-permute-start.12 = (bf16[128,640]{1,0:T(8,128)(2,1)S(1)}, bf16[128,640]{1,0:T(8,128)(2,1)S(1)}, u32[]{:S(2)}, u32[]{:S(2)}) collective-permute-start(bf16[128,640]{1,0:T(8,128)(2,1)S(1)} %get-tuple-element.42), channel_id=1, source_target_pairs={{0,16},{1,17},{2,18},{3,19},{4,20},{5,21},{6,22},{7,23},{8,24},{9,... | collective-permute-start | bytes 491528 | tf_op jit(solution)/shard_map/ppermute | solution.py:77
  99.1 7.1 %collective-permute-start.13 = (bf16[128,640]{1,0:T(8,128)(2,1)S(1)}, bf16[128,640]{1,0:T(8,128)(2,1)S(1)}, u32[]{:S(2)}, u32[]{:S(2)}) collective-permute-start(bf16[128,640]{1,0:T(8,128)(2,1)S(1)} %get-tuple-element.42), channel_id=1, source_target_pairs={{0,24},{1,25},{2,26},{3,27},{4,28},{5,29},{6,30},{7,31},{8,0},{9,1... | collective-permute-start | bytes 491528 | tf_op jit(solution)/shard_map/ppermute | solution.py:77
  105.8 6.8 %copy-start.7 = (f32[64]{0:T(128)S(1)}, f32[64]{0:T(128)}, u32[]{:S(2)}) copy-start(f32[64]{0:T(128)} %copy-done.6) | copy-start | bytes 772
  105.8 6.8 %copy-start.11 = (f32[256]{0:T(256)S(1)}, f32[256]{0:T(256)}, u32[]{:S(2)}) copy-start(f32[256]{0:T(256)} %copy-done.10) | copy-start | bytes 3076
  109.3 7.7 %copy-start.9 = (f32[640]{0:T(1024)S(1)}, f32[640]{0:T(1024)}, u32[]{:S(2)}) copy-start(f32[640]{0:T(1024)} %param.15) | copy-start | bytes 7684
  113.3 9.6 %copy-start.4 = (bf16[2,256,128]{2,1,0:T(8,128)(2,1)}, bf16[2,256,128]{2,1,0:T(8,128)(2,1)S(1)}, u32[]{:S(2)}) copy-start(bf16[2,256,128]{2,1,0:T(8,128)(2,1)S(1)} %pad_maximum_fusion.1) | copy-start | bytes 393220
  113.3 10.7 %collective-permute-start.15 = (bf16[2,256,128]{2,1,0:T(8,128)(2,1)S(1)}, bf16[2,256,128]{2,1,0:T(8,128)(2,1)S(1)}, u32[]{:S(2)}, u32[]{:S(2)}) collective-permute-start(bf16[2,256,128]{2,1,0:T(8,128)(2,1)S(1)} %pad_maximum_fusion.1), channel_id=1, source_target_pairs={{0,1},{1,0},{2,3},{3,2},{4,5},{5,4},{6,7},{7,6},{8,9},{9,8},{10,11... | collective-permute-start | bytes 393224 | tf_op jit(solution)/shard_map/ppermute | solution.py:13
  122.9 0.9 copy-start.2
  122.9 1.0 copy-start.3
  131.4 8.5 %copy-start.1 = (bf16[2,2048,128]{2,1,0:T(8,128)(2,1)S(1)}, bf16[2,2048,128]{2,1,0:T(8,128)(2,1)}, u32[]{:S(2)}) copy-start(bf16[2,2048,128]{2,1,0:T(8,128)(2,1)} %maximum_select_fusion) | copy-start | bytes 3145732
Sparse Core Ops, SparseCore 0:
  14.1 38.1 all-gather.1

commit v4 on v3

--- a/solution.py
+++ b/solution.py
@@ -86,8 +86,16 @@
     return ((z * 4 + y) * 2 + core) * rows
 
 
-def project(rows, w_query, kv_weight, b_query, kv_bias):
-    cols = lax.all_gather(rows, "kv", axis=1, tiled=True)
+def ring_columns(rows):
+    count = lax.axis_size("kv")
+    place = lax.axis_index("kv")
+    parts = [rows] + [lax.ppermute(rows, "kv", [(i, (i + s) % count) for i in range(count)]) for s in range(1, count)]
+    ordered = jnp.take(jnp.stack(parts), (place - jnp.arange(count)) % count, axis=0)
+    return jnp.transpose(ordered, (1, 0, 2)).reshape(rows.shape[0], count * rows.shape[1])
+
+
+def project(rows, w_query, kv_weight, b_query, kv_bias, ring=False):
+    cols = ring_columns(rows) if ring else lax.all_gather(rows, "kv", axis=1, tiled=True)
     query = jnp.dot(cols, w_query, preferred_element_type=jnp.float32) + b_query
     keyval = jnp.dot(cols, kv_weight, preferred_element_type=jnp.float32) + kv_bias
     return query, keyval
@@ -99,7 +107,7 @@
     kv_width = w_keyval.shape[2]
     kv_weight = w_keyval.reshape(w_keyval.shape[0], 2 * kv_width)
     kv_bias = b_keyval.reshape(2 * kv_width)
-    dec_q, dec_kv = project(dec_tokens, w_query, kv_weight, b_query, kv_bias)
+    dec_q, dec_kv = project(dec_tokens, w_query, kv_weight, b_query, kv_bias, ring=True)
     tok_place = lax.axis_index("tok")
     ids = jnp.stack([owner_slots // dec_count, owner_slots % dec_count], axis=1).astype(jnp.bfloat16)
     used = q_width + 2 * kv_width + 2

time: 155 us -> 155 us (level)
  blocking collectives: 9.84 us -> 0 us
  starting transfers between devices: 27.6 us -> 31.4 us
  other arithmetic: 27.3 us -> 29.9 us
  local copies, waits for them, and re-layouts: 32.2 us -> 34.3 us
    all_gather x1 -> x0, blocking collectives: 9.84 us -> none  [project(): cols = lax.all_gather(rows, 'kv', axis=1, tiled=True)]
    ppermute x0 -> x3, starting transfers between devices: none -> 5.63 us  [ring_columns(): lax.ppermute(rows, 'kv', [(i, (i + s) % count) for i in range(count)])]
    gather x0 -> x1, local copies, waits for them, and re-layouts: none -> 2.13 us  [ring_columns(): jnp.take(jnp.stack(parts), (place - jnp.arange(count)) % count, axis=0)]
    ppermute x14, starting transfers between devices: 22.4 us -> 20.3 us  [tree_gather(): parts.append(lax.ppermute(buffer, 'tok', pairs))]
    unnamed x60 -> x58, local copies, waits for them, and re-layouts: 18.3 us -> 18.3 us
  transfers between devices with their start and end apart: 17 -> 20, of which waited for: 9 -> 10; matrix products, arithmetic and copies ran while one was open for 37% -> 40% of each run, Pallas kernels for 0% -> 0%
where the time goes in v4:
time: 155 us; the launch traced here: 154 us
  local copies, waits for them, and re-layouts  34.3 us (22%)
  matrix products  32.4 us (21%)
  starting transfers between devices  31.4 us (20%)
  other arithmetic  29.9 us (19%)
  between operations  15.2 us (10%)
  waiting for transfers between devices  10.6 us (7%)
    ppermute x14, starting transfers between devices, tree_gather(): parts.append(lax.ppermute(buffer, 'tok', pairs))  20.3 us
    unnamed x58, local copies, waits for them, and re-layouts  18.3 us
    dot_general x2, matrix products, head_scores(): jnp.einsum('ngd,md->ngm', shaped, key_rows, preferred_element_type=jnp.fl...  10.8 us
    ppermute x14, waiting for transfers between devices, tree_gather(): parts.append(lax.ppermute(buffer, 'tok', pairs))  10.6 us
    dot_general x2, matrix products, project(): query = jnp.dot(cols, w_query, preferred_element_type=jnp.float32) + b_query  9.72 us
    reduce_sum x2, other arithmetic, head_mix(): totals = jnp.sum(powers, axis=-1)  9.29 us
    dot_general x2, matrix products, head_mix(): jnp.einsum('ngm,md->ngd', weights, value_rows, preferred_element_type=jnp...  7.83 us
    ppermute x3, starting transfers between devices, ring_columns(): lax.ppermute(rows, 'kv', [(i, (i + s) % count) for i in range(count)])  5.63 us
  transfers between devices with their start and end apart: 20, of which 10 were waited for; matrix products, arithmetic and copies ran while one was open for 40% of the time, Pallas kernels for 0%

profile of v4, /device:TPU:1, one launch (start us, length us, event | category | flops | bytes accessed | tf_op | source)
XLA Modules:
  0.0 153.8 jit_solution(10626463034952756302)
XLA Ops:
  7.3 6.7 %copy.129 = bf16[2,12288,128]{2,1,0:T(8,128)(2,1)} copy(bf16[2,12288,128]{2,1,0:T(8,128)(2,1)} %param.17) | data formatting | bytes 12582912
  14.0 2.0 %collective-permute-start = (bf16[16,1280]{1,0:T(8,128)(2,1)S(1)}, bf16[16,1280]{1,0:T(8,128)(2,1)}, u32[]{:S(2)}, u32[]{:S(2)}) collective-permute-start(bf16[16,1280]{1,0:T(8,128)(2,1)S(1)} %copy-done.5), channel_id=1, source_target_pairs={{0,32},{32,64},{64,96},{96,0},{1,33},{33,65},{65,97},{97,1},{2,34}... | collective-permute-start | bytes 122888 | tf_op jit(solution)/shard_map/ppermute | solution.py:92
  16.0 2.5 %collective-permute-start.1 = (bf16[16,1280]{1,0:T(8,128)(2,1)S(1)}, bf16[16,1280]{1,0:T(8,128)(2,1)}, u32[]{:S(2)}, u32[]{:S(2)}) collective-permute-start(bf16[16,1280]{1,0:T(8,128)(2,1)S(1)} %copy-done.5), channel_id=1, source_target_pairs={{0,64},{32,96},{64,0},{96,32},{1,65},{33,97},{65,1},{97,33},{2,66}... | collective-permute-start | bytes 122888 | tf_op jit(solution)/shard_map/ppermute | solution.py:92
  18.4 1.2 collective-permute-start.2
  19.6 1.6 %collective-permute-start.17 = (bf16[2,1024,128]{2,1,0:T(8,128)(2,1)}, bf16[2,1024,128]{2,1,0:T(8,128)(2,1)}, u32[]{:S(2)}, u32[]{:S(2)}) collective-permute-start(bf16[2,1024,128]{2,1,0:T(8,128)(2,1)} %param.20), channel_id=1, source_target_pairs={{0,1},{1,0},{2,3},{3,2},{4,5},{5,4},{6,7},{7,6},{8,9},{9,8},{10,11... | collective-permute-start | bytes 1572872 | tf_op jit(solution)/shard_map/ppermute | solution.py:13
  23.1 0.6 add_select_fusion
  23.8 0.7 fusion.68
  25.8 1.3 multiply_cosine_fusion.1
  27.1 0.6 compare_and_fusion.1
  28.0 1.2 compare_and_fusion
  29.4 1.5 pad_maximum_fusion.1
  30.9 2.1 %gather_fusion = bf16[4,16,1280]{2,1,0:T(8,128)(2,1)} fusion(bf16[4,16,1280]{2,1,0:T(8,128)(2,1)} %pad_maximum_fusion.1, s32[1024]{0:T(1024)S(1)} %pad_clamp_fusion.2), kind=kCustom, calls=%fused_computation | custom fusion | bytes 327696 | tf_op jit(solution)/shard_map/jit(_take)/gather | solution.py:93
  33.1 1.0 select_bitcast_fusion
  34.1 1.1 fusion.25
  35.2 3.9 %fusion.21 = bf16[16,640]{1,0:T(8,128)(2,1)S(1)} fusion(bf16[16,5120]{1,0:T(8,128)(2,1)S(1)} %bitcast.99, bf16[5120,640]{1,0:T(8,128)(2,1)} %param.13, f32[640]{0:T(1024)S(1)} %copy-done.8), kind=kOutput, calls=%fused_computation.32 | convolution fusion | flops 104878080 | bytes 6740480 | tf_op jit(solution)/shard_map/dot_general | solution.py:99
  40.4 1.3 collective-permute-start.4
  41.7 2.6 %collective-permute-start.5 = (bf16[32,1024]{1,0:T(8,128)(2,1)S(1)}, bf16[32,1024]{1,0:T(8,128)(2,1)S(1)}, u32[]{:S(2)}, u32[]{:S(2)}) collective-permute-start(bf16[32,1024]{1,0:T(8,128)(2,1)S(1)} %pad_maximum_fusion.3), channel_id=1, source_target_pairs={{0,4},{1,5},{2,6},{3,7},{4,0},{5,1},{6,2},{7,3},{8,12},{9,13},{10,... | collective-permute-start | bytes 196616 | tf_op jit(solution)/shard_map/ppermute | solution.py:77
  44.4 1.1 collective-permute-start.6
  46.1 0.7 constant_dynamic-update-slice_fusion.2
  46.7 1.1 collective-permute-done.5
  47.8 0.6 constant_dynamic-update-slice_fusion.1
  48.4 0.7 constant_dynamic-update-slice_fusion
  49.1 1.7 %collective-permute-start.7 = (bf16[128,1024]{1,0:T(8,128)(2,1)}, bf16[128,1024]{1,0:T(8,128)(2,1)}, u32[]{:S(2)}, u32[]{:S(2)}) collective-permute-start(bf16[128,1024]{1,0:T(8,128)(2,1)} %get-tuple-element.36), channel_id=1, source_target_pairs={{0,8},{1,9},{2,10},{3,11},{4,12},{5,13},{6,14},{7,15},{8,16},{9,17... | collective-permute-start | bytes 786440 | tf_op jit(solution)/shard_map/ppermute | solution.py:77
  50.8 0.8 multiply_cosine_fusion.3
  51.6 3.4 %collective-permute-start.8 = (bf16[128,1024]{1,0:T(8,128)(2,1)}, bf16[128,1024]{1,0:T(8,128)(2,1)}, u32[]{:S(2)}, u32[]{:S(2)}) collective-permute-start(bf16[128,1024]{1,0:T(8,128)(2,1)} %get-tuple-element.36), channel_id=1, source_target_pairs={{0,16},{1,17},{2,18},{3,19},{4,20},{5,21},{6,22},{7,23},{8,24},{9,... | collective-permute-start | bytes 786440 | tf_op jit(solution)/shard_map/ppermute | solution.py:77
  54.9 0.7 pad_clamp_fusion.1
  55.6 0.8 collective-permute-start.9
  56.9 1.9 %collective-permute-done.7 = bf16[128,1024]{1,0:T(8,128)(2,1)} collective-permute-done((bf16[128,1024]{1,0:T(8,128)(2,1)}, bf16[128,1024]{1,0:T(8,128)(2,1)}, u32[]{:S(2)}, u32[]{:S(2)}) %collective-permute-start.7) | collective-permute-done | bytes 262176 | tf_op jit(solution)/shard_map/ppermute | solution.py:77
  58.8 1.7 %constant_dynamic-update-slice_fusion.7 = bf16[512,1024]{1,0:T(8,128)(2,1)} fusion(bf16[512,1024]{1,0:T(8,128)(2,1)} %get-tuple-element.37, bf16[128,1024]{1,0:T(8,128)(2,1)} %collective-permute-done.7), kind=kLoop, calls=%fused_computation.86 | loop fusion | bytes 524288
  60.5 4.8 %collective-permute-done.8 = bf16[128,1024]{1,0:T(8,128)(2,1)} collective-permute-done((bf16[128,1024]{1,0:T(8,128)(2,1)}, bf16[128,1024]{1,0:T(8,128)(2,1)}, u32[]{:S(2)}, u32[]{:S(2)}) %collective-permute-start.8) | collective-permute-done | bytes 262176 | tf_op jit(solution)/shard_map/ppermute | solution.py:77
  65.3 1.7 %constant_dynamic-update-slice_fusion.6 = bf16[512,1024]{1,0:T(8,128)(2,1)} fusion(bf16[512,1024]{1,0:T(8,128)(2,1)} %constant_dynamic-update-slice_fusion.7, bf16[128,1024]{1,0:T(8,128)(2,1)} %collective-permute-done.8), kind=kLoop, calls=%fused_computation.85 | loop fusion | bytes 524288
  67.0 1.7 %constant_dynamic-update-slice_fusion.5 = bf16[512,1024]{1,0:T(8,128)(2,1)} fusion(bf16[512,1024]{1,0:T(8,128)(2,1)} %constant_dynamic-update-slice_fusion.6, bf16[128,1024]{1,0:T(8,128)(2,1)} %collective-permute-done.9), kind=kLoop, calls=%fused_computation.84 | loop fusion | bytes 524288 | tf_op jit(solution)/shard_map/concatenate | solution.py:78
  68.7 2.0 %gather_fusion.1 = bf16[16,1024]{1,0:T(8,128)(2,1)S(1)} fusion(bf16[512,1024]{1,0:T(8,128)(2,1)} %constant_dynamic-update-slice_fusion.5, s32[1024]{0:T(1024)S(1)} %pad_clamp_fusion.1), kind=kCustom, calls=%fused_computation.1 | custom fusion | bytes 65600 | tf_op jit(solution)/shard_map/jit(_take)/gather | solution.py:118
  70.7 0.7 broadcast_select_fusion
  71.4 0.6 slice_convert_fusion.1
  72.6 0.8 reshape.535
  73.4 0.7 fusion.100
  74.1 0.7 reshape.529
  74.9 0.8 fusion.78
  75.8 2.4 %scatter_fusion = bf16[2,12288,128]{2,1,0:T(8,128)(2,1)} fusion(bf16[2,12288,128]{2,1,0:T(8,128)(2,1)} %copy.129, s32[16]{0:T(128)} %get-tuple-element.22, bf16[16,2,128]{2,0,1:T(8,128)(2,1)S(1)} %maximum_bitcast_fusion), kind=kCustom, calls=%fused_computation.3 | custom fusion | bytes 24640 | tf_op jit(solution)/shard_map/scatter | solution.py:58
  78.2 1.0 subtract_convert_fusion.1
  79.3 3.5 %fusion.103 = (f32[16,5]{0,1:T(8,128)S(1)}, f32[16,5,12288]{2,0,1:T(8,128)S(1)}) fusion(bf16[2,12288,128]{2,1,0:T(8,128)(2,1)} %scatter_fusion, bf16[16,5,64]{2,0,1:T(8,128)(2,1)S(1)} %get-tuple-element.33, bf16[16,5,64]{2,0,1:T(8,128)(2,1)S(1)} %get-tuple-element.32, pred[16,12288]{1,0:T(8,128)(4,1)S(1)} %fusion.43), kind=kOutput, calls=%fused_computation.208 | convolution fusion | flops 254648240 | bytes 7295296 | tf_op jit(solution)/shard_map/ngd,md->ngm/dot_general | solution.py:34
  82.8 0.8 fusion.7
  83.6 0.9 fusion.34
  84.5 2.0 %collective-permute-start.10 = (bf16[16,640]{1,0:T(8,128)(2,1)S(1)}, bf16[16,640]{1,0:T(8,128)(2,1)S(1)}, u32[]{:S(2)}, u32[]{:S(2)}) collective-permute-start(bf16[16,640]{1,0:T(8,128)(2,1)S(1)} %bitcast.106), channel_id=1, source_target_pairs={{0,1},{1,0},{2,3},{3,2},{4,5},{5,4},{6,7},{7,6},{8,9},{9,8},{10,11... | collective-permute-start | bytes 61448 | tf_op jit(solution)/shard_map/ppermute | solution.py:77
  86.4 0.9 slice_convert_fusion
  87.6 0.7 iota_reduce_fusion
  89.8 2.6 %collective-permute-start.12 = (bf16[32,640]{1,0:T(8,128)(2,1)S(1)}, bf16[32,640]{1,0:T(8,128)(2,1)S(1)}, u32[]{:S(2)}, u32[]{:S(2)}) collective-permute-start(bf16[32,640]{1,0:T(8,128)(2,1)S(1)} %get-tuple-element.54), channel_id=1, source_target_pairs={{0,4},{1,5},{2,6},{3,7},{4,0},{5,1},{6,2},{7,3},{8,12},{9,13},{10,... | collective-permute-start | bytes 122888 | tf_op jit(solution)/shard_map/ppermute | solution.py:77
  92.5 0.8 collective-permute-start.13
  96.6 1.6 %collective-permute-start.15 = (bf16[128,640]{1,0:T(8,128)(2,1)S(1)}, bf16[128,640]{1,0:T(8,128)(2,1)S(1)}, u32[]{:S(2)}, u32[]{:S(2)}) collective-permute-start(bf16[128,640]{1,0:T(8,128)(2,1)S(1)} %get-tuple-element.42), channel_id=1, source_target_pairs={{0,16},{1,17},{2,18},{3,19},{4,20},{5,21},{6,22},{7,23},{8,24},{9,... | collective-permute-start | bytes 491528 | tf_op jit(solution)/shard_map/ppermute | solution.py:77
  98.3 1.7 %collective-permute-start.16 = (bf16[128,640]{1,0:T(8,128)(2,1)S(1)}, bf16[128,640]{1,0:T(8,128)(2,1)S(1)}, u32[]{:S(2)}, u32[]{:S(2)}) collective-permute-start(bf16[128,640]{1,0:T(8,128)(2,1)S(1)} %get-tuple-element.42), channel_id=1, source_target_pairs={{0,24},{1,25},{2,26},{3,27},{4,28},{5,29},{6,30},{7,31},{8,0},{9,1... | collective-permute-start | bytes 491528 | tf_op jit(solution)/shard_map/ppermute | solution.py:77
  100.0 2.8 %maximum_select_fusion = bf16[2,2048,128]{2,1,0:T(8,128)(2,1)} fusion(bf16[2,1024,128]{2,1,0:T(8,128)(2,1)} %collective-permute-done.17, bf16[2,1024,128]{2,1,0:T(8,128)(2,1)} %param.20, pred[]{:T(512)S(6)} %eq.34), kind=kLoop, calls=%fused_computation.38 | loop fusion | flops 4718592 | bytes 2097153 | tf_op jit(solution)/shard_map/jit(_where)/select_n | solution.py:152
  103.0 0.7 constant_dynamic-update-slice_fusion.22
  104.2 0.7 constant_dynamic-update-slice_fusion.21
  105.3 0.7 constant_dynamic-update-slice_fusion.20
  105.9 1.8 %gather_fusion.2 = bf16[16,640]{1,0:T(8,128)(2,1)S(1)} fusion(bf16[512,640]{1,0:T(8,128)(2,1)} %constant_dynamic-update-slice_fusion.20, s32[1024]{0:T(1024)S(1)} %pad_clamp_fusion), kind=kCustom, calls=%fused_computation.2 | custom fusion | bytes 41024 | tf_op jit(solution)/shard_map/jit(_take)/gather | solution.py:127
  107.7 0.7 broadcast_select_fusion.1
  108.4 2.9 %fusion.18 = f32[256,256]{0,1:T(8,128)S(1)} fusion(bf16[256,5120]{1,0:T(8,128)(2,1)} %all-gather.2.cloned.1.call-done, bf16[640,8,2,128]{3,2,1,0:T(2,128)(2,1)S(1)} %bitcast.96, f32[256]{0:T(256)S(1)} %bitcast.109), kind=kOutput, calls=%fused_computation.30 | convolution fusion | flops 671154176 | bytes 5506048 | tf_op jit(solution)/shard_map/dot_general | solution.py:100
  112.4 3.8 %collective-permute-start.18 = (bf16[2,256,128]{2,1,0:T(8,128)(2,1)S(1)}, bf16[2,256,128]{2,1,0:T(8,128)(2,1)S(1)}, u32[]{:S(2)}, u32[]{:S(2)}) collective-permute-start(bf16[2,256,128]{2,1,0:T(8,128)(2,1)S(1)} %pad_maximum_fusion.2), channel_id=1, source_target_pairs={{0,1},{1,0},{2,3},{3,2},{4,5},{5,4},{6,7},{7,6},{8,9},{9,8},{10,11... | collective-permute-start | bytes 393224 | tf_op jit(solution)/shard_map/ppermute | solution.py:13
  116.2 5.9 %convolution_add_fusion = f32[256,640]{1,0:T(8,128)S(1)} fusion(bf16[256,5120]{1,0:T(8,128)(2,1)} %all-gather.2.cloned.1.call-done, bf16[5120,640]{1,0:T(8,128)(2,1)} %param.13, f32[640]{0:T(1024)S(1)} %copy-done.9), kind=kOutput, calls=%fused_computation.29 | convolution fusion | flops 1677885440 | bytes 9832960 | tf_op jit(solution)/shard_map/dot_general | solution.py:99
  123.4 7.2 %fusion.1 = (f32[256,5]{0,1:T(8,128)S(1)}, f32[256,5,2560]{2,0,1:T(8,128)}) fusion(pred[256,2560]{1,0:T(8,128)(4,1)S(1)} %compare_and_fusion, bf16[2,2048,128]{2,1,0:T(8,128)(2,1)} %maximum_select_fusion, bf16[2,512,128]{2,1,0:T(8,128)(2,1)S(1)} %maximum_select_fusion.1, bf16[256,5,64]{2,0,1:T(8,128)(2,1)S(1)} %get-tuple-element.25, ...), kind=kOutput, calls=%fused_computation.8 | convolution fusion | flops 850656000 | bytes 15406080 | tf_op jit(solution)/shard_map/ngd,md->ngm/dot_general | solution.py:34
  130.6 8.5 %fusion.2 = f32[256,5]{0,1:T(8,128)S(1)} fusion(f32[256,5,2560]{2,0,1:T(8,128)} %get-tuple-element.72, f32[256,5]{0,1:T(8,128)S(1)} %get-tuple-element.71, pred[256,2560]{1,0:T(8,128)(4,1)S(1)} %compare_and_fusion), kind=kLoop, calls=%fused_computation.9 | loop fusion | flops 13105920 | bytes 13772800 | tf_op jit(solution)/shard_map/reduce_sum | solution.py:41
  139.1 7.0 %fusion.40 = bf16[256,5,128]{0,2,1:T(8,128)(2,1)S(1)} fusion(f32[256,5,2560]{2,0,1:T(8,128)} %get-tuple-element.72, f32[256,5]{0,1:T(8,128)S(1)} %get-tuple-element.71, pred[256,2560]{1,0:T(8,128)(4,1)S(1)} %compare_and_fusion, bf16[2,512,128]{2,1,0:T(8,128)(2,1)S(1)} %maximum_select_fusion.1, bf16[2,2048,128]{2,1,0:T(8,128)(2,1)S(1)} %copy-done.1, ...), kind=kOutput, calls=%fused_computation.40 | convolution fusion | flops 853606400 | bytes 15411200 | tf_op jit(solution)/shard_map/ngm,md->ngd/dot_general | solution.py:43
  146.1 0.9 copy.60
  (112 shorter events, 14.9 us)
Async XLA Ops:
  7.2 6.8 %copy-start.5 = (bf16[16,1280]{1,0:T(8,128)(2,1)S(1)}, bf16[16,1280]{1,0:T(8,128)(2,1)}, u32[]{:S(2)}) copy-start(bf16[16,1280]{1,0:T(8,128)(2,1)} %param.11) | copy-start | bytes 122884
  7.2 14.1 %copy-start.16 = (s32[16]{0:T(128)S(1)}, s32[16]{0:T(128)}, u32[]{:S(2)}) copy-start(s32[16]{0:T(128)} %param.21) | copy-start | bytes 196
  7.2 17.3 %copy-start.13 = (s32[16]{0:T(128)S(1)}, s32[16]{0:T(128)}, u32[]{:S(2)}) copy-start(s32[16]{0:T(128)} %param.19) | copy-start | bytes 196
  7.2 19.9 %copy-start.15 = (s32[16]{0:T(128)S(1)}, s32[16]{0:T(128)}, u32[]{:S(2)}) copy-start(s32[16]{0:T(128)} %param.18) | copy-start | bytes 196
  7.2 26.9 %copy-start = (bf16[5120,2,128]{2,1,0:T(2,128)(2,1)S(1)}, bf16[5120,2,128]{2,1,0:T(2,128)(2,1)}, u32[]{:S(2)}) copy-start(bf16[5120,2,128]{2,1,0:T(2,128)(2,1)} %param.14) | copy-start | bytes 7864324
  7.2 101.2 %all-gather.2.cloned.1.call-start = ((), (), s32[]{:S(2)}) async-start(), calls=%async_computation | async-start | bytes 3276800 | tf_op jit(solution)/shard_map/all_gather | solution.py:98
  14.0 21.3 %copy-start.8 = (f32[640]{0:T(1024)S(1)}, f32[640]{0:T(1024)}, u32[]{:S(2)}) copy-start(f32[640]{0:T(1024)} %param.15) | copy-start | bytes 7684
  14.0 15.4 %collective-permute-start = (bf16[16,1280]{1,0:T(8,128)(2,1)S(1)}, bf16[16,1280]{1,0:T(8,128)(2,1)}, u32[]{:S(2)}, u32[]{:S(2)}) collective-permute-start(bf16[16,1280]{1,0:T(8,128)(2,1)S(1)} %copy-done.5), channel_id=1, source_target_pairs={{0,32},{32,64},{64,96},{96,0},{1,33},{33,65},{65,97},{97,1},{2,34}... | collective-permute-start | bytes 122888 | tf_op jit(solution)/shard_map/ppermute | solution.py:92
  16.0 13.4 %collective-permute-start.1 = (bf16[16,1280]{1,0:T(8,128)(2,1)S(1)}, bf16[16,1280]{1,0:T(8,128)(2,1)}, u32[]{:S(2)}, u32[]{:S(2)}) collective-permute-start(bf16[16,1280]{1,0:T(8,128)(2,1)S(1)} %copy-done.5), channel_id=1, source_target_pairs={{0,64},{32,96},{64,0},{96,32},{1,65},{33,97},{65,1},{97,33},{2,66}... | collective-permute-start | bytes 122888 | tf_op jit(solution)/shard_map/ppermute | solution.py:92
  18.4 10.9 %collective-permute-start.2 = (bf16[16,1280]{1,0:T(8,128)(2,1)S(1)}, bf16[16,1280]{1,0:T(8,128)(2,1)}, u32[]{:S(2)}, u32[]{:S(2)}) collective-permute-start(bf16[16,1280]{1,0:T(8,128)(2,1)S(1)} %copy-done.5), channel_id=1, source_target_pairs={{0,96},{32,0},{64,32},{96,64},{1,97},{33,1},{65,33},{97,65},{2,98}... | collective-permute-start | bytes 122888 | tf_op jit(solution)/shard_map/ppermute | solution.py:92
  19.6 80.3 %collective-permute-start.17 = (bf16[2,1024,128]{2,1,0:T(8,128)(2,1)}, bf16[2,1024,128]{2,1,0:T(8,128)(2,1)}, u32[]{:S(2)}, u32[]{:S(2)}) collective-permute-start(bf16[2,1024,128]{2,1,0:T(8,128)(2,1)} %param.20), channel_id=1, source_target_pairs={{0,1},{1,0},{2,3},{3,2},{4,5},{5,4},{6,7},{7,6},{8,9},{9,8},{10,11... | collective-permute-start | bytes 1572872 | tf_op jit(solution)/shard_map/ppermute | solution.py:13
  21.2 6.5 %copy-start.6 = (f32[64]{0:T(128)}, f32[64]{0:T(128)S(1)}, u32[]{:S(2)}) copy-start(f32[64]{0:T(128)S(1)} %negate_power_fusion) | copy-start | bytes 772
  22.5 6.7 %copy-start.10 = (f32[256]{0:T(256)}, f32[256]{0:T(256)S(1)}, u32[]{:S(2)}) copy-start(f32[256]{0:T(256)S(1)} %fusion.90) | copy-start | bytes 3076
  39.2 1.2 collective-permute-start.3
  40.4 5.6 %collective-permute-start.4 = (bf16[32,1024]{1,0:T(8,128)(2,1)S(1)}, bf16[32,1024]{1,0:T(8,128)(2,1)S(1)}, u32[]{:S(2)}, u32[]{:S(2)}) collective-permute-start(bf16[32,1024]{1,0:T(8,128)(2,1)S(1)} %pad_maximum_fusion.3), channel_id=1, source_target_pairs={{0,2},{1,3},{2,4},{3,5},{4,6},{5,7},{6,0},{7,1},{8,10},{9,11},{10,... | collective-permute-start | bytes 196616 | tf_op jit(solution)/shard_map/ppermute | solution.py:77
  41.7 6.1 %collective-permute-start.5 = (bf16[32,1024]{1,0:T(8,128)(2,1)S(1)}, bf16[32,1024]{1,0:T(8,128)(2,1)S(1)}, u32[]{:S(2)}, u32[]{:S(2)}) collective-permute-start(bf16[32,1024]{1,0:T(8,128)(2,1)S(1)} %pad_maximum_fusion.3), channel_id=1, source_target_pairs={{0,4},{1,5},{2,6},{3,7},{4,0},{5,1},{6,2},{7,3},{8,12},{9,13},{10,... | collective-permute-start | bytes 196616 | tf_op jit(solution)/shard_map/ppermute | solution.py:77
  44.4 4.1 %collective-permute-start.6 = (bf16[32,1024]{1,0:T(8,128)(2,1)S(1)}, bf16[32,1024]{1,0:T(8,128)(2,1)S(1)}, u32[]{:S(2)}, u32[]{:S(2)}) collective-permute-start(bf16[32,1024]{1,0:T(8,128)(2,1)S(1)} %pad_maximum_fusion.3), channel_id=1, source_target_pairs={{0,6},{1,7},{2,0},{3,1},{4,2},{5,3},{6,4},{7,5},{8,14},{9,15},{10,... | collective-permute-start | bytes 196616 | tf_op jit(solution)/shard_map/ppermute | solution.py:77
  49.1 9.7 %collective-permute-start.7 = (bf16[128,1024]{1,0:T(8,128)(2,1)}, bf16[128,1024]{1,0:T(8,128)(2,1)}, u32[]{:S(2)}, u32[]{:S(2)}) collective-permute-start(bf16[128,1024]{1,0:T(8,128)(2,1)} %get-tuple-element.36), channel_id=1, source_target_pairs={{0,8},{1,9},{2,10},{3,11},{4,12},{5,13},{6,14},{7,15},{8,16},{9,17... | collective-permute-start | bytes 786440 | tf_op jit(solution)/shard_map/ppermute | solution.py:77
  51.6 13.8 %collective-permute-start.8 = (bf16[128,1024]{1,0:T(8,128)(2,1)}, bf16[128,1024]{1,0:T(8,128)(2,1)}, u32[]{:S(2)}, u32[]{:S(2)}) collective-permute-start(bf16[128,1024]{1,0:T(8,128)(2,1)} %get-tuple-element.36), channel_id=1, source_target_pairs={{0,16},{1,17},{2,18},{3,19},{4,20},{5,21},{6,22},{7,23},{8,24},{9,... | collective-permute-start | bytes 786440 | tf_op jit(solution)/shard_map/ppermute | solution.py:77
  55.6 11.4 %collective-permute-start.9 = (bf16[128,1024]{1,0:T(8,128)(2,1)}, bf16[128,1024]{1,0:T(8,128)(2,1)}, u32[]{:S(2)}, u32[]{:S(2)}) collective-permute-start(bf16[128,1024]{1,0:T(8,128)(2,1)} %get-tuple-element.36), channel_id=1, source_target_pairs={{0,24},{1,25},{2,26},{3,27},{4,28},{5,29},{6,30},{7,31},{8,0},{9,1... | collective-permute-start | bytes 786440 | tf_op jit(solution)/shard_map/ppermute | solution.py:77
  78.2 5.4 %slice-start = ((s8[6291456]{0:T(1024)(128)(4,1)}), s8[4194304]{0:T(1024)(128)(4,1)S(1)}, s32[]{:S(2)}) async-start(s8[6291456]{0:T(1024)(128)(4,1)} %bitcast.93), calls=%async_computation.1 | async-start | bytes 8388608
  79.2 4.3 %slice-start.1 = ((s8[6291456]{0:T(1024)(128)(4,1)}), s8[2097152]{0:T(1024)(128)(4,1)S(1)}, s32[]{:S(2)}) async-start(s8[6291456]{0:T(1024)(128)(4,1)} %bitcast.93), calls=%async_computation.2 | async-start | bytes 4194304
  83.6 4.0 %copy-start.14 = (s32[16]{0:T(128)S(1)}, s32[16]{0:T(128)}, u32[]{:S(2)}) copy-start(s32[16]{0:T(128)} %iota_add_fusion.1) | copy-start | bytes 196
  84.4 24.0 %copy-start.12 = (f32[2,128]{1,0:T(2,128)S(1)}, f32[2,128]{1,0:T(2,128)}, u32[]{:S(2)}) copy-start(f32[2,128]{1,0:T(2,128)} %param.16) | copy-start | bytes 3076
  84.5 4.5 %collective-permute-start.10 = (bf16[16,640]{1,0:T(8,128)(2,1)S(1)}, bf16[16,640]{1,0:T(8,128)(2,1)S(1)}, u32[]{:S(2)}, u32[]{:S(2)}) collective-permute-start(bf16[16,640]{1,0:T(8,128)(2,1)S(1)} %bitcast.106), channel_id=1, source_target_pairs={{0,1},{1,0},{2,3},{3,2},{4,5},{5,4},{6,7},{7,6},{8,9},{9,8},{10,11... | collective-permute-start | bytes 61448 | tf_op jit(solution)/shard_map/ppermute | solution.py:77
  89.5 4.1 %collective-permute-start.11 = (bf16[32,640]{1,0:T(8,128)(2,1)S(1)}, bf16[32,640]{1,0:T(8,128)(2,1)S(1)}, u32[]{:S(2)}, u32[]{:S(2)}) collective-permute-start(bf16[32,640]{1,0:T(8,128)(2,1)S(1)} %get-tuple-element.54), channel_id=1, source_target_pairs={{0,2},{1,3},{2,4},{3,5},{4,6},{5,7},{6,0},{7,1},{8,10},{9,11},{10,... | collective-permute-start | bytes 122888 | tf_op jit(solution)/shard_map/ppermute | solution.py:77
  89.8 4.9 %collective-permute-start.12 = (bf16[32,640]{1,0:T(8,128)(2,1)S(1)}, bf16[32,640]{1,0:T(8,128)(2,1)S(1)}, u32[]{:S(2)}, u32[]{:S(2)}) collective-permute-start(bf16[32,640]{1,0:T(8,128)(2,1)S(1)} %get-tuple-element.54), channel_id=1, source_target_pairs={{0,4},{1,5},{2,6},{3,7},{4,0},{5,1},{6,2},{7,3},{8,12},{9,13},{10,... | collective-permute-start | bytes 122888 | tf_op jit(solution)/shard_map/ppermute | solution.py:77
  92.5 3.0 %collective-permute-start.13 = (bf16[32,640]{1,0:T(8,128)(2,1)S(1)}, bf16[32,640]{1,0:T(8,128)(2,1)S(1)}, u32[]{:S(2)}, u32[]{:S(2)}) collective-permute-start(bf16[32,640]{1,0:T(8,128)(2,1)S(1)} %get-tuple-element.54), channel_id=1, source_target_pairs={{0,6},{1,7},{2,0},{3,1},{4,2},{5,3},{6,4},{7,5},{8,14},{9,15},{10,... | collective-permute-start | bytes 122888 | tf_op jit(solution)/shard_map/ppermute | solution.py:77
  96.1 6.9 %collective-permute-start.14 = (bf16[128,640]{1,0:T(8,128)(2,1)S(1)}, bf16[128,640]{1,0:T(8,128)(2,1)S(1)}, u32[]{:S(2)}, u32[]{:S(2)}) collective-permute-start(bf16[128,640]{1,0:T(8,128)(2,1)S(1)} %get-tuple-element.42), channel_id=1, source_target_pairs={{0,8},{1,9},{2,10},{3,11},{4,12},{5,13},{6,14},{7,15},{8,16},{9,17... | collective-permute-start | bytes 491528 | tf_op jit(solution)/shard_map/ppermute | solution.py:77
  96.6 7.6 %collective-permute-start.15 = (bf16[128,640]{1,0:T(8,128)(2,1)S(1)}, bf16[128,640]{1,0:T(8,128)(2,1)S(1)}, u32[]{:S(2)}, u32[]{:S(2)}) collective-permute-start(bf16[128,640]{1,0:T(8,128)(2,1)S(1)} %get-tuple-element.42), channel_id=1, source_target_pairs={{0,16},{1,17},{2,18},{3,19},{4,20},{5,21},{6,22},{7,23},{8,24},{9,... | collective-permute-start | bytes 491528 | tf_op jit(solution)/shard_map/ppermute | solution.py:77
  98.3 7.0 %collective-permute-start.16 = (bf16[128,640]{1,0:T(8,128)(2,1)S(1)}, bf16[128,640]{1,0:T(8,128)(2,1)S(1)}, u32[]{:S(2)}, u32[]{:S(2)}) collective-permute-start(bf16[128,640]{1,0:T(8,128)(2,1)S(1)} %get-tuple-element.42), channel_id=1, source_target_pairs={{0,24},{1,25},{2,26},{3,27},{4,28},{5,29},{6,30},{7,31},{8,0},{9,1... | collective-permute-start | bytes 491528 | tf_op jit(solution)/shard_map/ppermute | solution.py:77
  104.8 6.8 %copy-start.7 = (f32[64]{0:T(128)S(1)}, f32[64]{0:T(128)}, u32[]{:S(2)}) copy-start(f32[64]{0:T(128)} %copy-done.6) | copy-start | bytes 772
  104.8 6.8 %copy-start.11 = (f32[256]{0:T(256)S(1)}, f32[256]{0:T(256)}, u32[]{:S(2)}) copy-start(f32[256]{0:T(256)} %copy-done.10) | copy-start | bytes 3076
  108.4 7.8 %copy-start.9 = (f32[640]{0:T(1024)S(1)}, f32[640]{0:T(1024)}, u32[]{:S(2)}) copy-start(f32[640]{0:T(1024)} %param.15) | copy-start | bytes 7684
  112.4 9.7 %copy-start.4 = (bf16[2,256,128]{2,1,0:T(8,128)(2,1)}, bf16[2,256,128]{2,1,0:T(8,128)(2,1)S(1)}, u32[]{:S(2)}) copy-start(bf16[2,256,128]{2,1,0:T(8,128)(2,1)S(1)} %pad_maximum_fusion.2) | copy-start | bytes 393220
  112.4 10.8 %collective-permute-start.18 = (bf16[2,256,128]{2,1,0:T(8,128)(2,1)S(1)}, bf16[2,256,128]{2,1,0:T(8,128)(2,1)S(1)}, u32[]{:S(2)}, u32[]{:S(2)}) collective-permute-start(bf16[2,256,128]{2,1,0:T(8,128)(2,1)S(1)} %pad_maximum_fusion.2), channel_id=1, source_target_pairs={{0,1},{1,0},{2,3},{3,2},{4,5},{5,4},{6,7},{7,6},{8,9},{9,8},{10,11... | collective-permute-start | bytes 393224 | tf_op jit(solution)/shard_map/ppermute | solution.py:13
  122.1 0.9 copy-start.2
  122.1 1.0 copy-start.3
  130.6 8.5 %copy-start.1 = (bf16[2,2048,128]{2,1,0:T(8,128)(2,1)S(1)}, bf16[2,2048,128]{2,1,0:T(8,128)(2,1)}, u32[]{:S(2)}) copy-start(bf16[2,2048,128]{2,1,0:T(8,128)(2,1)} %maximum_select_fusion) | copy-start | bytes 3145732
Sparse Core Ops, SparseCore 0:
  19.7 35.7 all-gather.1

commit v5 on v3

--- a/solution.py
+++ b/solution.py
@@ -2,6 +2,7 @@
 import jax.numpy as jnp
 from jax import lax
 from jax.sharding import PartitionSpec as P
+from jax.experimental import pallas as pl
 
 HD = 128
 
@@ -25,6 +26,37 @@
     return jnp.concatenate(
         [former * cosine - latter * sine, latter * cosine + former * sine], axis=-1
     )
+
+
+def attend_kernel(q_ref, k_ref, v_ref, qpos_ref, kpos_ref, o_ref):
+    scores = lax.dot_general(
+        q_ref[...], k_ref[...], (((1,), (1,)), ((), ())), preferred_element_type=jnp.float32
+    ) * HD ** (-0.5)
+    allowed = kpos_ref[...] <= qpos_ref[...]
+    scores = jnp.where(allowed, scores, -jnp.inf)
+    top = jnp.max(scores, axis=1, keepdims=True)
+    powers = jnp.exp(scores - top)
+    total = jnp.sum(powers, axis=1, keepdims=True)
+    mixed = jnp.dot(powers.astype(jnp.bfloat16), v_ref[...], preferred_element_type=jnp.float32)
+    o_ref[...] = (mixed / total).astype(o_ref.dtype)
+
+
+def attend(queries, keys, values, query_pos, key_pos):
+    amount, width = queries.shape
+    length = keys.shape[0]
+    return pl.pallas_call(
+        attend_kernel,
+        grid=(width // HD,),
+        in_specs=[
+            pl.BlockSpec((amount, HD), lambda h: (0, h)),
+            pl.BlockSpec((length, HD), lambda h: (0, 0)),
+            pl.BlockSpec((length, HD), lambda h: (0, 0)),
+            pl.BlockSpec((amount, 1), lambda h: (0, 0)),
+            pl.BlockSpec((1, length), lambda h: (0, 0)),
+        ],
+        out_specs=pl.BlockSpec((amount, HD), lambda h: (0, h)),
+        out_shape=jax.ShapeDtypeStruct((amount, width), jnp.bfloat16),
+    )(queries, keys, values, query_pos.reshape(amount, 1), key_pos.reshape(1, length))
 
 
 def head_scores(queries, key_rows, allowed):
@@ -155,10 +187,8 @@
     key_slots = jnp.arange(key_rows.shape[1], dtype=jnp.int32)
     key_pos = jnp.where(key_slots < 2 * shard, key_slots, offset + key_slots - 2 * shard)
     usable = (key_slots < offset) | (key_slots >= 2 * shard)
-    allowed = usable[None, :] & (key_pos[None, :] <= positions[:, None])
-    scores = head_scores(turned, key_rows[0], allowed)
-    totals, mixed = head_mix(scores, jnp.max(scores, axis=-1), key_rows[1])
-    pre_attn = (mixed / totals[..., None]).astype(jnp.bfloat16).reshape(pre_count, q_width)
+    key_pos = jnp.where(usable, key_pos, jnp.int32(1 << 30))
+    pre_attn = attend(turned, key_rows[0], key_rows[1], positions, key_pos)
     return pre_attn, appended
 
 

time: 155 us -> 125 us (0.81)
  local copies, waits for them, and re-layouts: 32.2 us -> 13 us
  other arithmetic: 27.3 us -> 8.44 us
  waiting for transfers between devices: 10.5 us -> 28.4 us
  matrix products: 32 us -> 17.9 us
  Pallas kernels: 0 us -> 9.2 us
  starting transfers between devices: 27.6 us -> 22.5 us
    ppermute x14, waiting for transfers between devices: 10.5 us -> 28.3 us  [tree_gather(): parts.append(lax.ppermute(buffer, 'tok', pairs))]
    unnamed x60 -> x45, local copies, waits for them, and re-layouts: 18.3 us -> 7.23 us
    pallas_call x0 -> x1, Pallas kernels: none -> 9.2 us  [attend(): pl.pallas_call(attend_kernel, grid=(width // HD,), in_specs=[pl.BlockSpec...]
    reduce_sum x2 -> x1, other arithmetic: 9.29 us -> 0.79 us  [head_mix(): totals = jnp.sum(powers, axis=-1)]
    dot_general x2 -> x1, matrix products: 10.7 us -> 3.39 us  [head_scores(): jnp.einsum('ngd,md->ngm', shaped, key_rows, preferred_element_type=jnp.fl...]
    dot_general x2 -> x1, matrix products: 7.83 us -> 0.86 us  [head_mix(): jnp.einsum('ngm,md->ngd', weights, value_rows, preferred_element_type=jnp...]
    concatenate x4, local copies, waits for them, and re-layouts: 3.6 us -> 0.07 us  [tree_gather(): buffer = jnp.concatenate(parts, axis=0)]
    ppermute x2, starting transfers between devices: 5.17 us -> 1.9 us  [swapped(): lax.ppermute(value, axis, [(i, i ^ 1 << distance) for i in range(lax.axis...]
  transfers between devices with their start and end apart: 17 -> 17, of which waited for: 9 -> 7; matrix products, arithmetic and copies ran while one was open for 37% -> 17% of each run, Pallas kernels for 0% -> 0%
where the time goes in v5:
time: 125 us
  waiting for transfers between devices  28.4 us (23%)
  starting transfers between devices  22.5 us (18%)
  matrix products  17.9 us (14%)
  between operations  15.2 us (12%)
  local copies, waits for them, and re-layouts  13 us (10%)
  blocking collectives  10.4 us (8%)
  Pallas kernels  9.2 us (7%)
  other arithmetic  8.44 us (7%)
    ppermute x14, waiting for transfers between devices, tree_gather(): parts.append(lax.ppermute(buffer, 'tok', pairs))  28.3 us
    ppermute x14, starting transfers between devices, tree_gather(): parts.append(lax.ppermute(buffer, 'tok', pairs))  20.6 us
    all_gather x1, blocking collectives, project(): cols = lax.all_gather(rows, 'kv', axis=1, tiled=True)  10.4 us
    dot_general x2, matrix products, project(): query = jnp.dot(cols, w_query, preferred_element_type=jnp.float32) + b_query  9.31 us
    pallas_call x1, Pallas kernels, attend(): pl.pallas_call(attend_kernel, grid=(width // HD,), in_specs=[pl.BlockSpec...  9.2 us
    unnamed x45, local copies, waits for them, and re-layouts  7.23 us
    dot_general x2, matrix products, project(): jnp.dot(cols, kv_weight, preferred_element_type=jnp.float32) + kv_bias  4.3 us
    dot_general x1, matrix products, head_scores(): jnp.einsum('ngd,md->ngm', shaped, key_rows, preferred_element_type=jnp.fl...  3.39 us
  transfers between devices with their start and end apart: 17, of which 7 were waited for; matrix products, arithmetic and copies ran while one was open for 17% of the time, Pallas kernels for 0%

profile of v5, /device:TPU:1, one launch (start us, length us, event | category | flops | bytes accessed | tf_op | source)
XLA Modules:
  0.0 125.1 jit_solution(6152589150341039472)
XLA Ops:
  7.3 6.7 %copy.109 = bf16[2,12288,128]{2,1,0:T(8,128)(2,1)} copy(bf16[2,12288,128]{2,1,0:T(8,128)(2,1)} %param.17) | data formatting | bytes 12582912
  14.0 0.6 compare_and_fusion
  14.6 0.1 copy.34
  14.7 0.1 copy.33
  14.8 10.4 %all_gather.6 = bf16[16,5120]{1,0:T(8,128)(2,1)S(1)} all-gather(bf16[16,1280]{1,0:T(8,128)(2,1)S(1)} %copy-done.3), channel_id=1, replica_groups=mesh['kv'=4,'tok'=32] {'kv'}, dimensions={1}, use_global_device_ids=true | all-gather | bytes 204800 | tf_op jit(solution)/shard_map/all_gather | solution.py:122
  25.2 0.5 fusion.19
  25.7 4.3 %fusion.15 = bf16[16,640]{1,0:T(8,128)(2,1)S(1)} fusion(bf16[16,5120]{1,0:T(8,128)(2,1)S(1)} %all_gather.6, bf16[5120,640]{1,0:T(8,128)(2,1)} %param.13, f32[640]{0:T(1024)S(1)} %copy-done.4), kind=kOutput, calls=%fused_computation.23 | convolution fusion | flops 104878080 | bytes 6740480 | tf_op jit(solution)/shard_map/dot_general | solution.py:123
  29.9 0.1 concatenate.83
  30.0 3.1 %collective-permute-start = (bf16[16,1024]{1,0:T(8,128)(2,1)S(1)}, bf16[16,1024]{1,0:T(8,128)(2,1)S(1)}, u32[]{:S(2)}, u32[]{:S(2)}) collective-permute-start(bf16[16,1024]{1,0:T(8,128)(2,1)S(1)} %concatenate.83), channel_id=1, source_target_pairs={{0,1},{1,0},{2,3},{3,2},{4,5},{5,4},{6,7},{7,6},{8,9},{9,8},{10,11... | collective-permute-start | bytes 98312 | tf_op jit(solution)/shard_map/ppermute | solution.py:109
  33.2 0.1 collective-permute-start.14
  33.3 0.6 dynamic_slice.3
  33.9 1.3 %or_select_fusion.kpos_ref = s32[1,2560]{1,0:T(1,128)} fusion(s32[]{:T(128)} %bitcast.13), kind=kLoop, calls=%fused_computation.94 | loop fusion | flops 20480 | bytes 10244 | tf_op jit(solution)/shard_map/jit(_where)/select_n | solution.py:190
  35.8 0.1 copy.35
  36.0 0.1 reduce.19
  36.1 0.1 multiply_cosine_fusion.3
  36.2 0.3 multiply_cosine_fusion.1
  36.5 0.2 fusion.31
  36.8 2.8 %collective-permute-start.3 = (bf16[32,1024]{1,0:T(8,128)(2,1)S(1)}, bf16[32,1024]{1,0:T(8,128)(2,1)S(1)}, u32[]{:S(2)}, u32[]{:S(2)}) collective-permute-start(bf16[32,1024]{1,0:T(8,128)(2,1)S(1)} %pad_maximum_fusion.3), channel_id=1, source_target_pairs={{0,6},{1,7},{2,0},{3,1},{4,2},{5,3},{6,4},{7,5},{8,14},{9,15},{10,... | collective-permute-start | bytes 196616 | tf_op jit(solution)/shard_map/ppermute | solution.py:109
  39.6 0.4 collective-permute-start.2
  40.0 0.7 collective-permute-start.1
  40.6 5.5 %collective-permute-done.1 = bf16[32,1024]{1,0:T(8,128)(2,1)S(1)} collective-permute-done((bf16[32,1024]{1,0:T(8,128)(2,1)S(1)}, bf16[32,1024]{1,0:T(8,128)(2,1)S(1)}, u32[]{:S(2)}, u32[]{:S(2)}) %collective-permute-start.1) | collective-permute-done | bytes 65568 | tf_op jit(solution)/shard_map/ppermute | solution.py:109
  46.2 1.7 %collective-permute-start.4 = (bf16[128,1024]{1,0:T(8,128)(2,1)S(1)}, bf16[128,1024]{1,0:T(8,128)(2,1)S(1)}, u32[]{:S(2)}, u32[]{:S(2)}) collective-permute-start(bf16[128,1024]{1,0:T(8,128)(2,1)S(1)} %get-tuple-element.24), channel_id=1, source_target_pairs={{0,8},{1,9},{2,10},{3,11},{4,12},{5,13},{6,14},{7,15},{8,16},{9,17... | collective-permute-start | bytes 786440 | tf_op jit(solution)/shard_map/ppermute | solution.py:109
  47.9 0.7 iota_add_fusion.qpos_ref
  48.5 3.3 %collective-permute-start.5 = (bf16[128,1024]{1,0:T(8,128)(2,1)S(1)}, bf16[128,1024]{1,0:T(8,128)(2,1)S(1)}, u32[]{:S(2)}, u32[]{:S(2)}) collective-permute-start(bf16[128,1024]{1,0:T(8,128)(2,1)S(1)} %get-tuple-element.24), channel_id=1, source_target_pairs={{0,16},{1,17},{2,18},{3,19},{4,20},{5,21},{6,22},{7,23},{8,24},{9,... | collective-permute-start | bytes 786440 | tf_op jit(solution)/shard_map/ppermute | solution.py:109
  51.9 0.8 collective-permute-start.6
  52.7 3.1 %collective-permute-done.4 = bf16[128,1024]{1,0:T(8,128)(2,1)S(1)} collective-permute-done((bf16[128,1024]{1,0:T(8,128)(2,1)S(1)}, bf16[128,1024]{1,0:T(8,128)(2,1)S(1)}, u32[]{:S(2)}, u32[]{:S(2)}) %collective-permute-start.4) | collective-permute-done | bytes 262176 | tf_op jit(solution)/shard_map/ppermute | solution.py:109
  55.8 6.5 %collective-permute-done.5 = bf16[128,1024]{1,0:T(8,128)(2,1)S(1)} collective-permute-done((bf16[128,1024]{1,0:T(8,128)(2,1)S(1)}, bf16[128,1024]{1,0:T(8,128)(2,1)S(1)}, u32[]{:S(2)}, u32[]{:S(2)}) %collective-permute-start.5) | collective-permute-done | bytes 262176 | tf_op jit(solution)/shard_map/ppermute | solution.py:109
  62.3 0.3 collective-permute-done.6
  62.6 0.6 gather_fusion
  63.2 0.1 broadcast_select_fusion
  63.4 0.1 fusion.58
  63.5 0.1 fusion.71
  63.6 0.1 maximum_bitcast_fusion
  63.7 2.3 %scatter_fusion = bf16[2,12288,128]{2,1,0:T(8,128)(2,1)} fusion(bf16[2,12288,128]{2,1,0:T(8,128)(2,1)} %copy.109, s32[16]{0:T(128)S(1)} %get-tuple-element.10, bf16[16,2,128]{2,0,1:T(8,128)(2,1)S(1)} %maximum_bitcast_fusion), kind=kCustom, calls=%fused_computation.2 | custom fusion | bytes 24640 | tf_op jit(solution)/shard_map/scatter | solution.py:90
  66.1 3.4 %fusion.74 = (f32[16,5]{0,1:T(8,128)S(1)}, f32[16,5,12288]{2,0,1:T(8,128)S(1)}) fusion(bf16[2,12288,128]{2,1,0:T(8,128)(2,1)} %scatter_fusion, bf16[16,5,64]{2,0,1:T(8,128)(2,1)S(1)} %get-tuple-element.21, bf16[16,5,64]{2,0,1:T(8,128)(2,1)S(1)} %get-tuple-element.20, pred[16,12288]{1,0:T(8,128)(4,1)S(1)} %fusion.31), kind=kOutput, calls=%fused_computation.170 | convolution fusion | flops 254648240 | bytes 7295296 | tf_op jit(solution)/shard_map/ngd,md->ngm/dot_general | solution.py:66
  69.5 0.8 fusion.1
  70.2 0.9 fusion.28
  71.1 1.6 %collective-permute-start.7 = (bf16[16,640]{1,0:T(8,128)(2,1)S(1)}, bf16[16,640]{1,0:T(8,128)(2,1)S(1)}, u32[]{:S(2)}, u32[]{:S(2)}) collective-permute-start(bf16[16,640]{1,0:T(8,128)(2,1)S(1)} %bitcast.87), channel_id=1, source_target_pairs={{0,1},{1,0},{2,3},{3,2},{4,5},{5,4},{6,7},{7,6},{8,9},{9,8},{10,11... | collective-permute-start | bytes 61448 | tf_op jit(solution)/shard_map/ppermute | solution.py:109
  72.8 0.2 fusion.35
  73.0 0.7 iota_reduce_fusion
  73.9 2.7 %collective-permute-start.10 = (bf16[32,640]{1,0:T(8,128)(2,1)S(1)}, bf16[32,640]{1,0:T(8,128)(2,1)S(1)}, u32[]{:S(2)}, u32[]{:S(2)}) collective-permute-start(bf16[32,640]{1,0:T(8,128)(2,1)S(1)} %get-tuple-element.42), channel_id=1, source_target_pairs={{0,6},{1,7},{2,0},{3,1},{4,2},{5,3},{6,4},{7,5},{8,14},{9,15},{10,... | collective-permute-start | bytes 122888 | tf_op jit(solution)/shard_map/ppermute | solution.py:109
  76.6 1.4 %collective-permute-done.8 = bf16[32,640]{1,0:T(8,128)(2,1)S(1)} collective-permute-done((bf16[32,640]{1,0:T(8,128)(2,1)S(1)}, bf16[32,640]{1,0:T(8,128)(2,1)S(1)}, u32[]{:S(2)}, u32[]{:S(2)}) %collective-permute-start.8) | collective-permute-done | bytes 40992 | tf_op jit(solution)/shard_map/ppermute | solution.py:109
  78.0 3.0 %collective-permute-done.9 = bf16[32,640]{1,0:T(8,128)(2,1)S(1)} collective-permute-done((bf16[32,640]{1,0:T(8,128)(2,1)S(1)}, bf16[32,640]{1,0:T(8,128)(2,1)S(1)}, u32[]{:S(2)}, u32[]{:S(2)}) %collective-permute-start.9) | collective-permute-done | bytes 40992 | tf_op jit(solution)/shard_map/ppermute | solution.py:109
  81.0 2.4 %collective-permute-start.13 = (bf16[128,640]{1,0:T(8,128)(2,1)S(1)}, bf16[128,640]{1,0:T(8,128)(2,1)S(1)}, u32[]{:S(2)}, u32[]{:S(2)}) collective-permute-start(bf16[128,640]{1,0:T(8,128)(2,1)S(1)} %get-tuple-element.30), channel_id=1, source_target_pairs={{0,24},{1,25},{2,26},{3,27},{4,28},{5,29},{6,30},{7,31},{8,0},{9,1... | collective-permute-start | bytes 491528 | tf_op jit(solution)/shard_map/ppermute | solution.py:109
  83.4 0.9 collective-permute-start.12
  84.3 0.1 collective-permute-start.11
  84.4 0.3 maximum_select_fusion
  84.7 8.6 %collective-permute-done.11 = bf16[128,640]{1,0:T(8,128)(2,1)S(1)} collective-permute-done((bf16[128,640]{1,0:T(8,128)(2,1)S(1)}, bf16[128,640]{1,0:T(8,128)(2,1)S(1)}, u32[]{:S(2)}, u32[]{:S(2)}) %collective-permute-start.11) | collective-permute-done | bytes 163872 | tf_op jit(solution)/shard_map/ppermute | solution.py:109
  93.4 0.6 gather_fusion.1
  94.0 0.7 broadcast_select_fusion.1
  94.7 3.8 %fusion.12 = f32[256,256]{0,1:T(8,128)S(1)} fusion(bf16[256,5120]{1,0:T(8,128)(2,1)} %all-gather.2.cloned.1.call-done, bf16[640,8,2,128]{3,2,1,0:T(2,128)(2,1)} %bitcast.79, f32[256]{0:T(256)S(1)} %bitcast.90), kind=kOutput, calls=%fused_computation.21 | convolution fusion | flops 671154176 | bytes 5506048 | tf_op jit(solution)/shard_map/dot_general | solution.py:124
  98.6 5.1 %convolution_add_fusion = f32[256,640]{1,0:T(8,128)S(1)} fusion(bf16[256,5120]{1,0:T(8,128)(2,1)S(1)} %copy-done.10, bf16[5120,640]{1,0:T(8,128)(2,1)} %param.13, f32[640]{0:T(1024)S(1)} %copy-done.4), kind=kOutput, calls=%fused_computation.20 | convolution fusion | flops 1677885440 | bytes 9832960 | tf_op jit(solution)/shard_map/dot_general | solution.py:123
  103.6 0.2 copy.41
  103.9 0.1 copy.52
  104.0 0.1 copy.51
  104.1 0.1 copy.50
  104.2 0.6 fusion.45
  104.8 0.1 pad_maximum_fusion.2
  104.9 1.8 %collective-permute-start.15 = (bf16[2,256,128]{2,1,0:T(8,128)(2,1)S(1)}, bf16[2,256,128]{2,1,0:T(8,128)(2,1)S(1)}, u32[]{:S(2)}, u32[]{:S(2)}) collective-permute-start(bf16[2,256,128]{2,1,0:T(8,128)(2,1)S(1)} %pad_maximum_fusion.2), channel_id=1, source_target_pairs={{0,1},{1,0},{2,3},{3,2},{4,5},{5,4},{6,7},{7,6},{8,9},{9,8},{10,11... | collective-permute-start | bytes 393224 | tf_op jit(solution)/shard_map/ppermute | solution.py:14
  106.7 0.1 subtract_convert_fusion
  106.8 0.9 copy.45.q_ref
  107.7 0.1 maximum_select_fusion.1
  107.8 1.2 fusion.34
  109.0 9.2 %shard_map.138 = bf16[256,640]{1,0:T(8,128)(2,1)} custom-call(bf16[256,640]{1,0:T(8,128)(2,1)} %copy.45.q_ref, bf16[2560,128]{1,0:T(8,128)(2,1)} %get-tuple-element.13.k_ref, bf16[2560,128]{1,0:T(8,128)(2,1)} %get-tuple-element.12.v_ref, s32[256,1]{1,0:T(8,128)} %iota_add_fusion.qpos_ref, s32[1,2560]{1,0:T(1,128)} %or_select_fusion.kpos_ref), custom_call_target="tpu_custom_call" | custom-call | tf_op jit(solution)/shard_map/pallas_call | solution.py:47
  (85 shorter events, 0.7 us)
Async XLA Ops:
  7.2 6.9 %copy-start.9 = (s32[16]{0:T(128)S(1)}, s32[16]{0:T(128)}, u32[]{:S(2)}) copy-start(s32[16]{0:T(128)} %param.18) | copy-start | bytes 196
  7.2 7.6 %copy-start.3 = (bf16[16,1280]{1,0:T(8,128)(2,1)S(1)}, bf16[16,1280]{1,0:T(8,128)(2,1)}, u32[]{:S(2)}) copy-start(bf16[16,1280]{1,0:T(8,128)(2,1)} %param.11) | copy-start | bytes 122884
  7.2 18.0 %copy-start.6 = (f32[2,128]{1,0:T(2,128)S(1)}, f32[2,128]{1,0:T(2,128)}, u32[]{:S(2)}) copy-start(f32[2,128]{1,0:T(2,128)} %param.16) | copy-start | bytes 3076
  7.2 18.0 %copy-start = (bf16[5120,2,128]{2,1,0:T(2,128)(2,1)S(1)}, bf16[5120,2,128]{2,1,0:T(2,128)(2,1)}, u32[]{:S(2)}) copy-start(bf16[5120,2,128]{2,1,0:T(2,128)(2,1)} %param.14) | copy-start | bytes 7864324
  7.2 87.5 %all-gather.2.cloned.1.call-start = ((), (), s32[]{:S(2)}) async-start(), calls=%async_computation | async-start | bytes 3276800 | tf_op jit(solution)/shard_map/all_gather | solution.py:122
  13.9 11.7 %copy-start.4 = (f32[640]{0:T(1024)S(1)}, f32[640]{0:T(1024)}, u32[]{:S(2)}) copy-start(f32[640]{0:T(1024)} %param.15) | copy-start | bytes 7684
  25.6 7.6 %copy-start.1 = (bf16[2,1024,128]{2,1,0:T(8,128)(2,1)S(1)}, bf16[2,1024,128]{2,1,0:T(8,128)(2,1)}, u32[]{:S(2)}) copy-start(bf16[2,1024,128]{2,1,0:T(8,128)(2,1)} %param.20) | copy-start | bytes 1572868
  25.6 7.7 %copy-start.11 = (s32[16]{0:T(128)S(1)}, s32[16]{0:T(128)}, u32[]{:S(2)}) copy-start(s32[16]{0:T(128)} %param.21) | copy-start | bytes 196
  25.7 10.2 %copy-start.8 = (s32[16]{0:T(128)S(1)}, s32[16]{0:T(128)}, u32[]{:S(2)}) copy-start(s32[16]{0:T(128)} %param.19) | copy-start | bytes 196
  25.7 26.2 %copy-start.5 = (s32[16]{0:T(128)S(1)}, s32[16]{0:T(128)}, u32[]{:S(2)}) copy-start(s32[16]{0:T(128)} %get-tuple-element.7) | copy-start | bytes 196
  30.0 6.7 %collective-permute-start = (bf16[16,1024]{1,0:T(8,128)(2,1)S(1)}, bf16[16,1024]{1,0:T(8,128)(2,1)S(1)}, u32[]{:S(2)}, u32[]{:S(2)}) collective-permute-start(bf16[16,1024]{1,0:T(8,128)(2,1)S(1)} %concatenate.83), channel_id=1, source_target_pairs={{0,1},{1,0},{2,3},{3,2},{4,5},{5,4},{6,7},{7,6},{8,9},{9,8},{10,11... | collective-permute-start | bytes 98312 | tf_op jit(solution)/shard_map/ppermute | solution.py:109
  33.2 51.2 %collective-permute-start.14 = (bf16[2,1024,128]{2,1,0:T(8,128)(2,1)S(1)}, bf16[2,1024,128]{2,1,0:T(8,128)(2,1)S(1)}, u32[]{:S(2)}, u32[]{:S(2)}) collective-permute-start(bf16[2,1024,128]{2,1,0:T(8,128)(2,1)S(1)} %copy-done.1), channel_id=1, source_target_pairs={{0,1},{1,0},{2,3},{3,2},{4,5},{5,4},{6,7},{7,6},{8,9},{9,8},{10,11... | collective-permute-start | bytes 1572872 | tf_op jit(solution)/shard_map/ppermute | solution.py:14
  36.8 9.4 %collective-permute-start.3 = (bf16[32,1024]{1,0:T(8,128)(2,1)S(1)}, bf16[32,1024]{1,0:T(8,128)(2,1)S(1)}, u32[]{:S(2)}, u32[]{:S(2)}) collective-permute-start(bf16[32,1024]{1,0:T(8,128)(2,1)S(1)} %pad_maximum_fusion.3), channel_id=1, source_target_pairs={{0,6},{1,7},{2,0},{3,1},{4,2},{5,3},{6,4},{7,5},{8,14},{9,15},{10,... | collective-permute-start | bytes 196616 | tf_op jit(solution)/shard_map/ppermute | solution.py:109
  39.6 6.5 %collective-permute-start.2 = (bf16[32,1024]{1,0:T(8,128)(2,1)S(1)}, bf16[32,1024]{1,0:T(8,128)(2,1)S(1)}, u32[]{:S(2)}, u32[]{:S(2)}) collective-permute-start(bf16[32,1024]{1,0:T(8,128)(2,1)S(1)} %pad_maximum_fusion.3), channel_id=1, source_target_pairs={{0,4},{1,5},{2,6},{3,7},{4,0},{5,1},{6,2},{7,3},{8,12},{9,13},{10,... | collective-permute-start | bytes 196616 | tf_op jit(solution)/shard_map/ppermute | solution.py:109
  40.0 6.2 %collective-permute-start.1 = (bf16[32,1024]{1,0:T(8,128)(2,1)S(1)}, bf16[32,1024]{1,0:T(8,128)(2,1)S(1)}, u32[]{:S(2)}, u32[]{:S(2)}) collective-permute-start(bf16[32,1024]{1,0:T(8,128)(2,1)S(1)} %pad_maximum_fusion.3), channel_id=1, source_target_pairs={{0,2},{1,3},{2,4},{3,5},{4,6},{5,7},{6,0},{7,1},{8,10},{9,11},{10,... | collective-permute-start | bytes 196616 | tf_op jit(solution)/shard_map/ppermute | solution.py:109
  46.2 9.6 %collective-permute-start.4 = (bf16[128,1024]{1,0:T(8,128)(2,1)S(1)}, bf16[128,1024]{1,0:T(8,128)(2,1)S(1)}, u32[]{:S(2)}, u32[]{:S(2)}) collective-permute-start(bf16[128,1024]{1,0:T(8,128)(2,1)S(1)} %get-tuple-element.24), channel_id=1, source_target_pairs={{0,8},{1,9},{2,10},{3,11},{4,12},{5,13},{6,14},{7,15},{8,16},{9,17... | collective-permute-start | bytes 786440 | tf_op jit(solution)/shard_map/ppermute | solution.py:109
  48.5 13.8 %collective-permute-start.5 = (bf16[128,1024]{1,0:T(8,128)(2,1)S(1)}, bf16[128,1024]{1,0:T(8,128)(2,1)S(1)}, u32[]{:S(2)}, u32[]{:S(2)}) collective-permute-start(bf16[128,1024]{1,0:T(8,128)(2,1)S(1)} %get-tuple-element.24), channel_id=1, source_target_pairs={{0,16},{1,17},{2,18},{3,19},{4,20},{5,21},{6,22},{7,23},{8,24},{9,... | collective-permute-start | bytes 786440 | tf_op jit(solution)/shard_map/ppermute | solution.py:109
  51.9 10.8 %collective-permute-start.6 = (bf16[128,1024]{1,0:T(8,128)(2,1)S(1)}, bf16[128,1024]{1,0:T(8,128)(2,1)S(1)}, u32[]{:S(2)}, u32[]{:S(2)}) collective-permute-start(bf16[128,1024]{1,0:T(8,128)(2,1)S(1)} %get-tuple-element.24), channel_id=1, source_target_pairs={{0,24},{1,25},{2,26},{3,27},{4,28},{5,29},{6,30},{7,31},{8,0},{9,1... | collective-permute-start | bytes 786440 | tf_op jit(solution)/shard_map/ppermute | solution.py:109
  66.0 4.2 %slice-start = ((s8[6291456]{0:T(1024)(128)(4,1)}), s8[4194304]{0:T(1024)(128)(4,1)S(1)}, s32[]{:S(2)}) async-start(s8[6291456]{0:T(1024)(128)(4,1)} %bitcast.77), calls=%async_computation.1 | async-start | bytes 8388608
  66.0 4.2 %slice-start.1 = ((s8[6291456]{0:T(1024)(128)(4,1)}), s8[2097152]{0:T(1024)(128)(4,1)S(1)}, s32[]{:S(2)}) async-start(s8[6291456]{0:T(1024)(128)(4,1)} %bitcast.77), calls=%async_computation.2 | async-start | bytes 4194304
  71.1 23.6 %copy-start.7 = (f32[2,128]{1,0:T(2,128)S(1)}, f32[2,128]{1,0:T(2,128)}, u32[]{:S(2)}) copy-start(f32[2,128]{1,0:T(2,128)} %param.16) | copy-start | bytes 3076
  71.1 2.6 %collective-permute-start.7 = (bf16[16,640]{1,0:T(8,128)(2,1)S(1)}, bf16[16,640]{1,0:T(8,128)(2,1)S(1)}, u32[]{:S(2)}, u32[]{:S(2)}) collective-permute-start(bf16[16,640]{1,0:T(8,128)(2,1)S(1)} %bitcast.87), channel_id=1, source_target_pairs={{0,1},{1,0},{2,3},{3,2},{4,5},{5,4},{6,7},{7,6},{8,9},{9,8},{10,11... | collective-permute-start | bytes 61448 | tf_op jit(solution)/shard_map/ppermute | solution.py:109
  73.8 4.1 %collective-permute-start.8 = (bf16[32,640]{1,0:T(8,128)(2,1)S(1)}, bf16[32,640]{1,0:T(8,128)(2,1)S(1)}, u32[]{:S(2)}, u32[]{:S(2)}) collective-permute-start(bf16[32,640]{1,0:T(8,128)(2,1)S(1)} %get-tuple-element.42), channel_id=1, source_target_pairs={{0,2},{1,3},{2,4},{3,5},{4,6},{5,7},{6,0},{7,1},{8,10},{9,11},{10,... | collective-permute-start | bytes 122888 | tf_op jit(solution)/shard_map/ppermute | solution.py:109
  73.9 7.0 %collective-permute-start.10 = (bf16[32,640]{1,0:T(8,128)(2,1)S(1)}, bf16[32,640]{1,0:T(8,128)(2,1)S(1)}, u32[]{:S(2)}, u32[]{:S(2)}) collective-permute-start(bf16[32,640]{1,0:T(8,128)(2,1)S(1)} %get-tuple-element.42), channel_id=1, source_target_pairs={{0,6},{1,7},{2,0},{3,1},{4,2},{5,3},{6,4},{7,5},{8,14},{9,15},{10,... | collective-permute-start | bytes 122888 | tf_op jit(solution)/shard_map/ppermute | solution.py:109
  76.6 4.4 %collective-permute-start.9 = (bf16[32,640]{1,0:T(8,128)(2,1)S(1)}, bf16[32,640]{1,0:T(8,128)(2,1)S(1)}, u32[]{:S(2)}, u32[]{:S(2)}) collective-permute-start(bf16[32,640]{1,0:T(8,128)(2,1)S(1)} %get-tuple-element.42), channel_id=1, source_target_pairs={{0,4},{1,5},{2,6},{3,7},{4,0},{5,1},{6,2},{7,3},{8,12},{9,13},{10,... | collective-permute-start | bytes 122888 | tf_op jit(solution)/shard_map/ppermute | solution.py:109
  81.0 12.4 %collective-permute-start.13 = (bf16[128,640]{1,0:T(8,128)(2,1)S(1)}, bf16[128,640]{1,0:T(8,128)(2,1)S(1)}, u32[]{:S(2)}, u32[]{:S(2)}) collective-permute-start(bf16[128,640]{1,0:T(8,128)(2,1)S(1)} %get-tuple-element.30), channel_id=1, source_target_pairs={{0,24},{1,25},{2,26},{3,27},{4,28},{5,29},{6,30},{7,31},{8,0},{9,1... | collective-permute-start | bytes 491528 | tf_op jit(solution)/shard_map/ppermute | solution.py:109
  83.4 9.9 %collective-permute-start.12 = (bf16[128,640]{1,0:T(8,128)(2,1)S(1)}, bf16[128,640]{1,0:T(8,128)(2,1)S(1)}, u32[]{:S(2)}, u32[]{:S(2)}) collective-permute-start(bf16[128,640]{1,0:T(8,128)(2,1)S(1)} %get-tuple-element.30), channel_id=1, source_target_pairs={{0,16},{1,17},{2,18},{3,19},{4,20},{5,21},{6,22},{7,23},{8,24},{9,... | collective-permute-start | bytes 491528 | tf_op jit(solution)/shard_map/ppermute | solution.py:109
  84.3 9.0 %collective-permute-start.11 = (bf16[128,640]{1,0:T(8,128)(2,1)S(1)}, bf16[128,640]{1,0:T(8,128)(2,1)S(1)}, u32[]{:S(2)}, u32[]{:S(2)}) collective-permute-start(bf16[128,640]{1,0:T(8,128)(2,1)S(1)} %get-tuple-element.30), channel_id=1, source_target_pairs={{0,8},{1,9},{2,10},{3,11},{4,12},{5,13},{6,14},{7,15},{8,16},{9,17... | collective-permute-start | bytes 491528 | tf_op jit(solution)/shard_map/ppermute | solution.py:109
  94.7 3.9 %copy-start.10 = (bf16[256,5120]{1,0:T(8,128)(2,1)S(1)}, bf16[256,5120]{1,0:T(8,128)(2,1)}, u32[]{:S(2)}) copy-start(bf16[256,5120]{1,0:T(8,128)(2,1)} %all-gather.2.cloned.1.call-done) | copy-start | bytes 7864324
  104.9 13.3 %copy-start.2 = (bf16[2,256,128]{2,1,0:T(8,128)(2,1)}, bf16[2,256,128]{2,1,0:T(8,128)(2,1)S(1)}, u32[]{:S(2)}) copy-start(bf16[2,256,128]{2,1,0:T(8,128)(2,1)S(1)} %pad_maximum_fusion.2) | copy-start | bytes 393220
  104.9 2.8 %collective-permute-start.15 = (bf16[2,256,128]{2,1,0:T(8,128)(2,1)S(1)}, bf16[2,256,128]{2,1,0:T(8,128)(2,1)S(1)}, u32[]{:S(2)}, u32[]{:S(2)}) collective-permute-start(bf16[2,256,128]{2,1,0:T(8,128)(2,1)S(1)} %pad_maximum_fusion.2), channel_id=1, source_target_pairs={{0,1},{1,0},{2,3},{3,2},{4,5},{5,4},{6,7},{7,6},{8,9},{9,8},{10,11... | collective-permute-start | bytes 393224 | tf_op jit(solution)/shard_map/ppermute | solution.py:14
Sparse Core Ops, SparseCore 0:
  14.1 38.1 all-gather.1

commit v6 on v5

--- a/solution.py
+++ b/solution.py
@@ -86,14 +86,23 @@
     turned = turned.astype(jnp.bfloat16).reshape(amount, q_heads * HD)
     new_keys = rotate(keyval[:, 0].astype(jnp.float32).reshape(amount, kv_heads, HD), lengths)
     new_keys = new_keys.astype(jnp.bfloat16).reshape(amount, kv_heads * HD)
-    appended = jnp.stack([new_keys, keyval[:, 1]], axis=0)
-    cache_pool = cache_pool.at[:, starts + lengths].set(appended)
+    new_values = keyval[:, 1]
+    appended = jnp.stack([new_keys, new_values], axis=0)
+    new_pool = cache_pool.at[:, starts + lengths].set(appended)
     spots = jnp.arange(cache_pool.shape[1], dtype=jnp.int32)
-    allowed = (spots[None, :] >= starts[:, None]) & (spots[None, :] <= (starts + lengths)[:, None])
+    allowed = (spots[None, :] >= starts[:, None]) & (spots[None, :] < (starts + lengths)[:, None])
     scores = head_scores(turned, cache_pool[0], allowed)
-    totals, mixed = head_mix(scores, jnp.max(scores, axis=-1), cache_pool[1])
+    fresh = jnp.einsum(
+        "ngd,nd->ng", turned.reshape(amount, q_heads, HD), new_keys, preferred_element_type=jnp.float32
+    ) * HD ** (-0.5)
+    top = jnp.maximum(jnp.max(scores, axis=-1), fresh)
+    totals, mixed = head_mix(scores, top, cache_pool[1])
+    fresh_power = jnp.exp(fresh - top)
+    totals = totals + fresh_power
+    fresh_weight = fresh_power.astype(jnp.bfloat16).astype(jnp.float32)
+    mixed = mixed + fresh_weight[..., None] * new_values.astype(jnp.float32)[:, None, :]
     result = (mixed / totals[..., None]).astype(jnp.bfloat16).reshape(amount, q_heads * HD)
-    return (result, cache_pool)
+    return (result, new_pool)
 
 
 def tree_gather(value):
@@ -188,15 +197,15 @@
     key_pos = jnp.where(key_slots < 2 * shard, key_slots, offset + key_slots - 2 * shard)
     usable = (key_slots < offset) | (key_slots >= 2 * shard)
     key_pos = jnp.where(usable, key_pos, jnp.int32(1 << 30))
-    pre_attn = attend(turned, key_rows[0], key_rows[1], positions, key_pos)
-    return pre_attn, appended
+    return (turned, key_rows[0], key_rows[1], positions, key_pos), appended
 
 
 def body(dec_tokens, pre_tokens, w_query, w_keyval, b_query, b_keyval, dec_pool, owner_slots, dec_lengths, pre_cache, pre_offsets):
     dec_attn, new_pool, all_query, all_keyval = body_inner(
         dec_tokens, pre_tokens, w_query, w_keyval, b_query, b_keyval, dec_pool, owner_slots, dec_lengths
     )
-    pre_attn, appended = prefill(all_query, all_keyval, pre_tokens, w_query, w_keyval, pre_cache, pre_offsets)
+    operands, appended = prefill(all_query, all_keyval, pre_tokens, w_query, w_keyval, pre_cache, pre_offsets)
+    pre_attn = attend(*operands)
     return (dec_attn, pre_attn, new_pool, appended)
 
 

time: 125 us -> 127 us (1.016)
  waiting for transfers between devices: 28.4 us -> 16.5 us
  local copies, waits for them, and re-layouts: 13 us -> 22.1 us
  starting transfers between devices: 22.5 us -> 26.9 us
    ppermute x14, waiting for transfers between devices: 28.3 us -> 16.5 us  [tree_gather(): parts.append(lax.ppermute(buffer, 'tok', pairs))]
    unnamed x45 -> x42, local copies, waits for them, and re-layouts: 7.23 us -> 13.1 us
    ppermute x14, starting transfers between devices: 20.6 us -> 23.8 us  [tree_gather(): parts.append(lax.ppermute(buffer, 'tok', pairs))]
    concatenate x4, local copies, waits for them, and re-layouts: 0.07 us -> 1.96 us  [tree_gather(): buffer = jnp.concatenate(parts, axis=0)]
  transfers between devices with their start and end apart: 17 -> 17, of which waited for: 7 -> 8; matrix products, arithmetic and copies ran while one was open for 17% -> 21% of each run, Pallas kernels for 0% -> 0%
where the time goes in v6:
time: 127 us
  starting transfers between devices  26.9 us (21%)
  local copies, waits for them, and re-layouts  22.1 us (17%)
  matrix products  17.7 us (14%)
  waiting for transfers between devices  16.5 us (13%)
  between operations  15.1 us (12%)
  blocking collectives  10.4 us (8%)
  Pallas kernels  9.2 us (7%)
  other arithmetic  9.01 us (7%)
    ppermute x14, starting transfers between devices, tree_gather(): parts.append(lax.ppermute(buffer, 'tok', pairs))  23.8 us
    ppermute x14, waiting for transfers between devices, tree_gather(): parts.append(lax.ppermute(buffer, 'tok', pairs))  16.5 us
    unnamed x42, local copies, waits for them, and re-layouts  13.1 us
    all_gather x1, blocking collectives, project(): cols = lax.all_gather(rows, 'kv', axis=1, tiled=True)  10.4 us
    pallas_call x1, Pallas kernels, attend(): pl.pallas_call(attend_kernel, grid=(width // HD,), in_specs=[pl.BlockSpec...  9.2 us
    dot_general x2, matrix products, project(): query = jnp.dot(cols, w_query, preferred_element_type=jnp.float32) + b_query  9.02 us
    dot_general x2, matrix products, project(): jnp.dot(cols, kv_weight, preferred_element_type=jnp.float32) + kv_bias  4.3 us
    dot_general x1, matrix products, head_scores(): jnp.einsum('ngd,md->ngm', shaped, key_rows, preferred_element_type=jnp.fl...  3.33 us
  transfers between devices with their start and end apart: 17, of which 8 were waited for; matrix products, arithmetic and copies ran while one was open for 21% of the time, Pallas kernels for 0%

profile of v6, /device:TPU:1, one launch (start us, length us, event | category | flops | bytes accessed | tf_op | source)
XLA Modules:
  0.0 126.8 jit_solution(4809467704459450685)
XLA Ops:
  7.2 6.4 %copy.116 = bf16[2,12288,128]{2,1,0:T(8,128)(2,1)} copy(bf16[2,12288,128]{2,1,0:T(8,128)(2,1)} %param.17) | data formatting | bytes 12582912
  13.7 10.4 %all_gather.6 = bf16[16,5120]{1,0:T(8,128)(2,1)S(1)} all-gather(bf16[16,1280]{1,0:T(8,128)(2,1)S(1)} %copy-done.4), channel_id=1, replica_groups=mesh['kv'=4,'tok'=32] {'kv'}, dimensions={1}, use_global_device_ids=true | all-gather | bytes 204800 | tf_op jit(solution)/shard_map/all_gather | solution.py:131
  24.3 4.0 %fusion.24 = bf16[16,640]{1,0:T(8,128)(2,1)S(1)} fusion(bf16[16,5120]{1,0:T(8,128)(2,1)S(1)} %all_gather.6, bf16[5120,640]{1,0:T(8,128)(2,1)} %param.13, f32[640]{0:T(1024)S(1)} %copy-done.5), kind=kOutput, calls=%fused_computation.26 | convolution fusion | flops 104878080 | bytes 6740480 | tf_op jit(solution)/shard_map/dot_general | solution.py:132
  28.3 0.5 fusion.28
  28.9 3.5 %collective-permute-start = (bf16[16,1024]{1,0:T(8,128)(2,1)S(1)}, bf16[16,1024]{1,0:T(8,128)(2,1)S(1)}, u32[]{:S(2)}, u32[]{:S(2)}) collective-permute-start(bf16[16,1024]{1,0:T(8,128)(2,1)S(1)} %concatenate.91), channel_id=1, source_target_pairs={{0,1},{1,0},{2,3},{3,2},{4,5},{5,4},{6,7},{7,6},{8,9},{9,8},{10,11... | collective-permute-start | bytes 98312 | tf_op jit(solution)/shard_map/ppermute | solution.py:118
  32.4 0.4 collective-permute-start.14
  33.1 0.6 dynamic_slice.3
  33.7 1.3 or_select_fusion.kpos_ref
  35.8 0.3 multiply_cosine_fusion.1
  36.1 0.2 fusion.46
  36.3 0.6 constant_dynamic-update-slice_fusion.4
  36.9 1.4 %collective-permute-start.1 = (bf16[32,1024]{1,0:T(8,128)(2,1)S(1)}, bf16[32,1024]{1,0:T(8,128)(2,1)S(1)}, u32[]{:S(2)}, u32[]{:S(2)}) collective-permute-start(bf16[32,1024]{1,0:T(8,128)(2,1)S(1)} %pad_maximum_fusion.3), channel_id=1, source_target_pairs={{0,2},{1,3},{2,4},{3,5},{4,6},{5,7},{6,0},{7,1},{8,10},{9,11},{10,... | collective-permute-start | bytes 196616 | tf_op jit(solution)/shard_map/ppermute | solution.py:118
  38.3 2.6 %collective-permute-start.2 = (bf16[32,1024]{1,0:T(8,128)(2,1)S(1)}, bf16[32,1024]{1,0:T(8,128)(2,1)S(1)}, u32[]{:S(2)}, u32[]{:S(2)}) collective-permute-start(bf16[32,1024]{1,0:T(8,128)(2,1)S(1)} %pad_maximum_fusion.3), channel_id=1, source_target_pairs={{0,4},{1,5},{2,6},{3,7},{4,0},{5,1},{6,2},{7,3},{8,12},{9,13},{10,... | collective-permute-start | bytes 196616 | tf_op jit(solution)/shard_map/ppermute | solution.py:118
  40.9 1.1 collective-permute-start.3
  42.0 0.6 constant_dynamic-update-slice_fusion.3
  42.6 0.6 constant_dynamic-update-slice_fusion.2
  43.3 1.1 collective-permute-done.2
  44.3 0.6 constant_dynamic-update-slice_fusion.1
  45.0 0.6 constant_dynamic-update-slice_fusion
  45.6 1.6 %collective-permute-start.4 = (bf16[128,1024]{1,0:T(8,128)(2,1)}, bf16[128,1024]{1,0:T(8,128)(2,1)S(1)}, u32[]{:S(2)}, u32[]{:S(2)}) collective-permute-start(bf16[128,1024]{1,0:T(8,128)(2,1)} %get-tuple-element.24), channel_id=1, source_target_pairs={{0,8},{1,9},{2,10},{3,11},{4,12},{5,13},{6,14},{7,15},{8,16},{9,17... | collective-permute-start | bytes 786440 | tf_op jit(solution)/shard_map/ppermute | solution.py:118
  47.2 0.7 iota_add_fusion.qpos_ref
  47.9 3.3 %collective-permute-start.5 = (bf16[128,1024]{1,0:T(8,128)(2,1)}, bf16[128,1024]{1,0:T(8,128)(2,1)S(1)}, u32[]{:S(2)}, u32[]{:S(2)}) collective-permute-start(bf16[128,1024]{1,0:T(8,128)(2,1)} %get-tuple-element.24), channel_id=1, source_target_pairs={{0,16},{1,17},{2,18},{3,19},{4,20},{5,21},{6,22},{7,23},{8,24},{9,... | collective-permute-start | bytes 786440 | tf_op jit(solution)/shard_map/ppermute | solution.py:118
  51.2 0.7 collective-permute-start.6
  52.0 3.4 %collective-permute-done.4 = bf16[128,1024]{1,0:T(8,128)(2,1)S(1)} collective-permute-done((bf16[128,1024]{1,0:T(8,128)(2,1)}, bf16[128,1024]{1,0:T(8,128)(2,1)S(1)}, u32[]{:S(2)}, u32[]{:S(2)}) %collective-permute-start.4) | collective-permute-done | bytes 262176 | tf_op jit(solution)/shard_map/ppermute | solution.py:118
  55.3 6.4 %collective-permute-done.5 = bf16[128,1024]{1,0:T(8,128)(2,1)S(1)} collective-permute-done((bf16[128,1024]{1,0:T(8,128)(2,1)}, bf16[128,1024]{1,0:T(8,128)(2,1)S(1)}, u32[]{:S(2)}, u32[]{:S(2)}) %collective-permute-start.5) | collective-permute-done | bytes 262176 | tf_op jit(solution)/shard_map/ppermute | solution.py:118
  61.8 0.5 collective-permute-done.6
  62.3 0.6 gather_fusion
  63.5 0.1 fusion.61
  63.7 3.3 %fusion.87 = (f32[16,5]{0,1:T(8,128)S(1)}, f32[16,5,12288]{2,0,1:T(8,128)S(1)}) fusion(bf16[16,5,128]{2,0,1:T(8,128)(2,1)S(1)} %pad_maximum_fusion.4, bf16[2,12288,128]{2,1,0:T(8,128)(2,1)} %copy.116, pred[16,12288]{1,0:T(8,128)(4,1)S(1)} %fusion.46), kind=kOutput, calls=%fused_computation.177 | convolution fusion | flops 254607280 | bytes 7295296 | tf_op jit(solution)/shard_map/ngd,md->ngm/dot_general | solution.py:66
  67.0 0.8 fusion.1
  67.9 0.9 fusion.41
  68.8 1.5 %collective-permute-start.7 = (bf16[16,640]{1,0:T(8,128)(2,1)S(1)}, bf16[16,640]{1,0:T(8,128)(2,1)S(1)}, u32[]{:S(2)}, u32[]{:S(2)}) collective-permute-start(bf16[16,640]{1,0:T(8,128)(2,1)S(1)} %bitcast.111), channel_id=1, source_target_pairs={{0,1},{1,0},{2,3},{3,2},{4,5},{5,4},{6,7},{7,6},{8,9},{9,8},{10,11... | collective-permute-start | bytes 61448 | tf_op jit(solution)/shard_map/ppermute | solution.py:118
  70.3 0.9 slice_convert_fusion
  71.3 0.2 fusion.50
  71.5 0.7 iota_reduce_fusion
  72.2 0.6 constant_dynamic-update-slice_fusion.19
  72.9 0.6 constant_dynamic-update-slice_fusion.18
  73.5 2.3 %scatter_fusion = bf16[2,12288,128]{2,1,0:T(8,128)(2,1)} fusion(bf16[2,12288,128]{2,1,0:T(8,128)(2,1)} %copy.116, s32[16]{0:T(128)S(1)} %get-tuple-element.6, bf16[16,2,128]{2,0,1:T(8,128)(2,1)S(1)} %maximum_bitcast_fusion), kind=kCustom, calls=%fused_computation.2 | custom fusion | bytes 24640 | tf_op jit(solution)/shard_map/scatter | solution.py:91
  75.9 2.5 %collective-permute-start.9 = (bf16[32,640]{1,0:T(8,128)(2,1)S(1)}, bf16[32,640]{1,0:T(8,128)(2,1)S(1)}, u32[]{:S(2)}, u32[]{:S(2)}) collective-permute-start(bf16[32,640]{1,0:T(8,128)(2,1)S(1)} %get-tuple-element.42), channel_id=1, source_target_pairs={{0,4},{1,5},{2,6},{3,7},{4,0},{5,1},{6,2},{7,3},{8,12},{9,13},{10,... | collective-permute-start | bytes 122888 | tf_op jit(solution)/shard_map/ppermute | solution.py:118
  78.4 0.9 collective-permute-start.10
  79.2 0.6 constant_dynamic-update-slice_fusion.17
  79.9 0.3 collective-permute-done.9
  80.2 0.6 constant_dynamic-update-slice_fusion.16
  80.8 0.8 collective-permute-done.10
  81.6 0.6 constant_dynamic-update-slice_fusion.15
  82.2 1.5 %collective-permute-start.11 = (bf16[128,640]{1,0:T(8,128)(2,1)S(1)}, bf16[128,640]{1,0:T(8,128)(2,1)S(1)}, u32[]{:S(2)}, u32[]{:S(2)}) collective-permute-start(bf16[128,640]{1,0:T(8,128)(2,1)S(1)} %get-tuple-element.30), channel_id=1, source_target_pairs={{0,8},{1,9},{2,10},{3,11},{4,12},{5,13},{6,14},{7,15},{8,16},{9,17... | collective-permute-start | bytes 491528 | tf_op jit(solution)/shard_map/ppermute | solution.py:118
  83.7 2.0 %collective-permute-start.12 = (bf16[128,640]{1,0:T(8,128)(2,1)S(1)}, bf16[128,640]{1,0:T(8,128)(2,1)S(1)}, u32[]{:S(2)}, u32[]{:S(2)}) collective-permute-start(bf16[128,640]{1,0:T(8,128)(2,1)S(1)} %get-tuple-element.30), channel_id=1, source_target_pairs={{0,16},{1,17},{2,18},{3,19},{4,20},{5,21},{6,22},{7,23},{8,24},{9,... | collective-permute-start | bytes 491528 | tf_op jit(solution)/shard_map/ppermute | solution.py:118
  85.7 1.2 collective-permute-start.13
  86.9 0.3 maximum_select_fusion
  87.2 0.5 collective-permute-done.11
  87.6 0.7 constant_dynamic-update-slice_fusion.22
  88.3 3.5 %collective-permute-done.12 = bf16[128,640]{1,0:T(8,128)(2,1)S(1)} collective-permute-done((bf16[128,640]{1,0:T(8,128)(2,1)S(1)}, bf16[128,640]{1,0:T(8,128)(2,1)S(1)}, u32[]{:S(2)}, u32[]{:S(2)}) %collective-permute-start.12) | collective-permute-done | bytes 163872 | tf_op jit(solution)/shard_map/ppermute | solution.py:118
  91.8 0.7 constant_dynamic-update-slice_fusion.21
  92.5 0.7 constant_dynamic-update-slice_fusion.20
  93.2 1.8 %gather_fusion.1 = bf16[16,640]{1,0:T(8,128)(2,1)S(1)} fusion(bf16[512,640]{1,0:T(8,128)(2,1)} %constant_dynamic-update-slice_fusion.20, s32[1024]{0:T(1024)S(1)} %pad_clamp_fusion), kind=kCustom, calls=%fused_computation.1 | custom fusion | bytes 41024 | tf_op jit(solution)/shard_map/jit(_take)/gather | solution.py:160
  94.9 0.7 broadcast_select_fusion.1
  95.6 3.8 %fusion.16 = f32[256,256]{0,1:T(8,128)S(1)} fusion(bf16[256,5120]{1,0:T(8,128)(2,1)} %all-gather.2.cloned.1.call-done, bf16[640,8,2,128]{3,2,1,0:T(2,128)(2,1)} %bitcast.99, f32[256]{0:T(256)S(1)} %bitcast.113), kind=kOutput, calls=%fused_computation.23 | convolution fusion | flops 671154176 | bytes 5506048 | tf_op jit(solution)/shard_map/dot_general | solution.py:133
  99.5 5.1 %convolution_add_fusion = f32[256,640]{1,0:T(8,128)S(1)} fusion(bf16[256,5120]{1,0:T(8,128)(2,1)S(1)} %copy-done.9, bf16[5120,640]{1,0:T(8,128)(2,1)} %param.13, f32[640]{0:T(1024)S(1)} %copy-done.5), kind=kOutput, calls=%fused_computation.22 | convolution fusion | flops 1677885440 | bytes 9832960 | tf_op jit(solution)/shard_map/dot_general | solution.py:132
  104.6 0.2 copy.41
  105.2 0.6 fusion.60
  105.8 2.6 %collective-permute-start.15 = (bf16[2,256,128]{2,1,0:T(8,128)(2,1)S(1)}, bf16[2,256,128]{2,1,0:T(8,128)(2,1)S(1)}, u32[]{:S(2)}, u32[]{:S(2)}) collective-permute-start(bf16[2,256,128]{2,1,0:T(8,128)(2,1)S(1)} %pad_maximum_fusion.2), channel_id=1, source_target_pairs={{0,1},{1,0},{2,3},{3,2},{4,5},{5,4},{6,7},{7,6},{8,9},{9,8},{10,11... | collective-permute-start | bytes 393224 | tf_op jit(solution)/shard_map/ppermute | solution.py:14
  108.6 0.9 copy.45.q_ref
  109.6 1.2 fusion.49
  110.8 9.2 %shard_map.138 = bf16[256,640]{1,0:T(8,128)(2,1)} custom-call(bf16[256,640]{1,0:T(8,128)(2,1)} %copy.45.q_ref, bf16[2560,128]{1,0:T(8,128)(2,1)} %get-tuple-element.13.k_ref, bf16[2560,128]{1,0:T(8,128)(2,1)} %get-tuple-element.12.v_ref, s32[256,1]{1,0:T(8,128)} %iota_add_fusion.qpos_ref, s32[1,2560]{1,0:T(1,128)} %or_select_fusion.kpos_ref), custom_call_target="tpu_custom_call" | custom-call | tf_op jit(solution)/shard_map/pallas_call | solution.py:47
  (89 shorter events, 2.3 us)
Async XLA Ops:
  7.2 6.5 %copy-start.4 = (bf16[16,1280]{1,0:T(8,128)(2,1)S(1)}, bf16[16,1280]{1,0:T(8,128)(2,1)}, u32[]{:S(2)}) copy-start(bf16[16,1280]{1,0:T(8,128)(2,1)} %param.11) | copy-start | bytes 122884
  7.2 16.9 %copy-start.8 = (s32[16]{0:T(128)S(1)}, s32[16]{0:T(128)}, u32[]{:S(2)}) copy-start(s32[16]{0:T(128)} %param.18) | copy-start | bytes 196
  7.2 17.1 %copy-start.5 = (f32[640]{0:T(1024)S(1)}, f32[640]{0:T(1024)}, u32[]{:S(2)}) copy-start(f32[640]{0:T(1024)} %param.15) | copy-start | bytes 7684
  7.2 88.4 %all-gather.2.cloned.1.call-start = ((), (), s32[]{:S(2)}) async-start(), calls=%async_computation | async-start | bytes 3276800 | tf_op jit(solution)/shard_map/all_gather | solution.py:131
  24.3 4.0 %copy-start = (bf16[5120,2,128]{2,1,0:T(2,128)(2,1)S(1)}, bf16[5120,2,128]{2,1,0:T(2,128)(2,1)}, u32[]{:S(2)}) copy-start(bf16[5120,2,128]{2,1,0:T(2,128)(2,1)} %param.14) | copy-start | bytes 7864324
  24.3 4.0 %copy-start.6 = (f32[2,128]{1,0:T(2,128)S(1)}, f32[2,128]{1,0:T(2,128)}, u32[]{:S(2)}) copy-start(f32[2,128]{1,0:T(2,128)} %param.16) | copy-start | bytes 3076
  28.3 4.2 %copy-start.1 = (bf16[2,1024,128]{2,1,0:T(8,128)(2,1)S(1)}, bf16[2,1024,128]{2,1,0:T(8,128)(2,1)}, u32[]{:S(2)}) copy-start(bf16[2,1024,128]{2,1,0:T(8,128)(2,1)} %param.20) | copy-start | bytes 1572868
  28.3 4.6 %copy-start.7 = (s32[16]{0:T(128)S(1)}, s32[16]{0:T(128)}, u32[]{:S(2)}) copy-start(s32[16]{0:T(128)} %param.19) | copy-start | bytes 196
  28.3 4.8 %copy-start.10 = (s32[16]{0:T(128)S(1)}, s32[16]{0:T(128)}, u32[]{:S(2)}) copy-start(s32[16]{0:T(128)} %param.21) | copy-start | bytes 196
  28.9 8.1 %collective-permute-start = (bf16[16,1024]{1,0:T(8,128)(2,1)S(1)}, bf16[16,1024]{1,0:T(8,128)(2,1)S(1)}, u32[]{:S(2)}, u32[]{:S(2)}) collective-permute-start(bf16[16,1024]{1,0:T(8,128)(2,1)S(1)} %concatenate.91), channel_id=1, source_target_pairs={{0,1},{1,0},{2,3},{3,2},{4,5},{5,4},{6,7},{7,6},{8,9},{9,8},{10,11... | collective-permute-start | bytes 98312 | tf_op jit(solution)/shard_map/ppermute | solution.py:118
  32.4 54.4 %collective-permute-start.14 = (bf16[2,1024,128]{2,1,0:T(8,128)(2,1)S(1)}, bf16[2,1024,128]{2,1,0:T(8,128)(2,1)S(1)}, u32[]{:S(2)}, u32[]{:S(2)}) collective-permute-start(bf16[2,1024,128]{2,1,0:T(8,128)(2,1)S(1)} %copy-done.1), channel_id=1, source_target_pairs={{0,1},{1,0},{2,3},{3,2},{4,5},{5,4},{6,7},{7,6},{8,9},{9,8},{10,11... | collective-permute-start | bytes 1572872 | tf_op jit(solution)/shard_map/ppermute | solution.py:14
  36.9 5.7 %collective-permute-start.1 = (bf16[32,1024]{1,0:T(8,128)(2,1)S(1)}, bf16[32,1024]{1,0:T(8,128)(2,1)S(1)}, u32[]{:S(2)}, u32[]{:S(2)}) collective-permute-start(bf16[32,1024]{1,0:T(8,128)(2,1)S(1)} %pad_maximum_fusion.3), channel_id=1, source_target_pairs={{0,2},{1,3},{2,4},{3,5},{4,6},{5,7},{6,0},{7,1},{8,10},{9,11},{10,... | collective-permute-start | bytes 196616 | tf_op jit(solution)/shard_map/ppermute | solution.py:118
  38.3 6.0 %collective-permute-start.2 = (bf16[32,1024]{1,0:T(8,128)(2,1)S(1)}, bf16[32,1024]{1,0:T(8,128)(2,1)S(1)}, u32[]{:S(2)}, u32[]{:S(2)}) collective-permute-start(bf16[32,1024]{1,0:T(8,128)(2,1)S(1)} %pad_maximum_fusion.3), channel_id=1, source_target_pairs={{0,4},{1,5},{2,6},{3,7},{4,0},{5,1},{6,2},{7,3},{8,12},{9,13},{10,... | collective-permute-start | bytes 196616 | tf_op jit(solution)/shard_map/ppermute | solution.py:118
  40.9 4.0 %collective-permute-start.3 = (bf16[32,1024]{1,0:T(8,128)(2,1)S(1)}, bf16[32,1024]{1,0:T(8,128)(2,1)S(1)}, u32[]{:S(2)}, u32[]{:S(2)}) collective-permute-start(bf16[32,1024]{1,0:T(8,128)(2,1)S(1)} %pad_maximum_fusion.3), channel_id=1, source_target_pairs={{0,6},{1,7},{2,0},{3,1},{4,2},{5,3},{6,4},{7,5},{8,14},{9,15},{10,... | collective-permute-start | bytes 196616 | tf_op jit(solution)/shard_map/ppermute | solution.py:118
  45.6 9.7 %collective-permute-start.4 = (bf16[128,1024]{1,0:T(8,128)(2,1)}, bf16[128,1024]{1,0:T(8,128)(2,1)S(1)}, u32[]{:S(2)}, u32[]{:S(2)}) collective-permute-start(bf16[128,1024]{1,0:T(8,128)(2,1)} %get-tuple-element.24), channel_id=1, source_target_pairs={{0,8},{1,9},{2,10},{3,11},{4,12},{5,13},{6,14},{7,15},{8,16},{9,17... | collective-permute-start | bytes 786440 | tf_op jit(solution)/shard_map/ppermute | solution.py:118
  47.9 13.8 %collective-permute-start.5 = (bf16[128,1024]{1,0:T(8,128)(2,1)}, bf16[128,1024]{1,0:T(8,128)(2,1)S(1)}, u32[]{:S(2)}, u32[]{:S(2)}) collective-permute-start(bf16[128,1024]{1,0:T(8,128)(2,1)} %get-tuple-element.24), channel_id=1, source_target_pairs={{0,16},{1,17},{2,18},{3,19},{4,20},{5,21},{6,22},{7,23},{8,24},{9,... | collective-permute-start | bytes 786440 | tf_op jit(solution)/shard_map/ppermute | solution.py:118
  51.2 11.1 %collective-permute-start.6 = (bf16[128,1024]{1,0:T(8,128)(2,1)}, bf16[128,1024]{1,0:T(8,128)(2,1)S(1)}, u32[]{:S(2)}, u32[]{:S(2)}) collective-permute-start(bf16[128,1024]{1,0:T(8,128)(2,1)} %get-tuple-element.24), channel_id=1, source_target_pairs={{0,24},{1,25},{2,26},{3,27},{4,28},{5,29},{6,30},{7,31},{8,0},{9,1... | collective-permute-start | bytes 786440 | tf_op jit(solution)/shard_map/ppermute | solution.py:118
  62.3 1.1 copy-start.2
  63.5 4.4 %slice-start = ((s8[6291456]{0:T(1024)(128)(4,1)}), s8[2097152]{0:T(1024)(128)(4,1)S(1)}, s32[]{:S(2)}) async-start(s8[6291456]{0:T(1024)(128)(4,1)} %bitcast.97), calls=%async_computation.1 | async-start | bytes 4194304
  63.7 4.2 %slice-start.1 = ((s8[6291456]{0:T(1024)(128)(4,1)}), s8[4194304]{0:T(1024)(128)(4,1)S(1)}, s32[]{:S(2)}) async-start(s8[6291456]{0:T(1024)(128)(4,1)} %bitcast.97), calls=%async_computation.2 | async-start | bytes 8388608
  68.8 4.1 %collective-permute-start.7 = (bf16[16,640]{1,0:T(8,128)(2,1)S(1)}, bf16[16,640]{1,0:T(8,128)(2,1)S(1)}, u32[]{:S(2)}, u32[]{:S(2)}) collective-permute-start(bf16[16,640]{1,0:T(8,128)(2,1)S(1)} %bitcast.111), channel_id=1, source_target_pairs={{0,1},{1,0},{2,3},{3,2},{4,5},{5,4},{6,7},{7,6},{8,9},{9,8},{10,11... | collective-permute-start | bytes 61448 | tf_op jit(solution)/shard_map/ppermute | solution.py:118
  73.5 5.7 %collective-permute-start.8 = (bf16[32,640]{1,0:T(8,128)(2,1)S(1)}, bf16[32,640]{1,0:T(8,128)(2,1)S(1)}, u32[]{:S(2)}, u32[]{:S(2)}) collective-permute-start(bf16[32,640]{1,0:T(8,128)(2,1)S(1)} %get-tuple-element.42), channel_id=1, source_target_pairs={{0,2},{1,3},{2,4},{3,5},{4,6},{5,7},{6,0},{7,1},{8,10},{9,11},{10,... | collective-permute-start | bytes 122888 | tf_op jit(solution)/shard_map/ppermute | solution.py:118
  75.9 4.4 %collective-permute-start.9 = (bf16[32,640]{1,0:T(8,128)(2,1)S(1)}, bf16[32,640]{1,0:T(8,128)(2,1)S(1)}, u32[]{:S(2)}, u32[]{:S(2)}) collective-permute-start(bf16[32,640]{1,0:T(8,128)(2,1)S(1)} %get-tuple-element.42), channel_id=1, source_target_pairs={{0,4},{1,5},{2,6},{3,7},{4,0},{5,1},{6,2},{7,3},{8,12},{9,13},{10,... | collective-permute-start | bytes 122888 | tf_op jit(solution)/shard_map/ppermute | solution.py:118
  78.4 3.3 %collective-permute-start.10 = (bf16[32,640]{1,0:T(8,128)(2,1)S(1)}, bf16[32,640]{1,0:T(8,128)(2,1)S(1)}, u32[]{:S(2)}, u32[]{:S(2)}) collective-permute-start(bf16[32,640]{1,0:T(8,128)(2,1)S(1)} %get-tuple-element.42), channel_id=1, source_target_pairs={{0,6},{1,7},{2,0},{3,1},{4,2},{5,3},{6,4},{7,5},{8,14},{9,15},{10,... | collective-permute-start | bytes 122888 | tf_op jit(solution)/shard_map/ppermute | solution.py:118
  82.2 5.4 %collective-permute-start.11 = (bf16[128,640]{1,0:T(8,128)(2,1)S(1)}, bf16[128,640]{1,0:T(8,128)(2,1)S(1)}, u32[]{:S(2)}, u32[]{:S(2)}) collective-permute-start(bf16[128,640]{1,0:T(8,128)(2,1)S(1)} %get-tuple-element.30), channel_id=1, source_target_pairs={{0,8},{1,9},{2,10},{3,11},{4,12},{5,13},{6,14},{7,15},{8,16},{9,17... | collective-permute-start | bytes 491528 | tf_op jit(solution)/shard_map/ppermute | solution.py:118
  83.7 8.1 %collective-permute-start.12 = (bf16[128,640]{1,0:T(8,128)(2,1)S(1)}, bf16[128,640]{1,0:T(8,128)(2,1)S(1)}, u32[]{:S(2)}, u32[]{:S(2)}) collective-permute-start(bf16[128,640]{1,0:T(8,128)(2,1)S(1)} %get-tuple-element.30), channel_id=1, source_target_pairs={{0,16},{1,17},{2,18},{3,19},{4,20},{5,21},{6,22},{7,23},{8,24},{9,... | collective-permute-start | bytes 491528 | tf_op jit(solution)/shard_map/ppermute | solution.py:118
  85.7 6.8 %collective-permute-start.13 = (bf16[128,640]{1,0:T(8,128)(2,1)S(1)}, bf16[128,640]{1,0:T(8,128)(2,1)S(1)}, u32[]{:S(2)}, u32[]{:S(2)}) collective-permute-start(bf16[128,640]{1,0:T(8,128)(2,1)S(1)} %get-tuple-element.30), channel_id=1, source_target_pairs={{0,24},{1,25},{2,26},{3,27},{4,28},{5,29},{6,30},{7,31},{8,0},{9,1... | collective-permute-start | bytes 491528 | tf_op jit(solution)/shard_map/ppermute | solution.py:118
  95.6 3.9 %copy-start.9 = (bf16[256,5120]{1,0:T(8,128)(2,1)S(1)}, bf16[256,5120]{1,0:T(8,128)(2,1)}, u32[]{:S(2)}) copy-start(bf16[256,5120]{1,0:T(8,128)(2,1)} %all-gather.2.cloned.1.call-done) | copy-start | bytes 7864324
  105.8 14.2 %copy-start.3 = (bf16[2,256,128]{2,1,0:T(8,128)(2,1)}, bf16[2,256,128]{2,1,0:T(8,128)(2,1)S(1)}, u32[]{:S(2)}) copy-start(bf16[2,256,128]{2,1,0:T(8,128)(2,1)S(1)} %pad_maximum_fusion.2) | copy-start | bytes 393220
  105.8 3.7 %collective-permute-start.15 = (bf16[2,256,128]{2,1,0:T(8,128)(2,1)S(1)}, bf16[2,256,128]{2,1,0:T(8,128)(2,1)S(1)}, u32[]{:S(2)}, u32[]{:S(2)}) collective-permute-start(bf16[2,256,128]{2,1,0:T(8,128)(2,1)S(1)} %pad_maximum_fusion.2), channel_id=1, source_target_pairs={{0,1},{1,0},{2,3},{3,2},{4,5},{5,4},{6,7},{7,6},{8,9},{9,8},{10,11... | collective-permute-start | bytes 393224 | tf_op jit(solution)/shard_map/ppermute | solution.py:14
Sparse Core Ops, SparseCore 0:
  32.6 36.1 all-gather.1

commit v7 on v5

--- a/solution.py
+++ b/solution.py
@@ -98,7 +98,7 @@
 
 def tree_gather(value):
     buffer = value
-    for stride, count in ((1, 2), (2, 4), (8, 4)):
+    for level, stride, count in (("c", 1, 2), ("y", 2, 4), ("z", 8, 4)):
       parts = [buffer]
       for shift in range(1, count):
           pairs = []
@@ -107,8 +107,18 @@
               target = i + (((digit + shift) % count) - digit) * stride
               pairs.append((i, target))
           parts.append(lax.ppermute(buffer, "tok", pairs))
-      buffer = jnp.concatenate(parts, axis=0)
-    return buffer
+      if level != "z":
+          buffer = jnp.concatenate(parts, axis=0)
+    return parts
+
+
+def pick(parts, rows):
+    block = parts[0].shape[0]
+    out = None
+    for k, part in enumerate(parts):
+        got = jnp.take(part, rows % block, axis=0)
+        out = got if out is None else jnp.where((rows // block == k)[:, None], got, out)
+    return out
 
 
 def tree_row(place, source, rows):
@@ -139,16 +149,16 @@
     sent = jnp.concatenate([dec_q.astype(jnp.bfloat16), dec_kv.astype(jnp.bfloat16), ids, pad], axis=1)
     got = tree_gather(sent)
     rows = tree_row(tok_place, owner_slots // dec_count, dec_count) + owner_slots % dec_count
-    chosen = jnp.take(got, rows, axis=0)
+    chosen = pick(got, rows)
     dec_query = chosen[:, :q_width]
     dec_keyval = chosen[:, q_width:q_width + 2 * kv_width].reshape(dec_count, 2, kv_width)
     served, new_pool = serve_owner(dec_query, dec_keyval, dec_lengths, dec_pool)
     back = tree_gather(served)
-    got_ids = got[:, q_width + 2 * kv_width:used].astype(jnp.int32)
+    got_ids = jnp.concatenate([part[:, q_width + 2 * kv_width:used] for part in got], axis=0).astype(jnp.int32)
     requests = got_ids[:, 0] * dec_count + got_ids[:, 1]
     wanted = tok_place * dec_count + jnp.arange(dec_count, dtype=jnp.int32)
     where = jnp.argmax(requests[None, :] == wanted[:, None], axis=1)
-    dec_attn = jnp.take(back, where, axis=0)
+    dec_attn = pick(back, where.astype(jnp.int32))
     all_query, all_keyval = project(pre_tokens, w_query, kv_weight, b_query, kv_bias)
     return dec_attn, new_pool, all_query, all_keyval
 

time: 125 us -> 125 us (level)
  local copies, waits for them, and re-layouts: 13 us -> 16.8 us
  waiting for transfers between devices: 28.4 us -> 26 us
    gather x2 -> x8, local copies, waits for them, and re-layouts: 1.19 us -> 4.74 us  [pick(): got = jnp.take(part, rows % block, axis=0)]
    ppermute x14, starting transfers between devices: 20.6 us -> 17.8 us  [tree_gather(): parts.append(lax.ppermute(buffer, 'tok', pairs))]
    ppermute x14, waiting for transfers between devices: 28.3 us -> 26 us  [tree_gather(): parts.append(lax.ppermute(buffer, 'tok', pairs))]
    ppermute x2, starting transfers between devices: 1.9 us -> 3.68 us  [swapped(): lax.ppermute(value, axis, [(i, i ^ 1 << distance) for i in range(lax.axis...]
    unnamed x45 -> x36, local copies, waits for them, and re-layouts: 7.23 us -> 7.1 us
  transfers between devices with their start and end apart: 17 -> 17, of which waited for: 7 -> 9; matrix products, arithmetic and copies ran while one was open for 17% -> 19% of each run, Pallas kernels for 0% -> 0%
where the time goes in v7:
time: 125 us
  waiting for transfers between devices  26 us (21%)
  starting transfers between devices  21.5 us (17%)
  matrix products  17.9 us (14%)
  local copies, waits for them, and re-layouts  16.8 us (13%)
  between operations  15.2 us (12%)
  blocking collectives  10.4 us (8%)
  Pallas kernels  9.2 us (7%)
  other arithmetic  7.73 us (6%)
    ppermute x14, waiting for transfers between devices, tree_gather(): parts.append(lax.ppermute(buffer, 'tok', pairs))  26 us
    ppermute x14, starting transfers between devices, tree_gather(): parts.append(lax.ppermute(buffer, 'tok', pairs))  17.8 us
    all_gather x1, blocking collectives, project(): cols = lax.all_gather(rows, 'kv', axis=1, tiled=True)  10.4 us
    dot_general x2, matrix products, project(): query = jnp.dot(cols, w_query, preferred_element_type=jnp.float32) + b_query  9.37 us
    pallas_call x1, Pallas kernels, attend(): pl.pallas_call(attend_kernel, grid=(width // HD,), in_specs=[pl.BlockSpec...  9.2 us
    unnamed x36, local copies, waits for them, and re-layouts  7.1 us
    gather x8, local copies, waits for them, and re-layouts, pick(): got = jnp.take(part, rows % block, axis=0)  4.74 us
    dot_general x2, matrix products, project(): jnp.dot(cols, kv_weight, preferred_element_type=jnp.float32) + kv_bias  4.31 us
  transfers between devices with their start and end apart: 17, of which 9 were waited for; matrix products, arithmetic and copies ran while one was open for 19% of the time, Pallas kernels for 0%

profile of v7, /device:TPU:1, one launch (start us, length us, event | category | flops | bytes accessed | tf_op | source)
XLA Modules:
  0.0 124.8 jit_solution(13615368510317153351)
XLA Ops:
  7.3 6.7 %copy.114 = bf16[2,12288,128]{2,1,0:T(8,128)(2,1)} copy(bf16[2,12288,128]{2,1,0:T(8,128)(2,1)} %param.21) | data formatting | bytes 12582912
  14.1 0.1 copy.51
  14.2 0.1 copy.50
  14.3 10.4 %all_gather.6 = bf16[16,5120]{1,0:T(8,128)(2,1)S(1)} all-gather(bf16[16,1280]{1,0:T(8,128)(2,1)S(1)} %copy-done.3), channel_id=1, replica_groups=mesh['kv'=4,'tok'=32] {'kv'}, dimensions={1}, use_global_device_ids=true | all-gather | bytes 204800 | tf_op jit(solution)/shard_map/all_gather | solution.py:132
  24.7 0.5 fusion.19
  25.2 4.3 %fusion.15 = bf16[16,640]{1,0:T(8,128)(2,1)S(1)} fusion(bf16[16,5120]{1,0:T(8,128)(2,1)S(1)} %all_gather.6, bf16[5120,640]{1,0:T(8,128)(2,1)} %param.17, f32[640]{0:T(1024)S(1)} %copy-done.4), kind=kOutput, calls=%fused_computation.29 | convolution fusion | flops 104878080 | bytes 6740480 | tf_op jit(solution)/shard_map/dot_general | solution.py:133
  29.5 0.1 concatenate.78
  29.6 3.2 %collective-permute-start = (bf16[16,1024]{1,0:T(8,128)(2,1)S(1)}, bf16[16,1024]{1,0:T(8,128)(2,1)S(1)}, u32[]{:S(2)}, u32[]{:S(2)}) collective-permute-start(bf16[16,1024]{1,0:T(8,128)(2,1)S(1)} %concatenate.78), channel_id=1, source_target_pairs={{0,1},{1,0},{2,3},{3,2},{4,5},{5,4},{6,7},{7,6},{8,9},{9,8},{10,11... | collective-permute-start | bytes 98312 | tf_op jit(solution)/shard_map/ppermute | solution.py:109
  32.8 0.1 collective-permute-start.14
  32.9 0.6 dynamic_slice.3
  33.5 1.2 or_select_fusion.kpos_ref
  35.6 0.1 reduce.18
  35.7 0.7 iota_add_fusion.qpos_ref
  36.4 0.1 multiply_cosine_fusion.3
  36.5 0.2 fusion.31
  36.8 2.8 %collective-permute-start.3 = (bf16[32,1024]{1,0:T(8,128)(2,1)S(1)}, bf16[32,1024]{1,0:T(8,128)(2,1)S(1)}, u32[]{:S(2)}, u32[]{:S(2)}) collective-permute-start(bf16[32,1024]{1,0:T(8,128)(2,1)S(1)} %pad_maximum_fusion.3), channel_id=1, source_target_pairs={{0,6},{1,7},{2,0},{3,1},{4,2},{5,3},{6,4},{7,5},{8,14},{9,15},{10,... | collective-permute-start | bytes 196616 | tf_op jit(solution)/shard_map/ppermute | solution.py:109
  39.5 0.4 collective-permute-start.2
  39.9 0.7 collective-permute-start.1
  40.6 5.4 %collective-permute-done.1 = bf16[32,1024]{1,0:T(8,128)(2,1)S(1)} collective-permute-done((bf16[32,1024]{1,0:T(8,128)(2,1)S(1)}, bf16[32,1024]{1,0:T(8,128)(2,1)S(1)}, u32[]{:S(2)}, u32[]{:S(2)}) %collective-permute-start.1) | collective-permute-done | bytes 65568 | tf_op jit(solution)/shard_map/ppermute | solution.py:109
  46.1 3.8 %collective-permute-start.6 = (bf16[128,1024]{1,0:T(8,128)(2,1)S(1)}, bf16[128,1024]{1,0:T(8,128)(2,1)S(1)}, u32[]{:S(2)}, u32[]{:S(2)}) collective-permute-start(bf16[128,1024]{1,0:T(8,128)(2,1)S(1)} %constant_dynamic-update-slice_fusion), channel_id=1, source_target_pairs={{0,24},{1,25},{2,26},{3,27},{4,28},{5,29},{6,30},{7,31},{8,0},{9,1... | collective-permute-start | bytes 786440 | tf_op jit(solution)/shard_map/ppermute | solution.py:109
  49.9 0.7 collective-permute-start.4
  50.6 0.3 multiply_cosine_fusion.1
  50.9 0.6 gather_fusion.3
  51.6 8.5 %collective-permute-done.6 = bf16[128,1024]{1,0:T(8,128)(2,1)S(1)} collective-permute-done((bf16[128,1024]{1,0:T(8,128)(2,1)S(1)}, bf16[128,1024]{1,0:T(8,128)(2,1)S(1)}, u32[]{:S(2)}, u32[]{:S(2)}) %collective-permute-start.6) | collective-permute-done | bytes 262176 | tf_op jit(solution)/shard_map/ppermute | solution.py:109
  60.1 0.6 gather_fusion
  60.7 0.6 gather_fusion.1
  61.3 3.3 %collective-permute-done.4 = bf16[128,1024]{1,0:T(8,128)(2,1)S(1)} collective-permute-done((bf16[128,1024]{1,0:T(8,128)(2,1)S(1)}, bf16[128,1024]{1,0:T(8,128)(2,1)S(1)}, u32[]{:S(2)}, u32[]{:S(2)}) %collective-permute-start.4) | collective-permute-done | bytes 262176 | tf_op jit(solution)/shard_map/ppermute | solution.py:109
  64.6 0.6 gather_fusion.2
  65.2 0.1 fusion.46
  65.4 0.1 fusion.61
  65.9 2.3 %scatter_fusion = bf16[2,12288,128]{2,1,0:T(8,128)(2,1)} fusion(bf16[2,12288,128]{2,1,0:T(8,128)(2,1)} %copy.114, s32[16]{0:T(128)S(1)} %get-tuple-element.19, bf16[16,2,128]{2,0,1:T(8,128)(2,1)S(1)} %maximum_bitcast_fusion), kind=kCustom, calls=%fused_computation.8 | custom fusion | bytes 24640 | tf_op jit(solution)/shard_map/scatter | solution.py:90
  68.4 3.4 %fusion.77 = (f32[16,5]{0,1:T(8,128)S(1)}, f32[16,5,12288]{2,0,1:T(8,128)S(1)}) fusion(bf16[2,12288,128]{2,1,0:T(8,128)(2,1)} %scatter_fusion, bf16[16,5,64]{2,0,1:T(8,128)(2,1)S(1)} %get-tuple-element.30, bf16[16,5,64]{2,0,1:T(8,128)(2,1)S(1)} %get-tuple-element.29, pred[16,12288]{1,0:T(8,128)(4,1)S(1)} %fusion.31), kind=kOutput, calls=%fused_computation.180 | convolution fusion | flops 254648240 | bytes 7295296 | tf_op jit(solution)/shard_map/ngd,md->ngm/dot_general | solution.py:66
  71.8 0.8 fusion.1
  72.6 0.9 fusion.28
  73.5 0.9 collective-permute-start.7
  74.3 0.7 iota_reduce_fusion
  75.2 2.7 %collective-permute-start.10 = (bf16[32,640]{1,0:T(8,128)(2,1)S(1)}, bf16[32,640]{1,0:T(8,128)(2,1)S(1)}, u32[]{:S(2)}, u32[]{:S(2)}) collective-permute-start(bf16[32,640]{1,0:T(8,128)(2,1)S(1)} %get-tuple-element.33), channel_id=1, source_target_pairs={{0,6},{1,7},{2,0},{3,1},{4,2},{5,3},{6,4},{7,5},{8,14},{9,15},{10,... | collective-permute-start | bytes 122888 | tf_op jit(solution)/shard_map/ppermute | solution.py:109
  77.9 1.4 %collective-permute-done.8 = bf16[32,640]{1,0:T(8,128)(2,1)S(1)} collective-permute-done((bf16[32,640]{1,0:T(8,128)(2,1)S(1)}, bf16[32,640]{1,0:T(8,128)(2,1)S(1)}, u32[]{:S(2)}, u32[]{:S(2)}) %collective-permute-start.8) | collective-permute-done | bytes 40992 | tf_op jit(solution)/shard_map/ppermute | solution.py:109
  79.3 3.0 %collective-permute-done.9 = bf16[32,640]{1,0:T(8,128)(2,1)S(1)} collective-permute-done((bf16[32,640]{1,0:T(8,128)(2,1)S(1)}, bf16[32,640]{1,0:T(8,128)(2,1)S(1)}, u32[]{:S(2)}, u32[]{:S(2)}) %collective-permute-start.9) | collective-permute-done | bytes 40992 | tf_op jit(solution)/shard_map/ppermute | solution.py:109
  82.3 2.4 %collective-permute-start.12 = (bf16[128,640]{1,0:T(8,128)(2,1)S(1)}, bf16[128,640]{1,0:T(8,128)(2,1)S(1)}, u32[]{:S(2)}, u32[]{:S(2)}) collective-permute-start(bf16[128,640]{1,0:T(8,128)(2,1)S(1)} %constant_dynamic-update-slice_fusion.7), channel_id=1, source_target_pairs={{0,16},{1,17},{2,18},{3,19},{4,20},{5,21},{6,22},{7,23},{8,24},{9,... | collective-permute-start | bytes 491528 | tf_op jit(solution)/shard_map/ppermute | solution.py:109
  84.7 0.3 collective-permute-start.11
  85.0 0.6 gather_fusion.7
  85.6 0.3 maximum_select_fusion
  85.9 3.4 %collective-permute-done.13 = bf16[128,640]{1,0:T(8,128)(2,1)S(1)} collective-permute-done((bf16[128,640]{1,0:T(8,128)(2,1)S(1)}, bf16[128,640]{1,0:T(8,128)(2,1)S(1)}, u32[]{:S(2)}, u32[]{:S(2)}) %collective-permute-start.13) | collective-permute-done | bytes 163872 | tf_op jit(solution)/shard_map/ppermute | solution.py:109
  89.3 0.6 gather_fusion.6
  89.9 0.3 collective-permute-done.12
  90.2 0.6 gather_fusion.5
  90.8 0.6 collective-permute-done.11
  91.4 0.6 gather_fusion.4
  92.0 0.7 fusion.51
  92.7 3.8 %fusion.12 = f32[256,256]{0,1:T(8,128)S(1)} fusion(bf16[256,5120]{1,0:T(8,128)(2,1)} %all-gather.2.cloned.1.call-done, bf16[640,8,2,128]{3,2,1,0:T(2,128)(2,1)} %bitcast.78, f32[256]{0:T(256)S(1)} %bitcast.90), kind=kOutput, calls=%fused_computation.27 | convolution fusion | flops 671154176 | bytes 5506048 | tf_op jit(solution)/shard_map/dot_general | solution.py:134
  96.6 5.1 %convolution_add_fusion = f32[256,640]{1,0:T(8,128)S(1)} fusion(bf16[256,5120]{1,0:T(8,128)(2,1)S(1)} %copy-done.8, bf16[5120,640]{1,0:T(8,128)(2,1)} %param.17, f32[640]{0:T(1024)S(1)} %copy-done.4), kind=kOutput, calls=%fused_computation.26 | convolution fusion | flops 1677885440 | bytes 9832960 | tf_op jit(solution)/shard_map/dot_general | solution.py:133
  101.6 0.2 copy.62
  101.9 0.1 copy.73
  102.0 0.1 copy.72
  102.1 0.1 copy.71
  102.2 0.6 fusion.44
  102.8 0.1 pad_maximum_fusion.2
  102.9 3.6 %collective-permute-start.15 = (bf16[2,256,128]{2,1,0:T(8,128)(2,1)S(1)}, bf16[2,256,128]{2,1,0:T(8,128)(2,1)S(1)}, u32[]{:S(2)}, u32[]{:S(2)}) collective-permute-start(bf16[2,256,128]{2,1,0:T(8,128)(2,1)S(1)} %pad_maximum_fusion.2), channel_id=1, source_target_pairs={{0,1},{1,0},{2,3},{3,2},{4,5},{5,4},{6,7},{7,6},{8,9},{9,8},{10,11... | collective-permute-start | bytes 393224 | tf_op jit(solution)/shard_map/ppermute | solution.py:14
  106.5 0.1 subtract_convert_fusion
  106.6 0.9 copy.66.q_ref
  107.5 0.1 maximum_select_fusion.1
  107.6 1.2 fusion.34
  108.8 9.2 %shard_map.138 = bf16[256,640]{1,0:T(8,128)(2,1)} custom-call(bf16[256,640]{1,0:T(8,128)(2,1)} %copy.66.q_ref, bf16[2560,128]{1,0:T(8,128)(2,1)} %get-tuple-element.22.k_ref, bf16[2560,128]{1,0:T(8,128)(2,1)} %get-tuple-element.21.v_ref, s32[256,1]{1,0:T(8,128)} %iota_add_fusion.qpos_ref, s32[1,2560]{1,0:T(1,128)} %or_select_fusion.kpos_ref), custom_call_target="tpu_custom_call" | custom-call | tf_op jit(solution)/shard_map/pallas_call | solution.py:47
  (90 shorter events, 1.3 us)
Async XLA Ops:
  7.2 6.9 %copy-start.6 = (s32[16]{0:T(128)S(1)}, s32[16]{0:T(128)}, u32[]{:S(2)}) copy-start(s32[16]{0:T(128)} %param.22) | copy-start | bytes 196
  7.2 7.1 %copy-start.3 = (bf16[16,1280]{1,0:T(8,128)(2,1)S(1)}, bf16[16,1280]{1,0:T(8,128)(2,1)}, u32[]{:S(2)}) copy-start(bf16[16,1280]{1,0:T(8,128)(2,1)} %param.15) | copy-start | bytes 122884
  7.2 17.5 %copy-start.5 = (f32[2,128]{1,0:T(2,128)S(1)}, f32[2,128]{1,0:T(2,128)}, u32[]{:S(2)}) copy-start(f32[2,128]{1,0:T(2,128)} %param.20) | copy-start | bytes 3076
  7.2 17.5 %copy-start = (bf16[5120,2,128]{2,1,0:T(2,128)(2,1)S(1)}, bf16[5120,2,128]{2,1,0:T(2,128)(2,1)}, u32[]{:S(2)}) copy-start(bf16[5120,2,128]{2,1,0:T(2,128)(2,1)} %param.18) | copy-start | bytes 7864324
  7.2 85.5 %all-gather.2.cloned.1.call-start = ((), (), s32[]{:S(2)}) async-start(), calls=%async_computation | async-start | bytes 3276800 | tf_op jit(solution)/shard_map/all_gather | solution.py:132
  13.9 11.2 %copy-start.4 = (f32[640]{0:T(1024)S(1)}, f32[640]{0:T(1024)}, u32[]{:S(2)}) copy-start(f32[640]{0:T(1024)} %param.19) | copy-start | bytes 7684
  25.1 7.6 %copy-start.1 = (bf16[2,1024,128]{2,1,0:T(8,128)(2,1)S(1)}, bf16[2,1024,128]{2,1,0:T(8,128)(2,1)}, u32[]{:S(2)}) copy-start(bf16[2,1024,128]{2,1,0:T(8,128)(2,1)} %param.24) | copy-start | bytes 1572868
  25.1 7.8 %copy-start.9 = (s32[16]{0:T(128)S(1)}, s32[16]{0:T(128)}, u32[]{:S(2)}) copy-start(s32[16]{0:T(128)} %param.25) | copy-start | bytes 196
  25.2 10.2 %copy-start.7 = (s32[16]{0:T(128)S(1)}, s32[16]{0:T(128)}, u32[]{:S(2)}) copy-start(s32[16]{0:T(128)} %param.23) | copy-start | bytes 196
  29.6 7.2 %collective-permute-start = (bf16[16,1024]{1,0:T(8,128)(2,1)S(1)}, bf16[16,1024]{1,0:T(8,128)(2,1)S(1)}, u32[]{:S(2)}, u32[]{:S(2)}) collective-permute-start(bf16[16,1024]{1,0:T(8,128)(2,1)S(1)} %concatenate.78), channel_id=1, source_target_pairs={{0,1},{1,0},{2,3},{3,2},{4,5},{5,4},{6,7},{7,6},{8,9},{9,8},{10,11... | collective-permute-start | bytes 98312 | tf_op jit(solution)/shard_map/ppermute | solution.py:109
  32.8 52.8 %collective-permute-start.14 = (bf16[2,1024,128]{2,1,0:T(8,128)(2,1)S(1)}, bf16[2,1024,128]{2,1,0:T(8,128)(2,1)S(1)}, u32[]{:S(2)}, u32[]{:S(2)}) collective-permute-start(bf16[2,1024,128]{2,1,0:T(8,128)(2,1)S(1)} %copy-done.1), channel_id=1, source_target_pairs={{0,1},{1,0},{2,3},{3,2},{4,5},{5,4},{6,7},{7,6},{8,9},{9,8},{10,11... | collective-permute-start | bytes 1572872 | tf_op jit(solution)/shard_map/ppermute | solution.py:14
  36.8 9.3 %collective-permute-start.3 = (bf16[32,1024]{1,0:T(8,128)(2,1)S(1)}, bf16[32,1024]{1,0:T(8,128)(2,1)S(1)}, u32[]{:S(2)}, u32[]{:S(2)}) collective-permute-start(bf16[32,1024]{1,0:T(8,128)(2,1)S(1)} %pad_maximum_fusion.3), channel_id=1, source_target_pairs={{0,6},{1,7},{2,0},{3,1},{4,2},{5,3},{6,4},{7,5},{8,14},{9,15},{10,... | collective-permute-start | bytes 196616 | tf_op jit(solution)/shard_map/ppermute | solution.py:109
  39.5 6.5 %collective-permute-start.2 = (bf16[32,1024]{1,0:T(8,128)(2,1)S(1)}, bf16[32,1024]{1,0:T(8,128)(2,1)S(1)}, u32[]{:S(2)}, u32[]{:S(2)}) collective-permute-start(bf16[32,1024]{1,0:T(8,128)(2,1)S(1)} %pad_maximum_fusion.3), channel_id=1, source_target_pairs={{0,4},{1,5},{2,6},{3,7},{4,0},{5,1},{6,2},{7,3},{8,12},{9,13},{10,... | collective-permute-start | bytes 196616 | tf_op jit(solution)/shard_map/ppermute | solution.py:109
  39.9 6.1 %collective-permute-start.1 = (bf16[32,1024]{1,0:T(8,128)(2,1)S(1)}, bf16[32,1024]{1,0:T(8,128)(2,1)S(1)}, u32[]{:S(2)}, u32[]{:S(2)}) collective-permute-start(bf16[32,1024]{1,0:T(8,128)(2,1)S(1)} %pad_maximum_fusion.3), channel_id=1, source_target_pairs={{0,2},{1,3},{2,4},{3,5},{4,6},{5,7},{6,0},{7,1},{8,10},{9,11},{10,... | collective-permute-start | bytes 196616 | tf_op jit(solution)/shard_map/ppermute | solution.py:109
  46.1 14.0 %collective-permute-start.6 = (bf16[128,1024]{1,0:T(8,128)(2,1)S(1)}, bf16[128,1024]{1,0:T(8,128)(2,1)S(1)}, u32[]{:S(2)}, u32[]{:S(2)}) collective-permute-start(bf16[128,1024]{1,0:T(8,128)(2,1)S(1)} %constant_dynamic-update-slice_fusion), channel_id=1, source_target_pairs={{0,24},{1,25},{2,26},{3,27},{4,28},{5,29},{6,30},{7,31},{8,0},{9,1... | collective-permute-start | bytes 786440 | tf_op jit(solution)/shard_map/ppermute | solution.py:109
  49.9 10.8 %collective-permute-start.5 = (bf16[128,1024]{1,0:T(8,128)(2,1)S(1)}, bf16[128,1024]{1,0:T(8,128)(2,1)S(1)}, u32[]{:S(2)}, u32[]{:S(2)}) collective-permute-start(bf16[128,1024]{1,0:T(8,128)(2,1)S(1)} %constant_dynamic-update-slice_fusion), channel_id=1, source_target_pairs={{0,16},{1,17},{2,18},{3,19},{4,20},{5,21},{6,22},{7,23},{8,24},{9,... | collective-permute-start | bytes 786440 | tf_op jit(solution)/shard_map/ppermute | solution.py:109
  49.9 14.8 %collective-permute-start.4 = (bf16[128,1024]{1,0:T(8,128)(2,1)S(1)}, bf16[128,1024]{1,0:T(8,128)(2,1)S(1)}, u32[]{:S(2)}, u32[]{:S(2)}) collective-permute-start(bf16[128,1024]{1,0:T(8,128)(2,1)S(1)} %constant_dynamic-update-slice_fusion), channel_id=1, source_target_pairs={{0,8},{1,9},{2,10},{3,11},{4,12},{5,13},{6,14},{7,15},{8,16},{9,17... | collective-permute-start | bytes 786440 | tf_op jit(solution)/shard_map/ppermute | solution.py:109
  68.3 4.2 %slice-start = ((s8[6291456]{0:T(1024)(128)(4,1)}), s8[4194304]{0:T(1024)(128)(4,1)S(1)}, s32[]{:S(2)}) async-start(s8[6291456]{0:T(1024)(128)(4,1)} %bitcast.76), calls=%async_computation.1 | async-start | bytes 8388608
  68.4 4.2 %slice-start.1 = ((s8[6291456]{0:T(1024)(128)(4,1)}), s8[2097152]{0:T(1024)(128)(4,1)S(1)}, s32[]{:S(2)}) async-start(s8[6291456]{0:T(1024)(128)(4,1)} %bitcast.76), calls=%async_computation.2 | async-start | bytes 4194304
  73.5 1.7 %collective-permute-start.7 = (bf16[16,640]{1,0:T(8,128)(2,1)S(1)}, bf16[16,640]{1,0:T(8,128)(2,1)S(1)}, u32[]{:S(2)}, u32[]{:S(2)}) collective-permute-start(bf16[16,640]{1,0:T(8,128)(2,1)S(1)} %bitcast.86), channel_id=1, source_target_pairs={{0,1},{1,0},{2,3},{3,2},{4,5},{5,4},{6,7},{7,6},{8,9},{9,8},{10,11... | collective-permute-start | bytes 61448 | tf_op jit(solution)/shard_map/ppermute | solution.py:109
  75.2 4.1 %collective-permute-start.8 = (bf16[32,640]{1,0:T(8,128)(2,1)S(1)}, bf16[32,640]{1,0:T(8,128)(2,1)S(1)}, u32[]{:S(2)}, u32[]{:S(2)}) collective-permute-start(bf16[32,640]{1,0:T(8,128)(2,1)S(1)} %get-tuple-element.33), channel_id=1, source_target_pairs={{0,2},{1,3},{2,4},{3,5},{4,6},{5,7},{6,0},{7,1},{8,10},{9,11},{10,... | collective-permute-start | bytes 122888 | tf_op jit(solution)/shard_map/ppermute | solution.py:109
  75.2 7.0 %collective-permute-start.10 = (bf16[32,640]{1,0:T(8,128)(2,1)S(1)}, bf16[32,640]{1,0:T(8,128)(2,1)S(1)}, u32[]{:S(2)}, u32[]{:S(2)}) collective-permute-start(bf16[32,640]{1,0:T(8,128)(2,1)S(1)} %get-tuple-element.33), channel_id=1, source_target_pairs={{0,6},{1,7},{2,0},{3,1},{4,2},{5,3},{6,4},{7,5},{8,14},{9,15},{10,... | collective-permute-start | bytes 122888 | tf_op jit(solution)/shard_map/ppermute | solution.py:109
  77.9 4.4 %collective-permute-start.9 = (bf16[32,640]{1,0:T(8,128)(2,1)S(1)}, bf16[32,640]{1,0:T(8,128)(2,1)S(1)}, u32[]{:S(2)}, u32[]{:S(2)}) collective-permute-start(bf16[32,640]{1,0:T(8,128)(2,1)S(1)} %get-tuple-element.33), channel_id=1, source_target_pairs={{0,4},{1,5},{2,6},{3,7},{4,0},{5,1},{6,2},{7,3},{8,12},{9,13},{10,... | collective-permute-start | bytes 122888 | tf_op jit(solution)/shard_map/ppermute | solution.py:109
  82.3 7.1 %collective-permute-start.13 = (bf16[128,640]{1,0:T(8,128)(2,1)S(1)}, bf16[128,640]{1,0:T(8,128)(2,1)S(1)}, u32[]{:S(2)}, u32[]{:S(2)}) collective-permute-start(bf16[128,640]{1,0:T(8,128)(2,1)S(1)} %constant_dynamic-update-slice_fusion.7), channel_id=1, source_target_pairs={{0,8},{1,9},{2,10},{3,11},{4,12},{5,13},{6,14},{7,15},{8,16},{9,17... | collective-permute-start | bytes 491528 | tf_op jit(solution)/shard_map/ppermute | solution.py:109
  82.3 7.8 %collective-permute-start.12 = (bf16[128,640]{1,0:T(8,128)(2,1)S(1)}, bf16[128,640]{1,0:T(8,128)(2,1)S(1)}, u32[]{:S(2)}, u32[]{:S(2)}) collective-permute-start(bf16[128,640]{1,0:T(8,128)(2,1)S(1)} %constant_dynamic-update-slice_fusion.7), channel_id=1, source_target_pairs={{0,16},{1,17},{2,18},{3,19},{4,20},{5,21},{6,22},{7,23},{8,24},{9,... | collective-permute-start | bytes 491528 | tf_op jit(solution)/shard_map/ppermute | solution.py:109
  84.7 6.7 %collective-permute-start.11 = (bf16[128,640]{1,0:T(8,128)(2,1)S(1)}, bf16[128,640]{1,0:T(8,128)(2,1)S(1)}, u32[]{:S(2)}, u32[]{:S(2)}) collective-permute-start(bf16[128,640]{1,0:T(8,128)(2,1)S(1)} %constant_dynamic-update-slice_fusion.7), channel_id=1, source_target_pairs={{0,24},{1,25},{2,26},{3,27},{4,28},{5,29},{6,30},{7,31},{8,0},{9,1... | collective-permute-start | bytes 491528 | tf_op jit(solution)/shard_map/ppermute | solution.py:109
  92.7 3.9 %copy-start.8 = (bf16[256,5120]{1,0:T(8,128)(2,1)S(1)}, bf16[256,5120]{1,0:T(8,128)(2,1)}, u32[]{:S(2)}) copy-start(bf16[256,5120]{1,0:T(8,128)(2,1)} %all-gather.2.cloned.1.call-done) | copy-start | bytes 7864324
  102.9 15.1 %copy-start.2 = (bf16[2,256,128]{2,1,0:T(8,128)(2,1)}, bf16[2,256,128]{2,1,0:T(8,128)(2,1)S(1)}, u32[]{:S(2)}) copy-start(bf16[2,256,128]{2,1,0:T(8,128)(2,1)S(1)} %pad_maximum_fusion.2) | copy-start | bytes 393220
  102.9 4.6 %collective-permute-start.15 = (bf16[2,256,128]{2,1,0:T(8,128)(2,1)S(1)}, bf16[2,256,128]{2,1,0:T(8,128)(2,1)S(1)}, u32[]{:S(2)}, u32[]{:S(2)}) collective-permute-start(bf16[2,256,128]{2,1,0:T(8,128)(2,1)S(1)} %pad_maximum_fusion.2), channel_id=1, source_target_pairs={{0,1},{1,0},{2,3},{3,2},{4,5},{5,4},{6,7},{7,6},{8,9},{9,8},{10,11... | collective-permute-start | bytes 393224 | tf_op jit(solution)/shard_map/ppermute | solution.py:14
Sparse Core Ops, SparseCore 0:
  14.1 38.1 all-gather.1

commit v8 on v5

--- a/solution.py
+++ b/solution.py
@@ -118,8 +118,17 @@
     return ((z * 4 + y) * 2 + core) * rows
 
 
-def project(rows, w_query, kv_weight, b_query, kv_bias):
-    cols = lax.all_gather(rows, "kv", axis=1, tiled=True)
+def ring_columns(rows):
+    count = lax.axis_size("kv")
+    place = lax.axis_index("kv")
+    parts = [rows] + [lax.ppermute(rows, "kv", [(i, (i + s) % count) for i in range(count)]) for s in range(1, count)]
+    ordered = jnp.take(jnp.stack(parts), (place - jnp.arange(count)) % count, axis=0)
+    return jnp.transpose(ordered, (1, 0, 2)).reshape(rows.shape[0], count * rows.shape[1])
+
+
+def project(rows, w_query, kv_weight, b_query, kv_bias, cols=None):
+    if cols is None:
+        cols = lax.all_gather(rows, "kv", axis=1, tiled=True)
     query = jnp.dot(cols, w_query, preferred_element_type=jnp.float32) + b_query
     keyval = jnp.dot(cols, kv_weight, preferred_element_type=jnp.float32) + kv_bias
     return query, keyval
@@ -131,6 +140,7 @@
     kv_width = w_keyval.shape[2]
     kv_weight = w_keyval.reshape(w_keyval.shape[0], 2 * kv_width)
     kv_bias = b_keyval.reshape(2 * kv_width)
+    pre_cols = ring_columns(pre_tokens)
     dec_q, dec_kv = project(dec_tokens, w_query, kv_weight, b_query, kv_bias)
     tok_place = lax.axis_index("tok")
     ids = jnp.stack([owner_slots // dec_count, owner_slots % dec_count], axis=1).astype(jnp.bfloat16)
@@ -149,7 +159,7 @@
     wanted = tok_place * dec_count + jnp.arange(dec_count, dtype=jnp.int32)
     where = jnp.argmax(requests[None, :] == wanted[:, None], axis=1)
     dec_attn = jnp.take(back, where, axis=0)
-    all_query, all_keyval = project(pre_tokens, w_query, kv_weight, b_query, kv_bias)
+    all_query, all_keyval = project(pre_tokens, w_query, kv_weight, b_query, kv_bias, cols=pre_cols)
     return dec_attn, new_pool, all_query, all_keyval
 
 

time: 125 us -> 154 us (1.23)
  local copies, waits for them, and re-layouts: 13 us -> 32.1 us
  between operations: 15.2 us -> 1.7 us
  blocking collectives: 10.4 us -> 19.3 us
  other arithmetic: 8.44 us -> 15.2 us
  starting transfers between devices: 22.5 us -> 27.2 us
  waiting for transfers between devices: 28.4 us -> 32.4 us
    all_gather x1, blocking collectives: 10.4 us -> 19.3 us  [project(): cols = lax.all_gather(rows, 'kv', axis=1, tiled=True)]
    unnamed x45, local copies, waits for them, and re-layouts: 7.23 us -> 16 us
    ppermute x2, starting transfers between devices: 1.9 us -> 7.47 us  [swapped(): lax.ppermute(value, axis, [(i, i ^ 1 << distance) for i in range(lax.axis...]
    ppermute x14, starting transfers between devices: 20.6 us -> 15.1 us  [tree_gather(): parts.append(lax.ppermute(buffer, 'tok', pairs))]
    ppermute x0 -> x3, starting transfers between devices: none -> 4.56 us  [ring_columns(): lax.ppermute(rows, 'kv', [(i, (i + s) % count) for i in range(count)])]
    ppermute x14, waiting for transfers between devices: 28.3 us -> 32.4 us  [tree_gather(): parts.append(lax.ppermute(buffer, 'tok', pairs))]
    select_n x0 -> x2, other arithmetic: none -> 3.57 us  [ring_columns(): jnp.take(jnp.stack(parts), (place - jnp.arange(count)) % count, axis=0)]
    select_n x0 -> x1, local copies, waits for them, and re-layouts: none -> 2.96 us  [ring_columns(): jnp.take(jnp.stack(parts), (place - jnp.arange(count)) % count, axis=0)]
  transfers between devices with their start and end apart: 17 -> 19, of which waited for: 7 -> 9; matrix products, arithmetic and copies ran while one was open for 17% -> 23% of each run, Pallas kernels for 0% -> 0%
where the time goes in v8:
time: 154 us
  waiting for transfers between devices  32.4 us (21%)
  local copies, waits for them, and re-layouts  32.1 us (21%)
  starting transfers between devices  27.2 us (18%)
  blocking collectives  19.3 us (13%)
  matrix products  16.6 us (11%)
  other arithmetic  15.2 us (10%)
  Pallas kernels  9.2 us (6%)
  between operations  1.7 us (1%)
    ppermute x14, waiting for transfers between devices, tree_gather(): parts.append(lax.ppermute(buffer, 'tok', pairs))  32.4 us
    all_gather x1, blocking collectives, project(): cols = lax.all_gather(rows, 'kv', axis=1, tiled=True)  19.3 us
    unnamed x45, local copies, waits for them, and re-layouts  16 us
    ppermute x14, starting transfers between devices, tree_gather(): parts.append(lax.ppermute(buffer, 'tok', pairs))  15.1 us
    pallas_call x1, Pallas kernels, attend(): pl.pallas_call(attend_kernel, grid=(width // HD,), in_specs=[pl.BlockSpec...  9.2 us
    dot_general x2, matrix products, project(): query = jnp.dot(cols, w_query, preferred_element_type=jnp.float32) + b_query  8.96 us
    ppermute x2, starting transfers between devices, swapped(): lax.ppermute(value, axis, [(i, i ^ 1 << distance) for i in range(lax.axis...  7.47 us
    ppermute x3, starting transfers between devices, ring_columns(): lax.ppermute(rows, 'kv', [(i, (i + s) % count) for i in range(count)])  4.56 us
  transfers between devices with their start and end apart: 19, of which 9 were waited for; matrix products, arithmetic and copies ran while one was open for 23% of the time, Pallas kernels for 0%

profile of v8, /device:TPU:1, one launch (start us, length us, event | category | flops | bytes accessed | tf_op | source)
XLA Modules:
  0.0 153.7 jit_solution(13607774594107686301)
XLA Ops:
  0.7 6.9 %copy.124 = bf16[2,12288,128]{2,1,0:T(8,128)(2,1)} copy(bf16[2,12288,128]{2,1,0:T(8,128)(2,1)} %param.17) | data formatting | bytes 12582912
  7.6 2.0 %collective-permute-start.14 = (bf16[256,1280]{1,0:T(8,128)(2,1)S(1)}, bf16[256,1280]{1,0:T(8,128)(2,1)}, u32[]{:S(2)}, u32[]{:S(2)}) collective-permute-start(bf16[256,1280]{1,0:T(8,128)(2,1)S(1)} %copy-done.2), channel_id=1, source_target_pairs={{0,32},{32,64},{64,96},{96,0},{1,33},{33,65},{65,97},{97,1},{2,34}... | collective-permute-start | bytes 1966088 | tf_op jit(solution)/shard_map/ppermute | solution.py:124
  9.6 1.3 collective-permute-start.16
  11.2 19.3 %all_gather.3 = bf16[16,5120]{1,0:T(8,128)(2,1)S(1)} all-gather(bf16[16,1280]{1,0:T(8,128)(2,1)S(1)} %copy-done.6), channel_id=1, replica_groups=mesh['kv'=4,'tok'=32] {'kv'}, dimensions={1}, use_global_device_ids=true | all-gather | bytes 204800 | tf_op jit(solution)/shard_map/all_gather | solution.py:131
  31.1 3.9 %fusion.15 = bf16[16,640]{1,0:T(8,128)(2,1)S(1)} fusion(bf16[16,5120]{1,0:T(8,128)(2,1)S(1)} %all_gather.3, bf16[5120,640]{1,0:T(8,128)(2,1)} %param.13, f32[640]{0:T(1024)S(1)} %copy-done.7), kind=kOutput, calls=%fused_computation.26 | convolution fusion | flops 104878080 | bytes 6740480 | tf_op jit(solution)/shard_map/dot_general | solution.py:132
  35.0 3.3 %collective-permute-start = (bf16[16,1024]{1,0:T(8,128)(2,1)S(1)}, bf16[16,1024]{1,0:T(8,128)(2,1)S(1)}, u32[]{:S(2)}, u32[]{:S(2)}) collective-permute-start(bf16[16,1024]{1,0:T(8,128)(2,1)S(1)} %concatenate.83), channel_id=1, source_target_pairs={{0,1},{1,0},{2,3},{3,2},{4,5},{5,4},{6,7},{7,6},{8,9},{9,8},{10,11... | collective-permute-start | bytes 98312 | tf_op jit(solution)/shard_map/ppermute | solution.py:109
  38.3 0.6 dynamic_slice.3
  38.9 1.3 or_select_fusion.kpos_ref
  40.8 0.7 iota_add_fusion.qpos_ref
  41.5 0.6 constant_dynamic-update-slice_fusion.4
  43.1 2.8 %collective-permute-start.3 = (bf16[32,1024]{1,0:T(8,128)(2,1)S(1)}, bf16[32,1024]{1,0:T(8,128)(2,1)S(1)}, u32[]{:S(2)}, u32[]{:S(2)}) collective-permute-start(bf16[32,1024]{1,0:T(8,128)(2,1)S(1)} %pad_maximum_fusion.4), channel_id=1, source_target_pairs={{0,6},{1,7},{2,0},{3,1},{4,2},{5,3},{6,4},{7,5},{8,14},{9,15},{10,... | collective-permute-start | bytes 196616 | tf_op jit(solution)/shard_map/ppermute | solution.py:109
  46.2 0.7 collective-permute-start.1
  46.9 0.6 constant_dynamic-update-slice_fusion.3
  47.5 5.1 %collective-permute-done.1 = bf16[32,1024]{1,0:T(8,128)(2,1)S(1)} collective-permute-done((bf16[32,1024]{1,0:T(8,128)(2,1)S(1)}, bf16[32,1024]{1,0:T(8,128)(2,1)S(1)}, u32[]{:S(2)}, u32[]{:S(2)}) %collective-permute-start.1) | collective-permute-done | bytes 65568 | tf_op jit(solution)/shard_map/ppermute | solution.py:109
  52.7 0.7 constant_dynamic-update-slice_fusion.2
  53.3 0.6 constant_dynamic-update-slice_fusion.1
  54.0 0.7 constant_dynamic-update-slice_fusion
  54.6 1.6 %collective-permute-start.4 = (bf16[128,1024]{1,0:T(8,128)(2,1)}, bf16[128,1024]{1,0:T(8,128)(2,1)S(1)}, u32[]{:S(2)}, u32[]{:S(2)}) collective-permute-start(bf16[128,1024]{1,0:T(8,128)(2,1)} %get-tuple-element.24), channel_id=1, source_target_pairs={{0,8},{1,9},{2,10},{3,11},{4,12},{5,13},{6,14},{7,15},{8,16},{9,17... | collective-permute-start | bytes 786440 | tf_op jit(solution)/shard_map/ppermute | solution.py:109
  56.3 3.3 %collective-permute-start.5 = (bf16[128,1024]{1,0:T(8,128)(2,1)}, bf16[128,1024]{1,0:T(8,128)(2,1)S(1)}, u32[]{:S(2)}, u32[]{:S(2)}) collective-permute-start(bf16[128,1024]{1,0:T(8,128)(2,1)} %get-tuple-element.24), channel_id=1, source_target_pairs={{0,16},{1,17},{2,18},{3,19},{4,20},{5,21},{6,22},{7,23},{8,24},{9,... | collective-permute-start | bytes 786440 | tf_op jit(solution)/shard_map/ppermute | solution.py:109
  59.6 0.8 collective-permute-start.6
  60.4 4.2 %collective-permute-done.4 = bf16[128,1024]{1,0:T(8,128)(2,1)S(1)} collective-permute-done((bf16[128,1024]{1,0:T(8,128)(2,1)}, bf16[128,1024]{1,0:T(8,128)(2,1)S(1)}, u32[]{:S(2)}, u32[]{:S(2)}) %collective-permute-start.4) | collective-permute-done | bytes 262176 | tf_op jit(solution)/shard_map/ppermute | solution.py:109
  64.6 1.2 collective-permute-start.15
  65.8 0.7 constant_dynamic-update-slice_fusion.7
  66.6 4.6 %collective-permute-done.5 = bf16[128,1024]{1,0:T(8,128)(2,1)S(1)} collective-permute-done((bf16[128,1024]{1,0:T(8,128)(2,1)}, bf16[128,1024]{1,0:T(8,128)(2,1)S(1)}, u32[]{:S(2)}, u32[]{:S(2)}) %collective-permute-start.5) | collective-permute-done | bytes 262176 | tf_op jit(solution)/shard_map/ppermute | solution.py:109
  71.2 1.5 collective-permute-start.17
  72.7 0.7 constant_dynamic-update-slice_fusion.6
  73.4 0.7 constant_dynamic-update-slice_fusion.5
  74.1 0.9 slice_convert_fusion
  75.1 2.0 %gather_fusion = bf16[16,1024]{1,0:T(8,128)(2,1)S(1)} fusion(bf16[512,1024]{1,0:T(8,128)(2,1)} %constant_dynamic-update-slice_fusion.5, s32[1024]{0:T(1024)S(1)} %pad_clamp_fusion.2), kind=kCustom, calls=%fused_computation | custom fusion | bytes 65600 | tf_op jit(solution)/shard_map/jit(_take)/gather | solution.py:152
  77.5 2.3 %scatter_fusion = bf16[2,12288,128]{2,1,0:T(8,128)(2,1)} fusion(bf16[2,12288,128]{2,1,0:T(8,128)(2,1)} %copy.124, s32[16]{0:T(128)S(1)} %get-tuple-element.10, bf16[16,2,128]{2,0,1:T(8,128)(2,1)S(1)} %maximum_bitcast_fusion), kind=kCustom, calls=%fused_computation.3 | custom fusion | bytes 24640 | tf_op jit(solution)/shard_map/scatter | solution.py:90
  79.9 3.4 %fusion.77 = (f32[16,5]{0,1:T(8,128)S(1)}, f32[16,5,12288]{2,0,1:T(8,128)S(1)}) fusion(bf16[2,12288,128]{2,1,0:T(8,128)(2,1)} %scatter_fusion, bf16[16,5,64]{2,0,1:T(8,128)(2,1)S(1)} %get-tuple-element.21, bf16[16,5,64]{2,0,1:T(8,128)(2,1)S(1)} %get-tuple-element.20, pred[16,12288]{1,0:T(8,128)(4,1)S(1)} %fusion.31), kind=kOutput, calls=%fused_computation.186 | convolution fusion | flops 254648240 | bytes 7295296 | tf_op jit(solution)/shard_map/ngd,md->ngm/dot_general | solution.py:66
  83.2 0.8 fusion.1
  84.0 0.9 fusion.28
  84.9 0.6 constant_dynamic-update-slice_fusion.19
  85.8 0.7 iota_reduce_fusion
  86.5 1.2 collective-permute-done.7
  87.7 0.6 constant_dynamic-update-slice_fusion.18
  88.3 4.1 %collective-permute-done.8 = bf16[32,640]{1,0:T(8,128)(2,1)S(1)} collective-permute-done((bf16[32,640]{1,0:T(8,128)(2,1)S(1)}, bf16[32,640]{1,0:T(8,128)(2,1)S(1)}, u32[]{:S(2)}, u32[]{:S(2)}) %collective-permute-start.8) | collective-permute-done | bytes 40992 | tf_op jit(solution)/shard_map/ppermute | solution.py:109
  92.3 0.6 constant_dynamic-update-slice_fusion.17
  93.0 3.7 %collective-permute-done.9 = bf16[32,640]{1,0:T(8,128)(2,1)S(1)} collective-permute-done((bf16[32,640]{1,0:T(8,128)(2,1)S(1)}, bf16[32,640]{1,0:T(8,128)(2,1)S(1)}, u32[]{:S(2)}, u32[]{:S(2)}) %collective-permute-start.9) | collective-permute-done | bytes 40992 | tf_op jit(solution)/shard_map/ppermute | solution.py:109
  96.7 0.6 constant_dynamic-update-slice_fusion.16
  97.3 2.2 %collective-permute-done.10 = bf16[32,640]{1,0:T(8,128)(2,1)S(1)} collective-permute-done((bf16[32,640]{1,0:T(8,128)(2,1)S(1)}, bf16[32,640]{1,0:T(8,128)(2,1)S(1)}, u32[]{:S(2)}, u32[]{:S(2)}) %collective-permute-start.10) | collective-permute-done | bytes 40992 | tf_op jit(solution)/shard_map/ppermute | solution.py:109
  99.6 0.6 constant_dynamic-update-slice_fusion.15
  100.2 2.3 %collective-permute-start.12 = (bf16[128,640]{1,0:T(8,128)(2,1)S(1)}, bf16[128,640]{1,0:T(8,128)(2,1)S(1)}, u32[]{:S(2)}, u32[]{:S(2)}) collective-permute-start(bf16[128,640]{1,0:T(8,128)(2,1)S(1)} %get-tuple-element.30), channel_id=1, source_target_pairs={{0,16},{1,17},{2,18},{3,19},{4,20},{5,21},{6,22},{7,23},{8,24},{9,... | collective-permute-start | bytes 491528 | tf_op jit(solution)/shard_map/ppermute | solution.py:109
  102.5 1.3 maximum_select_fusion
  103.7 4.1 %collective-permute-done.11 = bf16[128,640]{1,0:T(8,128)(2,1)S(1)} collective-permute-done((bf16[128,640]{1,0:T(8,128)(2,1)S(1)}, bf16[128,640]{1,0:T(8,128)(2,1)S(1)}, u32[]{:S(2)}, u32[]{:S(2)}) %collective-permute-start.11) | collective-permute-done | bytes 163872 | tf_op jit(solution)/shard_map/ppermute | solution.py:109
  107.9 0.7 constant_dynamic-update-slice_fusion.22
  108.6 0.7 constant_dynamic-update-slice_fusion.21
  109.2 3.1 %collective-permute-done.13 = bf16[128,640]{1,0:T(8,128)(2,1)S(1)} collective-permute-done((bf16[128,640]{1,0:T(8,128)(2,1)S(1)}, bf16[128,640]{1,0:T(8,128)(2,1)S(1)}, u32[]{:S(2)}, u32[]{:S(2)}) %collective-permute-start.13) | collective-permute-done | bytes 163872 | tf_op jit(solution)/shard_map/ppermute | solution.py:109
  112.3 0.7 constant_dynamic-update-slice_fusion.20
  113.0 1.8 %gather_fusion.1 = bf16[16,640]{1,0:T(8,128)(2,1)S(1)} fusion(bf16[512,640]{1,0:T(8,128)(2,1)} %constant_dynamic-update-slice_fusion.20, s32[1024]{0:T(1024)S(1)} %pad_clamp_fusion.1), kind=kCustom, calls=%fused_computation.1 | custom fusion | bytes 41024 | tf_op jit(solution)/shard_map/jit(_take)/gather | solution.py:161
  114.8 0.7 broadcast_select_fusion.1
  115.5 0.8 copy-done.3
  116.3 1.8 %pad_maximum_fusion = bf16[4,256,1280]{2,1,0:T(8,128)(2,1)S(1)} fusion(bf16[1,256,1280]{2,1,0:T(8,128)(2,1)} %bitcast.15, bf16[1,256,1280]{2,1,0:T(8,128)(2,1)} %bitcast.95, bf16[1,256,1280]{2,1,0:T(8,128)(2,1)} %bitcast.13, bf16[1,256,1280]{2,1,0:T(8,128)(2,1)S(1)} %bitcast.94), kind=kLoop, calls=%fused_computation.16 | loop fusion | flops 3932160 | bytes 5242880 | tf_op jit(solution)/shard_map/stack | solution.py:125
  118.1 2.2 %gather_fusion.2 = bf16[4,256,1280]{2,1,0:T(8,128)(2,1)} fusion(bf16[4,256,1280]{2,1,0:T(8,128)(2,1)S(1)} %pad_maximum_fusion, s32[1024]{0:T(1024)S(1)} %pad_clamp_fusion), kind=kCustom, calls=%fused_computation.2 | custom fusion | bytes 5242896 | tf_op jit(solution)/shard_map/jit(_take)/gather | solution.py:125
  120.4 3.6 %select_bitcast_fusion = bf16[256,4,1280]{2,0,1:T(8,128)(2,1)} fusion(bf16[4,256,1280]{2,1,0:T(8,128)(2,1)} %gather_fusion.2, pred[4]{0:T(512)(128)(4,1)S(1)} %compare_and_fusion), kind=kLoop, calls=%fused_computation.17 | loop fusion | flops 1310720 | bytes 5242884 | tf_op jit(solution)/shard_map/jit(_take)/select_n | solution.py:125
  123.9 3.0 %copy.55 = bf16[256,4,1280]{0,2,1:T(8,128)(2,1)S(1)} copy(bf16[256,4,1280]{2,0,1:T(8,128)(2,1)} %select_bitcast_fusion) | data formatting | bytes 5242880 | tf_op jit(solution)/shard_map/jit(_take)/select_n | solution.py:125
  126.9 2.9 %fusion.12 = f32[256,256]{0,1:T(8,128)S(1)} fusion(bf16[256,5120]{0,1:T(8,128)(2,1)S(1)} %bitcast.88, bf16[640,8,2,128]{3,2,1,0:T(2,128)(2,1)} %bitcast.90, f32[256]{0:T(256)S(1)} %bitcast.103), kind=kOutput, calls=%fused_computation.24 | convolution fusion | flops 671154176 | bytes 5506048 | tf_op jit(solution)/shard_map/dot_general | solution.py:133
  129.8 5.1 %convolution_add_fusion = f32[256,640]{1,0:T(8,128)S(1)} fusion(bf16[256,5120]{0,1:T(8,128)(2,1)S(1)} %bitcast.89, bf16[5120,640]{1,0:T(8,128)(2,1)} %param.13, f32[640]{0:T(1024)S(1)} %copy-done.7), kind=kOutput, calls=%fused_computation.23 | convolution fusion | flops 1677885440 | bytes 9832960 | tf_op jit(solution)/shard_map/dot_general | solution.py:132
  135.5 0.6 fusion.45
  136.2 6.0 %collective-permute-start.18 = (bf16[2,256,128]{2,1,0:T(8,128)(2,1)S(1)}, bf16[2,256,128]{2,1,0:T(8,128)(2,1)S(1)}, u32[]{:S(2)}, u32[]{:S(2)}) collective-permute-start(bf16[2,256,128]{2,1,0:T(8,128)(2,1)S(1)} %pad_maximum_fusion.3), channel_id=1, source_target_pairs={{0,1},{1,0},{2,3},{3,2},{4,5},{5,4},{6,7},{7,6},{8,9},{9,8},{10,11... | collective-permute-start | bytes 393224 | tf_op jit(solution)/shard_map/ppermute | solution.py:14
  142.3 0.9 copy.60.q_ref
  143.3 1.2 fusion.34
  144.5 9.2 %shard_map.138 = bf16[256,640]{1,0:T(8,128)(2,1)} custom-call(bf16[256,640]{1,0:T(8,128)(2,1)} %copy.60.q_ref, bf16[2560,128]{1,0:T(8,128)(2,1)} %get-tuple-element.13.k_ref, bf16[2560,128]{1,0:T(8,128)(2,1)} %get-tuple-element.12.v_ref, s32[256,1]{1,0:T(8,128)} %iota_add_fusion.qpos_ref, s32[1,2560]{1,0:T(1,128)} %or_select_fusion.kpos_ref), custom_call_target="tpu_custom_call" | custom-call | tf_op jit(solution)/shard_map/pallas_call | solution.py:47
  (95 shorter events, 3.8 us)
Async XLA Ops:
  0.6 10.6 %copy-start.6 = (bf16[16,1280]{1,0:T(8,128)(2,1)S(1)}, bf16[16,1280]{1,0:T(8,128)(2,1)}, u32[]{:S(2)}) copy-start(bf16[16,1280]{1,0:T(8,128)(2,1)} %param.11) | copy-start | bytes 122884
  0.6 7.0 %copy-start.2 = (bf16[256,1280]{1,0:T(8,128)(2,1)S(1)}, bf16[256,1280]{1,0:T(8,128)(2,1)}, u32[]{:S(2)}) copy-start(bf16[256,1280]{1,0:T(8,128)(2,1)} %param.12) | copy-start | bytes 1966084
  0.7 29.9 %copy-start.1 = (bf16[5120,2,128]{2,1,0:T(2,128)(2,1)S(1)}, bf16[5120,2,128]{2,1,0:T(2,128)(2,1)}, u32[]{:S(2)}) copy-start(bf16[5120,2,128]{2,1,0:T(2,128)(2,1)} %param.14) | copy-start | bytes 7864324
  0.7 29.9 %copy-start.8 = (f32[2,128]{1,0:T(2,128)S(1)}, f32[2,128]{1,0:T(2,128)}, u32[]{:S(2)}) copy-start(f32[2,128]{1,0:T(2,128)} %param.16) | copy-start | bytes 3076
  0.7 10.3 %copy-start.10 = (s32[16]{0:T(128)S(1)}, s32[16]{0:T(128)}, u32[]{:S(2)}) copy-start(s32[16]{0:T(128)} %param.18) | copy-start | bytes 196
  7.6 23.4 %copy-start.7 = (f32[640]{0:T(1024)S(1)}, f32[640]{0:T(1024)}, u32[]{:S(2)}) copy-start(f32[640]{0:T(1024)} %param.15) | copy-start | bytes 7684
  7.6 107.9 %collective-permute-start.14 = (bf16[256,1280]{1,0:T(8,128)(2,1)S(1)}, bf16[256,1280]{1,0:T(8,128)(2,1)}, u32[]{:S(2)}, u32[]{:S(2)}) collective-permute-start(bf16[256,1280]{1,0:T(8,128)(2,1)S(1)} %copy-done.2), channel_id=1, source_target_pairs={{0,32},{32,64},{64,96},{96,0},{1,33},{33,65},{65,97},{97,1},{2,34}... | collective-permute-start | bytes 1966088 | tf_op jit(solution)/shard_map/ppermute | solution.py:124
  9.6 105.8 %collective-permute-start.16 = (bf16[256,1280]{1,0:T(8,128)(2,1)S(1)}, bf16[256,1280]{1,0:T(8,128)(2,1)}, u32[]{:S(2)}, u32[]{:S(2)}) collective-permute-start(bf16[256,1280]{1,0:T(8,128)(2,1)S(1)} %copy-done.2), channel_id=1, source_target_pairs={{0,96},{32,0},{64,32},{96,64},{1,97},{33,1},{65,33},{97,65},{2,98}... | collective-permute-start | bytes 1966088 | tf_op jit(solution)/shard_map/ppermute | solution.py:124
  31.0 7.3 %copy-start.11 = (s32[16]{0:T(128)S(1)}, s32[16]{0:T(128)}, u32[]{:S(2)}) copy-start(s32[16]{0:T(128)} %param.21) | copy-start | bytes 196
  31.0 11.1 %copy-start.9 = (s32[16]{0:T(128)S(1)}, s32[16]{0:T(128)}, u32[]{:S(2)}) copy-start(s32[16]{0:T(128)} %param.19) | copy-start | bytes 196
  31.1 40.1 %copy-start.4 = (bf16[2,1024,128]{2,1,0:T(8,128)(2,1)S(1)}, bf16[2,1024,128]{2,1,0:T(8,128)(2,1)}, u32[]{:S(2)}) copy-start(bf16[2,1024,128]{2,1,0:T(8,128)(2,1)} %param.20) | copy-start | bytes 1572868
  35.0 8.0 %collective-permute-start = (bf16[16,1024]{1,0:T(8,128)(2,1)S(1)}, bf16[16,1024]{1,0:T(8,128)(2,1)S(1)}, u32[]{:S(2)}, u32[]{:S(2)}) collective-permute-start(bf16[16,1024]{1,0:T(8,128)(2,1)S(1)} %concatenate.83), channel_id=1, source_target_pairs={{0,1},{1,0},{2,3},{3,2},{4,5},{5,4},{6,7},{7,6},{8,9},{9,8},{10,11... | collective-permute-start | bytes 98312 | tf_op jit(solution)/shard_map/ppermute | solution.py:109
  43.1 10.9 %collective-permute-start.3 = (bf16[32,1024]{1,0:T(8,128)(2,1)S(1)}, bf16[32,1024]{1,0:T(8,128)(2,1)S(1)}, u32[]{:S(2)}, u32[]{:S(2)}) collective-permute-start(bf16[32,1024]{1,0:T(8,128)(2,1)S(1)} %pad_maximum_fusion.4), channel_id=1, source_target_pairs={{0,6},{1,7},{2,0},{3,1},{4,2},{5,3},{6,4},{7,5},{8,14},{9,15},{10,... | collective-permute-start | bytes 196616 | tf_op jit(solution)/shard_map/ppermute | solution.py:109
  45.9 7.4 %collective-permute-start.2 = (bf16[32,1024]{1,0:T(8,128)(2,1)S(1)}, bf16[32,1024]{1,0:T(8,128)(2,1)S(1)}, u32[]{:S(2)}, u32[]{:S(2)}) collective-permute-start(bf16[32,1024]{1,0:T(8,128)(2,1)S(1)} %pad_maximum_fusion.4), channel_id=1, source_target_pairs={{0,4},{1,5},{2,6},{3,7},{4,0},{5,1},{6,2},{7,3},{8,12},{9,13},{10,... | collective-permute-start | bytes 196616 | tf_op jit(solution)/shard_map/ppermute | solution.py:109
  46.2 6.4 %collective-permute-start.1 = (bf16[32,1024]{1,0:T(8,128)(2,1)S(1)}, bf16[32,1024]{1,0:T(8,128)(2,1)S(1)}, u32[]{:S(2)}, u32[]{:S(2)}) collective-permute-start(bf16[32,1024]{1,0:T(8,128)(2,1)S(1)} %pad_maximum_fusion.4), channel_id=1, source_target_pairs={{0,2},{1,3},{2,4},{3,5},{4,6},{5,7},{6,0},{7,1},{8,10},{9,11},{10,... | collective-permute-start | bytes 196616 | tf_op jit(solution)/shard_map/ppermute | solution.py:109
  54.6 10.0 %collective-permute-start.4 = (bf16[128,1024]{1,0:T(8,128)(2,1)}, bf16[128,1024]{1,0:T(8,128)(2,1)S(1)}, u32[]{:S(2)}, u32[]{:S(2)}) collective-permute-start(bf16[128,1024]{1,0:T(8,128)(2,1)} %get-tuple-element.24), channel_id=1, source_target_pairs={{0,8},{1,9},{2,10},{3,11},{4,12},{5,13},{6,14},{7,15},{8,16},{9,17... | collective-permute-start | bytes 786440 | tf_op jit(solution)/shard_map/ppermute | solution.py:109
  56.3 14.9 %collective-permute-start.5 = (bf16[128,1024]{1,0:T(8,128)(2,1)}, bf16[128,1024]{1,0:T(8,128)(2,1)S(1)}, u32[]{:S(2)}, u32[]{:S(2)}) collective-permute-start(bf16[128,1024]{1,0:T(8,128)(2,1)} %get-tuple-element.24), channel_id=1, source_target_pairs={{0,16},{1,17},{2,18},{3,19},{4,20},{5,21},{6,22},{7,23},{8,24},{9,... | collective-permute-start | bytes 786440 | tf_op jit(solution)/shard_map/ppermute | solution.py:109
  59.6 13.8 %collective-permute-start.6 = (bf16[128,1024]{1,0:T(8,128)(2,1)}, bf16[128,1024]{1,0:T(8,128)(2,1)S(1)}, u32[]{:S(2)}, u32[]{:S(2)}) collective-permute-start(bf16[128,1024]{1,0:T(8,128)(2,1)} %get-tuple-element.24), channel_id=1, source_target_pairs={{0,24},{1,25},{2,26},{3,27},{4,28},{5,29},{6,30},{7,31},{8,0},{9,1... | collective-permute-start | bytes 786440 | tf_op jit(solution)/shard_map/ppermute | solution.py:109
  64.6 50.8 %collective-permute-start.15 = (bf16[256,1280]{1,0:T(8,128)(2,1)S(1)}, bf16[256,1280]{1,0:T(8,128)(2,1)S(1)}, u32[]{:S(2)}, u32[]{:S(2)}) collective-permute-start(bf16[256,1280]{1,0:T(8,128)(2,1)S(1)} %copy-done.2), channel_id=1, source_target_pairs={{0,64},{32,96},{64,0},{96,32},{1,65},{33,97},{65,1},{97,33},{2,66}... | collective-permute-start | bytes 1966088 | tf_op jit(solution)/shard_map/ppermute | solution.py:124
  71.2 31.3 %collective-permute-start.17 = (bf16[2,1024,128]{2,1,0:T(8,128)(2,1)S(1)}, bf16[2,1024,128]{2,1,0:T(8,128)(2,1)S(1)}, u32[]{:S(2)}, u32[]{:S(2)}) collective-permute-start(bf16[2,1024,128]{2,1,0:T(8,128)(2,1)S(1)} %copy-done.4), channel_id=1, source_target_pairs={{0,1},{1,0},{2,3},{3,2},{4,5},{5,4},{6,7},{7,6},{8,9},{9,8},{10,11... | collective-permute-start | bytes 1572872 | tf_op jit(solution)/shard_map/ppermute | solution.py:14
  79.8 4.2 %slice-start = ((s8[6291456]{0:T(1024)(128)(4,1)}), s8[4194304]{0:T(1024)(128)(4,1)S(1)}, s32[]{:S(2)}) async-start(s8[6291456]{0:T(1024)(128)(4,1)} %bitcast.86), calls=%async_computation | async-start | bytes 8388608
  79.8 4.2 %slice-start.1 = ((s8[6291456]{0:T(1024)(128)(4,1)}), s8[2097152]{0:T(1024)(128)(4,1)S(1)}, s32[]{:S(2)}) async-start(s8[6291456]{0:T(1024)(128)(4,1)} %bitcast.86), calls=%async_computation.1 | async-start | bytes 4194304
  86.5 1.2 collective-permute-start.7
  88.3 4.1 %collective-permute-start.8 = (bf16[32,640]{1,0:T(8,128)(2,1)S(1)}, bf16[32,640]{1,0:T(8,128)(2,1)S(1)}, u32[]{:S(2)}, u32[]{:S(2)}) collective-permute-start(bf16[32,640]{1,0:T(8,128)(2,1)S(1)} %get-tuple-element.42), channel_id=1, source_target_pairs={{0,2},{1,3},{2,4},{3,5},{4,6},{5,7},{6,0},{7,1},{8,10},{9,11},{10,... | collective-permute-start | bytes 122888 | tf_op jit(solution)/shard_map/ppermute | solution.py:109
  92.3 4.4 %collective-permute-start.9 = (bf16[32,640]{1,0:T(8,128)(2,1)S(1)}, bf16[32,640]{1,0:T(8,128)(2,1)S(1)}, u32[]{:S(2)}, u32[]{:S(2)}) collective-permute-start(bf16[32,640]{1,0:T(8,128)(2,1)S(1)} %get-tuple-element.42), channel_id=1, source_target_pairs={{0,4},{1,5},{2,6},{3,7},{4,0},{5,1},{6,2},{7,3},{8,12},{9,13},{10,... | collective-permute-start | bytes 122888 | tf_op jit(solution)/shard_map/ppermute | solution.py:109
  96.7 2.9 %collective-permute-start.10 = (bf16[32,640]{1,0:T(8,128)(2,1)S(1)}, bf16[32,640]{1,0:T(8,128)(2,1)S(1)}, u32[]{:S(2)}, u32[]{:S(2)}) collective-permute-start(bf16[32,640]{1,0:T(8,128)(2,1)S(1)} %get-tuple-element.42), channel_id=1, source_target_pairs={{0,6},{1,7},{2,0},{3,1},{4,2},{5,3},{6,4},{7,5},{8,14},{9,15},{10,... | collective-permute-start | bytes 122888 | tf_op jit(solution)/shard_map/ppermute | solution.py:109
  100.2 8.4 %collective-permute-start.12 = (bf16[128,640]{1,0:T(8,128)(2,1)S(1)}, bf16[128,640]{1,0:T(8,128)(2,1)S(1)}, u32[]{:S(2)}, u32[]{:S(2)}) collective-permute-start(bf16[128,640]{1,0:T(8,128)(2,1)S(1)} %get-tuple-element.30), channel_id=1, source_target_pairs={{0,16},{1,17},{2,18},{3,19},{4,20},{5,21},{6,22},{7,23},{8,24},{9,... | collective-permute-start | bytes 491528 | tf_op jit(solution)/shard_map/ppermute | solution.py:109
  102.5 5.4 %collective-permute-start.11 = (bf16[128,640]{1,0:T(8,128)(2,1)S(1)}, bf16[128,640]{1,0:T(8,128)(2,1)S(1)}, u32[]{:S(2)}, u32[]{:S(2)}) collective-permute-start(bf16[128,640]{1,0:T(8,128)(2,1)S(1)} %get-tuple-element.30), channel_id=1, source_target_pairs={{0,8},{1,9},{2,10},{3,11},{4,12},{5,13},{6,14},{7,15},{8,16},{9,17... | collective-permute-start | bytes 491528 | tf_op jit(solution)/shard_map/ppermute | solution.py:109
  107.9 4.5 %collective-permute-start.13 = (bf16[128,640]{1,0:T(8,128)(2,1)S(1)}, bf16[128,640]{1,0:T(8,128)(2,1)S(1)}, u32[]{:S(2)}, u32[]{:S(2)}) collective-permute-start(bf16[128,640]{1,0:T(8,128)(2,1)S(1)} %get-tuple-element.30), channel_id=1, source_target_pairs={{0,24},{1,25},{2,26},{3,27},{4,28},{5,29},{6,30},{7,31},{8,0},{9,1... | collective-permute-start | bytes 491528 | tf_op jit(solution)/shard_map/ppermute | solution.py:109
  115.5 0.8 copy-start.3
  134.9 8.4 %copy-start = (bf16[2,2048,128]{2,1,0:T(8,128)(2,1)S(1)}, bf16[2,2048,128]{2,1,0:T(8,128)(2,1)}, u32[]{:S(2)}) copy-start(bf16[2,2048,128]{2,1,0:T(8,128)(2,1)} %maximum_select_fusion) | copy-start | bytes 3145732
  136.2 8.3 %copy-start.5 = (bf16[2,256,128]{2,1,0:T(8,128)(2,1)}, bf16[2,256,128]{2,1,0:T(8,128)(2,1)S(1)}, u32[]{:S(2)}) copy-start(bf16[2,256,128]{2,1,0:T(8,128)(2,1)S(1)} %pad_maximum_fusion.3) | copy-start | bytes 393220
  136.2 7.0 %collective-permute-start.18 = (bf16[2,256,128]{2,1,0:T(8,128)(2,1)S(1)}, bf16[2,256,128]{2,1,0:T(8,128)(2,1)S(1)}, u32[]{:S(2)}, u32[]{:S(2)}) collective-permute-start(bf16[2,256,128]{2,1,0:T(8,128)(2,1)S(1)} %pad_maximum_fusion.3), channel_id=1, source_target_pairs={{0,1},{1,0},{2,3},{3,2},{4,5},{5,4},{6,7},{7,6},{8,9},{9,8},{10,11... | collective-permute-start | bytes 393224 | tf_op jit(solution)/shard_map/ppermute | solution.py:14

commit v9 on v8

--- a/solution.py
+++ b/solution.py
@@ -118,12 +118,30 @@
     return ((z * 4 + y) * 2 + core) * rows
 
 
-def ring_columns(rows):
+def ring_parts(rows):
     count = lax.axis_size("kv")
-    place = lax.axis_index("kv")
-    parts = [rows] + [lax.ppermute(rows, "kv", [(i, (i + s) % count) for i in range(count)]) for s in range(1, count)]
-    ordered = jnp.take(jnp.stack(parts), (place - jnp.arange(count)) % count, axis=0)
-    return jnp.transpose(ordered, (1, 0, 2)).reshape(rows.shape[0], count * rows.shape[1])
+    return [rows] + [lax.ppermute(rows, "kv", [(i, (i + s) % count) for i in range(count)]) for s in range(1, count)]
+
+
+def ring_project(parts, w_query, kv_weight, b_query, kv_bias):
+    count = len(parts)
+    width = parts[0].shape[1]
+
+    def branch(place):
+        def run(*blocks):
+            query = None
+            keyval = None
+            for shift, block in enumerate(blocks):
+                source = (place - shift) % count
+                part_q = jnp.dot(block, w_query[source * width:(source + 1) * width], preferred_element_type=jnp.float32)
+                part_kv = jnp.dot(block, kv_weight[source * width:(source + 1) * width], preferred_element_type=jnp.float32)
+                query = part_q if query is None else query + part_q
+                keyval = part_kv if keyval is None else keyval + part_kv
+            return query + b_query, keyval + kv_bias
+
+        return run
+
+    return lax.switch(lax.axis_index("kv"), [branch(p) for p in range(count)], *parts)
 
 
 def project(rows, w_query, kv_weight, b_query, kv_bias, cols=None):
@@ -140,7 +158,7 @@
     kv_width = w_keyval.shape[2]
     kv_weight = w_keyval.reshape(w_keyval.shape[0], 2 * kv_width)
     kv_bias = b_keyval.reshape(2 * kv_width)
-    pre_cols = ring_columns(pre_tokens)
+    pre_parts = ring_parts(pre_tokens)
     dec_q, dec_kv = project(dec_tokens, w_query, kv_weight, b_query, kv_bias)
     tok_place = lax.axis_index("tok")
     ids = jnp.stack([owner_slots // dec_count, owner_slots % dec_count], axis=1).astype(jnp.bfloat16)
@@ -159,7 +177,7 @@
     wanted = tok_place * dec_count + jnp.arange(dec_count, dtype=jnp.int32)
     where = jnp.argmax(requests[None, :] == wanted[:, None], axis=1)
     dec_attn = jnp.take(back, where, axis=0)
-    all_query, all_keyval = project(pre_tokens, w_query, kv_weight, b_query, kv_bias, cols=pre_cols)
+    all_query, all_keyval = ring_project(pre_parts, w_query, kv_weight, b_query, kv_bias)
     return dec_attn, new_pool, all_query, all_keyval
 
 

time: 154 us -> 178 us (1.16)
  blocking collectives: 19.3 us -> 33.3 us
  other arithmetic: 15.2 us -> 21 us
  local copies, waits for them, and re-layouts: 32.1 us -> 36.4 us
  waiting for transfers between devices: 32.4 us -> 28.2 us
  matrix products: 16.6 us -> 20.4 us
    all_gather x1, blocking collectives: 19.3 us -> 33.3 us  [project(): cols = lax.all_gather(rows, 'kv', axis=1, tiled=True)]
    dot_general x0 -> x8, matrix products: none -> 11.7 us  [the longest x4 6.8 us: run(): jnp.dot(block, w_query[source * width:(source + 1) * width], preferred_el...]
    dot_general x2 -> x1, matrix products: 8.96 us -> 3.82 us  [project(): query = jnp.dot(cols, w_query, preferred_element_type=jnp.float32) + b_query]
    ppermute x14, waiting for transfers between devices: 32.4 us -> 28.2 us  [tree_gather(): parts.append(lax.ppermute(buffer, 'tok', pairs))]
    select_n x2 -> x0, other arithmetic: 3.57 us -> none  [ring_columns(): jnp.take(jnp.stack(parts), (place - jnp.arange(count)) % count, axis=0)]
    select_n x1 -> x0, local copies, waits for them, and re-layouts: 2.96 us -> none  [ring_columns(): jnp.take(jnp.stack(parts), (place - jnp.arange(count)) % count, axis=0)]
    dot_general x2 -> x1, matrix products: 3.37 us -> 0.46 us  [project(): jnp.dot(cols, kv_weight, preferred_element_type=jnp.float32) + kv_bias]
    unnamed x45 -> x57, local copies, waits for them, and re-layouts: 16 us -> 18.4 us
  transfers between devices with their start and end apart: 19 -> 19, of which waited for: 9 -> 9; matrix products, arithmetic and copies ran while one was open for 23% -> 31% of each run, Pallas kernels for 0% -> 0%
where the time goes in v9:
time: 178 us; the launch traced here: 177 us
  local copies, waits for them, and re-layouts  36.4 us (20%)
  blocking collectives  33.3 us (19%)
  waiting for transfers between devices  28.2 us (16%)
  starting transfers between devices  26.8 us (15%)
  other arithmetic  21 us (12%)
  matrix products  20.4 us (11%)
  Pallas kernels  9.2 us (5%)
    all_gather x1, blocking collectives, project(): cols = lax.all_gather(rows, 'kv', axis=1, tiled=True)  33.3 us
    ppermute x14, waiting for transfers between devices, tree_gather(): parts.append(lax.ppermute(buffer, 'tok', pairs))  28.2 us
    unnamed x57, local copies, waits for them, and re-layouts  18.4 us
    ppermute x14, starting transfers between devices, tree_gather(): parts.append(lax.ppermute(buffer, 'tok', pairs))  15.6 us
    pallas_call x1, Pallas kernels, attend(): pl.pallas_call(attend_kernel, grid=(width // HD,), in_specs=[pl.BlockSpec...  9.2 us
    dot_general x4, matrix products, run(): jnp.dot(block, w_query[source * width:(source + 1) * width], preferred_el...  6.8 us
    ppermute x2, starting transfers between devices, swapped(): lax.ppermute(value, axis, [(i, i ^ 1 << distance) for i in range(lax.axis...  6 us
    ppermute x3, starting transfers between devices, ring_parts(): lax.ppermute(rows, 'kv', [(i, (i + s) % count) for i in range(count)])  5.21 us
  transfers between devices with their start and end apart: 19, of which 9 were waited for; matrix products, arithmetic and copies ran while one was open for 31% of the time, Pallas kernels for 0%

profile of v9, /device:TPU:1, one launch (start us, length us, event | category | flops | bytes accessed | tf_op | source)
XLA Modules:
  0.0 177.4 jit_solution(9774532665233792787)
XLA Ops:
  0.7 6.9 %copy.161 = bf16[2,12288,128]{2,1,0:T(8,128)(2,1)} copy(bf16[2,12288,128]{2,1,0:T(8,128)(2,1)} %param.21) | data formatting | bytes 12582912
  7.6 3.6 %collective-permute-start.15 = (bf16[256,1280]{1,0:T(8,128)(2,1)S(1)}, bf16[256,1280]{1,0:T(8,128)(2,1)}, u32[]{:S(2)}, u32[]{:S(2)}) collective-permute-start(bf16[256,1280]{1,0:T(8,128)(2,1)S(1)} %copy-done), channel_id=1, source_target_pairs={{0,64},{32,96},{64,0},{96,32},{1,65},{33,97},{65,1},{97,33},{2,66}... | collective-permute-start | bytes 1966088 | tf_op jit(solution)/shard_map/ppermute | solution.py:123
  12.2 33.3 %all_gather.3 = bf16[16,5120]{1,0:T(8,128)(2,1)S(1)} all-gather(bf16[16,1280]{1,0:T(8,128)(2,1)S(1)} %copy-done.11), channel_id=1, replica_groups=mesh['kv'=4,'tok'=32] {'kv'}, dimensions={1}, use_global_device_ids=true | all-gather | bytes 204800 | tf_op jit(solution)/shard_map/all_gather | solution.py:149
  46.0 3.8 %fusion.114 = bf16[16,640]{1,0:T(8,128)(2,1)S(1)} fusion(bf16[16,5120]{1,0:T(8,128)(2,1)S(1)} %all_gather.3, bf16[5120,640]{1,0:T(8,128)(2,1)} %param.17, f32[640]{0:T(1024)S(1)} %copy-done.10), kind=kOutput, calls=%fused_computation.108 | convolution fusion | flops 104878080 | bytes 6740480 | tf_op jit(solution)/shard_map/dot_general | solution.py:150
  50.0 2.3 %collective-permute-start = (bf16[16,1024]{1,0:T(8,128)(2,1)S(1)}, bf16[16,1024]{1,0:T(8,128)(2,1)S(1)}, u32[]{:S(2)}, u32[]{:S(2)}) collective-permute-start(bf16[16,1024]{1,0:T(8,128)(2,1)S(1)} %concatenate.83), channel_id=1, source_target_pairs={{0,1},{1,0},{2,3},{3,2},{4,5},{5,4},{6,7},{7,6},{8,9},{9,8},{10,11... | collective-permute-start | bytes 98312 | tf_op jit(solution)/shard_map/ppermute | solution.py:109
  52.8 1.3 or_select_fusion.kpos_ref
  55.6 0.7 multiply_cosine_fusion.3
  56.3 1.0 multiply_cosine_fusion.1
  57.3 0.9 fusion.125
  58.8 3.0 %collective-permute-start.3 = (bf16[32,1024]{1,0:T(8,128)(2,1)S(1)}, bf16[32,1024]{1,0:T(8,128)(2,1)S(1)}, u32[]{:S(2)}, u32[]{:S(2)}) collective-permute-start(bf16[32,1024]{1,0:T(8,128)(2,1)S(1)} %pad_maximum_fusion.3), channel_id=1, source_target_pairs={{0,6},{1,7},{2,0},{3,1},{4,2},{5,3},{6,4},{7,5},{8,14},{9,15},{10,... | collective-permute-start | bytes 196616 | tf_op jit(solution)/shard_map/ppermute | solution.py:109
  62.2 0.7 collective-permute-start.1
  63.5 5.1 %collective-permute-done.1 = bf16[32,1024]{1,0:T(8,128)(2,1)S(1)} collective-permute-done((bf16[32,1024]{1,0:T(8,128)(2,1)S(1)}, bf16[32,1024]{1,0:T(8,128)(2,1)S(1)}, u32[]{:S(2)}, u32[]{:S(2)}) %collective-permute-start.1) | collective-permute-done | bytes 65568 | tf_op jit(solution)/shard_map/ppermute | solution.py:109
  70.6 1.6 collective-permute-start.4
  72.9 3.3 %collective-permute-start.5 = (bf16[128,1024]{1,0:T(8,128)(2,1)}, bf16[128,1024]{1,0:T(8,128)(2,1)S(1)}, u32[]{:S(2)}, u32[]{:S(2)}) collective-permute-start(bf16[128,1024]{1,0:T(8,128)(2,1)} %get-tuple-element.404), channel_id=1, source_target_pairs={{0,16},{1,17},{2,18},{3,19},{4,20},{5,21},{6,22},{7,23},{8,24},{9,... | collective-permute-start | bytes 786440 | tf_op jit(solution)/shard_map/ppermute | solution.py:109
  76.2 0.8 collective-permute-start.6
  77.6 2.1 %copy.113 = bf16[640,8,2,128]{3,1,2,0:T(8,128)(2,1)S(1)} copy(bf16[640,8,2,128]{3,2,1,0:T(2,128)(2,1)} %bitcast.120) | data formatting | bytes 5242880
  79.7 1.0 collective-permute-done.4
  80.7 1.3 collective-permute-start.16
  82.1 1.7 constant_dynamic-update-slice_fusion.7
  83.7 3.4 %collective-permute-done.5 = bf16[128,1024]{1,0:T(8,128)(2,1)S(1)} collective-permute-done((bf16[128,1024]{1,0:T(8,128)(2,1)}, bf16[128,1024]{1,0:T(8,128)(2,1)S(1)}, u32[]{:S(2)}, u32[]{:S(2)}) %collective-permute-start.5) | collective-permute-done | bytes 262176 | tf_op jit(solution)/shard_map/ppermute | solution.py:109
  87.1 1.5 collective-permute-start.17
  88.6 0.7 constant_dynamic-update-slice_fusion.6
  89.3 1.7 constant_dynamic-update-slice_fusion.5
  91.0 0.9 slice_convert_fusion.4
  91.9 2.6 %gather_fusion = bf16[16,1024]{1,0:T(8,128)(2,1)} fusion(bf16[512,1024]{1,0:T(8,128)(2,1)} %constant_dynamic-update-slice_fusion.5, s32[1024]{0:T(1024)S(1)} %pad_clamp_fusion.1), kind=kCustom, calls=%fused_computation | custom fusion | bytes 65600 | tf_op jit(solution)/shard_map/jit(_take)/gather | solution.py:170
  94.5 0.8 broadcast_select_fusion
  96.6 0.7 reshape.559
  97.3 1.4 fusion.152
  99.3 1.4 reshape.570
  100.7 1.6 fusion.172
  102.3 0.8 maximum_bitcast_fusion
  103.1 2.4 %scatter_fusion = bf16[2,12288,128]{2,1,0:T(8,128)(2,1)} fusion(bf16[2,12288,128]{2,1,0:T(8,128)(2,1)} %copy.161, s32[16]{0:T(128)} %get-tuple-element.376, bf16[16,2,128]{2,0,1:T(8,128)(2,1)S(1)} %maximum_bitcast_fusion), kind=kCustom, calls=%fused_computation.2 | custom fusion | bytes 24640 | tf_op jit(solution)/shard_map/scatter | solution.py:90
  105.5 1.0 subtract_convert_fusion.1
  106.6 3.6 %fusion.175 = (f32[16,5]{0,1:T(8,128)S(1)}, f32[16,5,12288]{2,0,1:T(8,128)S(1)}) fusion(bf16[2,12288,128]{2,1,0:T(8,128)(2,1)} %scatter_fusion, bf16[16,5,64]{2,0,1:T(8,128)(2,1)S(1)} %get-tuple-element.401, bf16[16,5,64]{2,0,1:T(8,128)(2,1)S(1)} %get-tuple-element.400, pred[16,12288]{1,0:T(8,128)(4,1)} %fusion.125), kind=kOutput, calls=%fused_computation.261 | convolution fusion | flops 254648240 | bytes 7295296 | tf_op jit(solution)/shard_map/ngd,md->ngm/dot_general | solution.py:66
  110.2 0.8 fusion.109
  111.0 0.9 fusion.122
  112.7 0.7 iota_reduce_fusion
  113.4 1.2 collective-permute-done.7
  115.2 4.1 %collective-permute-done.8 = bf16[32,640]{1,0:T(8,128)(2,1)S(1)} collective-permute-done((bf16[32,640]{1,0:T(8,128)(2,1)S(1)}, bf16[32,640]{1,0:T(8,128)(2,1)S(1)}, u32[]{:S(2)}, u32[]{:S(2)}) %collective-permute-start.8) | collective-permute-done | bytes 40992 | tf_op jit(solution)/shard_map/ppermute | solution.py:109
  119.9 3.7 %collective-permute-done.9 = bf16[32,640]{1,0:T(8,128)(2,1)S(1)} collective-permute-done((bf16[32,640]{1,0:T(8,128)(2,1)S(1)}, bf16[32,640]{1,0:T(8,128)(2,1)S(1)}, u32[]{:S(2)}, u32[]{:S(2)}) %collective-permute-start.9) | collective-permute-done | bytes 40992 | tf_op jit(solution)/shard_map/ppermute | solution.py:109
  124.2 2.2 %collective-permute-done.10 = bf16[32,640]{1,0:T(8,128)(2,1)S(1)} collective-permute-done((bf16[32,640]{1,0:T(8,128)(2,1)S(1)}, bf16[32,640]{1,0:T(8,128)(2,1)S(1)}, u32[]{:S(2)}, u32[]{:S(2)}) %collective-permute-start.10) | collective-permute-done | bytes 40992 | tf_op jit(solution)/shard_map/ppermute | solution.py:109
  127.1 3.5 %collective-permute-start.12 = (bf16[128,640]{1,0:T(8,128)(2,1)S(1)}, bf16[128,640]{1,0:T(8,128)(2,1)S(1)}, u32[]{:S(2)}, u32[]{:S(2)}) collective-permute-start(bf16[128,640]{1,0:T(8,128)(2,1)S(1)} %get-tuple-element.410), channel_id=1, source_target_pairs={{0,16},{1,17},{2,18},{3,19},{4,20},{5,21},{6,22},{7,23},{8,24},{9,... | collective-permute-start | bytes 491528 | tf_op jit(solution)/shard_map/ppermute | solution.py:109
  130.6 2.5 %maximum_select_fusion = bf16[2,2048,128]{2,1,0:T(8,128)(2,1)} fusion(bf16[2,1024,128]{2,1,0:T(8,128)(2,1)} %collective-permute-done.17, bf16[2,1024,128]{2,1,0:T(8,128)(2,1)S(1)} %copy-done.8, pred[]{:T(512)S(6)} %eq.32), kind=kLoop, calls=%fused_computation.114 | loop fusion | flops 4718592 | bytes 2097153 | tf_op jit(solution)/shard_map/jit(_where)/select_n | solution.py:204
  133.1 4.6 %collective-permute-done.11 = bf16[128,640]{1,0:T(8,128)(2,1)S(1)} collective-permute-done((bf16[128,640]{1,0:T(8,128)(2,1)S(1)}, bf16[128,640]{1,0:T(8,128)(2,1)S(1)}, u32[]{:S(2)}, u32[]{:S(2)}) %collective-permute-start.11) | collective-permute-done | bytes 163872 | tf_op jit(solution)/shard_map/ppermute | solution.py:109
  137.8 0.7 constant_dynamic-update-slice_fusion.22
  139.1 2.8 %collective-permute-done.13 = bf16[128,640]{1,0:T(8,128)(2,1)S(1)} collective-permute-done((bf16[128,640]{1,0:T(8,128)(2,1)S(1)}, bf16[128,640]{1,0:T(8,128)(2,1)S(1)}, u32[]{:S(2)}, u32[]{:S(2)}) %collective-permute-start.13) | collective-permute-done | bytes 163872 | tf_op jit(solution)/shard_map/ppermute | solution.py:109
  141.9 0.7 constant_dynamic-update-slice_fusion.20
  142.6 1.8 gather_fusion.1
  144.4 0.7 broadcast_select_fusion.1
  145.1 13.5 %conditional.1 = (f32[256,5,64]{0,2,1:T(8,128)}, f32[256,5,64]{0,2,1:T(8,128)}, f32[256,1,64]{2,0,1:T(8,128)S(1)}, f32[256,1,64]{2,0,1:T(8,128)S(1)}, bf16[1,256,128]{2,1,0:T(8,128)(2,1)S(1)}) conditional(s32[]{:T(128)} %clamp.3, (bf16[5120,640]{1,0:T(8,128)(2,1)}, bf16[256,1280]{1,0:T(8,128)(2,1)S(1)}, ...), branch_computations={%region_5.6_spmd.clone, %region_6.7_spmd.clone, %region_7.8_spmd.c... | conditional | flops 2349727744 | bytes 50467908 | solution.py:144
  145.5 1.5 convolution_add_fusion.2
  147.0 2.5 %fusion.4 = f32[256,640]{1,0:T(8,128)S(1)} fusion(bf16[256,1280]{1,0:T(8,128)(2,1)} %get-tuple-element.319, bf16[5120,640]{1,0:T(8,128)(2,1)} %get-tuple-element.318), kind=kOutput, calls=%fused_computation.7 | convolution fusion | flops 419430400 | bytes 2949120 | tf_op jit(solution)/shard_map/cond/branch_0_fun/dot_general | solution.py:136
  149.5 1.6 convolution_add_fusion.1
  151.0 1.5 fusion.20
  152.5 1.8 %fusion = f32[256,640]{1,0:T(8,128)S(1)} fusion(bf16[256,1280]{1,0:T(8,128)(2,1)} %get-tuple-element.321, bf16[5120,640]{1,0:T(8,128)(2,1)S(1)} %copy-done.1), kind=kOutput, calls=%fused_computation.3 | convolution fusion | flops 419430400 | bytes 2949120 | tf_op jit(solution)/shard_map/cond/branch_0_fun/dot_general | solution.py:136
  154.3 1.8 %fusion.2 = f32[256,640]{1,0:T(8,128)S(1)} fusion(bf16[256,1280]{1,0:T(8,128)(2,1)} %get-tuple-element.320, bf16[5120,640]{1,0:T(8,128)(2,1)S(1)} %copy-done.1), kind=kOutput, calls=%fused_computation.5 | convolution fusion | flops 419430400 | bytes 2949120 | tf_op jit(solution)/shard_map/cond/branch_0_fun/dot_general | solution.py:136
  156.1 0.8 fusion.17
  157.1 0.9 fusion.164
  159.4 4.5 %collective-permute-start.18 = (bf16[2,256,128]{2,1,0:T(8,128)(2,1)S(1)}, bf16[2,256,128]{2,1,0:T(8,128)(2,1)S(1)}, u32[]{:S(2)}, u32[]{:S(2)}) collective-permute-start(bf16[2,256,128]{2,1,0:T(8,128)(2,1)S(1)} %pad_maximum_fusion.2), channel_id=1, source_target_pairs={{0,1},{1,0},{2,3},{3,2},{4,5},{5,4},{6,7},{7,6},{8,9},{9,8},{10,11... | collective-permute-start | bytes 393224 | tf_op jit(solution)/shard_map/ppermute | solution.py:14
  163.9 1.2 subtract_convert_fusion
  165.1 0.9 copy.79.q_ref
  166.0 1.0 maximum_select_fusion.1
  167.0 1.2 fusion.128
  168.2 9.2 %shard_map.138 = bf16[256,640]{1,0:T(8,128)(2,1)} custom-call(bf16[256,640]{1,0:T(8,128)(2,1)} %copy.79.q_ref, bf16[2560,128]{1,0:T(8,128)(2,1)} %get-tuple-element.395.k_ref, bf16[2560,128]{1,0:T(8,128)(2,1)} %get-tuple-element.394.v_ref, s32[256,1]{1,0:T(8,128)} %iota_add_fusion.qpos_ref, s32[1,2560]{1,0:T(1,128)} %or_select_fusion.kpos_ref), custom_call_target="tpu_custom_call" | custom-call | tf_op jit(solution)/shard_map/pallas_call | solution.py:47
  (113 shorter events, 15.4 us)
Async XLA Ops:
  0.6 11.6 %copy-start.11 = (bf16[16,1280]{1,0:T(8,128)(2,1)S(1)}, bf16[16,1280]{1,0:T(8,128)(2,1)}, u32[]{:S(2)}) copy-start(bf16[16,1280]{1,0:T(8,128)(2,1)} %param.15) | copy-start | bytes 122884
  0.6 7.0 %copy-start = (bf16[256,1280]{1,0:T(8,128)(2,1)S(1)}, bf16[256,1280]{1,0:T(8,128)(2,1)}, u32[]{:S(2)}) copy-start(bf16[256,1280]{1,0:T(8,128)(2,1)} %param.16) | copy-start | bytes 1966084
  0.7 44.9 %copy-start.5 = (bf16[5120,2,128]{2,1,0:T(2,128)(2,1)S(1)}, bf16[5120,2,128]{2,1,0:T(2,128)(2,1)}, u32[]{:S(2)}) copy-start(bf16[5120,2,128]{2,1,0:T(2,128)(2,1)} %param.18) | copy-start | bytes 7864324
  0.7 44.9 %copy-start.12 = (f32[2,128]{1,0:T(2,128)S(1)}, f32[2,128]{1,0:T(2,128)}, u32[]{:S(2)}) copy-start(f32[2,128]{1,0:T(2,128)} %param.20) | copy-start | bytes 3076
  0.7 10.8 %copy-start.21 = (s32[16]{0:T(128)S(1)}, s32[16]{0:T(128)}, u32[]{:S(2)}) copy-start(s32[16]{0:T(128)} %param.22) | copy-start | bytes 196
  7.6 38.4 %copy-start.10 = (f32[640]{0:T(1024)S(1)}, f32[640]{0:T(1024)}, u32[]{:S(2)}) copy-start(f32[640]{0:T(1024)} %param.19) | copy-start | bytes 7684
  7.6 137.4 %collective-permute-start.15 = (bf16[256,1280]{1,0:T(8,128)(2,1)S(1)}, bf16[256,1280]{1,0:T(8,128)(2,1)}, u32[]{:S(2)}, u32[]{:S(2)}) collective-permute-start(bf16[256,1280]{1,0:T(8,128)(2,1)S(1)} %copy-done), channel_id=1, source_target_pairs={{0,64},{32,96},{64,0},{96,32},{1,65},{33,97},{65,1},{97,33},{2,66}... | collective-permute-start | bytes 1966088 | tf_op jit(solution)/shard_map/ppermute | solution.py:123
  11.2 133.9 %collective-permute-start.14 = (bf16[256,1280]{1,0:T(8,128)(2,1)S(1)}, bf16[256,1280]{1,0:T(8,128)(2,1)}, u32[]{:S(2)}, u32[]{:S(2)}) collective-permute-start(bf16[256,1280]{1,0:T(8,128)(2,1)S(1)} %copy-done), channel_id=1, source_target_pairs={{0,32},{32,64},{64,96},{96,0},{1,33},{33,65},{65,97},{97,1},{2,34}... | collective-permute-start | bytes 1966088 | tf_op jit(solution)/shard_map/ppermute | solution.py:123
  46.0 6.2 %copy-start.22 = (s32[16]{0:T(128)S(1)}, s32[16]{0:T(128)}, u32[]{:S(2)}) copy-start(s32[16]{0:T(128)} %param.25) | copy-start | bytes 196
  46.0 8.7 %copy-start.19 = (s32[16]{0:T(128)S(1)}, s32[16]{0:T(128)}, u32[]{:S(2)}) copy-start(s32[16]{0:T(128)} %param.23) | copy-start | bytes 196
  46.0 30.2 %copy-start.18 = (s32[16]{0:T(128)S(1)}, s32[16]{0:T(128)}, u32[]{:S(2)}) copy-start(s32[16]{0:T(128)} %get-tuple-element.373) | copy-start | bytes 196
  50.0 8.8 %collective-permute-start = (bf16[16,1024]{1,0:T(8,128)(2,1)S(1)}, bf16[16,1024]{1,0:T(8,128)(2,1)S(1)}, u32[]{:S(2)}, u32[]{:S(2)}) collective-permute-start(bf16[16,1024]{1,0:T(8,128)(2,1)S(1)} %concatenate.83), channel_id=1, source_target_pairs={{0,1},{1,0},{2,3},{3,2},{4,5},{5,4},{6,7},{7,6},{8,9},{9,8},{10,11... | collective-permute-start | bytes 98312 | tf_op jit(solution)/shard_map/ppermute | solution.py:109
  52.2 27.4 %copy-start.13 = (f32[64]{0:T(128)}, f32[64]{0:T(128)S(1)}, u32[]{:S(2)}) copy-start(f32[64]{0:T(128)S(1)} %negate_power_fusion) | copy-start | bytes 772
  54.8 21.4 %copy-start.15 = (f32[256]{0:T(256)}, f32[256]{0:T(256)S(1)}, u32[]{:S(2)}) copy-start(f32[256]{0:T(256)S(1)} %add_convert_fusion.2) | copy-start | bytes 3076
  54.8 4.0 %copy-start.17 = (f32[16]{0:T(128)}, f32[16]{0:T(128)S(1)}, u32[]{:S(2)}) copy-start(f32[16]{0:T(128)S(1)} %get-tuple-element.435) | copy-start | bytes 196
  58.8 11.1 %collective-permute-start.3 = (bf16[32,1024]{1,0:T(8,128)(2,1)S(1)}, bf16[32,1024]{1,0:T(8,128)(2,1)S(1)}, u32[]{:S(2)}, u32[]{:S(2)}) collective-permute-start(bf16[32,1024]{1,0:T(8,128)(2,1)S(1)} %pad_maximum_fusion.3), channel_id=1, source_target_pairs={{0,6},{1,7},{2,0},{3,1},{4,2},{5,3},{6,4},{7,5},{8,14},{9,15},{10,... | collective-permute-start | bytes 196616 | tf_op jit(solution)/shard_map/ppermute | solution.py:109
  61.8 7.5 %collective-permute-start.2 = (bf16[32,1024]{1,0:T(8,128)(2,1)S(1)}, bf16[32,1024]{1,0:T(8,128)(2,1)S(1)}, u32[]{:S(2)}, u32[]{:S(2)}) collective-permute-start(bf16[32,1024]{1,0:T(8,128)(2,1)S(1)} %pad_maximum_fusion.3), channel_id=1, source_target_pairs={{0,4},{1,5},{2,6},{3,7},{4,0},{5,1},{6,2},{7,3},{8,12},{9,13},{10,... | collective-permute-start | bytes 196616 | tf_op jit(solution)/shard_map/ppermute | solution.py:109
  62.2 6.4 %collective-permute-start.1 = (bf16[32,1024]{1,0:T(8,128)(2,1)S(1)}, bf16[32,1024]{1,0:T(8,128)(2,1)S(1)}, u32[]{:S(2)}, u32[]{:S(2)}) collective-permute-start(bf16[32,1024]{1,0:T(8,128)(2,1)S(1)} %pad_maximum_fusion.3), channel_id=1, source_target_pairs={{0,2},{1,3},{2,4},{3,5},{4,6},{5,7},{6,0},{7,1},{8,10},{9,11},{10,... | collective-permute-start | bytes 196616 | tf_op jit(solution)/shard_map/ppermute | solution.py:109
  70.6 10.1 %collective-permute-start.4 = (bf16[128,1024]{1,0:T(8,128)(2,1)}, bf16[128,1024]{1,0:T(8,128)(2,1)}, u32[]{:S(2)}, u32[]{:S(2)}) collective-permute-start(bf16[128,1024]{1,0:T(8,128)(2,1)} %get-tuple-element.404), channel_id=1, source_target_pairs={{0,8},{1,9},{2,10},{3,11},{4,12},{5,13},{6,14},{7,15},{8,16},{9,17... | collective-permute-start | bytes 786440 | tf_op jit(solution)/shard_map/ppermute | solution.py:109
  72.9 14.2 %collective-permute-start.5 = (bf16[128,1024]{1,0:T(8,128)(2,1)}, bf16[128,1024]{1,0:T(8,128)(2,1)S(1)}, u32[]{:S(2)}, u32[]{:S(2)}) collective-permute-start(bf16[128,1024]{1,0:T(8,128)(2,1)} %get-tuple-element.404), channel_id=1, source_target_pairs={{0,16},{1,17},{2,18},{3,19},{4,20},{5,21},{6,22},{7,23},{8,24},{9,... | collective-permute-start | bytes 786440 | tf_op jit(solution)/shard_map/ppermute | solution.py:109
  76.2 13.1 %collective-permute-start.6 = (bf16[128,1024]{1,0:T(8,128)(2,1)}, bf16[128,1024]{1,0:T(8,128)(2,1)}, u32[]{:S(2)}, u32[]{:S(2)}) collective-permute-start(bf16[128,1024]{1,0:T(8,128)(2,1)} %get-tuple-element.404), channel_id=1, source_target_pairs={{0,24},{1,25},{2,26},{3,27},{4,28},{5,29},{6,30},{7,31},{8,0},{9,1... | collective-permute-start | bytes 786440 | tf_op jit(solution)/shard_map/ppermute | solution.py:109
  80.7 64.3 %collective-permute-start.16 = (bf16[256,1280]{1,0:T(8,128)(2,1)S(1)}, bf16[256,1280]{1,0:T(8,128)(2,1)}, u32[]{:S(2)}, u32[]{:S(2)}) collective-permute-start(bf16[256,1280]{1,0:T(8,128)(2,1)S(1)} %copy-done), channel_id=1, source_target_pairs={{0,96},{32,0},{64,32},{96,64},{1,97},{33,1},{65,33},{97,65},{2,98}... | collective-permute-start | bytes 1966088 | tf_op jit(solution)/shard_map/ppermute | solution.py:123
  87.1 43.5 %collective-permute-start.17 = (bf16[2,1024,128]{2,1,0:T(8,128)(2,1)}, bf16[2,1024,128]{2,1,0:T(8,128)(2,1)}, u32[]{:S(2)}, u32[]{:S(2)}) collective-permute-start(bf16[2,1024,128]{2,1,0:T(8,128)(2,1)} %param.24), channel_id=1, source_target_pairs={{0,1},{1,0},{2,3},{3,2},{4,5},{5,4},{6,7},{7,6},{8,9},{9,8},{10,11... | collective-permute-start | bytes 1572872 | tf_op jit(solution)/shard_map/ppermute | solution.py:14
  105.5 5.4 %slice-start = ((s8[6291456]{0:T(1024)(128)(4,1)}), s8[4194304]{0:T(1024)(128)(4,1)S(1)}, s32[]{:S(2)}) async-start(s8[6291456]{0:T(1024)(128)(4,1)} %bitcast.118), calls=%async_computation | async-start | bytes 8388608
  106.6 4.4 %slice-start.1 = ((s8[6291456]{0:T(1024)(128)(4,1)}), s8[2097152]{0:T(1024)(128)(4,1)S(1)}, s32[]{:S(2)}) async-start(s8[6291456]{0:T(1024)(128)(4,1)} %bitcast.118), calls=%async_computation.1 | async-start | bytes 4194304
  111.0 1.7 copy-start.20
  111.0 19.7 %copy-start.8 = (bf16[2,1024,128]{2,1,0:T(8,128)(2,1)S(1)}, bf16[2,1024,128]{2,1,0:T(8,128)(2,1)}, u32[]{:S(2)}) copy-start(bf16[2,1024,128]{2,1,0:T(8,128)(2,1)} %param.24) | copy-start | bytes 1572868
  113.4 1.2 collective-permute-start.7
  115.2 4.1 %collective-permute-start.8 = (bf16[32,640]{1,0:T(8,128)(2,1)S(1)}, bf16[32,640]{1,0:T(8,128)(2,1)S(1)}, u32[]{:S(2)}, u32[]{:S(2)}) collective-permute-start(bf16[32,640]{1,0:T(8,128)(2,1)S(1)} %get-tuple-element.422), channel_id=1, source_target_pairs={{0,2},{1,3},{2,4},{3,5},{4,6},{5,7},{6,0},{7,1},{8,10},{9,11},{10,... | collective-permute-start | bytes 122888 | tf_op jit(solution)/shard_map/ppermute | solution.py:109
  119.3 4.4 %collective-permute-start.9 = (bf16[32,640]{1,0:T(8,128)(2,1)S(1)}, bf16[32,640]{1,0:T(8,128)(2,1)S(1)}, u32[]{:S(2)}, u32[]{:S(2)}) collective-permute-start(bf16[32,640]{1,0:T(8,128)(2,1)S(1)} %get-tuple-element.422), channel_id=1, source_target_pairs={{0,4},{1,5},{2,6},{3,7},{4,0},{5,1},{6,2},{7,3},{8,12},{9,13},{10,... | collective-permute-start | bytes 122888 | tf_op jit(solution)/shard_map/ppermute | solution.py:109
  123.6 2.9 %collective-permute-start.10 = (bf16[32,640]{1,0:T(8,128)(2,1)S(1)}, bf16[32,640]{1,0:T(8,128)(2,1)S(1)}, u32[]{:S(2)}, u32[]{:S(2)}) collective-permute-start(bf16[32,640]{1,0:T(8,128)(2,1)S(1)} %get-tuple-element.422), channel_id=1, source_target_pairs={{0,6},{1,7},{2,0},{3,1},{4,2},{5,3},{6,4},{7,5},{8,14},{9,15},{10,... | collective-permute-start | bytes 122888 | tf_op jit(solution)/shard_map/ppermute | solution.py:109
  127.1 11.3 %collective-permute-start.12 = (bf16[128,640]{1,0:T(8,128)(2,1)S(1)}, bf16[128,640]{1,0:T(8,128)(2,1)S(1)}, u32[]{:S(2)}, u32[]{:S(2)}) collective-permute-start(bf16[128,640]{1,0:T(8,128)(2,1)S(1)} %get-tuple-element.410), channel_id=1, source_target_pairs={{0,16},{1,17},{2,18},{3,19},{4,20},{5,21},{6,22},{7,23},{8,24},{9,... | collective-permute-start | bytes 491528 | tf_op jit(solution)/shard_map/ppermute | solution.py:109
  130.6 7.1 %collective-permute-start.11 = (bf16[128,640]{1,0:T(8,128)(2,1)S(1)}, bf16[128,640]{1,0:T(8,128)(2,1)S(1)}, u32[]{:S(2)}, u32[]{:S(2)}) collective-permute-start(bf16[128,640]{1,0:T(8,128)(2,1)S(1)} %get-tuple-element.410), channel_id=1, source_target_pairs={{0,8},{1,9},{2,10},{3,11},{4,12},{5,13},{6,14},{7,15},{8,16},{9,17... | collective-permute-start | bytes 491528 | tf_op jit(solution)/shard_map/ppermute | solution.py:109
  137.8 4.2 %collective-permute-start.13 = (bf16[128,640]{1,0:T(8,128)(2,1)S(1)}, bf16[128,640]{1,0:T(8,128)(2,1)S(1)}, u32[]{:S(2)}, u32[]{:S(2)}) collective-permute-start(bf16[128,640]{1,0:T(8,128)(2,1)S(1)} %get-tuple-element.410), channel_id=1, source_target_pairs={{0,24},{1,25},{2,26},{3,27},{4,28},{5,29},{6,30},{7,31},{8,0},{9,1... | collective-permute-start | bytes 491528 | tf_op jit(solution)/shard_map/ppermute | solution.py:109
  145.1 13.6 %copy-start.14 = (f32[64]{0:T(128)S(1)}, f32[64]{0:T(128)}, u32[]{:S(2)}) copy-start(f32[64]{0:T(128)} %copy-done.13) | copy-start | bytes 772
  145.1 13.6 %copy-start.16 = (f32[256]{0:T(256)S(1)}, f32[256]{0:T(256)}, u32[]{:S(2)}) copy-start(f32[256]{0:T(256)} %copy-done.15) | copy-start | bytes 3076
  147.0 5.5 %copy-start.1 = (bf16[5120,640]{1,0:T(8,128)(2,1)S(1)}, bf16[5120,640]{1,0:T(8,128)(2,1)}, u32[]{:S(2)}) copy-start(bf16[5120,640]{1,0:T(8,128)(2,1)} %get-tuple-element.318) | copy-start | bytes 19660804 | tf_op jit(solution)/shard_map/cond
  158.6 6.4 %copy-start.7 = (bf16[1,256,128]{2,1,0:T(8,128)(2,1)}, bf16[1,256,128]{2,1,0:T(8,128)(2,1)S(1)}, u32[]{:S(2)}) copy-start(bf16[1,256,128]{2,1,0:T(8,128)(2,1)S(1)} %get-tuple-element.371) | copy-start | bytes 196612
  158.6 8.4 %copy-start.6 = (bf16[2,2048,128]{2,1,0:T(8,128)(2,1)S(1)}, bf16[2,2048,128]{2,1,0:T(8,128)(2,1)}, u32[]{:S(2)}) copy-start(bf16[2,2048,128]{2,1,0:T(8,128)(2,1)} %maximum_select_fusion) | copy-start | bytes 3145732
  159.4 8.9 %copy-start.9 = (bf16[2,256,128]{2,1,0:T(8,128)(2,1)}, bf16[2,256,128]{2,1,0:T(8,128)(2,1)S(1)}, u32[]{:S(2)}) copy-start(bf16[2,256,128]{2,1,0:T(8,128)(2,1)S(1)} %pad_maximum_fusion.2) | copy-start | bytes 393220
  159.4 6.6 %collective-permute-start.18 = (bf16[2,256,128]{2,1,0:T(8,128)(2,1)S(1)}, bf16[2,256,128]{2,1,0:T(8,128)(2,1)S(1)}, u32[]{:S(2)}, u32[]{:S(2)}) collective-permute-start(bf16[2,256,128]{2,1,0:T(8,128)(2,1)S(1)} %pad_maximum_fusion.2), channel_id=1, source_target_pairs={{0,1},{1,0},{2,3},{3,2},{4,5},{5,4},{6,7},{7,6},{8,9},{9,8},{10,11... | collective-permute-start | bytes 393224 | tf_op jit(solution)/shard_map/ppermute | solution.py:14

commit v10 on v5

--- a/solution.py
+++ b/solution.py
@@ -118,8 +118,15 @@
     return ((z * 4 + y) * 2 + core) * rows
 
 
-def project(rows, w_query, kv_weight, b_query, kv_bias):
-    cols = lax.all_gather(rows, "kv", axis=1, tiled=True)
+def swap_columns(rows):
+    count = lax.axis_size("kv")
+    tiled = jnp.broadcast_to(rows[None], (count,) + rows.shape)
+    blocks = lax.all_to_all(tiled, "kv", 0, 0, tiled=False)
+    return jnp.transpose(blocks, (1, 0, 2)).reshape(rows.shape[0], count * rows.shape[1])
+
+
+def project(rows, w_query, kv_weight, b_query, kv_bias, small=False):
+    cols = swap_columns(rows) if small else lax.all_gather(rows, "kv", axis=1, tiled=True)
     query = jnp.dot(cols, w_query, preferred_element_type=jnp.float32) + b_query
     keyval = jnp.dot(cols, kv_weight, preferred_element_type=jnp.float32) + kv_bias
     return query, keyval
@@ -131,7 +138,7 @@
     kv_width = w_keyval.shape[2]
     kv_weight = w_keyval.reshape(w_keyval.shape[0], 2 * kv_width)
     kv_bias = b_keyval.reshape(2 * kv_width)
-    dec_q, dec_kv = project(dec_tokens, w_query, kv_weight, b_query, kv_bias)
+    dec_q, dec_kv = project(dec_tokens, w_query, kv_weight, b_query, kv_bias, small=True)
     tok_place = lax.axis_index("tok")
     ids = jnp.stack([owner_slots // dec_count, owner_slots % dec_count], axis=1).astype(jnp.bfloat16)
     used = q_width + 2 * kv_width + 2
@@ -188,15 +195,15 @@
     key_pos = jnp.where(key_slots < 2 * shard, key_slots, offset + key_slots - 2 * shard)
     usable = (key_slots < offset) | (key_slots >= 2 * shard)
     key_pos = jnp.where(usable, key_pos, jnp.int32(1 << 30))
-    pre_attn = attend(turned, key_rows[0], key_rows[1], positions, key_pos)
-    return pre_attn, appended
+    return (turned, key_rows[0], key_rows[1], positions, key_pos), appended
 
 
 def body(dec_tokens, pre_tokens, w_query, w_keyval, b_query, b_keyval, dec_pool, owner_slots, dec_lengths, pre_cache, pre_offsets):
     dec_attn, new_pool, all_query, all_keyval = body_inner(
         dec_tokens, pre_tokens, w_query, w_keyval, b_query, b_keyval, dec_pool, owner_slots, dec_lengths
     )
-    pre_attn, appended = prefill(all_query, all_keyval, pre_tokens, w_query, w_keyval, pre_cache, pre_offsets)
+    operands, appended = prefill(all_query, all_keyval, pre_tokens, w_query, w_keyval, pre_cache, pre_offsets)
+    pre_attn = attend(*operands)
     return (dec_attn, pre_attn, new_pool, appended)
 
 

time: 125 us -> 120 us (0.960)
  blocking collectives: 10.4 us -> 0 us
  starting transfers between devices: 22.5 us -> 28.4 us
  waiting for transfers between devices: 28.4 us -> 24 us
  other arithmetic: 8.44 us -> 10.3 us
    all_gather x1 -> x0, blocking collectives: 10.4 us -> none  [project(): cols = lax.all_gather(rows, 'kv', axis=1, tiled=True)]
    all_to_all x0 -> x1, starting transfers between devices: none -> 4.83 us  [swap_columns(): blocks = lax.all_to_all(tiled, 'kv', 0, 0, tiled=False)]
    ppermute x14, waiting for transfers between devices: 28.3 us -> 24 us  [tree_gather(): parts.append(lax.ppermute(buffer, 'tok', pairs))]
    unnamed x45 -> x47, local copies, waits for them, and re-layouts: 7.23 us -> 7.38 us
  transfers between devices with their start and end apart: 17 -> 18, of which waited for: 7 -> 8; matrix products, arithmetic and copies ran while one was open for 17% -> 20% of each run, Pallas kernels for 0% -> 0%
where the time goes in v10:
time: 120 us
  starting transfers between devices  28.4 us (24%)
  waiting for transfers between devices  24 us (20%)
  matrix products  18.6 us (16%)
  between operations  15.2 us (13%)
  local copies, waits for them, and re-layouts  13.9 us (12%)
  other arithmetic  10.3 us (9%)
  Pallas kernels  9.2 us (8%)
    ppermute x14, waiting for transfers between devices, tree_gather(): parts.append(lax.ppermute(buffer, 'tok', pairs))  24 us
    ppermute x14, starting transfers between devices, tree_gather(): parts.append(lax.ppermute(buffer, 'tok', pairs))  20.5 us
    dot_general x2, matrix products, project(): query = jnp.dot(cols, w_query, preferred_element_type=jnp.float32) + b_query  9.32 us
    pallas_call x1, Pallas kernels, attend(): pl.pallas_call(attend_kernel, grid=(width // HD,), in_specs=[pl.BlockSpec...  9.2 us
    unnamed x47, local copies, waits for them, and re-layouts  7.38 us
    dot_general x2, matrix products, project(): jnp.dot(cols, kv_weight, preferred_element_type=jnp.float32) + kv_bias  4.98 us
    all_to_all x1, starting transfers between devices, swap_columns(): blocks = lax.all_to_all(tiled, 'kv', 0, 0, tiled=False)  4.83 us
    dot_general x1, matrix products, head_scores(): jnp.einsum('ngd,md->ngm', shaped, key_rows, preferred_element_type=jnp.fl...  3.39 us
  transfers between devices with their start and end apart: 18, of which 8 were waited for; matrix products, arithmetic and copies ran while one was open for 20% of the time, Pallas kernels for 0%

profile of v10, /device:TPU:1, one launch (start us, length us, event | category | flops | bytes accessed | tf_op | source)
XLA Modules:
  0.0 119.6 jit_solution(16100844168519137240)
XLA Ops:
  7.3 6.8 %copy.125 = bf16[2,12288,128]{2,1,0:T(8,128)(2,1)} copy(bf16[2,12288,128]{2,1,0:T(8,128)(2,1)} %param.17) | data formatting | bytes 12582912
  14.2 0.7 broadcast_in_dim.45
  14.8 4.8 %all-to-all-start = ((bf16[4,16,1280]{2,1,0:T(8,128)(2,1)}), bf16[4,16,1280]{2,1,0:T(8,128)(2,1)S(1)}, u32[]{:S(2)}, u32[]{:S(2)}) async-start(bf16[4,16,1280]{2,1,0:T(8,128)(2,1)} %broadcast_in_dim.45), calls=%async_computation | async-start | bytes 327680 | tf_op jit(solution)/shard_map/all_to_all | solution.py:124
  19.7 1.0 collective-permute-start.14
  20.6 0.6 dynamic_slice.3
  21.2 1.3 %or_select_fusion.kpos_ref = s32[1,2560]{1,0:T(1,128)} fusion(s32[]{:T(128)} %bitcast.14), kind=kLoop, calls=%fused_computation.94 | loop fusion | flops 20480 | bytes 10244 | tf_op jit(solution)/shard_map/jit(_where)/select_n | solution.py:197
  23.2 0.6 compare_and_fusion
  23.8 0.1 copy.49
  23.9 0.1 copy.48
  23.9 0.1 copy.50
  24.1 0.1 reduce.19
  24.2 1.0 multiply_cosine_fusion.1
  25.2 0.2 fusion.31
  25.4 0.1 multiply_cosine_fusion.3
  25.6 1.1 fusion.19
  26.7 4.2 %fusion.15 = bf16[16,640]{1,0:T(8,128)(2,1)S(1)} fusion(bf16[16,5120]{1,0:T(8,128)(2,1)S(1)} %bitcast.86, bf16[5120,640]{1,0:T(8,128)(2,1)} %param.13, f32[640]{0:T(1024)S(1)} %copy-done.6), kind=kOutput, calls=%fused_computation.23 | convolution fusion | flops 104878080 | bytes 6740480 | tf_op jit(solution)/shard_map/dot_general | solution.py:130
  31.0 0.1 concatenate.83
  31.1 1.1 collective-permute-start
  32.2 0.9 collective-permute-done
  33.0 2.7 %collective-permute-start.3 = (bf16[32,1024]{1,0:T(8,128)(2,1)S(1)}, bf16[32,1024]{1,0:T(8,128)(2,1)S(1)}, u32[]{:S(2)}, u32[]{:S(2)}) collective-permute-start(bf16[32,1024]{1,0:T(8,128)(2,1)S(1)} %pad_maximum_fusion.3), channel_id=1, source_target_pairs={{0,6},{1,7},{2,0},{3,1},{4,2},{5,3},{6,4},{7,5},{8,14},{9,15},{10,... | collective-permute-start | bytes 196616 | tf_op jit(solution)/shard_map/ppermute | solution.py:109
  35.7 0.4 collective-permute-start.2
  36.1 0.7 collective-permute-start.1
  36.8 5.5 %collective-permute-done.1 = bf16[32,1024]{1,0:T(8,128)(2,1)S(1)} collective-permute-done((bf16[32,1024]{1,0:T(8,128)(2,1)S(1)}, bf16[32,1024]{1,0:T(8,128)(2,1)S(1)}, u32[]{:S(2)}, u32[]{:S(2)}) %collective-permute-start.1) | collective-permute-done | bytes 65568 | tf_op jit(solution)/shard_map/ppermute | solution.py:109
  42.4 1.7 %collective-permute-start.4 = (bf16[128,1024]{1,0:T(8,128)(2,1)S(1)}, bf16[128,1024]{1,0:T(8,128)(2,1)S(1)}, u32[]{:S(2)}, u32[]{:S(2)}) collective-permute-start(bf16[128,1024]{1,0:T(8,128)(2,1)S(1)} %get-tuple-element.24), channel_id=1, source_target_pairs={{0,8},{1,9},{2,10},{3,11},{4,12},{5,13},{6,14},{7,15},{8,16},{9,17... | collective-permute-start | bytes 786440 | tf_op jit(solution)/shard_map/ppermute | solution.py:109
  44.1 0.7 iota_add_fusion.qpos_ref
  44.7 3.1 %collective-permute-start.5 = (bf16[128,1024]{1,0:T(8,128)(2,1)S(1)}, bf16[128,1024]{1,0:T(8,128)(2,1)S(1)}, u32[]{:S(2)}, u32[]{:S(2)}) collective-permute-start(bf16[128,1024]{1,0:T(8,128)(2,1)S(1)} %get-tuple-element.24), channel_id=1, source_target_pairs={{0,16},{1,17},{2,18},{3,19},{4,20},{5,21},{6,22},{7,23},{8,24},{9,... | collective-permute-start | bytes 786440 | tf_op jit(solution)/shard_map/ppermute | solution.py:109
  47.9 0.9 collective-permute-start.6
  48.7 3.2 %collective-permute-done.4 = bf16[128,1024]{1,0:T(8,128)(2,1)S(1)} collective-permute-done((bf16[128,1024]{1,0:T(8,128)(2,1)S(1)}, bf16[128,1024]{1,0:T(8,128)(2,1)S(1)}, u32[]{:S(2)}, u32[]{:S(2)}) %collective-permute-start.4) | collective-permute-done | bytes 262176 | tf_op jit(solution)/shard_map/ppermute | solution.py:109
  51.9 6.4 %collective-permute-done.5 = bf16[128,1024]{1,0:T(8,128)(2,1)S(1)} collective-permute-done((bf16[128,1024]{1,0:T(8,128)(2,1)S(1)}, bf16[128,1024]{1,0:T(8,128)(2,1)S(1)}, u32[]{:S(2)}, u32[]{:S(2)}) %collective-permute-start.5) | collective-permute-done | bytes 262176 | tf_op jit(solution)/shard_map/ppermute | solution.py:109
  58.3 0.3 collective-permute-done.6
  58.6 0.6 gather_fusion
  59.4 0.1 fusion.58
  59.5 0.1 fusion.71
  59.7 2.3 %scatter_fusion = bf16[2,12288,128]{2,1,0:T(8,128)(2,1)} fusion(bf16[2,12288,128]{2,1,0:T(8,128)(2,1)} %copy.125, s32[16]{0:T(128)S(1)} %get-tuple-element.10, bf16[16,2,128]{2,0,1:T(8,128)(2,1)S(1)} %maximum_bitcast_fusion), kind=kCustom, calls=%fused_computation.2 | custom fusion | bytes 24640 | tf_op jit(solution)/shard_map/scatter | solution.py:90
  62.0 3.4 %fusion.74 = (f32[16,5]{0,1:T(8,128)S(1)}, f32[16,5,12288]{2,0,1:T(8,128)S(1)}) fusion(bf16[2,12288,128]{2,1,0:T(8,128)(2,1)} %scatter_fusion, bf16[16,5,64]{2,0,1:T(8,128)(2,1)S(1)} %get-tuple-element.21, bf16[16,5,64]{2,0,1:T(8,128)(2,1)S(1)} %get-tuple-element.20, pred[16,12288]{1,0:T(8,128)(4,1)S(1)} %fusion.31), kind=kOutput, calls=%fused_computation.170 | convolution fusion | flops 254648240 | bytes 7295296 | tf_op jit(solution)/shard_map/ngd,md->ngm/dot_general | solution.py:66
  65.4 0.8 fusion.1
  66.2 0.9 fusion.28
  67.1 1.6 %collective-permute-start.7 = (bf16[16,640]{1,0:T(8,128)(2,1)S(1)}, bf16[16,640]{1,0:T(8,128)(2,1)S(1)}, u32[]{:S(2)}, u32[]{:S(2)}) collective-permute-start(bf16[16,640]{1,0:T(8,128)(2,1)S(1)} %bitcast.93), channel_id=1, source_target_pairs={{0,1},{1,0},{2,3},{3,2},{4,5},{5,4},{6,7},{7,6},{8,9},{9,8},{10,11... | collective-permute-start | bytes 61448 | tf_op jit(solution)/shard_map/ppermute | solution.py:109
  68.8 0.2 fusion.35
  69.0 0.7 iota_reduce_fusion
  69.9 2.7 %collective-permute-start.10 = (bf16[32,640]{1,0:T(8,128)(2,1)S(1)}, bf16[32,640]{1,0:T(8,128)(2,1)S(1)}, u32[]{:S(2)}, u32[]{:S(2)}) collective-permute-start(bf16[32,640]{1,0:T(8,128)(2,1)S(1)} %get-tuple-element.42), channel_id=1, source_target_pairs={{0,6},{1,7},{2,0},{3,1},{4,2},{5,3},{6,4},{7,5},{8,14},{9,15},{10,... | collective-permute-start | bytes 122888 | tf_op jit(solution)/shard_map/ppermute | solution.py:109
  72.6 1.4 %collective-permute-done.8 = bf16[32,640]{1,0:T(8,128)(2,1)S(1)} collective-permute-done((bf16[32,640]{1,0:T(8,128)(2,1)S(1)}, bf16[32,640]{1,0:T(8,128)(2,1)S(1)}, u32[]{:S(2)}, u32[]{:S(2)}) %collective-permute-start.8) | collective-permute-done | bytes 40992 | tf_op jit(solution)/shard_map/ppermute | solution.py:109
  74.0 3.0 %collective-permute-done.9 = bf16[32,640]{1,0:T(8,128)(2,1)S(1)} collective-permute-done((bf16[32,640]{1,0:T(8,128)(2,1)S(1)}, bf16[32,640]{1,0:T(8,128)(2,1)S(1)}, u32[]{:S(2)}, u32[]{:S(2)}) %collective-permute-start.9) | collective-permute-done | bytes 40992 | tf_op jit(solution)/shard_map/ppermute | solution.py:109
  77.0 2.7 %collective-permute-start.12 = (bf16[128,640]{1,0:T(8,128)(2,1)S(1)}, bf16[128,640]{1,0:T(8,128)(2,1)S(1)}, u32[]{:S(2)}, u32[]{:S(2)}) collective-permute-start(bf16[128,640]{1,0:T(8,128)(2,1)S(1)} %get-tuple-element.30), channel_id=1, source_target_pairs={{0,16},{1,17},{2,18},{3,19},{4,20},{5,21},{6,22},{7,23},{8,24},{9,... | collective-permute-start | bytes 491528 | tf_op jit(solution)/shard_map/ppermute | solution.py:109
  79.6 0.3 collective-permute-start.11
  80.0 1.5 %maximum_select_fusion = bf16[2,2048,128]{2,1,0:T(8,128)(2,1)S(1)} fusion(bf16[2,1024,128]{2,1,0:T(8,128)(2,1)} %collective-permute-done.14, bf16[2,1024,128]{2,1,0:T(8,128)(2,1)S(1)} %copy-done.1, pred[]{:T(512)S(6)} %eq.32), kind=kLoop, calls=%fused_computation.29 | loop fusion | flops 4718592 | bytes 2097153 | tf_op jit(solution)/shard_map/jit(_where)/select_n | solution.py:183
  81.4 2.6 %collective-permute-start.13 = (bf16[128,640]{1,0:T(8,128)(2,1)S(1)}, bf16[128,640]{1,0:T(8,128)(2,1)S(1)}, u32[]{:S(2)}, u32[]{:S(2)}) collective-permute-start(bf16[128,640]{1,0:T(8,128)(2,1)S(1)} %get-tuple-element.30), channel_id=1, source_target_pairs={{0,24},{1,25},{2,26},{3,27},{4,28},{5,29},{6,30},{7,31},{8,0},{9,1... | collective-permute-start | bytes 491528 | tf_op jit(solution)/shard_map/ppermute | solution.py:109
  84.0 3.5 %collective-permute-done.11 = bf16[128,640]{1,0:T(8,128)(2,1)S(1)} collective-permute-done((bf16[128,640]{1,0:T(8,128)(2,1)S(1)}, bf16[128,640]{1,0:T(8,128)(2,1)S(1)}, u32[]{:S(2)}, u32[]{:S(2)}) %collective-permute-start.11) | collective-permute-done | bytes 163872 | tf_op jit(solution)/shard_map/ppermute | solution.py:109
  87.6 0.6 gather_fusion.1
  88.2 0.7 broadcast_select_fusion.1
  88.9 3.8 %fusion.12 = f32[256,256]{0,1:T(8,128)S(1)} fusion(bf16[256,5120]{1,0:T(8,128)(2,1)} %all-gather.2.cloned.1.call-done, bf16[640,8,2,128]{3,2,1,0:T(2,128)(2,1)} %bitcast.82, f32[256]{0:T(256)S(1)} %bitcast.96), kind=kOutput, calls=%fused_computation.21 | convolution fusion | flops 671154176 | bytes 5506048 | tf_op jit(solution)/shard_map/dot_general | solution.py:131
  92.8 5.1 %convolution_add_fusion = f32[256,640]{1,0:T(8,128)S(1)} fusion(bf16[256,5120]{1,0:T(8,128)(2,1)S(1)} %copy-done.11, bf16[5120,640]{1,0:T(8,128)(2,1)} %param.13, f32[640]{0:T(1024)S(1)} %copy-done.6), kind=kOutput, calls=%fused_computation.20 | convolution fusion | flops 1677885440 | bytes 9832960 | tf_op jit(solution)/shard_map/dot_general | solution.py:130
  97.9 0.2 copy.56
  98.1 0.1 copy.67
  98.2 0.1 copy.66
  98.3 0.1 copy.65
  98.4 0.6 fusion.45
  99.0 0.1 pad_maximum_fusion.2
  99.1 2.1 %collective-permute-start.15 = (bf16[2,256,128]{2,1,0:T(8,128)(2,1)S(1)}, bf16[2,256,128]{2,1,0:T(8,128)(2,1)S(1)}, u32[]{:S(2)}, u32[]{:S(2)}) collective-permute-start(bf16[2,256,128]{2,1,0:T(8,128)(2,1)S(1)} %pad_maximum_fusion.2), channel_id=1, source_target_pairs={{0,1},{1,0},{2,3},{3,2},{4,5},{5,4},{6,7},{7,6},{8,9},{9,8},{10,11... | collective-permute-start | bytes 393224 | tf_op jit(solution)/shard_map/ppermute | solution.py:14
  101.2 0.1 subtract_convert_fusion
  101.4 0.9 copy.60.q_ref
  102.3 0.1 maximum_select_fusion.1
  102.4 1.2 fusion.34
  103.6 9.2 %shard_map.138 = bf16[256,640]{1,0:T(8,128)(2,1)} custom-call(bf16[256,640]{1,0:T(8,128)(2,1)} %copy.60.q_ref, bf16[2560,128]{1,0:T(8,128)(2,1)} %get-tuple-element.13.k_ref, bf16[2560,128]{1,0:T(8,128)(2,1)} %get-tuple-element.12.v_ref, s32[256,1]{1,0:T(8,128)} %iota_add_fusion.qpos_ref, s32[1,2560]{1,0:T(1,128)} %or_select_fusion.kpos_ref), custom_call_target="tpu_custom_call" | custom-call | tf_op jit(solution)/shard_map/pallas_call | solution.py:47
  (90 shorter events, 0.9 us)
Async XLA Ops:
  7.2 7.0 %copy-start.5 = (bf16[16,1280]{1,0:T(8,128)(2,1)S(1)}, bf16[16,1280]{1,0:T(8,128)(2,1)}, u32[]{:S(2)}) copy-start(bf16[16,1280]{1,0:T(8,128)(2,1)} %param.11) | copy-start | bytes 122884
  7.2 12.5 %copy-start.1 = (bf16[2,1024,128]{2,1,0:T(8,128)(2,1)S(1)}, bf16[2,1024,128]{2,1,0:T(8,128)(2,1)}, u32[]{:S(2)}) copy-start(bf16[2,1024,128]{2,1,0:T(8,128)(2,1)} %param.20) | copy-start | bytes 1572868
  7.2 13.5 %copy-start.12 = (s32[16]{0:T(128)S(1)}, s32[16]{0:T(128)}, u32[]{:S(2)}) copy-start(s32[16]{0:T(128)} %param.21) | copy-start | bytes 196
  7.2 16.0 %copy-start.9 = (s32[16]{0:T(128)S(1)}, s32[16]{0:T(128)}, u32[]{:S(2)}) copy-start(s32[16]{0:T(128)} %param.19) | copy-start | bytes 196
  7.2 16.0 %copy-start.10 = (s32[16]{0:T(128)S(1)}, s32[16]{0:T(128)}, u32[]{:S(2)}) copy-start(s32[16]{0:T(128)} %param.18) | copy-start | bytes 196
  7.2 18.3 %copy-start = (bf16[5120,2,128]{2,1,0:T(2,128)(2,1)S(1)}, bf16[5120,2,128]{2,1,0:T(2,128)(2,1)}, u32[]{:S(2)}) copy-start(bf16[5120,2,128]{2,1,0:T(2,128)(2,1)} %param.14) | copy-start | bytes 7864324
  7.2 81.6 %all-gather.2.cloned.1.call-start = ((), (), s32[]{:S(2)}) async-start(), calls=%async_computation.1 | async-start | bytes 3276800 | tf_op jit(solution)/shard_map/all_gather | solution.py:129
  14.1 12.6 %copy-start.6 = (f32[640]{0:T(1024)S(1)}, f32[640]{0:T(1024)}, u32[]{:S(2)}) copy-start(f32[640]{0:T(1024)} %param.15) | copy-start | bytes 7684
  14.8 10.7 %all-to-all-start = ((bf16[4,16,1280]{2,1,0:T(8,128)(2,1)}), bf16[4,16,1280]{2,1,0:T(8,128)(2,1)S(1)}, u32[]{:S(2)}, u32[]{:S(2)}) async-start(bf16[4,16,1280]{2,1,0:T(8,128)(2,1)} %broadcast_in_dim.45), calls=%async_computation | async-start | bytes 327680 | tf_op jit(solution)/shard_map/all_to_all | solution.py:124
  19.7 60.3 %collective-permute-start.14 = (bf16[2,1024,128]{2,1,0:T(8,128)(2,1)S(1)}, bf16[2,1024,128]{2,1,0:T(8,128)(2,1)}, u32[]{:S(2)}, u32[]{:S(2)}) collective-permute-start(bf16[2,1024,128]{2,1,0:T(8,128)(2,1)S(1)} %copy-done.1), channel_id=1, source_target_pairs={{0,1},{1,0},{2,3},{3,2},{4,5},{5,4},{6,7},{7,6},{8,9},{9,8},{10,11... | collective-permute-start | bytes 1572872 | tf_op jit(solution)/shard_map/ppermute | solution.py:14
  26.7 21.1 %copy-start.7 = (s32[16]{0:T(128)S(1)}, s32[16]{0:T(128)}, u32[]{:S(2)}) copy-start(s32[16]{0:T(128)} %get-tuple-element.7) | copy-start | bytes 196
  31.1 2.0 %collective-permute-start = (bf16[16,1024]{1,0:T(8,128)(2,1)S(1)}, bf16[16,1024]{1,0:T(8,128)(2,1)S(1)}, u32[]{:S(2)}, u32[]{:S(2)}) collective-permute-start(bf16[16,1024]{1,0:T(8,128)(2,1)S(1)} %concatenate.83), channel_id=1, source_target_pairs={{0,1},{1,0},{2,3},{3,2},{4,5},{5,4},{6,7},{7,6},{8,9},{9,8},{10,11... | collective-permute-start | bytes 98312 | tf_op jit(solution)/shard_map/ppermute | solution.py:109
  33.0 9.3 %collective-permute-start.3 = (bf16[32,1024]{1,0:T(8,128)(2,1)S(1)}, bf16[32,1024]{1,0:T(8,128)(2,1)S(1)}, u32[]{:S(2)}, u32[]{:S(2)}) collective-permute-start(bf16[32,1024]{1,0:T(8,128)(2,1)S(1)} %pad_maximum_fusion.3), channel_id=1, source_target_pairs={{0,6},{1,7},{2,0},{3,1},{4,2},{5,3},{6,4},{7,5},{8,14},{9,15},{10,... | collective-permute-start | bytes 196616 | tf_op jit(solution)/shard_map/ppermute | solution.py:109
  35.7 6.6 %collective-permute-start.2 = (bf16[32,1024]{1,0:T(8,128)(2,1)S(1)}, bf16[32,1024]{1,0:T(8,128)(2,1)S(1)}, u32[]{:S(2)}, u32[]{:S(2)}) collective-permute-start(bf16[32,1024]{1,0:T(8,128)(2,1)S(1)} %pad_maximum_fusion.3), channel_id=1, source_target_pairs={{0,4},{1,5},{2,6},{3,7},{4,0},{5,1},{6,2},{7,3},{8,12},{9,13},{10,... | collective-permute-start | bytes 196616 | tf_op jit(solution)/shard_map/ppermute | solution.py:109
  36.1 6.2 %collective-permute-start.1 = (bf16[32,1024]{1,0:T(8,128)(2,1)S(1)}, bf16[32,1024]{1,0:T(8,128)(2,1)S(1)}, u32[]{:S(2)}, u32[]{:S(2)}) collective-permute-start(bf16[32,1024]{1,0:T(8,128)(2,1)S(1)} %pad_maximum_fusion.3), channel_id=1, source_target_pairs={{0,2},{1,3},{2,4},{3,5},{4,6},{5,7},{6,0},{7,1},{8,10},{9,11},{10,... | collective-permute-start | bytes 196616 | tf_op jit(solution)/shard_map/ppermute | solution.py:109
  42.4 9.5 %collective-permute-start.4 = (bf16[128,1024]{1,0:T(8,128)(2,1)S(1)}, bf16[128,1024]{1,0:T(8,128)(2,1)S(1)}, u32[]{:S(2)}, u32[]{:S(2)}) collective-permute-start(bf16[128,1024]{1,0:T(8,128)(2,1)S(1)} %get-tuple-element.24), channel_id=1, source_target_pairs={{0,8},{1,9},{2,10},{3,11},{4,12},{5,13},{6,14},{7,15},{8,16},{9,17... | collective-permute-start | bytes 786440 | tf_op jit(solution)/shard_map/ppermute | solution.py:109
  44.7 13.6 %collective-permute-start.5 = (bf16[128,1024]{1,0:T(8,128)(2,1)S(1)}, bf16[128,1024]{1,0:T(8,128)(2,1)S(1)}, u32[]{:S(2)}, u32[]{:S(2)}) collective-permute-start(bf16[128,1024]{1,0:T(8,128)(2,1)S(1)} %get-tuple-element.24), channel_id=1, source_target_pairs={{0,16},{1,17},{2,18},{3,19},{4,20},{5,21},{6,22},{7,23},{8,24},{9,... | collective-permute-start | bytes 786440 | tf_op jit(solution)/shard_map/ppermute | solution.py:109
  47.9 10.8 %collective-permute-start.6 = (bf16[128,1024]{1,0:T(8,128)(2,1)S(1)}, bf16[128,1024]{1,0:T(8,128)(2,1)S(1)}, u32[]{:S(2)}, u32[]{:S(2)}) collective-permute-start(bf16[128,1024]{1,0:T(8,128)(2,1)S(1)} %get-tuple-element.24), channel_id=1, source_target_pairs={{0,24},{1,25},{2,26},{3,27},{4,28},{5,29},{6,30},{7,31},{8,0},{9,1... | collective-permute-start | bytes 786440 | tf_op jit(solution)/shard_map/ppermute | solution.py:109
  62.0 4.2 %slice-start = ((s8[6291456]{0:T(1024)(128)(4,1)}), s8[4194304]{0:T(1024)(128)(4,1)S(1)}, s32[]{:S(2)}) async-start(s8[6291456]{0:T(1024)(128)(4,1)} %bitcast.80), calls=%async_computation.2 | async-start | bytes 8388608
  62.0 4.2 %slice-start.1 = ((s8[6291456]{0:T(1024)(128)(4,1)}), s8[2097152]{0:T(1024)(128)(4,1)S(1)}, s32[]{:S(2)}) async-start(s8[6291456]{0:T(1024)(128)(4,1)} %bitcast.80), calls=%async_computation.3 | async-start | bytes 4194304
  67.1 21.8 %copy-start.8 = (f32[2,128]{1,0:T(2,128)S(1)}, f32[2,128]{1,0:T(2,128)}, u32[]{:S(2)}) copy-start(f32[2,128]{1,0:T(2,128)} %param.16) | copy-start | bytes 3076
  67.1 2.6 %collective-permute-start.7 = (bf16[16,640]{1,0:T(8,128)(2,1)S(1)}, bf16[16,640]{1,0:T(8,128)(2,1)S(1)}, u32[]{:S(2)}, u32[]{:S(2)}) collective-permute-start(bf16[16,640]{1,0:T(8,128)(2,1)S(1)} %bitcast.93), channel_id=1, source_target_pairs={{0,1},{1,0},{2,3},{3,2},{4,5},{5,4},{6,7},{7,6},{8,9},{9,8},{10,11... | collective-permute-start | bytes 61448 | tf_op jit(solution)/shard_map/ppermute | solution.py:109
  69.8 4.1 %collective-permute-start.8 = (bf16[32,640]{1,0:T(8,128)(2,1)S(1)}, bf16[32,640]{1,0:T(8,128)(2,1)S(1)}, u32[]{:S(2)}, u32[]{:S(2)}) collective-permute-start(bf16[32,640]{1,0:T(8,128)(2,1)S(1)} %get-tuple-element.42), channel_id=1, source_target_pairs={{0,2},{1,3},{2,4},{3,5},{4,6},{5,7},{6,0},{7,1},{8,10},{9,11},{10,... | collective-permute-start | bytes 122888 | tf_op jit(solution)/shard_map/ppermute | solution.py:109
  69.9 7.0 %collective-permute-start.10 = (bf16[32,640]{1,0:T(8,128)(2,1)S(1)}, bf16[32,640]{1,0:T(8,128)(2,1)S(1)}, u32[]{:S(2)}, u32[]{:S(2)}) collective-permute-start(bf16[32,640]{1,0:T(8,128)(2,1)S(1)} %get-tuple-element.42), channel_id=1, source_target_pairs={{0,6},{1,7},{2,0},{3,1},{4,2},{5,3},{6,4},{7,5},{8,14},{9,15},{10,... | collective-permute-start | bytes 122888 | tf_op jit(solution)/shard_map/ppermute | solution.py:109
  72.6 4.4 %collective-permute-start.9 = (bf16[32,640]{1,0:T(8,128)(2,1)S(1)}, bf16[32,640]{1,0:T(8,128)(2,1)S(1)}, u32[]{:S(2)}, u32[]{:S(2)}) collective-permute-start(bf16[32,640]{1,0:T(8,128)(2,1)S(1)} %get-tuple-element.42), channel_id=1, source_target_pairs={{0,4},{1,5},{2,6},{3,7},{4,0},{5,1},{6,2},{7,3},{8,12},{9,13},{10,... | collective-permute-start | bytes 122888 | tf_op jit(solution)/shard_map/ppermute | solution.py:109
  77.0 10.6 %collective-permute-start.12 = (bf16[128,640]{1,0:T(8,128)(2,1)S(1)}, bf16[128,640]{1,0:T(8,128)(2,1)S(1)}, u32[]{:S(2)}, u32[]{:S(2)}) collective-permute-start(bf16[128,640]{1,0:T(8,128)(2,1)S(1)} %get-tuple-element.30), channel_id=1, source_target_pairs={{0,16},{1,17},{2,18},{3,19},{4,20},{5,21},{6,22},{7,23},{8,24},{9,... | collective-permute-start | bytes 491528 | tf_op jit(solution)/shard_map/ppermute | solution.py:109
  79.6 7.9 %collective-permute-start.11 = (bf16[128,640]{1,0:T(8,128)(2,1)S(1)}, bf16[128,640]{1,0:T(8,128)(2,1)S(1)}, u32[]{:S(2)}, u32[]{:S(2)}) collective-permute-start(bf16[128,640]{1,0:T(8,128)(2,1)S(1)} %get-tuple-element.30), channel_id=1, source_target_pairs={{0,8},{1,9},{2,10},{3,11},{4,12},{5,13},{6,14},{7,15},{8,16},{9,17... | collective-permute-start | bytes 491528 | tf_op jit(solution)/shard_map/ppermute | solution.py:109
  81.4 6.1 %collective-permute-start.13 = (bf16[128,640]{1,0:T(8,128)(2,1)S(1)}, bf16[128,640]{1,0:T(8,128)(2,1)S(1)}, u32[]{:S(2)}, u32[]{:S(2)}) collective-permute-start(bf16[128,640]{1,0:T(8,128)(2,1)S(1)} %get-tuple-element.30), channel_id=1, source_target_pairs={{0,24},{1,25},{2,26},{3,27},{4,28},{5,29},{6,30},{7,31},{8,0},{9,1... | collective-permute-start | bytes 491528 | tf_op jit(solution)/shard_map/ppermute | solution.py:109
  88.9 3.9 %copy-start.11 = (bf16[256,5120]{1,0:T(8,128)(2,1)S(1)}, bf16[256,5120]{1,0:T(8,128)(2,1)}, u32[]{:S(2)}) copy-start(bf16[256,5120]{1,0:T(8,128)(2,1)} %all-gather.2.cloned.1.call-done) | copy-start | bytes 7864324
  92.8 8.5 %copy-start.2 = (f32[256,64]{0,1:T(8,128)S(1)}, f32[256,64]{0,1:T(8,128)}, u32[]{:S(2)}) copy-start(f32[256,64]{0,1:T(8,128)} %get-tuple-element.50) | copy-start | bytes 196612
  92.8 8.5 %copy-start.3 = (f32[256,64]{0,1:T(8,128)S(1)}, f32[256,64]{0,1:T(8,128)}, u32[]{:S(2)}) copy-start(f32[256,64]{0,1:T(8,128)} %get-tuple-element.51) | copy-start | bytes 196612
  99.1 13.6 %copy-start.4 = (bf16[2,256,128]{2,1,0:T(8,128)(2,1)}, bf16[2,256,128]{2,1,0:T(8,128)(2,1)S(1)}, u32[]{:S(2)}) copy-start(bf16[2,256,128]{2,1,0:T(8,128)(2,1)S(1)} %pad_maximum_fusion.2) | copy-start | bytes 393220
  99.1 3.1 %collective-permute-start.15 = (bf16[2,256,128]{2,1,0:T(8,128)(2,1)S(1)}, bf16[2,256,128]{2,1,0:T(8,128)(2,1)S(1)}, u32[]{:S(2)}, u32[]{:S(2)}) collective-permute-start(bf16[2,256,128]{2,1,0:T(8,128)(2,1)S(1)} %pad_maximum_fusion.2), channel_id=1, source_target_pairs={{0,1},{1,0},{2,3},{3,2},{4,5},{5,4},{6,7},{7,6},{8,9},{9,8},{10,11... | collective-permute-start | bytes 393224 | tf_op jit(solution)/shard_map/ppermute | solution.py:14
Sparse Core Ops, SparseCore 0:
  14.3 38.1 all-gather.1

commit v11 on v10

--- a/solution.py
+++ b/solution.py
@@ -125,11 +125,20 @@
     return jnp.transpose(blocks, (1, 0, 2)).reshape(rows.shape[0], count * rows.shape[1])
 
 
-def project(rows, w_query, kv_weight, b_query, kv_bias, small=False):
-    cols = swap_columns(rows) if small else lax.all_gather(rows, "kv", axis=1, tiled=True)
-    query = jnp.dot(cols, w_query, preferred_element_type=jnp.float32) + b_query
-    keyval = jnp.dot(cols, kv_weight, preferred_element_type=jnp.float32) + kv_bias
-    return query, keyval
+def block_project(rows, after, w_query, kv_weight, b_query, kv_bias):
+    count = lax.axis_size("kv")
+    width = rows.shape[1]
+    tiled = jnp.broadcast_to(rows[None], (count,) + rows.shape)
+    tiled, after = lax.optimization_barrier((tiled, after))
+    blocks = lax.all_to_all(tiled, "kv", 0, 0, tiled=False)
+    query = None
+    keyval = None
+    for source in range(count):
+        part_q = jnp.dot(blocks[source], w_query[source * width:(source + 1) * width], preferred_element_type=jnp.float32)
+        part_kv = jnp.dot(blocks[source], kv_weight[source * width:(source + 1) * width], preferred_element_type=jnp.float32)
+        query = part_q if query is None else query + part_q
+        keyval = part_kv if keyval is None else keyval + part_kv
+    return query + b_query, keyval + kv_bias, after
 
 
 def body_inner(dec_tokens, pre_tokens, w_query, w_keyval, b_query, b_keyval, dec_pool, owner_slots, dec_lengths):
@@ -138,7 +147,10 @@
     kv_width = w_keyval.shape[2]
     kv_weight = w_keyval.reshape(w_keyval.shape[0], 2 * kv_width)
     kv_bias = b_keyval.reshape(2 * kv_width)
-    dec_q, dec_kv = project(dec_tokens, w_query, kv_weight, b_query, kv_bias, small=True)
+    dec_cols = swap_columns(dec_tokens)
+    pre_q, pre_kv, dec_cols = block_project(pre_tokens, dec_cols, w_query, kv_weight, b_query, kv_bias)
+    dec_q = jnp.dot(dec_cols, w_query, preferred_element_type=jnp.float32) + b_query
+    dec_kv = jnp.dot(dec_cols, kv_weight, preferred_element_type=jnp.float32) + kv_bias
     tok_place = lax.axis_index("tok")
     ids = jnp.stack([owner_slots // dec_count, owner_slots % dec_count], axis=1).astype(jnp.bfloat16)
     used = q_width + 2 * kv_width + 2
@@ -156,7 +168,7 @@
     wanted = tok_place * dec_count + jnp.arange(dec_count, dtype=jnp.int32)
     where = jnp.argmax(requests[None, :] == wanted[:, None], axis=1)
     dec_attn = jnp.take(back, where, axis=0)
-    all_query, all_keyval = project(pre_tokens, w_query, kv_weight, b_query, kv_bias)
+    all_query, all_keyval = pre_q, pre_kv
     return dec_attn, new_pool, all_query, all_keyval
 
 

time: 120 us -> 129 us (1.075)
  local copies, waits for them, and re-layouts: 13.9 us -> 30.6 us
  between operations: 15.2 us -> 1.83 us
  matrix products: 18.6 us -> 24.3 us
  waiting for transfers between devices: 24 us -> 19.8 us
  starting transfers between devices: 28.4 us -> 31 us
    unnamed x47 -> x59, local copies, waits for them, and re-layouts: 7.38 us -> 13.7 us
    dot_general x4 -> x10, matrix products: 14.3 us -> 20.1 us  [the longest x4 8.55 us: block_project(): jnp.dot(blocks[source], w_query[source * width:(source + 1) * width], pre...]
    all_to_all x0 -> x1, starting transfers between devices: none -> 4.54 us  [block_project(): blocks = lax.all_to_all(tiled, 'kv', 0, 0, tiled=False)]
    ppermute x14, waiting for transfers between devices: 24 us -> 19.8 us  [tree_gather(): parts.append(lax.ppermute(buffer, 'tok', pairs))]
    slice x0 -> x1, local copies, waits for them, and re-layouts: none -> 2.85 us  [block_project(): kv_weight[source * width:(source + 1) * width]]
    broadcast_in_dim x0 -> x1, local copies, waits for them, and re-layouts: none -> 2.77 us  [block_project(): tiled = jnp.broadcast_to(rows[None], (count,) + rows.shape)]
    ppermute x14, starting transfers between devices: 20.5 us -> 19.2 us  [tree_gather(): parts.append(lax.ppermute(buffer, 'tok', pairs))]
  transfers between devices with their start and end apart: 18 -> 18, of which waited for: 8 -> 7; matrix products, arithmetic and copies ran while one was open for 20% -> 28% of each run, Pallas kernels for 0% -> 0%
where the time goes in v11:
time: 129 us; the launch traced here: 128 us
  starting transfers between devices  31 us (24%)
  local copies, waits for them, and re-layouts  30.6 us (24%)
  matrix products  24.3 us (19%)
  waiting for transfers between devices  19.8 us (15%)
  other arithmetic  10.8 us (8%)
  Pallas kernels  9.2 us (7%)
  between operations  1.83 us (1%)
    ppermute x14, waiting for transfers between devices, tree_gather(): parts.append(lax.ppermute(buffer, 'tok', pairs))  19.8 us
    ppermute x14, starting transfers between devices, tree_gather(): parts.append(lax.ppermute(buffer, 'tok', pairs))  19.2 us
    unnamed x59, local copies, waits for them, and re-layouts  13.7 us
    pallas_call x1, Pallas kernels, attend(): pl.pallas_call(attend_kernel, grid=(width // HD,), in_specs=[pl.BlockSpec...  9.2 us
    dot_general x4, matrix products, block_project(): jnp.dot(blocks[source], w_query[source * width:(source + 1) * width], pre...  8.55 us
    dot_general x4, matrix products, block_project(): jnp.dot(blocks[source], kv_weight[source * width:(source + 1) * width], p...  6.57 us
    all_to_all x1, starting transfers between devices, swap_columns(): blocks = lax.all_to_all(tiled, 'kv', 0, 0, tiled=False)  4.83 us
    all_to_all x1, starting transfers between devices, block_project(): blocks = lax.all_to_all(tiled, 'kv', 0, 0, tiled=False)  4.54 us
  transfers between devices with their start and end apart: 18, of which 7 were waited for; matrix products, arithmetic and copies ran while one was open for 28% of the time, Pallas kernels for 0%

profile of v11, /device:TPU:1, one launch (start us, length us, event | category | flops | bytes accessed | tf_op | source)
XLA Modules:
  0.0 127.6 jit_solution(5434991648099554145)
XLA Ops:
  0.7 6.9 %copy.139 = bf16[2,12288,128]{2,1,0:T(8,128)(2,1)} copy(bf16[2,12288,128]{2,1,0:T(8,128)(2,1)} %param.17) | data formatting | bytes 12582912
  7.6 0.7 broadcast_in_dim.45
  8.3 4.8 %all-to-all-start = ((bf16[4,16,1280]{2,1,0:T(8,128)(2,1)}), bf16[4,16,1280]{2,1,0:T(8,128)(2,1)S(1)}, u32[]{:S(2)}, u32[]{:S(2)}) async-start(bf16[4,16,1280]{2,1,0:T(8,128)(2,1)} %broadcast_in_dim.45), calls=%async_computation | async-start | bytes 327680 | tf_op jit(solution)/shard_map/all_to_all | solution.py:124
  13.1 1.0 collective-permute-start.14
  14.1 0.6 dynamic_slice.3
  14.7 1.3 or_select_fusion.kpos_ref
  18.1 2.8 %fusion.94 = (bf16[1280,2,128]{2,1,0:T(2,128)(2,1)}, bf16[1280,2,128]{2,1,0:T(2,128)(2,1)}, bf16[1280,2,128]{2,1,0:T(2,128)(2,1)}, bf16[1280,2,128]{2,1,0:T(2,128)(2,1)}) fusion(bf16[5120,2,128]{2,1,0:T(2,128)(2,1)S(1)} %copy-done), kind=kLoop, calls=%fused_computation.190 | loop fusion | bytes 5242880 | tf_op jit(solution)/shard_map/slice | solution.py:138
  21.0 1.0 multiply_cosine_fusion.1
  22.3 2.8 %broadcast_in_dim.44 = bf16[4,256,1280]{2,1,0:T(8,128)(2,1)} broadcast(bf16[256,1280]{1,0:T(8,128)(2,1)} %param.12), dimensions={1,2} | broadcast | bytes 3276800 | tf_op jit(solution)/shard_map/broadcast_in_dim | solution.py:131
  25.1 1.1 fusion.34
  26.3 3.8 %fusion.30 = bf16[16,640]{1,0:T(8,128)(2,1)S(1)} fusion(bf16[16,5120]{1,0:T(8,128)(2,1)S(1)} %bitcast.112, bf16[5120,640]{1,0:T(8,128)(2,1)} %param.13, f32[640]{0:T(1024)S(1)} %copy-done.9), kind=kOutput, calls=%fused_computation.34 | convolution fusion | flops 104878080 | bytes 6740480 | tf_op jit(solution)/shard_map/dot_general | solution.py:152
  30.3 1.1 collective-permute-done
  31.4 2.7 %collective-permute-start.3 = (bf16[32,1024]{1,0:T(8,128)(2,1)S(1)}, bf16[32,1024]{1,0:T(8,128)(2,1)S(1)}, u32[]{:S(2)}, u32[]{:S(2)}) collective-permute-start(bf16[32,1024]{1,0:T(8,128)(2,1)S(1)} %pad_maximum_fusion.3), channel_id=1, source_target_pairs={{0,6},{1,7},{2,0},{3,1},{4,2},{5,3},{6,4},{7,5},{8,14},{9,15},{10,... | collective-permute-start | bytes 196616 | tf_op jit(solution)/shard_map/ppermute | solution.py:109
  34.5 0.7 collective-permute-start.1
  35.2 5.6 %collective-permute-done.1 = bf16[32,1024]{1,0:T(8,128)(2,1)S(1)} collective-permute-done((bf16[32,1024]{1,0:T(8,128)(2,1)S(1)}, bf16[32,1024]{1,0:T(8,128)(2,1)S(1)}, u32[]{:S(2)}, u32[]{:S(2)}) %collective-permute-start.1) | collective-permute-done | bytes 65568 | tf_op jit(solution)/shard_map/ppermute | solution.py:109
  40.9 1.7 %collective-permute-start.4 = (bf16[128,1024]{1,0:T(8,128)(2,1)S(1)}, bf16[128,1024]{1,0:T(8,128)(2,1)S(1)}, u32[]{:S(2)}, u32[]{:S(2)}) collective-permute-start(bf16[128,1024]{1,0:T(8,128)(2,1)S(1)} %get-tuple-element.32), channel_id=1, source_target_pairs={{0,8},{1,9},{2,10},{3,11},{4,12},{5,13},{6,14},{7,15},{8,16},{9,17... | collective-permute-start | bytes 786440 | tf_op jit(solution)/shard_map/ppermute | solution.py:109
  42.6 0.7 iota_add_fusion.qpos_ref
  43.3 3.3 %collective-permute-start.5 = (bf16[128,1024]{1,0:T(8,128)(2,1)S(1)}, bf16[128,1024]{1,0:T(8,128)(2,1)S(1)}, u32[]{:S(2)}, u32[]{:S(2)}) collective-permute-start(bf16[128,1024]{1,0:T(8,128)(2,1)S(1)} %get-tuple-element.32), channel_id=1, source_target_pairs={{0,16},{1,17},{2,18},{3,19},{4,20},{5,21},{6,22},{7,23},{8,24},{9,... | collective-permute-start | bytes 786440 | tf_op jit(solution)/shard_map/ppermute | solution.py:109
  46.6 0.8 collective-permute-start.6
  47.4 4.5 %all-to-all-start.1 = ((bf16[4,256,1280]{2,1,0:T(8,128)(2,1)}), bf16[4,256,1280]{2,1,0:T(8,128)(2,1)}, u32[]{:S(2)}, u32[]{:S(2)}) async-start(bf16[4,256,1280]{2,1,0:T(8,128)(2,1)} %broadcast_in_dim.44), calls=%async_computation.1 | async-start | bytes 5242880 | tf_op jit(solution)/shard_map/all_to_all | solution.py:133
  52.0 5.2 %collective-permute-done.5 = bf16[128,1024]{1,0:T(8,128)(2,1)S(1)} collective-permute-done((bf16[128,1024]{1,0:T(8,128)(2,1)S(1)}, bf16[128,1024]{1,0:T(8,128)(2,1)S(1)}, u32[]{:S(2)}, u32[]{:S(2)}) %collective-permute-start.5) | collective-permute-done | bytes 262176 | tf_op jit(solution)/shard_map/ppermute | solution.py:109
  57.4 0.6 gather_fusion
  58.7 2.3 %scatter_fusion = bf16[2,12288,128]{2,1,0:T(8,128)(2,1)} fusion(bf16[2,12288,128]{2,1,0:T(8,128)(2,1)} %copy.139, s32[16]{0:T(128)S(1)} %get-tuple-element.14, bf16[16,2,128]{2,0,1:T(8,128)(2,1)S(1)} %maximum_bitcast_fusion), kind=kCustom, calls=%fused_computation.2 | custom fusion | bytes 24640 | tf_op jit(solution)/shard_map/scatter | solution.py:90
  61.1 3.4 %fusion.99 = (f32[16,5]{0,1:T(8,128)S(1)}, f32[16,5,12288]{2,0,1:T(8,128)S(1)}) fusion(bf16[2,12288,128]{2,1,0:T(8,128)(2,1)} %scatter_fusion, bf16[16,5,64]{2,0,1:T(8,128)(2,1)S(1)} %get-tuple-element.29, bf16[16,5,64]{2,0,1:T(8,128)(2,1)S(1)} %get-tuple-element.28, pred[16,12288]{1,0:T(8,128)(4,1)S(1)} %fusion.46), kind=kOutput, calls=%fused_computation.195 | convolution fusion | flops 254648240 | bytes 7295296 | tf_op jit(solution)/shard_map/ngd,md->ngm/dot_general | solution.py:66
  64.5 0.8 fusion.1
  65.3 0.9 fusion.43
  66.2 1.6 %collective-permute-start.7 = (bf16[16,640]{1,0:T(8,128)(2,1)S(1)}, bf16[16,640]{1,0:T(8,128)(2,1)S(1)}, u32[]{:S(2)}, u32[]{:S(2)}) collective-permute-start(bf16[16,640]{1,0:T(8,128)(2,1)S(1)} %bitcast.123), channel_id=1, source_target_pairs={{0,1},{1,0},{2,3},{3,2},{4,5},{5,4},{6,7},{7,6},{8,9},{9,8},{10,11... | collective-permute-start | bytes 61448 | tf_op jit(solution)/shard_map/ppermute | solution.py:109
  67.8 0.7 iota_reduce_fusion
  68.5 0.6 constant_dynamic-update-slice_fusion.19
  69.1 0.6 constant_dynamic-update-slice_fusion.18
  69.7 2.7 %collective-permute-start.10 = (bf16[32,640]{1,0:T(8,128)(2,1)S(1)}, bf16[32,640]{1,0:T(8,128)(2,1)S(1)}, u32[]{:S(2)}, u32[]{:S(2)}) collective-permute-start(bf16[32,640]{1,0:T(8,128)(2,1)S(1)} %get-tuple-element.50), channel_id=1, source_target_pairs={{0,6},{1,7},{2,0},{3,1},{4,2},{5,3},{6,4},{7,5},{8,14},{9,15},{10,... | collective-permute-start | bytes 122888 | tf_op jit(solution)/shard_map/ppermute | solution.py:109
  72.4 1.8 %collective-permute-done.8 = bf16[32,640]{1,0:T(8,128)(2,1)S(1)} collective-permute-done((bf16[32,640]{1,0:T(8,128)(2,1)S(1)}, bf16[32,640]{1,0:T(8,128)(2,1)S(1)}, u32[]{:S(2)}, u32[]{:S(2)}) %collective-permute-start.8) | collective-permute-done | bytes 40992 | tf_op jit(solution)/shard_map/ppermute | solution.py:109
  74.1 0.6 constant_dynamic-update-slice_fusion.17
  74.8 2.3 %collective-permute-done.9 = bf16[32,640]{1,0:T(8,128)(2,1)S(1)} collective-permute-done((bf16[32,640]{1,0:T(8,128)(2,1)S(1)}, bf16[32,640]{1,0:T(8,128)(2,1)S(1)}, u32[]{:S(2)}, u32[]{:S(2)}) %collective-permute-start.9) | collective-permute-done | bytes 40992 | tf_op jit(solution)/shard_map/ppermute | solution.py:109
  77.1 0.6 constant_dynamic-update-slice_fusion.16
  77.7 0.6 constant_dynamic-update-slice_fusion.15
  78.4 2.5 %collective-permute-start.12 = (bf16[128,640]{1,0:T(8,128)(2,1)S(1)}, bf16[128,640]{1,0:T(8,128)(2,1)S(1)}, u32[]{:S(2)}, u32[]{:S(2)}) collective-permute-start(bf16[128,640]{1,0:T(8,128)(2,1)S(1)} %get-tuple-element.38), channel_id=1, source_target_pairs={{0,16},{1,17},{2,18},{3,19},{4,20},{5,21},{6,22},{7,23},{8,24},{9,... | collective-permute-start | bytes 491528 | tf_op jit(solution)/shard_map/ppermute | solution.py:109
  81.3 1.5 %maximum_select_fusion = bf16[2,2048,128]{2,1,0:T(8,128)(2,1)S(1)} fusion(bf16[2,1024,128]{2,1,0:T(8,128)(2,1)} %collective-permute-done.14, bf16[2,1024,128]{2,1,0:T(8,128)(2,1)S(1)} %copy-done.4, pred[]{:T(512)S(6)} %eq.32), kind=kLoop, calls=%fused_computation.40 | loop fusion | flops 4718592 | bytes 2097153 | tf_op jit(solution)/shard_map/jit(_where)/select_n | solution.py:195
  82.8 2.3 %collective-permute-start.13 = (bf16[128,640]{1,0:T(8,128)(2,1)S(1)}, bf16[128,640]{1,0:T(8,128)(2,1)S(1)}, u32[]{:S(2)}, u32[]{:S(2)}) collective-permute-start(bf16[128,640]{1,0:T(8,128)(2,1)S(1)} %get-tuple-element.38), channel_id=1, source_target_pairs={{0,24},{1,25},{2,26},{3,27},{4,28},{5,29},{6,30},{7,31},{8,0},{9,1... | collective-permute-start | bytes 491528 | tf_op jit(solution)/shard_map/ppermute | solution.py:109
  85.1 3.5 %collective-permute-done.11 = bf16[128,640]{1,0:T(8,128)(2,1)S(1)} collective-permute-done((bf16[128,640]{1,0:T(8,128)(2,1)S(1)}, bf16[128,640]{1,0:T(8,128)(2,1)S(1)}, u32[]{:S(2)}, u32[]{:S(2)}) %collective-permute-start.11) | collective-permute-done | bytes 163872 | tf_op jit(solution)/shard_map/ppermute | solution.py:109
  88.6 0.7 constant_dynamic-update-slice_fusion.22
  89.3 0.7 constant_dynamic-update-slice_fusion.21
  90.0 0.7 constant_dynamic-update-slice_fusion.20
  90.7 1.8 %gather_fusion.1 = bf16[16,640]{1,0:T(8,128)(2,1)S(1)} fusion(bf16[512,640]{1,0:T(8,128)(2,1)} %constant_dynamic-update-slice_fusion.20, s32[1024]{0:T(1024)S(1)} %pad_clamp_fusion), kind=kCustom, calls=%fused_computation.1 | custom fusion | bytes 41024 | tf_op jit(solution)/shard_map/jit(_take)/gather | solution.py:170
  92.5 0.7 broadcast_select_fusion.1
  93.2 1.8 %fusion.55 = f32[256,256]{0,1:T(8,128)S(1)} fusion(bf16[160,8,2,128]{3,2,1,0:T(2,128)(2,1)} %bitcast.117, bf16[4,256,1280]{2,1,0:T(8,128)(2,1)} %all-to-all-done.1), kind=kOutput, calls=%fused_computation.52 | convolution fusion | flops 167772160 | bytes 1572864 | tf_op jit(solution)/shard_map/dot_general | solution.py:138
  94.9 1.7 %convolution_add_fusion.2 = f32[256,256]{0,1:T(8,128)S(1)} fusion(f32[256,256]{0,1:T(8,128)S(1)} %fusion.55, bf16[160,8,2,128]{3,2,1,0:T(2,128)(2,1)} %bitcast.116, bf16[4,256,1280]{2,1,0:T(8,128)(2,1)} %all-to-all-done.1), kind=kOutput, calls=%fused_computation.32 | convolution fusion | flops 167837696 | bytes 1835008 | tf_op jit(solution)/shard_map/dot_general | solution.py:138
  96.7 1.6 %convolution_add_fusion.1 = f32[256,256]{0,1:T(8,128)S(1)} fusion(f32[256,256]{0,1:T(8,128)S(1)} %convolution_add_fusion.2, bf16[160,8,2,128]{3,2,1,0:T(2,128)(2,1)S(1)} %bitcast.115, bf16[4,256,1280]{2,1,0:T(8,128)(2,1)} %all-to-all-done.1), kind=kOutput, calls=%fused_computation.31 | convolution fusion | flops 167837696 | bytes 1835008 | tf_op jit(solution)/shard_map/dot_general | solution.py:138
  98.3 1.5 %fusion.29 = f32[256,256]{0,1:T(8,128)S(1)} fusion(f32[256,256]{0,1:T(8,128)S(1)} %convolution_add_fusion.1, bf16[160,8,2,128]{3,2,1,0:T(2,128)(2,1)S(1)} %bitcast.114, bf16[4,256,1280]{2,1,0:T(8,128)(2,1)} %all-to-all-done.1, f32[256]{0:T(256)S(1)} %bitcast.126), kind=kOutput, calls=%fused_computation.30 | convolution fusion | flops 167903232 | bytes 1836032 | tf_op jit(solution)/shard_map/dot_general | solution.py:138
  99.8 0.6 slice.177
  100.4 0.6 fusion.95
  101.1 2.3 %fusion.9 = f32[256,640]{1,0:T(8,128)S(1)} fusion(bf16[5120,640]{1,0:T(8,128)(2,1)} %param.13, bf16[4,256,1280]{2,1,0:T(8,128)(2,1)} %all-to-all-done.1), kind=kOutput, calls=%fused_computation.15 | convolution fusion | flops 419430400 | bytes 2949120 | tf_op jit(solution)/shard_map/dot_general | solution.py:137
  103.4 1.8 %fusion.11 = f32[256,640]{1,0:T(8,128)S(1)} fusion(bf16[5120,640]{1,0:T(8,128)(2,1)S(1)} %bitcast.109, bf16[4,256,1280]{2,1,0:T(8,128)(2,1)} %all-to-all-done.1), kind=kOutput, calls=%fused_computation.17 | convolution fusion | flops 419430400 | bytes 2949120 | tf_op jit(solution)/shard_map/dot_general | solution.py:137
  105.2 1.8 %fusion.13 = f32[256,640]{1,0:T(8,128)S(1)} fusion(bf16[5120,640]{1,0:T(8,128)(2,1)S(1)} %bitcast.109, bf16[4,256,1280]{2,1,0:T(8,128)(2,1)} %all-to-all-done.1), kind=kOutput, calls=%fused_computation.19 | convolution fusion | flops 419430400 | bytes 2949120 | tf_op jit(solution)/shard_map/dot_general | solution.py:137
  107.0 2.7 %fusion.26 = f32[256,640]{1,0:T(8,128)} fusion(f32[256,640]{1,0:T(8,128)S(1)} %fusion.9, f32[256,640]{1,0:T(8,128)S(1)} %fusion.11, f32[256,640]{1,0:T(8,128)S(1)} %fusion.13, bf16[5120,640]{1,0:T(8,128)(2,1)S(1)} %bitcast.109, bf16[4,256,1280]{2,1,0:T(8,128)(2,1)} %all-to-all-done.1, f32[640]{0:T(1024)S(1)} %copy-done.9), kind=kOutput, calls=%fused_computation.28 | convolution fusion | flops 420085760 | bytes 4919296 | tf_op jit(solution)/shard_map/dot_general | solution.py:137
  109.7 1.3 %copy.56 = f32[256,640]{0,1:T(8,128)S(1)} copy(f32[256,640]{1,0:T(8,128)} %fusion.26) | data formatting | bytes 1310720 | tf_op jit(solution)/shard_map/add | solution.py:141
  111.0 1.0 copy.67
  112.0 0.9 copy.66
  112.9 0.9 copy.65
  113.9 0.6 fusion.69
  114.5 1.5 %collective-permute-start.15 = (bf16[2,256,128]{2,1,0:T(8,128)(2,1)S(1)}, bf16[2,256,128]{2,1,0:T(8,128)(2,1)S(1)}, u32[]{:S(2)}, u32[]{:S(2)}) collective-permute-start(bf16[2,256,128]{2,1,0:T(8,128)(2,1)S(1)} %pad_maximum_fusion.2), channel_id=1, source_target_pairs={{0,1},{1,0},{2,3},{3,2},{4,5},{5,4},{6,7},{7,6},{8,9},{9,8},{10,11... | collective-permute-start | bytes 393224 | tf_op jit(solution)/shard_map/ppermute | solution.py:14
  116.2 0.9 copy.60.q_ref
  117.2 1.2 fusion.58
  118.4 9.2 %shard_map.138 = bf16[256,640]{1,0:T(8,128)(2,1)} custom-call(bf16[256,640]{1,0:T(8,128)(2,1)} %copy.60.q_ref, bf16[2560,128]{1,0:T(8,128)(2,1)} %get-tuple-element.21.k_ref, bf16[2560,128]{1,0:T(8,128)(2,1)} %get-tuple-element.20.v_ref, s32[256,1]{1,0:T(8,128)} %iota_add_fusion.qpos_ref, s32[1,2560]{1,0:T(1,128)} %or_select_fusion.kpos_ref), custom_call_target="tpu_custom_call" | custom-call | tf_op jit(solution)/shard_map/pallas_call | solution.py:47
  (110 shorter events, 4.3 us)
Async XLA Ops:
  0.6 7.0 %copy-start.8 = (bf16[16,1280]{1,0:T(8,128)(2,1)S(1)}, bf16[16,1280]{1,0:T(8,128)(2,1)}, u32[]{:S(2)}) copy-start(bf16[16,1280]{1,0:T(8,128)(2,1)} %param.11) | copy-start | bytes 122884
  0.6 12.5 %copy-start.3 = (bf16[2,1024,128]{2,1,0:T(8,128)(2,1)S(1)}, bf16[2,1024,128]{2,1,0:T(8,128)(2,1)}, u32[]{:S(2)}) copy-start(bf16[2,1024,128]{2,1,0:T(8,128)(2,1)} %param.20) | copy-start | bytes 1572868
  0.7 13.4 %copy-start.16 = (s32[16]{0:T(128)S(1)}, s32[16]{0:T(128)}, u32[]{:S(2)}) copy-start(s32[16]{0:T(128)} %param.21) | copy-start | bytes 196
  0.7 15.9 %copy-start.14 = (s32[16]{0:T(128)S(1)}, s32[16]{0:T(128)}, u32[]{:S(2)}) copy-start(s32[16]{0:T(128)} %param.19) | copy-start | bytes 196
  0.7 16.4 %copy-start.15 = (s32[16]{0:T(128)S(1)}, s32[16]{0:T(128)}, u32[]{:S(2)}) copy-start(s32[16]{0:T(128)} %param.18) | copy-start | bytes 196
  0.7 17.4 %copy-start = (bf16[5120,2,128]{2,1,0:T(2,128)(2,1)S(1)}, bf16[5120,2,128]{2,1,0:T(2,128)(2,1)}, u32[]{:S(2)}) copy-start(bf16[5120,2,128]{2,1,0:T(2,128)(2,1)} %param.14) | copy-start | bytes 7864324
  8.3 14.0 %all-to-all-start = ((bf16[4,16,1280]{2,1,0:T(8,128)(2,1)}), bf16[4,16,1280]{2,1,0:T(8,128)(2,1)S(1)}, u32[]{:S(2)}, u32[]{:S(2)}) async-start(bf16[4,16,1280]{2,1,0:T(8,128)(2,1)} %broadcast_in_dim.45), calls=%async_computation | async-start | bytes 327680 | tf_op jit(solution)/shard_map/all_to_all | solution.py:124
  13.1 68.2 %collective-permute-start.14 = (bf16[2,1024,128]{2,1,0:T(8,128)(2,1)S(1)}, bf16[2,1024,128]{2,1,0:T(8,128)(2,1)}, u32[]{:S(2)}, u32[]{:S(2)}) collective-permute-start(bf16[2,1024,128]{2,1,0:T(8,128)(2,1)S(1)} %copy-done.3), channel_id=1, source_target_pairs={{0,1},{1,0},{2,3},{3,2},{4,5},{5,4},{6,7},{7,6},{8,9},{9,8},{10,11... | collective-permute-start | bytes 1572872 | tf_op jit(solution)/shard_map/ppermute | solution.py:14
  18.1 4.1 %copy-start.10 = (f32[16]{0:T(128)S(1)}, f32[16]{0:T(128)}, u32[]{:S(2)}) copy-start(f32[16]{0:T(128)} %get-tuple-element.63) | copy-start | bytes 196
  22.3 3.9 %copy-start.9 = (f32[640]{0:T(1024)S(1)}, f32[640]{0:T(1024)}, u32[]{:S(2)}) copy-start(f32[640]{0:T(1024)} %param.15) | copy-start | bytes 7684
  26.3 20.3 %copy-start.12 = (s32[16]{0:T(128)S(1)}, s32[16]{0:T(128)}, u32[]{:S(2)}) copy-start(s32[16]{0:T(128)} %get-tuple-element.11) | copy-start | bytes 196
  30.2 1.2 collective-permute-start
  31.4 9.4 %collective-permute-start.3 = (bf16[32,1024]{1,0:T(8,128)(2,1)S(1)}, bf16[32,1024]{1,0:T(8,128)(2,1)S(1)}, u32[]{:S(2)}, u32[]{:S(2)}) collective-permute-start(bf16[32,1024]{1,0:T(8,128)(2,1)S(1)} %pad_maximum_fusion.3), channel_id=1, source_target_pairs={{0,6},{1,7},{2,0},{3,1},{4,2},{5,3},{6,4},{7,5},{8,14},{9,15},{10,... | collective-permute-start | bytes 196616 | tf_op jit(solution)/shard_map/ppermute | solution.py:109
  34.2 6.7 %collective-permute-start.2 = (bf16[32,1024]{1,0:T(8,128)(2,1)S(1)}, bf16[32,1024]{1,0:T(8,128)(2,1)S(1)}, u32[]{:S(2)}, u32[]{:S(2)}) collective-permute-start(bf16[32,1024]{1,0:T(8,128)(2,1)S(1)} %pad_maximum_fusion.3), channel_id=1, source_target_pairs={{0,4},{1,5},{2,6},{3,7},{4,0},{5,1},{6,2},{7,3},{8,12},{9,13},{10,... | collective-permute-start | bytes 196616 | tf_op jit(solution)/shard_map/ppermute | solution.py:109
  34.5 6.3 %collective-permute-start.1 = (bf16[32,1024]{1,0:T(8,128)(2,1)S(1)}, bf16[32,1024]{1,0:T(8,128)(2,1)S(1)}, u32[]{:S(2)}, u32[]{:S(2)}) collective-permute-start(bf16[32,1024]{1,0:T(8,128)(2,1)S(1)} %pad_maximum_fusion.3), channel_id=1, source_target_pairs={{0,2},{1,3},{2,4},{3,5},{4,6},{5,7},{6,0},{7,1},{8,10},{9,11},{10,... | collective-permute-start | bytes 196616 | tf_op jit(solution)/shard_map/ppermute | solution.py:109
  40.9 11.0 %collective-permute-start.4 = (bf16[128,1024]{1,0:T(8,128)(2,1)S(1)}, bf16[128,1024]{1,0:T(8,128)(2,1)S(1)}, u32[]{:S(2)}, u32[]{:S(2)}) collective-permute-start(bf16[128,1024]{1,0:T(8,128)(2,1)S(1)} %get-tuple-element.32), channel_id=1, source_target_pairs={{0,8},{1,9},{2,10},{3,11},{4,12},{5,13},{6,14},{7,15},{8,16},{9,17... | collective-permute-start | bytes 786440 | tf_op jit(solution)/shard_map/ppermute | solution.py:109
  43.3 13.9 %collective-permute-start.5 = (bf16[128,1024]{1,0:T(8,128)(2,1)S(1)}, bf16[128,1024]{1,0:T(8,128)(2,1)S(1)}, u32[]{:S(2)}, u32[]{:S(2)}) collective-permute-start(bf16[128,1024]{1,0:T(8,128)(2,1)S(1)} %get-tuple-element.32), channel_id=1, source_target_pairs={{0,16},{1,17},{2,18},{3,19},{4,20},{5,21},{6,22},{7,23},{8,24},{9,... | collective-permute-start | bytes 786440 | tf_op jit(solution)/shard_map/ppermute | solution.py:109
  46.6 10.8 %collective-permute-start.6 = (bf16[128,1024]{1,0:T(8,128)(2,1)S(1)}, bf16[128,1024]{1,0:T(8,128)(2,1)S(1)}, u32[]{:S(2)}, u32[]{:S(2)}) collective-permute-start(bf16[128,1024]{1,0:T(8,128)(2,1)S(1)} %get-tuple-element.32), channel_id=1, source_target_pairs={{0,24},{1,25},{2,26},{3,27},{4,28},{5,29},{6,30},{7,31},{8,0},{9,1... | collective-permute-start | bytes 786440 | tf_op jit(solution)/shard_map/ppermute | solution.py:109
  47.4 45.8 %all-to-all-start.1 = ((bf16[4,256,1280]{2,1,0:T(8,128)(2,1)}), bf16[4,256,1280]{2,1,0:T(8,128)(2,1)}, u32[]{:S(2)}, u32[]{:S(2)}) async-start(bf16[4,256,1280]{2,1,0:T(8,128)(2,1)} %broadcast_in_dim.44), calls=%async_computation.1 | async-start | bytes 5242880 | tf_op jit(solution)/shard_map/all_to_all | solution.py:133
  51.9 6.5 %copy-start.11 = (f32[16]{0:T(128)S(1)}, f32[16]{0:T(128)}, u32[]{:S(2)}) copy-start(f32[16]{0:T(128)} %get-tuple-element.63) | copy-start | bytes 196
  61.1 4.2 %slice-start = ((s8[6291456]{0:T(1024)(128)(4,1)}), s8[4194304]{0:T(1024)(128)(4,1)S(1)}, s32[]{:S(2)}) async-start(s8[6291456]{0:T(1024)(128)(4,1)} %bitcast.105), calls=%async_computation.2 | async-start | bytes 8388608
  61.1 4.2 %slice-start.1 = ((s8[6291456]{0:T(1024)(128)(4,1)}), s8[2097152]{0:T(1024)(128)(4,1)S(1)}, s32[]{:S(2)}) async-start(s8[6291456]{0:T(1024)(128)(4,1)} %bitcast.105), calls=%async_computation.3 | async-start | bytes 4194304
  65.3 16.0 %copy-start.4 = (bf16[2,1024,128]{2,1,0:T(8,128)(2,1)S(1)}, bf16[2,1024,128]{2,1,0:T(8,128)(2,1)}, u32[]{:S(2)}) copy-start(bf16[2,1024,128]{2,1,0:T(8,128)(2,1)} %param.20) | copy-start | bytes 1572868
  66.2 2.9 %collective-permute-start.7 = (bf16[16,640]{1,0:T(8,128)(2,1)S(1)}, bf16[16,640]{1,0:T(8,128)(2,1)S(1)}, u32[]{:S(2)}, u32[]{:S(2)}) collective-permute-start(bf16[16,640]{1,0:T(8,128)(2,1)S(1)} %bitcast.123), channel_id=1, source_target_pairs={{0,1},{1,0},{2,3},{3,2},{4,5},{5,4},{6,7},{7,6},{8,9},{9,8},{10,11... | collective-permute-start | bytes 61448 | tf_op jit(solution)/shard_map/ppermute | solution.py:109
  69.7 4.5 %collective-permute-start.8 = (bf16[32,640]{1,0:T(8,128)(2,1)S(1)}, bf16[32,640]{1,0:T(8,128)(2,1)S(1)}, u32[]{:S(2)}, u32[]{:S(2)}) collective-permute-start(bf16[32,640]{1,0:T(8,128)(2,1)S(1)} %get-tuple-element.50), channel_id=1, source_target_pairs={{0,2},{1,3},{2,4},{3,5},{4,6},{5,7},{6,0},{7,1},{8,10},{9,11},{10,... | collective-permute-start | bytes 122888 | tf_op jit(solution)/shard_map/ppermute | solution.py:109
  69.7 8.1 %collective-permute-start.10 = (bf16[32,640]{1,0:T(8,128)(2,1)S(1)}, bf16[32,640]{1,0:T(8,128)(2,1)S(1)}, u32[]{:S(2)}, u32[]{:S(2)}) collective-permute-start(bf16[32,640]{1,0:T(8,128)(2,1)S(1)} %get-tuple-element.50), channel_id=1, source_target_pairs={{0,6},{1,7},{2,0},{3,1},{4,2},{5,3},{6,4},{7,5},{8,14},{9,15},{10,... | collective-permute-start | bytes 122888 | tf_op jit(solution)/shard_map/ppermute | solution.py:109
  72.4 4.8 %collective-permute-start.9 = (bf16[32,640]{1,0:T(8,128)(2,1)S(1)}, bf16[32,640]{1,0:T(8,128)(2,1)S(1)}, u32[]{:S(2)}, u32[]{:S(2)}) collective-permute-start(bf16[32,640]{1,0:T(8,128)(2,1)S(1)} %get-tuple-element.50), channel_id=1, source_target_pairs={{0,4},{1,5},{2,6},{3,7},{4,0},{5,1},{6,2},{7,3},{8,12},{9,13},{10,... | collective-permute-start | bytes 122888 | tf_op jit(solution)/shard_map/ppermute | solution.py:109
  78.4 10.9 %collective-permute-start.12 = (bf16[128,640]{1,0:T(8,128)(2,1)S(1)}, bf16[128,640]{1,0:T(8,128)(2,1)S(1)}, u32[]{:S(2)}, u32[]{:S(2)}) collective-permute-start(bf16[128,640]{1,0:T(8,128)(2,1)S(1)} %get-tuple-element.38), channel_id=1, source_target_pairs={{0,16},{1,17},{2,18},{3,19},{4,20},{5,21},{6,22},{7,23},{8,24},{9,... | collective-permute-start | bytes 491528 | tf_op jit(solution)/shard_map/ppermute | solution.py:109
  80.9 7.8 %collective-permute-start.11 = (bf16[128,640]{1,0:T(8,128)(2,1)S(1)}, bf16[128,640]{1,0:T(8,128)(2,1)S(1)}, u32[]{:S(2)}, u32[]{:S(2)}) collective-permute-start(bf16[128,640]{1,0:T(8,128)(2,1)S(1)} %get-tuple-element.38), channel_id=1, source_target_pairs={{0,8},{1,9},{2,10},{3,11},{4,12},{5,13},{6,14},{7,15},{8,16},{9,17... | collective-permute-start | bytes 491528 | tf_op jit(solution)/shard_map/ppermute | solution.py:109
  82.8 7.2 %collective-permute-start.13 = (bf16[128,640]{1,0:T(8,128)(2,1)S(1)}, bf16[128,640]{1,0:T(8,128)(2,1)S(1)}, u32[]{:S(2)}, u32[]{:S(2)}) collective-permute-start(bf16[128,640]{1,0:T(8,128)(2,1)S(1)} %get-tuple-element.38), channel_id=1, source_target_pairs={{0,24},{1,25},{2,26},{3,27},{4,28},{5,29},{6,30},{7,31},{8,0},{9,1... | collective-permute-start | bytes 491528 | tf_op jit(solution)/shard_map/ppermute | solution.py:109
  89.3 14.1 %slice-start.2 = ((s8[6553600]{0:T(1024)(128)(4,1)}), s8[2359296]{0:T(1024)(128)(4,1)S(1)}, s32[]{:S(2)}) async-start(s8[6553600]{0:T(1024)(128)(4,1)} %bitcast.108), calls=%async_computation.4 | async-start | bytes 4718592
  93.1 3.5 %copy-start.2 = (bf16[1280,2,128]{2,1,0:T(2,128)(2,1)S(1)}, bf16[1280,2,128]{2,1,0:T(2,128)(2,1)}, u32[]{:S(2)}) copy-start(bf16[1280,2,128]{2,1,0:T(2,128)(2,1)} %get-tuple-element.19) | copy-start | bytes 1966084
  93.1 5.1 %copy-start.1 = (bf16[1280,2,128]{2,1,0:T(2,128)(2,1)S(1)}, bf16[1280,2,128]{2,1,0:T(2,128)(2,1)}, u32[]{:S(2)}) copy-start(bf16[1280,2,128]{2,1,0:T(2,128)(2,1)} %get-tuple-element.16) | copy-start | bytes 1966084
  93.2 5.2 %copy-start.13 = (f32[2,128]{1,0:T(2,128)S(1)}, f32[2,128]{1,0:T(2,128)}, u32[]{:S(2)}) copy-start(f32[2,128]{1,0:T(2,128)} %param.16) | copy-start | bytes 3076
  96.6 6.8 %slice-start.3 = ((s8[6553600]{0:T(1024)(128)(4,1)}), s8[4194304]{0:T(1024)(128)(4,1)S(1)}, s32[]{:S(2)}) async-start(s8[6553600]{0:T(1024)(128)(4,1)} %bitcast.108), calls=%async_computation.5 | async-start | bytes 8388608
  107.0 9.1 %copy-start.5 = (f32[256,64]{0,1:T(8,128)S(1)}, f32[256,64]{0,1:T(8,128)}, u32[]{:S(2)}) copy-start(f32[256,64]{0,1:T(8,128)} %get-tuple-element.58) | copy-start | bytes 196612
  107.0 9.1 %copy-start.6 = (f32[256,64]{0,1:T(8,128)S(1)}, f32[256,64]{0,1:T(8,128)}, u32[]{:S(2)}) copy-start(f32[256,64]{0,1:T(8,128)} %get-tuple-element.59) | copy-start | bytes 196612
  114.5 3.9 %copy-start.7 = (bf16[2,256,128]{2,1,0:T(8,128)(2,1)}, bf16[2,256,128]{2,1,0:T(8,128)(2,1)S(1)}, u32[]{:S(2)}) copy-start(bf16[2,256,128]{2,1,0:T(8,128)(2,1)S(1)} %pad_maximum_fusion.2) | copy-start | bytes 393220
  114.5 2.6 %collective-permute-start.15 = (bf16[2,256,128]{2,1,0:T(8,128)(2,1)S(1)}, bf16[2,256,128]{2,1,0:T(8,128)(2,1)S(1)}, u32[]{:S(2)}, u32[]{:S(2)}) collective-permute-start(bf16[2,256,128]{2,1,0:T(8,128)(2,1)S(1)} %pad_maximum_fusion.2), channel_id=1, source_target_pairs={{0,1},{1,0},{2,3},{3,2},{4,5},{5,4},{6,7},{7,6},{8,9},{9,8},{10,11... | collective-permute-start | bytes 393224 | tf_op jit(solution)/shard_map/ppermute | solution.py:14

commit v12 on v11

--- a/solution.py
+++ b/solution.py
@@ -131,14 +131,10 @@
     tiled = jnp.broadcast_to(rows[None], (count,) + rows.shape)
     tiled, after = lax.optimization_barrier((tiled, after))
     blocks = lax.all_to_all(tiled, "kv", 0, 0, tiled=False)
-    query = None
-    keyval = None
-    for source in range(count):
-        part_q = jnp.dot(blocks[source], w_query[source * width:(source + 1) * width], preferred_element_type=jnp.float32)
-        part_kv = jnp.dot(blocks[source], kv_weight[source * width:(source + 1) * width], preferred_element_type=jnp.float32)
-        query = part_q if query is None else query + part_q
-        keyval = part_kv if keyval is None else keyval + part_kv
-    return query + b_query, keyval + kv_bias, after
+    cols = jnp.transpose(blocks, (1, 0, 2)).reshape(rows.shape[0], count * width)
+    query = jnp.dot(cols, w_query, preferred_element_type=jnp.float32) + b_query
+    keyval = jnp.dot(cols, kv_weight, preferred_element_type=jnp.float32) + kv_bias
+    return query, keyval, after
 
 
 def body_inner(dec_tokens, pre_tokens, w_query, w_keyval, b_query, b_keyval, dec_pool, owner_slots, dec_lengths):

time: 129 us -> 123 us (0.953)
  matrix products: 24.3 us -> 16.6 us
  other arithmetic: 10.8 us -> 14.3 us
  waiting for transfers between devices: 19.8 us -> 16.9 us
  local copies, waits for them, and re-layouts: 30.6 us -> 32.4 us
    dot_general x8 -> x2, matrix products: 15.1 us -> 8.04 us  [the longest x1 5.12 us: block_project(): query = jnp.dot(cols, w_query, preferred_element_type=jnp.float32) + b_query]
    ppermute x14, waiting for transfers between devices: 19.8 us -> 16.9 us  [tree_gather(): parts.append(lax.ppermute(buffer, 'tok', pairs))]
    slice x1 -> x0, local copies, waits for them, and re-layouts: 2.85 us -> none  [block_project(): kv_weight[source * width:(source + 1) * width]]
    unnamed x59 -> x68, local copies, waits for them, and re-layouts: 13.7 us -> 16 us
    concatenate x4, local copies, waits for them, and re-layouts: 1.33 us -> 3.64 us  [tree_gather(): buffer = jnp.concatenate(parts, axis=0)]
    gather x1, local copies, waits for them, and re-layouts: 0.59 us -> 1.97 us  [body_inner(): chosen = jnp.take(got, rows, axis=0)]
    select_n x1, other arithmetic: 1.48 us -> 2.83 us  [prefill(): jnp.where(is_lower, jnp.concatenate([pre_cache, other_cache], axis=1), jn...]
  transfers between devices with their start and end apart: 18 -> 18, of which waited for: 7 -> 6; matrix products, arithmetic and copies ran while one was open for 28% -> 37% of each run, Pallas kernels for 0% -> 0%
where the time goes in v12:
time: 123 us; the launch traced here: 122 us
  local copies, waits for them, and re-layouts  32.4 us (26%)
  starting transfers between devices  30.6 us (25%)
  waiting for transfers between devices  16.9 us (14%)
  matrix products  16.6 us (13%)
  other arithmetic  14.3 us (12%)
  Pallas kernels  9.2 us (7%)
  between operations  1.81 us (1%)
    ppermute x14, starting transfers between devices, tree_gather(): parts.append(lax.ppermute(buffer, 'tok', pairs))  18.6 us
    ppermute x14, waiting for transfers between devices, tree_gather(): parts.append(lax.ppermute(buffer, 'tok', pairs))  16.9 us
    unnamed x68, local copies, waits for them, and re-layouts  16 us
    pallas_call x1, Pallas kernels, attend(): pl.pallas_call(attend_kernel, grid=(width // HD,), in_specs=[pl.BlockSpec...  9.2 us
    dot_general x1, matrix products, block_project(): query = jnp.dot(cols, w_query, preferred_element_type=jnp.float32) + b_query  5.12 us
    all_to_all x1, starting transfers between devices, swap_columns(): blocks = lax.all_to_all(tiled, 'kv', 0, 0, tiled=False)  4.96 us
    all_to_all x1, starting transfers between devices, block_project(): blocks = lax.all_to_all(tiled, 'kv', 0, 0, tiled=False)  4.53 us
    dot_general x1, matrix products, body_inner(): jnp.dot(dec_cols, w_query, preferred_element_type=jnp.float32) + b_query  3.82 us
  transfers between devices with their start and end apart: 18, of which 6 were waited for; matrix products, arithmetic and copies ran while one was open for 37% of the time, Pallas kernels for 0%

profile of v12, /device:TPU:1, one launch (start us, length us, event | category | flops | bytes accessed | tf_op | source)
XLA Modules:
  0.0 121.9 jit_solution(17361054650055433672)
XLA Ops:
  0.7 6.4 %copy.128 = bf16[2,12288,128]{2,1,0:T(8,128)(2,1)} copy(bf16[2,12288,128]{2,1,0:T(8,128)(2,1)} %param.17) | data formatting | bytes 12582912
  7.1 0.7 broadcast_in_dim.45
  7.8 5.0 %all-to-all-start = ((bf16[4,16,1280]{2,1,0:T(8,128)(2,1)}), bf16[4,16,1280]{2,1,0:T(8,128)(2,1)}, u32[]{:S(2)}, u32[]{:S(2)}) async-start(bf16[4,16,1280]{2,1,0:T(8,128)(2,1)} %broadcast_in_dim.45), calls=%async_computation | async-start | bytes 327680 | tf_op jit(solution)/shard_map/all_to_all | solution.py:124
  12.8 1.0 collective-permute-start.14
  13.8 0.6 dynamic_slice.3
  14.4 1.3 %or_select_fusion.kpos_ref = s32[1,2560]{1,0:T(1,128)} fusion(s32[]{:T(128)} %bitcast.16), kind=kLoop, calls=%fused_computation.94 | loop fusion | flops 20480 | bytes 10244 | tf_op jit(solution)/shard_map/jit(_where)/select_n | solution.py:205
  16.8 0.6 compare_and_fusion
  17.5 0.7 copy.52
  18.2 0.7 copy.51
  19.1 0.6 compare_select_fusion.1
  19.7 1.3 %copy.49 = bf16[256,1280]{0,1:T(8,128)(2,1)S(1)} copy(bf16[256,1280]{1,0:T(8,128)(2,1)} %param.12) | data formatting | bytes 1310720 | tf_op args[1]
  21.0 0.9 multiply_cosine_fusion.1
  22.2 0.7 multiply_cosine_fusion.3
  22.9 0.9 copy.71
  23.9 1.6 %broadcast_in_dim.44 = bf16[4,256,1280]{1,2,0:T(8,128)(2,1)} broadcast(bf16[256,1280]{0,1:T(8,128)(2,1)S(1)} %copy.49), dimensions={1,2} | broadcast | bytes 3276800 | tf_op jit(solution)/shard_map/broadcast_in_dim | solution.py:131
  26.0 3.8 %fusion.15 = bf16[16,640]{1,0:T(8,128)(2,1)S(1)} fusion(bf16[16,5120]{1,0:T(8,128)(2,1)S(1)} %bitcast.91, bf16[5120,640]{1,0:T(8,128)(2,1)} %param.13, f32[640]{0:T(1024)S(1)} %copy-done.5), kind=kOutput, calls=%fused_computation.23 | convolution fusion | flops 104878080 | bytes 6740480 | tf_op jit(solution)/shard_map/dot_general | solution.py:148
  30.0 0.6 constant_dynamic-update-slice_fusion.4
  31.2 2.7 %collective-permute-start.3 = (bf16[32,1024]{1,0:T(8,128)(2,1)S(1)}, bf16[32,1024]{1,0:T(8,128)(2,1)S(1)}, u32[]{:S(2)}, u32[]{:S(2)}) collective-permute-start(bf16[32,1024]{1,0:T(8,128)(2,1)S(1)} %pad_maximum_fusion.3), channel_id=1, source_target_pairs={{0,6},{1,7},{2,0},{3,1},{4,2},{5,3},{6,4},{7,5},{8,14},{9,15},{10,... | collective-permute-start | bytes 196616 | tf_op jit(solution)/shard_map/ppermute | solution.py:109
  34.3 0.7 collective-permute-start.1
  35.0 0.6 constant_dynamic-update-slice_fusion.3
  35.6 5.0 %collective-permute-done.1 = bf16[32,1024]{1,0:T(8,128)(2,1)S(1)} collective-permute-done((bf16[32,1024]{1,0:T(8,128)(2,1)S(1)}, bf16[32,1024]{1,0:T(8,128)(2,1)S(1)}, u32[]{:S(2)}, u32[]{:S(2)}) %collective-permute-start.1) | collective-permute-done | bytes 65568 | tf_op jit(solution)/shard_map/ppermute | solution.py:109
  40.6 0.7 constant_dynamic-update-slice_fusion.2
  41.2 0.7 constant_dynamic-update-slice_fusion.1
  41.9 0.7 constant_dynamic-update-slice_fusion
  42.6 1.6 %collective-permute-start.4 = (bf16[128,1024]{1,0:T(8,128)(2,1)}, bf16[128,1024]{1,0:T(8,128)(2,1)S(1)}, u32[]{:S(2)}, u32[]{:S(2)}) collective-permute-start(bf16[128,1024]{1,0:T(8,128)(2,1)} %get-tuple-element.28), channel_id=1, source_target_pairs={{0,8},{1,9},{2,10},{3,11},{4,12},{5,13},{6,14},{7,15},{8,16},{9,17... | collective-permute-start | bytes 786440 | tf_op jit(solution)/shard_map/ppermute | solution.py:109
  44.2 0.7 iota_add_fusion.qpos_ref
  44.9 3.3 %collective-permute-start.5 = (bf16[128,1024]{1,0:T(8,128)(2,1)}, bf16[128,1024]{1,0:T(8,128)(2,1)S(1)}, u32[]{:S(2)}, u32[]{:S(2)}) collective-permute-start(bf16[128,1024]{1,0:T(8,128)(2,1)} %get-tuple-element.28), channel_id=1, source_target_pairs={{0,16},{1,17},{2,18},{3,19},{4,20},{5,21},{6,22},{7,23},{8,24},{9,... | collective-permute-start | bytes 786440 | tf_op jit(solution)/shard_map/ppermute | solution.py:109
  48.2 0.8 collective-permute-start.6
  49.0 4.5 %all-to-all-start.1 = ((bf16[4,256,1280]{1,2,0:T(8,128)(2,1)}), bf16[4,256,1280]{1,2,0:T(8,128)(2,1)S(1)}, u32[]{:S(2)}, u32[]{:S(2)}) async-start(bf16[4,256,1280]{1,2,0:T(8,128)(2,1)} %broadcast_in_dim.44), calls=%async_computation.1 | async-start | bytes 5242880 | tf_op jit(solution)/shard_map/all_to_all | solution.py:133
  53.6 0.7 constant_dynamic-update-slice_fusion.7
  54.3 4.7 %collective-permute-done.5 = bf16[128,1024]{1,0:T(8,128)(2,1)S(1)} collective-permute-done((bf16[128,1024]{1,0:T(8,128)(2,1)}, bf16[128,1024]{1,0:T(8,128)(2,1)S(1)}, u32[]{:S(2)}, u32[]{:S(2)}) %collective-permute-start.5) | collective-permute-done | bytes 262176 | tf_op jit(solution)/shard_map/ppermute | solution.py:109
  59.0 0.7 constant_dynamic-update-slice_fusion.6
  59.7 1.7 %constant_dynamic-update-slice_fusion.5 = bf16[512,1024]{1,0:T(8,128)(2,1)} fusion(bf16[512,1024]{1,0:T(8,128)(2,1)} %constant_dynamic-update-slice_fusion.6, bf16[128,1024]{1,0:T(8,128)(2,1)} %collective-permute-done.6), kind=kLoop, calls=%fused_computation.68 | loop fusion | bytes 524288 | tf_op jit(solution)/shard_map/concatenate | solution.py:110
  61.4 0.9 slice_convert_fusion
  62.3 2.0 %gather_fusion = bf16[16,1024]{1,0:T(8,128)(2,1)S(1)} fusion(bf16[512,1024]{1,0:T(8,128)(2,1)} %constant_dynamic-update-slice_fusion.5, s32[1024]{0:T(1024)S(1)} %pad_clamp_fusion.1), kind=kCustom, calls=%fused_computation | custom fusion | bytes 65600 | tf_op jit(solution)/shard_map/jit(_take)/gather | solution.py:157
  65.0 2.3 %scatter_fusion = bf16[2,12288,128]{2,1,0:T(8,128)(2,1)} fusion(bf16[2,12288,128]{2,1,0:T(8,128)(2,1)} %copy.128, s32[16]{0:T(128)S(1)} %copy-done.14, bf16[16,2,128]{2,0,1:T(8,128)(2,1)S(1)} %maximum_bitcast_fusion), kind=kCustom, calls=%fused_computation.2 | custom fusion | bytes 24640 | tf_op jit(solution)/shard_map/scatter | solution.py:90
  67.4 3.4 %fusion.74 = (f32[16,5]{0,1:T(8,128)S(1)}, f32[16,5,12288]{2,0,1:T(8,128)S(1)}) fusion(bf16[2,12288,128]{2,1,0:T(8,128)(2,1)} %scatter_fusion, bf16[16,5,64]{2,0,1:T(8,128)(2,1)S(1)} %get-tuple-element.25, bf16[16,5,64]{2,0,1:T(8,128)(2,1)S(1)} %get-tuple-element.24, pred[16,12288]{1,0:T(8,128)(4,1)S(1)} %fusion.31), kind=kOutput, calls=%fused_computation.170 | convolution fusion | flops 254648240 | bytes 7295296 | tf_op jit(solution)/shard_map/ngd,md->ngm/dot_general | solution.py:66
  70.8 0.8 fusion.1
  71.6 0.9 fusion.28
  72.5 1.7 %collective-permute-start.7 = (bf16[16,640]{1,0:T(8,128)(2,1)S(1)}, bf16[16,640]{1,0:T(8,128)(2,1)S(1)}, u32[]{:S(2)}, u32[]{:S(2)}) collective-permute-start(bf16[16,640]{1,0:T(8,128)(2,1)S(1)} %bitcast.97), channel_id=1, source_target_pairs={{0,1},{1,0},{2,3},{3,2},{4,5},{5,4},{6,7},{7,6},{8,9},{9,8},{10,11... | collective-permute-start | bytes 61448 | tf_op jit(solution)/shard_map/ppermute | solution.py:109
  74.2 0.7 iota_reduce_fusion
  74.9 0.6 constant_dynamic-update-slice_fusion.19
  75.5 0.6 constant_dynamic-update-slice_fusion.18
  76.1 2.7 %collective-permute-start.10 = (bf16[32,640]{1,0:T(8,128)(2,1)S(1)}, bf16[32,640]{1,0:T(8,128)(2,1)S(1)}, u32[]{:S(2)}, u32[]{:S(2)}) collective-permute-start(bf16[32,640]{1,0:T(8,128)(2,1)S(1)} %get-tuple-element.46), channel_id=1, source_target_pairs={{0,6},{1,7},{2,0},{3,1},{4,2},{5,3},{6,4},{7,5},{8,14},{9,15},{10,... | collective-permute-start | bytes 122888 | tf_op jit(solution)/shard_map/ppermute | solution.py:109
  78.8 1.7 %collective-permute-done.8 = bf16[32,640]{1,0:T(8,128)(2,1)S(1)} collective-permute-done((bf16[32,640]{1,0:T(8,128)(2,1)S(1)}, bf16[32,640]{1,0:T(8,128)(2,1)S(1)}, u32[]{:S(2)}, u32[]{:S(2)}) %collective-permute-start.8) | collective-permute-done | bytes 40992 | tf_op jit(solution)/shard_map/ppermute | solution.py:109
  80.4 0.6 constant_dynamic-update-slice_fusion.17
  81.1 2.4 %collective-permute-done.9 = bf16[32,640]{1,0:T(8,128)(2,1)S(1)} collective-permute-done((bf16[32,640]{1,0:T(8,128)(2,1)S(1)}, bf16[32,640]{1,0:T(8,128)(2,1)S(1)}, u32[]{:S(2)}, u32[]{:S(2)}) %collective-permute-start.9) | collective-permute-done | bytes 40992 | tf_op jit(solution)/shard_map/ppermute | solution.py:109
  83.4 0.6 constant_dynamic-update-slice_fusion.16
  84.0 0.6 constant_dynamic-update-slice_fusion.15
  84.7 2.0 %collective-permute-start.12 = (bf16[128,640]{1,0:T(8,128)(2,1)S(1)}, bf16[128,640]{1,0:T(8,128)(2,1)S(1)}, u32[]{:S(2)}, u32[]{:S(2)}) collective-permute-start(bf16[128,640]{1,0:T(8,128)(2,1)S(1)} %get-tuple-element.34), channel_id=1, source_target_pairs={{0,16},{1,17},{2,18},{3,19},{4,20},{5,21},{6,22},{7,23},{8,24},{9,... | collective-permute-start | bytes 491528 | tf_op jit(solution)/shard_map/ppermute | solution.py:109
  87.1 2.8 %maximum_select_fusion = bf16[2,2048,128]{2,1,0:T(8,128)(2,1)} fusion(bf16[2,1024,128]{2,1,0:T(8,128)(2,1)} %collective-permute-done.14, bf16[2,1024,128]{2,1,0:T(8,128)(2,1)} %param.20, pred[]{:T(512)S(6)} %eq.32), kind=kLoop, calls=%fused_computation.29 | loop fusion | flops 4718592 | bytes 2097153 | tf_op jit(solution)/shard_map/jit(_where)/select_n | solution.py:191
  89.9 2.3 %collective-permute-start.13 = (bf16[128,640]{1,0:T(8,128)(2,1)S(1)}, bf16[128,640]{1,0:T(8,128)(2,1)S(1)}, u32[]{:S(2)}, u32[]{:S(2)}) collective-permute-start(bf16[128,640]{1,0:T(8,128)(2,1)S(1)} %get-tuple-element.34), channel_id=1, source_target_pairs={{0,24},{1,25},{2,26},{3,27},{4,28},{5,29},{6,30},{7,31},{8,0},{9,1... | collective-permute-start | bytes 491528 | tf_op jit(solution)/shard_map/ppermute | solution.py:109
  92.1 2.6 %collective-permute-done.11 = bf16[128,640]{1,0:T(8,128)(2,1)S(1)} collective-permute-done((bf16[128,640]{1,0:T(8,128)(2,1)S(1)}, bf16[128,640]{1,0:T(8,128)(2,1)S(1)}, u32[]{:S(2)}, u32[]{:S(2)}) %collective-permute-start.11) | collective-permute-done | bytes 163872 | tf_op jit(solution)/shard_map/ppermute | solution.py:109
  94.8 0.7 constant_dynamic-update-slice_fusion.22
  95.4 0.7 constant_dynamic-update-slice_fusion.21
  96.1 0.7 constant_dynamic-update-slice_fusion.20
  96.8 1.8 %gather_fusion.1 = bf16[16,640]{1,0:T(8,128)(2,1)S(1)} fusion(bf16[512,640]{1,0:T(8,128)(2,1)} %constant_dynamic-update-slice_fusion.20, s32[1024]{0:T(1024)S(1)} %pad_clamp_fusion), kind=kCustom, calls=%fused_computation.1 | custom fusion | bytes 41024 | tf_op jit(solution)/shard_map/jit(_take)/gather | solution.py:166
  98.6 0.7 broadcast_select_fusion.1
  99.3 2.9 %fusion.12 = f32[256,256]{0,1:T(8,128)S(1)} fusion(bf16[256,5120]{0,1:T(8,128)(2,1)S(1)} %bitcast.85, bf16[640,8,2,128]{3,2,1,0:T(2,128)(2,1)} %bitcast.87, f32[256]{0:T(256)S(1)} %bitcast.100), kind=kOutput, calls=%fused_computation.21 | convolution fusion | flops 671154176 | bytes 5506048 | tf_op jit(solution)/shard_map/dot_general | solution.py:136
  102.3 5.1 %convolution_add_fusion = f32[256,640]{1,0:T(8,128)S(1)} fusion(bf16[256,5120]{0,1:T(8,128)(2,1)S(1)} %bitcast.86, bf16[5120,640]{1,0:T(8,128)(2,1)} %param.13, f32[640]{0:T(1024)S(1)} %copy-done.6), kind=kOutput, calls=%fused_computation.20 | convolution fusion | flops 1677885440 | bytes 9832960 | tf_op jit(solution)/shard_map/dot_general | solution.py:135
  108.7 1.6 %collective-permute-start.15 = (bf16[2,256,128]{2,1,0:T(8,128)(2,1)S(1)}, bf16[2,256,128]{2,1,0:T(8,128)(2,1)S(1)}, u32[]{:S(2)}, u32[]{:S(2)}) collective-permute-start(bf16[2,256,128]{2,1,0:T(8,128)(2,1)S(1)} %pad_maximum_fusion.2), channel_id=1, source_target_pairs={{0,1},{1,0},{2,3},{3,2},{4,5},{5,4},{6,7},{7,6},{8,9},{9,8},{10,11... | collective-permute-start | bytes 393224 | tf_op jit(solution)/shard_map/ppermute | solution.py:14
  110.4 0.9 copy.63.q_ref
  111.5 1.2 fusion.34
  112.7 9.2 %shard_map.138 = bf16[256,640]{1,0:T(8,128)(2,1)} custom-call(bf16[256,640]{1,0:T(8,128)(2,1)} %copy.63.q_ref, bf16[2560,128]{1,0:T(8,128)(2,1)} %get-tuple-element.17.k_ref, bf16[2560,128]{1,0:T(8,128)(2,1)} %get-tuple-element.16.v_ref, s32[256,1]{1,0:T(8,128)} %iota_add_fusion.qpos_ref, s32[1,2560]{1,0:T(1,128)} %or_select_fusion.kpos_ref), custom_call_target="tpu_custom_call" | custom-call | tf_op jit(solution)/shard_map/pallas_call | solution.py:47
  (111 shorter events, 5.2 us)
Async XLA Ops:
  0.6 6.5 %copy-start.4 = (bf16[16,1280]{1,0:T(8,128)(2,1)S(1)}, bf16[16,1280]{1,0:T(8,128)(2,1)}, u32[]{:S(2)}) copy-start(bf16[16,1280]{1,0:T(8,128)(2,1)} %param.11) | copy-start | bytes 122884
  0.6 13.1 %copy-start.22 = (s32[16]{0:T(128)S(1)}, s32[16]{0:T(128)}, u32[]{:S(2)}) copy-start(s32[16]{0:T(128)} %param.21) | copy-start | bytes 196
  0.7 15.6 %copy-start.20 = (s32[16]{0:T(128)S(1)}, s32[16]{0:T(128)}, u32[]{:S(2)}) copy-start(s32[16]{0:T(128)} %param.19) | copy-start | bytes 196
  0.7 16.2 %copy-start.21 = (s32[16]{0:T(128)S(1)}, s32[16]{0:T(128)}, u32[]{:S(2)}) copy-start(s32[16]{0:T(128)} %param.18) | copy-start | bytes 196
  7.1 18.4 %copy-start.1 = (bf16[5120,2,128]{2,1,0:T(2,128)(2,1)S(1)}, bf16[5120,2,128]{2,1,0:T(2,128)(2,1)}, u32[]{:S(2)}) copy-start(bf16[5120,2,128]{2,1,0:T(2,128)(2,1)} %param.14) | copy-start | bytes 7864324
  7.8 15.1 %all-to-all-start = ((bf16[4,16,1280]{2,1,0:T(8,128)(2,1)}), bf16[4,16,1280]{2,1,0:T(8,128)(2,1)}, u32[]{:S(2)}, u32[]{:S(2)}) async-start(bf16[4,16,1280]{2,1,0:T(8,128)(2,1)} %broadcast_in_dim.45), calls=%async_computation | async-start | bytes 327680 | tf_op jit(solution)/shard_map/all_to_all | solution.py:124
  12.8 74.3 %collective-permute-start.14 = (bf16[2,1024,128]{2,1,0:T(8,128)(2,1)}, bf16[2,1024,128]{2,1,0:T(8,128)(2,1)}, u32[]{:S(2)}, u32[]{:S(2)}) collective-permute-start(bf16[2,1024,128]{2,1,0:T(8,128)(2,1)} %param.20), channel_id=1, source_target_pairs={{0,1},{1,0},{2,3},{3,2},{4,5},{5,4},{6,7},{7,6},{8,9},{9,8},{10,11... | collective-permute-start | bytes 1572872 | tf_op jit(solution)/shard_map/ppermute | solution.py:14
  13.7 8.2 %copy-start.9 = (f32[64]{0:T(128)}, f32[64]{0:T(128)S(1)}, u32[]{:S(2)}) copy-start(f32[64]{0:T(128)S(1)} %negate_power_fusion) | copy-start | bytes 772
  16.3 5.6 %copy-start.12 = (f32[256]{0:T(256)}, f32[256]{0:T(256)S(1)}, u32[]{:S(2)}) copy-start(f32[256]{0:T(256)S(1)} %add_convert_fusion.2) | copy-start | bytes 3076
  22.9 2.6 %copy-start.18 = (f32[2,128]{1,0:T(2,128)S(1)}, f32[2,128]{1,0:T(2,128)}, u32[]{:S(2)}) copy-start(f32[2,128]{1,0:T(2,128)} %param.16) | copy-start | bytes 3076
  22.9 3.1 %copy-start.5 = (f32[640]{0:T(1024)S(1)}, f32[640]{0:T(1024)}, u32[]{:S(2)}) copy-start(f32[640]{0:T(1024)} %param.15) | copy-start | bytes 7684
  26.0 3.9 %copy-start.7 = (bf16[16,1]{1,0:T(8,128)(2,1)S(1)}, bf16[16,1]{1,0:T(8,128)(2,1)}, u32[]{:S(2)}) copy-start(bf16[16,1]{1,0:T(8,128)(2,1)} %copy.52) | copy-start | bytes 100
  26.0 3.9 %copy-start.8 = (bf16[16,1]{1,0:T(8,128)(2,1)S(1)}, bf16[16,1]{1,0:T(8,128)(2,1)}, u32[]{:S(2)}) copy-start(bf16[16,1]{1,0:T(8,128)(2,1)} %copy.51) | copy-start | bytes 100
  26.0 22.2 %copy-start.17 = (s32[16]{0:T(128)S(1)}, s32[16]{0:T(128)}, u32[]{:S(2)}) copy-start(s32[16]{0:T(128)} %get-tuple-element.11) | copy-start | bytes 196
  30.0 1.2 %collective-permute-start = (bf16[16,1024]{1,0:T(8,128)(2,1)S(1)}, bf16[16,1024]{1,0:T(8,128)(2,1)S(1)}, u32[]{:S(2)}, u32[]{:S(2)}) collective-permute-start(bf16[16,1024]{1,0:T(8,128)(2,1)S(1)} %concatenate.83), channel_id=1, source_target_pairs={{0,1},{1,0},{2,3},{3,2},{4,5},{5,4},{6,7},{7,6},{8,9},{9,8},{10,11... | collective-permute-start | bytes 98312 | tf_op jit(solution)/shard_map/ppermute | solution.py:109
  31.2 10.7 %collective-permute-start.3 = (bf16[32,1024]{1,0:T(8,128)(2,1)S(1)}, bf16[32,1024]{1,0:T(8,128)(2,1)S(1)}, u32[]{:S(2)}, u32[]{:S(2)}) collective-permute-start(bf16[32,1024]{1,0:T(8,128)(2,1)S(1)} %pad_maximum_fusion.3), channel_id=1, source_target_pairs={{0,6},{1,7},{2,0},{3,1},{4,2},{5,3},{6,4},{7,5},{8,14},{9,15},{10,... | collective-permute-start | bytes 196616 | tf_op jit(solution)/shard_map/ppermute | solution.py:109
  33.9 7.3 %collective-permute-start.2 = (bf16[32,1024]{1,0:T(8,128)(2,1)S(1)}, bf16[32,1024]{1,0:T(8,128)(2,1)S(1)}, u32[]{:S(2)}, u32[]{:S(2)}) collective-permute-start(bf16[32,1024]{1,0:T(8,128)(2,1)S(1)} %pad_maximum_fusion.3), channel_id=1, source_target_pairs={{0,4},{1,5},{2,6},{3,7},{4,0},{5,1},{6,2},{7,3},{8,12},{9,13},{10,... | collective-permute-start | bytes 196616 | tf_op jit(solution)/shard_map/ppermute | solution.py:109
  34.3 6.3 %collective-permute-start.1 = (bf16[32,1024]{1,0:T(8,128)(2,1)S(1)}, bf16[32,1024]{1,0:T(8,128)(2,1)S(1)}, u32[]{:S(2)}, u32[]{:S(2)}) collective-permute-start(bf16[32,1024]{1,0:T(8,128)(2,1)S(1)} %pad_maximum_fusion.3), channel_id=1, source_target_pairs={{0,2},{1,3},{2,4},{3,5},{4,6},{5,7},{6,0},{7,1},{8,10},{9,11},{10,... | collective-permute-start | bytes 196616 | tf_op jit(solution)/shard_map/ppermute | solution.py:109
  42.6 11.0 %collective-permute-start.4 = (bf16[128,1024]{1,0:T(8,128)(2,1)}, bf16[128,1024]{1,0:T(8,128)(2,1)S(1)}, u32[]{:S(2)}, u32[]{:S(2)}) collective-permute-start(bf16[128,1024]{1,0:T(8,128)(2,1)} %get-tuple-element.28), channel_id=1, source_target_pairs={{0,8},{1,9},{2,10},{3,11},{4,12},{5,13},{6,14},{7,15},{8,16},{9,17... | collective-permute-start | bytes 786440 | tf_op jit(solution)/shard_map/ppermute | solution.py:109
  44.9 14.1 %collective-permute-start.5 = (bf16[128,1024]{1,0:T(8,128)(2,1)}, bf16[128,1024]{1,0:T(8,128)(2,1)S(1)}, u32[]{:S(2)}, u32[]{:S(2)}) collective-permute-start(bf16[128,1024]{1,0:T(8,128)(2,1)} %get-tuple-element.28), channel_id=1, source_target_pairs={{0,16},{1,17},{2,18},{3,19},{4,20},{5,21},{6,22},{7,23},{8,24},{9,... | collective-permute-start | bytes 786440 | tf_op jit(solution)/shard_map/ppermute | solution.py:109
  48.2 11.5 %collective-permute-start.6 = (bf16[128,1024]{1,0:T(8,128)(2,1)}, bf16[128,1024]{1,0:T(8,128)(2,1)}, u32[]{:S(2)}, u32[]{:S(2)}) collective-permute-start(bf16[128,1024]{1,0:T(8,128)(2,1)} %get-tuple-element.28), channel_id=1, source_target_pairs={{0,24},{1,25},{2,26},{3,27},{4,28},{5,29},{6,30},{7,31},{8,0},{9,1... | collective-permute-start | bytes 786440 | tf_op jit(solution)/shard_map/ppermute | solution.py:109
  49.0 15.3 %copy-start.15 = (pred[16]{0:T(512)(128)(4,1)S(1)}, pred[16]{0:T(512)(128)(4,1)}, u32[]{:S(2)}) copy-start(pred[16]{0:T(512)(128)(4,1)} %get-tuple-element.10) | copy-start | bytes 52
  49.0 15.7 %copy-start.10 = (f32[64]{0:T(128)S(1)}, f32[64]{0:T(128)}, u32[]{:S(2)}) copy-start(f32[64]{0:T(128)} %copy-done.9) | copy-start | bytes 772
  49.0 15.7 %copy-start.16 = (f32[16]{0:T(128)S(1)}, f32[16]{0:T(128)}, u32[]{:S(2)}) copy-start(f32[16]{0:T(128)} %get-tuple-element.59) | copy-start | bytes 196
  49.0 16.0 %copy-start.14 = (s32[16]{0:T(128)S(1)}, s32[16]{0:T(128)}, u32[]{:S(2)}) copy-start(s32[16]{0:T(128)} %get-tuple-element.14) | copy-start | bytes 196
  49.0 50.3 %all-to-all-start.1 = ((bf16[4,256,1280]{1,2,0:T(8,128)(2,1)}), bf16[4,256,1280]{1,2,0:T(8,128)(2,1)S(1)}, u32[]{:S(2)}, u32[]{:S(2)}) async-start(bf16[4,256,1280]{1,2,0:T(8,128)(2,1)} %broadcast_in_dim.44), calls=%async_computation.1 | async-start | bytes 5242880 | tf_op jit(solution)/shard_map/all_to_all | solution.py:133
  67.3 4.2 %slice-start = ((s8[6291456]{0:T(1024)(128)(4,1)}), s8[4194304]{0:T(1024)(128)(4,1)S(1)}, s32[]{:S(2)}) async-start(s8[6291456]{0:T(1024)(128)(4,1)} %bitcast.83), calls=%async_computation.2 | async-start | bytes 8388608
  67.4 4.2 %slice-start.1 = ((s8[6291456]{0:T(1024)(128)(4,1)}), s8[2097152]{0:T(1024)(128)(4,1)S(1)}, s32[]{:S(2)}) async-start(s8[6291456]{0:T(1024)(128)(4,1)} %bitcast.83), calls=%async_computation.3 | async-start | bytes 4194304
  72.4 26.9 %copy-start.19 = (f32[2,128]{1,0:T(2,128)S(1)}, f32[2,128]{1,0:T(2,128)}, u32[]{:S(2)}) copy-start(f32[2,128]{1,0:T(2,128)} %param.16) | copy-start | bytes 3076
  72.5 3.0 %collective-permute-start.7 = (bf16[16,640]{1,0:T(8,128)(2,1)S(1)}, bf16[16,640]{1,0:T(8,128)(2,1)S(1)}, u32[]{:S(2)}, u32[]{:S(2)}) collective-permute-start(bf16[16,640]{1,0:T(8,128)(2,1)S(1)} %bitcast.97), channel_id=1, source_target_pairs={{0,1},{1,0},{2,3},{3,2},{4,5},{5,4},{6,7},{7,6},{8,9},{9,8},{10,11... | collective-permute-start | bytes 61448 | tf_op jit(solution)/shard_map/ppermute | solution.py:109
  76.1 4.4 %collective-permute-start.8 = (bf16[32,640]{1,0:T(8,128)(2,1)S(1)}, bf16[32,640]{1,0:T(8,128)(2,1)S(1)}, u32[]{:S(2)}, u32[]{:S(2)}) collective-permute-start(bf16[32,640]{1,0:T(8,128)(2,1)S(1)} %get-tuple-element.46), channel_id=1, source_target_pairs={{0,2},{1,3},{2,4},{3,5},{4,6},{5,7},{6,0},{7,1},{8,10},{9,11},{10,... | collective-permute-start | bytes 122888 | tf_op jit(solution)/shard_map/ppermute | solution.py:109
  76.1 7.9 %collective-permute-start.10 = (bf16[32,640]{1,0:T(8,128)(2,1)S(1)}, bf16[32,640]{1,0:T(8,128)(2,1)S(1)}, u32[]{:S(2)}, u32[]{:S(2)}) collective-permute-start(bf16[32,640]{1,0:T(8,128)(2,1)S(1)} %get-tuple-element.46), channel_id=1, source_target_pairs={{0,6},{1,7},{2,0},{3,1},{4,2},{5,3},{6,4},{7,5},{8,14},{9,15},{10,... | collective-permute-start | bytes 122888 | tf_op jit(solution)/shard_map/ppermute | solution.py:109
  78.8 4.7 %collective-permute-start.9 = (bf16[32,640]{1,0:T(8,128)(2,1)S(1)}, bf16[32,640]{1,0:T(8,128)(2,1)S(1)}, u32[]{:S(2)}, u32[]{:S(2)}) collective-permute-start(bf16[32,640]{1,0:T(8,128)(2,1)S(1)} %get-tuple-element.46), channel_id=1, source_target_pairs={{0,4},{1,5},{2,6},{3,7},{4,0},{5,1},{6,2},{7,3},{8,12},{9,13},{10,... | collective-permute-start | bytes 122888 | tf_op jit(solution)/shard_map/ppermute | solution.py:109
  84.7 10.8 %collective-permute-start.12 = (bf16[128,640]{1,0:T(8,128)(2,1)S(1)}, bf16[128,640]{1,0:T(8,128)(2,1)S(1)}, u32[]{:S(2)}, u32[]{:S(2)}) collective-permute-start(bf16[128,640]{1,0:T(8,128)(2,1)S(1)} %get-tuple-element.34), channel_id=1, source_target_pairs={{0,16},{1,17},{2,18},{3,19},{4,20},{5,21},{6,22},{7,23},{8,24},{9,... | collective-permute-start | bytes 491528 | tf_op jit(solution)/shard_map/ppermute | solution.py:109
  86.6 8.1 %collective-permute-start.11 = (bf16[128,640]{1,0:T(8,128)(2,1)S(1)}, bf16[128,640]{1,0:T(8,128)(2,1)S(1)}, u32[]{:S(2)}, u32[]{:S(2)}) collective-permute-start(bf16[128,640]{1,0:T(8,128)(2,1)S(1)} %get-tuple-element.34), channel_id=1, source_target_pairs={{0,8},{1,9},{2,10},{3,11},{4,12},{5,13},{6,14},{7,15},{8,16},{9,17... | collective-permute-start | bytes 491528 | tf_op jit(solution)/shard_map/ppermute | solution.py:109
  89.9 6.3 %collective-permute-start.13 = (bf16[128,640]{1,0:T(8,128)(2,1)S(1)}, bf16[128,640]{1,0:T(8,128)(2,1)S(1)}, u32[]{:S(2)}, u32[]{:S(2)}) collective-permute-start(bf16[128,640]{1,0:T(8,128)(2,1)S(1)} %get-tuple-element.34), channel_id=1, source_target_pairs={{0,24},{1,25},{2,26},{3,27},{4,28},{5,29},{6,30},{7,31},{8,0},{9,1... | collective-permute-start | bytes 491528 | tf_op jit(solution)/shard_map/ppermute | solution.py:109
  99.3 2.9 %copy-start.6 = (f32[640]{0:T(1024)S(1)}, f32[640]{0:T(1024)}, u32[]{:S(2)}) copy-start(f32[640]{0:T(1024)} %param.15) | copy-start | bytes 7684
  102.2 5.8 %copy-start.11 = (f32[64]{0:T(128)S(1)}, f32[64]{0:T(128)}, u32[]{:S(2)}) copy-start(f32[64]{0:T(128)} %copy-done.9) | copy-start | bytes 772
  102.2 5.8 %copy-start.13 = (f32[256]{0:T(256)S(1)}, f32[256]{0:T(256)}, u32[]{:S(2)}) copy-start(f32[256]{0:T(256)} %copy-done.12) | copy-start | bytes 3076
  102.3 8.0 %copy-start.2 = (f32[256,64]{0,1:T(8,128)S(1)}, f32[256,64]{0,1:T(8,128)}, u32[]{:S(2)}) copy-start(f32[256,64]{0,1:T(8,128)} %get-tuple-element.55) | copy-start | bytes 196612
  107.4 4.1 %copy-start = (bf16[2,2048,128]{2,1,0:T(8,128)(2,1)S(1)}, bf16[2,2048,128]{2,1,0:T(8,128)(2,1)}, u32[]{:S(2)}) copy-start(bf16[2,2048,128]{2,1,0:T(8,128)(2,1)} %maximum_select_fusion) | copy-start | bytes 3145732
  108.7 13.2 %copy-start.3 = (bf16[2,256,128]{2,1,0:T(8,128)(2,1)}, bf16[2,256,128]{2,1,0:T(8,128)(2,1)S(1)}, u32[]{:S(2)}) copy-start(bf16[2,256,128]{2,1,0:T(8,128)(2,1)S(1)} %pad_maximum_fusion.2) | copy-start | bytes 393220
  108.7 2.7 %collective-permute-start.15 = (bf16[2,256,128]{2,1,0:T(8,128)(2,1)S(1)}, bf16[2,256,128]{2,1,0:T(8,128)(2,1)S(1)}, u32[]{:S(2)}, u32[]{:S(2)}) collective-permute-start(bf16[2,256,128]{2,1,0:T(8,128)(2,1)S(1)} %pad_maximum_fusion.2), channel_id=1, source_target_pairs={{0,1},{1,0},{2,3},{3,2},{4,5},{5,4},{6,7},{7,6},{8,9},{9,8},{10,11... | collective-permute-start | bytes 393224 | tf_op jit(solution)/shard_map/ppermute | solution.py:14

commit v13 on v12

--- a/solution.py
+++ b/solution.py
@@ -28,12 +28,10 @@
     )
 
 
-def attend_kernel(q_ref, k_ref, v_ref, qpos_ref, kpos_ref, o_ref):
+def attend_kernel(q_ref, k_ref, v_ref, bias_ref, o_ref):
     scores = lax.dot_general(
         q_ref[...], k_ref[...], (((1,), (1,)), ((), ())), preferred_element_type=jnp.float32
-    ) * HD ** (-0.5)
-    allowed = kpos_ref[...] <= qpos_ref[...]
-    scores = jnp.where(allowed, scores, -jnp.inf)
+    ) * HD ** (-0.5) + bias_ref[...]
     top = jnp.max(scores, axis=1, keepdims=True)
     powers = jnp.exp(scores - top)
     total = jnp.sum(powers, axis=1, keepdims=True)
@@ -41,7 +39,7 @@
     o_ref[...] = (mixed / total).astype(o_ref.dtype)
 
 
-def attend(queries, keys, values, query_pos, key_pos):
+def attend(queries, keys, values, bias):
     amount, width = queries.shape
     length = keys.shape[0]
     return pl.pallas_call(
@@ -51,12 +49,11 @@
             pl.BlockSpec((amount, HD), lambda h: (0, h)),
             pl.BlockSpec((length, HD), lambda h: (0, 0)),
             pl.BlockSpec((length, HD), lambda h: (0, 0)),
-            pl.BlockSpec((amount, 1), lambda h: (0, 0)),
-            pl.BlockSpec((1, length), lambda h: (0, 0)),
+            pl.BlockSpec((amount, length), lambda h: (0, 0)),
         ],
         out_specs=pl.BlockSpec((amount, HD), lambda h: (0, h)),
         out_shape=jax.ShapeDtypeStruct((amount, width), jnp.bfloat16),
-    )(queries, keys, values, query_pos.reshape(amount, 1), key_pos.reshape(1, length))
+    )(queries, keys, values, bias)
 
 
 def head_scores(queries, key_rows, allowed):
@@ -203,7 +200,8 @@
     key_pos = jnp.where(key_slots < 2 * shard, key_slots, offset + key_slots - 2 * shard)
     usable = (key_slots < offset) | (key_slots >= 2 * shard)
     key_pos = jnp.where(usable, key_pos, jnp.int32(1 << 30))
-    return (turned, key_rows[0], key_rows[1], positions, key_pos), appended
+    bias = jnp.where(key_pos[None, :] <= positions[:, None], jnp.float32(0), -jnp.inf)
+    return (turned, key_rows[0], key_rows[1], bias), appended
 
 
 def body(dec_tokens, pre_tokens, w_query, w_keyval, b_query, b_keyval, dec_pool, owner_slots, dec_lengths, pre_cache, pre_offsets):

time: 123 us -> 122 us (level)
  local copies, waits for them, and re-layouts: 32.4 us -> 30.2 us
    select_n x0 -> x1, other arithmetic: none -> 1.73 us  [prefill(): jnp.where(key_pos[None, :] <= positions[:, None], jnp.float32(0), -jnp.inf)]
    unnamed x68 -> x56, local copies, waits for them, and re-layouts: 16 us -> 14.9 us
  transfers between devices with their start and end apart: 18 -> 18, of which waited for: 6 -> 6; matrix products, arithmetic and copies ran while one was open for 37% -> 36% of each run, Pallas kernels for 0% -> 0%
where the time goes in v13:
time: 122 us; the launch traced here: 121 us
  local copies, waits for them, and re-layouts  30.2 us (25%)
  starting transfers between devices  30.1 us (25%)
  waiting for transfers between devices  18 us (15%)
  matrix products  17.2 us (14%)
  other arithmetic  14 us (11%)
  Pallas kernels  9.69 us (8%)
  between operations  1.73 us (1%)
    ppermute x14, starting transfers between devices, tree_gather(): parts.append(lax.ppermute(buffer, 'tok', pairs))  18.2 us
    ppermute x14, waiting for transfers between devices, tree_gather(): parts.append(lax.ppermute(buffer, 'tok', pairs))  18 us
    unnamed x56, local copies, waits for them, and re-layouts  14.9 us
    pallas_call x1, Pallas kernels, attend(): pl.pallas_call(attend_kernel, grid=(width // HD,), in_specs=[pl.BlockSpec...  9.69 us
    dot_general x1, matrix products, block_project(): query = jnp.dot(cols, w_query, preferred_element_type=jnp.float32) + b_query  5.09 us
    all_to_all x1, starting transfers between devices, swap_columns(): blocks = lax.all_to_all(tiled, 'kv', 0, 0, tiled=False)  4.83 us
    all_to_all x1, starting transfers between devices, block_project(): blocks = lax.all_to_all(tiled, 'kv', 0, 0, tiled=False)  4.65 us
    dot_general x1, matrix products, body_inner(): jnp.dot(dec_cols, w_query, preferred_element_type=jnp.float32) + b_query  3.81 us
  transfers between devices with their start and end apart: 18, of which 6 were waited for; matrix products, arithmetic and copies ran while one was open for 36% of the time, Pallas kernels for 0%

profile of v13, /device:TPU:1, one launch (start us, length us, event | category | flops | bytes accessed | tf_op | source)
XLA Modules:
  0.0 120.9 jit_solution(10718853730275373568)
XLA Ops:
  0.7 6.5 %copy.128 = bf16[2,12288,128]{2,1,0:T(8,128)(2,1)} copy(bf16[2,12288,128]{2,1,0:T(8,128)(2,1)} %param.17) | data formatting | bytes 12582912
  7.2 0.7 broadcast_in_dim.54
  7.9 4.8 %all-to-all-start = ((bf16[4,16,1280]{2,1,0:T(8,128)(2,1)}), bf16[4,16,1280]{2,1,0:T(8,128)(2,1)}, u32[]{:S(2)}, u32[]{:S(2)}) async-start(bf16[4,16,1280]{2,1,0:T(8,128)(2,1)} %broadcast_in_dim.54), calls=%async_computation | async-start | bytes 327680 | tf_op jit(solution)/shard_map/all_to_all | solution.py:121
  12.7 1.0 collective-permute-start.14
  13.7 0.6 dynamic_slice.3
  14.9 0.7 select_select_fusion
  15.6 0.5 fusion.75
  16.1 0.6 compare_and_fusion
  17.2 0.6 compare_select_fusion.1
  18.2 1.7 %compare_select_fusion.bias_ref = f32[256,2560]{1,0:T(8,128)} fusion(s32[2560]{0:T(1024)S(1)} %select_select_fusion, s32[256]{0:T(256)S(1)} %iota_add_fusion), kind=kLoop, calls=%fused_computation.15 | loop fusion | flops 1310720 | bytes 2632704 | tf_op jit(solution)/shard_map/jit(_where)/select_n | solution.py:203
  20.0 0.9 multiply_cosine_fusion.1
  20.9 0.9 copy.71
  21.9 1.7 %broadcast_in_dim.53 = bf16[4,256,1280]{1,2,0:T(8,128)(2,1)} broadcast(bf16[256,1280]{0,1:T(8,128)(2,1)S(1)} %copy.49), dimensions={1,2} | broadcast | bytes 3276800 | tf_op jit(solution)/shard_map/broadcast_in_dim | solution.py:128
  23.6 1.1 fusion.19
  24.7 3.8 %fusion.15 = bf16[16,640]{1,0:T(8,128)(2,1)S(1)} fusion(bf16[16,5120]{1,0:T(8,128)(2,1)S(1)} %bitcast.91, bf16[5120,640]{1,0:T(8,128)(2,1)} %param.13, f32[640]{0:T(1024)S(1)} %copy-done.6), kind=kOutput, calls=%fused_computation.24 | convolution fusion | flops 104878080 | bytes 6740480 | tf_op jit(solution)/shard_map/dot_general | solution.py:145
  28.7 0.6 constant_dynamic-update-slice_fusion.4
  29.3 0.5 collective-permute-done
  29.9 2.7 %collective-permute-start.3 = (bf16[32,1024]{1,0:T(8,128)(2,1)S(1)}, bf16[32,1024]{1,0:T(8,128)(2,1)S(1)}, u32[]{:S(2)}, u32[]{:S(2)}) collective-permute-start(bf16[32,1024]{1,0:T(8,128)(2,1)S(1)} %pad_maximum_fusion.3), channel_id=1, source_target_pairs={{0,6},{1,7},{2,0},{3,1},{4,2},{5,3},{6,4},{7,5},{8,14},{9,15},{10,... | collective-permute-start | bytes 196616 | tf_op jit(solution)/shard_map/ppermute | solution.py:106
  33.0 0.7 collective-permute-start.1
  33.7 0.6 constant_dynamic-update-slice_fusion.3
  34.3 5.0 %collective-permute-done.1 = bf16[32,1024]{1,0:T(8,128)(2,1)S(1)} collective-permute-done((bf16[32,1024]{1,0:T(8,128)(2,1)S(1)}, bf16[32,1024]{1,0:T(8,128)(2,1)S(1)}, u32[]{:S(2)}, u32[]{:S(2)}) %collective-permute-start.1) | collective-permute-done | bytes 65568 | tf_op jit(solution)/shard_map/ppermute | solution.py:106
  39.3 0.7 constant_dynamic-update-slice_fusion.2
  39.9 0.7 constant_dynamic-update-slice_fusion.1
  40.6 0.7 constant_dynamic-update-slice_fusion
  41.3 1.6 %collective-permute-start.4 = (bf16[128,1024]{1,0:T(8,128)(2,1)}, bf16[128,1024]{1,0:T(8,128)(2,1)S(1)}, u32[]{:S(2)}, u32[]{:S(2)}) collective-permute-start(bf16[128,1024]{1,0:T(8,128)(2,1)} %get-tuple-element.28), channel_id=1, source_target_pairs={{0,8},{1,9},{2,10},{3,11},{4,12},{5,13},{6,14},{7,15},{8,16},{9,17... | collective-permute-start | bytes 786440 | tf_op jit(solution)/shard_map/ppermute | solution.py:106
  43.0 3.4 %collective-permute-start.5 = (bf16[128,1024]{1,0:T(8,128)(2,1)}, bf16[128,1024]{1,0:T(8,128)(2,1)S(1)}, u32[]{:S(2)}, u32[]{:S(2)}) collective-permute-start(bf16[128,1024]{1,0:T(8,128)(2,1)} %get-tuple-element.28), channel_id=1, source_target_pairs={{0,16},{1,17},{2,18},{3,19},{4,20},{5,21},{6,22},{7,23},{8,24},{9,... | collective-permute-start | bytes 786440 | tf_op jit(solution)/shard_map/ppermute | solution.py:106
  46.4 0.8 collective-permute-start.6
  47.2 4.6 %all-to-all-start.1 = ((bf16[4,256,1280]{1,2,0:T(8,128)(2,1)}), bf16[4,256,1280]{1,2,0:T(8,128)(2,1)S(1)}, u32[]{:S(2)}, u32[]{:S(2)}) async-start(bf16[4,256,1280]{1,2,0:T(8,128)(2,1)} %broadcast_in_dim.53), calls=%async_computation.1 | async-start | bytes 5242880 | tf_op jit(solution)/shard_map/all_to_all | solution.py:130
  51.9 0.7 constant_dynamic-update-slice_fusion.7
  52.6 5.1 %collective-permute-done.5 = bf16[128,1024]{1,0:T(8,128)(2,1)S(1)} collective-permute-done((bf16[128,1024]{1,0:T(8,128)(2,1)}, bf16[128,1024]{1,0:T(8,128)(2,1)S(1)}, u32[]{:S(2)}, u32[]{:S(2)}) %collective-permute-start.5) | collective-permute-done | bytes 262176 | tf_op jit(solution)/shard_map/ppermute | solution.py:106
  57.7 0.7 constant_dynamic-update-slice_fusion.6
  58.4 1.7 %constant_dynamic-update-slice_fusion.5 = bf16[512,1024]{1,0:T(8,128)(2,1)} fusion(bf16[512,1024]{1,0:T(8,128)(2,1)} %constant_dynamic-update-slice_fusion.6, bf16[128,1024]{1,0:T(8,128)(2,1)} %collective-permute-done.6), kind=kLoop, calls=%fused_computation.68 | loop fusion | bytes 524288 | tf_op jit(solution)/shard_map/concatenate | solution.py:107
  60.1 0.9 slice_convert_fusion
  61.0 2.0 %gather_fusion = bf16[16,1024]{1,0:T(8,128)(2,1)S(1)} fusion(bf16[512,1024]{1,0:T(8,128)(2,1)} %constant_dynamic-update-slice_fusion.5, s32[1024]{0:T(1024)S(1)} %pad_clamp_fusion.1), kind=kCustom, calls=%fused_computation | custom fusion | bytes 65600 | tf_op jit(solution)/shard_map/jit(_take)/gather | solution.py:154
  63.7 2.3 %scatter_fusion = bf16[2,12288,128]{2,1,0:T(8,128)(2,1)} fusion(bf16[2,12288,128]{2,1,0:T(8,128)(2,1)} %copy.128, s32[16]{0:T(128)S(1)} %copy-done.9, bf16[16,2,128]{2,0,1:T(8,128)(2,1)S(1)} %maximum_bitcast_fusion), kind=kCustom, calls=%fused_computation.2 | custom fusion | bytes 24640 | tf_op jit(solution)/shard_map/scatter | solution.py:87
  66.1 3.4 %fusion.76 = (f32[16,5]{0,1:T(8,128)S(1)}, f32[16,5,12288]{2,0,1:T(8,128)S(1)}) fusion(bf16[2,12288,128]{2,1,0:T(8,128)(2,1)} %scatter_fusion, bf16[16,5,64]{2,0,1:T(8,128)(2,1)S(1)} %get-tuple-element.25, bf16[16,5,64]{2,0,1:T(8,128)(2,1)S(1)} %get-tuple-element.24, pred[16,12288]{1,0:T(8,128)(4,1)S(1)} %fusion.31), kind=kOutput, calls=%fused_computation.174 | convolution fusion | flops 254648240 | bytes 7295296 | tf_op jit(solution)/shard_map/ngd,md->ngm/dot_general | solution.py:63
  69.5 0.8 fusion.1
  70.3 0.9 fusion.28
  71.1 1.7 %collective-permute-start.7 = (bf16[16,640]{1,0:T(8,128)(2,1)S(1)}, bf16[16,640]{1,0:T(8,128)(2,1)S(1)}, u32[]{:S(2)}, u32[]{:S(2)}) collective-permute-start(bf16[16,640]{1,0:T(8,128)(2,1)S(1)} %bitcast.97), channel_id=1, source_target_pairs={{0,1},{1,0},{2,3},{3,2},{4,5},{5,4},{6,7},{7,6},{8,9},{9,8},{10,11... | collective-permute-start | bytes 61448 | tf_op jit(solution)/shard_map/ppermute | solution.py:106
  72.8 0.7 iota_reduce_fusion
  73.6 0.6 constant_dynamic-update-slice_fusion.19
  74.2 0.6 constant_dynamic-update-slice_fusion.18
  74.8 2.7 %collective-permute-start.10 = (bf16[32,640]{1,0:T(8,128)(2,1)S(1)}, bf16[32,640]{1,0:T(8,128)(2,1)S(1)}, u32[]{:S(2)}, u32[]{:S(2)}) collective-permute-start(bf16[32,640]{1,0:T(8,128)(2,1)S(1)} %get-tuple-element.46), channel_id=1, source_target_pairs={{0,6},{1,7},{2,0},{3,1},{4,2},{5,3},{6,4},{7,5},{8,14},{9,15},{10,... | collective-permute-start | bytes 122888 | tf_op jit(solution)/shard_map/ppermute | solution.py:106
  77.5 1.7 %collective-permute-done.8 = bf16[32,640]{1,0:T(8,128)(2,1)S(1)} collective-permute-done((bf16[32,640]{1,0:T(8,128)(2,1)S(1)}, bf16[32,640]{1,0:T(8,128)(2,1)S(1)}, u32[]{:S(2)}, u32[]{:S(2)}) %collective-permute-start.8) | collective-permute-done | bytes 40992 | tf_op jit(solution)/shard_map/ppermute | solution.py:106
  79.1 0.6 constant_dynamic-update-slice_fusion.17
  79.7 2.4 %collective-permute-done.9 = bf16[32,640]{1,0:T(8,128)(2,1)S(1)} collective-permute-done((bf16[32,640]{1,0:T(8,128)(2,1)S(1)}, bf16[32,640]{1,0:T(8,128)(2,1)S(1)}, u32[]{:S(2)}, u32[]{:S(2)}) %collective-permute-start.9) | collective-permute-done | bytes 40992 | tf_op jit(solution)/shard_map/ppermute | solution.py:106
  82.1 0.6 constant_dynamic-update-slice_fusion.16
  82.7 0.6 constant_dynamic-update-slice_fusion.15
  83.3 1.6 %collective-permute-start.12 = (bf16[128,640]{1,0:T(8,128)(2,1)S(1)}, bf16[128,640]{1,0:T(8,128)(2,1)S(1)}, u32[]{:S(2)}, u32[]{:S(2)}) collective-permute-start(bf16[128,640]{1,0:T(8,128)(2,1)S(1)} %get-tuple-element.34), channel_id=1, source_target_pairs={{0,16},{1,17},{2,18},{3,19},{4,20},{5,21},{6,22},{7,23},{8,24},{9,... | collective-permute-start | bytes 491528 | tf_op jit(solution)/shard_map/ppermute | solution.py:106
  85.3 2.8 %maximum_select_fusion = bf16[2,2048,128]{2,1,0:T(8,128)(2,1)} fusion(bf16[2,1024,128]{2,1,0:T(8,128)(2,1)} %collective-permute-done.14, bf16[2,1024,128]{2,1,0:T(8,128)(2,1)} %param.20, pred[]{:T(512)S(6)} %eq.32), kind=kLoop, calls=%fused_computation.30 | loop fusion | flops 4718592 | bytes 2097153 | tf_op jit(solution)/shard_map/jit(_where)/select_n | solution.py:188
  88.1 2.3 %collective-permute-start.13 = (bf16[128,640]{1,0:T(8,128)(2,1)S(1)}, bf16[128,640]{1,0:T(8,128)(2,1)S(1)}, u32[]{:S(2)}, u32[]{:S(2)}) collective-permute-start(bf16[128,640]{1,0:T(8,128)(2,1)S(1)} %get-tuple-element.34), channel_id=1, source_target_pairs={{0,24},{1,25},{2,26},{3,27},{4,28},{5,29},{6,30},{7,31},{8,0},{9,1... | collective-permute-start | bytes 491528 | tf_op jit(solution)/shard_map/ppermute | solution.py:106
  90.4 3.3 %collective-permute-done.11 = bf16[128,640]{1,0:T(8,128)(2,1)S(1)} collective-permute-done((bf16[128,640]{1,0:T(8,128)(2,1)S(1)}, bf16[128,640]{1,0:T(8,128)(2,1)S(1)}, u32[]{:S(2)}, u32[]{:S(2)}) %collective-permute-start.11) | collective-permute-done | bytes 163872 | tf_op jit(solution)/shard_map/ppermute | solution.py:106
  93.7 0.7 constant_dynamic-update-slice_fusion.22
  94.4 0.7 constant_dynamic-update-slice_fusion.21
  95.1 0.7 constant_dynamic-update-slice_fusion.20
  95.7 1.8 %gather_fusion.1 = bf16[16,640]{1,0:T(8,128)(2,1)S(1)} fusion(bf16[512,640]{1,0:T(8,128)(2,1)} %constant_dynamic-update-slice_fusion.20, s32[1024]{0:T(1024)S(1)} %pad_clamp_fusion), kind=kCustom, calls=%fused_computation.1 | custom fusion | bytes 41024 | tf_op jit(solution)/shard_map/jit(_take)/gather | solution.py:163
  97.5 0.7 broadcast_select_fusion.1
  98.2 2.9 %fusion.12 = f32[256,256]{0,1:T(8,128)S(1)} fusion(bf16[256,5120]{0,1:T(8,128)(2,1)S(1)} %bitcast.85, bf16[640,8,2,128]{3,2,1,0:T(2,128)(2,1)} %bitcast.87, f32[256]{0:T(256)S(1)} %bitcast.100), kind=kOutput, calls=%fused_computation.22 | convolution fusion | flops 671154176 | bytes 5506048 | tf_op jit(solution)/shard_map/dot_general | solution.py:133
  101.1 5.1 %convolution_add_fusion = f32[256,640]{1,0:T(8,128)S(1)} fusion(bf16[256,5120]{0,1:T(8,128)(2,1)S(1)} %bitcast.86, bf16[5120,640]{1,0:T(8,128)(2,1)} %param.13, f32[640]{0:T(1024)S(1)} %copy-done.6), kind=kOutput, calls=%fused_computation.21 | convolution fusion | flops 1677885440 | bytes 9832960 | tf_op jit(solution)/shard_map/dot_general | solution.py:132
  106.8 0.6 fusion.45
  107.5 1.4 %collective-permute-start.15 = (bf16[2,256,128]{2,1,0:T(8,128)(2,1)S(1)}, bf16[2,256,128]{2,1,0:T(8,128)(2,1)S(1)}, u32[]{:S(2)}, u32[]{:S(2)}) collective-permute-start(bf16[2,256,128]{2,1,0:T(8,128)(2,1)S(1)} %pad_maximum_fusion.2), channel_id=1, source_target_pairs={{0,1},{1,0},{2,3},{3,2},{4,5},{5,4},{6,7},{7,6},{8,9},{9,8},{10,11... | collective-permute-start | bytes 393224 | tf_op jit(solution)/shard_map/ppermute | solution.py:14
  109.0 0.9 copy.63.q_ref
  110.1 1.1 fusion.34
  111.2 9.7 %shard_map.138 = bf16[256,640]{1,0:T(8,128)(2,1)} custom-call(bf16[256,640]{1,0:T(8,128)(2,1)} %copy.63.q_ref, bf16[2560,128]{1,0:T(8,128)(2,1)} %get-tuple-element.17.k_ref, bf16[2560,128]{1,0:T(8,128)(2,1)} %get-tuple-element.16.v_ref, f32[256,2560]{1,0:T(8,128)} %compare_select_fusion.bias_ref), custom_call_target="tpu_custom_call" | custom-call | tf_op jit(solution)/shard_map/pallas_call | solution.py:45
  (100 shorter events, 3.6 us)
Async XLA Ops:
  0.6 6.6 %copy-start.5 = (bf16[16,1280]{1,0:T(8,128)(2,1)S(1)}, bf16[16,1280]{1,0:T(8,128)(2,1)}, u32[]{:S(2)}) copy-start(bf16[16,1280]{1,0:T(8,128)(2,1)} %param.11) | copy-start | bytes 122884
  0.6 13.0 %copy-start.16 = (s32[16]{0:T(128)S(1)}, s32[16]{0:T(128)}, u32[]{:S(2)}) copy-start(s32[16]{0:T(128)} %param.21) | copy-start | bytes 196
  0.7 15.0 %copy-start.14 = (s32[16]{0:T(128)S(1)}, s32[16]{0:T(128)}, u32[]{:S(2)}) copy-start(s32[16]{0:T(128)} %param.19) | copy-start | bytes 196
  0.7 15.5 %copy-start.15 = (s32[16]{0:T(128)S(1)}, s32[16]{0:T(128)}, u32[]{:S(2)}) copy-start(s32[16]{0:T(128)} %param.18) | copy-start | bytes 196
  0.7 17.1 %copy-start.2 = (bf16[256,1280]{1,0:T(8,128)(2,1)S(1)}, bf16[256,1280]{1,0:T(8,128)(2,1)}, u32[]{:S(2)}) copy-start(bf16[256,1280]{1,0:T(8,128)(2,1)} %param.12) | copy-start | bytes 1966084
  7.9 13.1 %all-to-all-start = ((bf16[4,16,1280]{2,1,0:T(8,128)(2,1)}), bf16[4,16,1280]{2,1,0:T(8,128)(2,1)}, u32[]{:S(2)}, u32[]{:S(2)}) async-start(bf16[4,16,1280]{2,1,0:T(8,128)(2,1)} %broadcast_in_dim.54), calls=%async_computation | async-start | bytes 327680 | tf_op jit(solution)/shard_map/all_to_all | solution.py:121
  12.7 72.6 %collective-permute-start.14 = (bf16[2,1024,128]{2,1,0:T(8,128)(2,1)}, bf16[2,1024,128]{2,1,0:T(8,128)(2,1)}, u32[]{:S(2)}, u32[]{:S(2)}) collective-permute-start(bf16[2,1024,128]{2,1,0:T(8,128)(2,1)} %param.20), channel_id=1, source_target_pairs={{0,1},{1,0},{2,3},{3,2},{4,5},{5,4},{6,7},{7,6},{8,9},{9,8},{10,11... | collective-permute-start | bytes 1572872 | tf_op jit(solution)/shard_map/ppermute | solution.py:14
  14.9 6.9 %copy-start.7 = (f32[256]{0:T(256)}, f32[256]{0:T(256)S(1)}, u32[]{:S(2)}) copy-start(f32[256]{0:T(256)S(1)} %fusion.68) | copy-start | bytes 3076
  18.2 5.4 %copy-start.1 = (bf16[5120,2,128]{2,1,0:T(2,128)(2,1)S(1)}, bf16[5120,2,128]{2,1,0:T(2,128)(2,1)}, u32[]{:S(2)}) copy-start(bf16[5120,2,128]{2,1,0:T(2,128)(2,1)} %param.14) | copy-start | bytes 7864324
  21.9 2.9 %copy-start.6 = (f32[640]{0:T(1024)S(1)}, f32[640]{0:T(1024)}, u32[]{:S(2)}) copy-start(f32[640]{0:T(1024)} %param.15) | copy-start | bytes 7684
  24.7 18.2 %copy-start.11 = (f32[16]{0:T(128)S(1)}, f32[16]{0:T(128)}, u32[]{:S(2)}) copy-start(f32[16]{0:T(128)} %get-tuple-element.59) | copy-start | bytes 196
  24.7 21.7 %copy-start.12 = (s32[16]{0:T(128)S(1)}, s32[16]{0:T(128)}, u32[]{:S(2)}) copy-start(s32[16]{0:T(128)} %get-tuple-element.11) | copy-start | bytes 196
  28.7 1.2 %collective-permute-start = (bf16[16,1024]{1,0:T(8,128)(2,1)S(1)}, bf16[16,1024]{1,0:T(8,128)(2,1)S(1)}, u32[]{:S(2)}, u32[]{:S(2)}) collective-permute-start(bf16[16,1024]{1,0:T(8,128)(2,1)S(1)} %concatenate.83), channel_id=1, source_target_pairs={{0,1},{1,0},{2,3},{3,2},{4,5},{5,4},{6,7},{7,6},{8,9},{9,8},{10,11... | collective-permute-start | bytes 98312 | tf_op jit(solution)/shard_map/ppermute | solution.py:106
  29.9 10.7 %collective-permute-start.3 = (bf16[32,1024]{1,0:T(8,128)(2,1)S(1)}, bf16[32,1024]{1,0:T(8,128)(2,1)S(1)}, u32[]{:S(2)}, u32[]{:S(2)}) collective-permute-start(bf16[32,1024]{1,0:T(8,128)(2,1)S(1)} %pad_maximum_fusion.3), channel_id=1, source_target_pairs={{0,6},{1,7},{2,0},{3,1},{4,2},{5,3},{6,4},{7,5},{8,14},{9,15},{10,... | collective-permute-start | bytes 196616 | tf_op jit(solution)/shard_map/ppermute | solution.py:106
  32.6 7.3 %collective-permute-start.2 = (bf16[32,1024]{1,0:T(8,128)(2,1)S(1)}, bf16[32,1024]{1,0:T(8,128)(2,1)S(1)}, u32[]{:S(2)}, u32[]{:S(2)}) collective-permute-start(bf16[32,1024]{1,0:T(8,128)(2,1)S(1)} %pad_maximum_fusion.3), channel_id=1, source_target_pairs={{0,4},{1,5},{2,6},{3,7},{4,0},{5,1},{6,2},{7,3},{8,12},{9,13},{10,... | collective-permute-start | bytes 196616 | tf_op jit(solution)/shard_map/ppermute | solution.py:106
  33.0 6.3 %collective-permute-start.1 = (bf16[32,1024]{1,0:T(8,128)(2,1)S(1)}, bf16[32,1024]{1,0:T(8,128)(2,1)S(1)}, u32[]{:S(2)}, u32[]{:S(2)}) collective-permute-start(bf16[32,1024]{1,0:T(8,128)(2,1)S(1)} %pad_maximum_fusion.3), channel_id=1, source_target_pairs={{0,2},{1,3},{2,4},{3,5},{4,6},{5,7},{6,0},{7,1},{8,10},{9,11},{10,... | collective-permute-start | bytes 196616 | tf_op jit(solution)/shard_map/ppermute | solution.py:106
  41.3 10.6 %collective-permute-start.4 = (bf16[128,1024]{1,0:T(8,128)(2,1)}, bf16[128,1024]{1,0:T(8,128)(2,1)S(1)}, u32[]{:S(2)}, u32[]{:S(2)}) collective-permute-start(bf16[128,1024]{1,0:T(8,128)(2,1)} %get-tuple-element.28), channel_id=1, source_target_pairs={{0,8},{1,9},{2,10},{3,11},{4,12},{5,13},{6,14},{7,15},{8,16},{9,17... | collective-permute-start | bytes 786440 | tf_op jit(solution)/shard_map/ppermute | solution.py:106
  43.0 14.6 %collective-permute-start.5 = (bf16[128,1024]{1,0:T(8,128)(2,1)}, bf16[128,1024]{1,0:T(8,128)(2,1)S(1)}, u32[]{:S(2)}, u32[]{:S(2)}) collective-permute-start(bf16[128,1024]{1,0:T(8,128)(2,1)} %get-tuple-element.28), channel_id=1, source_target_pairs={{0,16},{1,17},{2,18},{3,19},{4,20},{5,21},{6,22},{7,23},{8,24},{9,... | collective-permute-start | bytes 786440 | tf_op jit(solution)/shard_map/ppermute | solution.py:106
  46.4 12.0 %collective-permute-start.6 = (bf16[128,1024]{1,0:T(8,128)(2,1)}, bf16[128,1024]{1,0:T(8,128)(2,1)}, u32[]{:S(2)}, u32[]{:S(2)}) collective-permute-start(bf16[128,1024]{1,0:T(8,128)(2,1)} %get-tuple-element.28), channel_id=1, source_target_pairs={{0,24},{1,25},{2,26},{3,27},{4,28},{5,29},{6,30},{7,31},{8,0},{9,1... | collective-permute-start | bytes 786440 | tf_op jit(solution)/shard_map/ppermute | solution.py:106
  47.2 15.8 %copy-start.10 = (pred[16]{0:T(512)(128)(4,1)S(1)}, pred[16]{0:T(512)(128)(4,1)}, u32[]{:S(2)}) copy-start(pred[16]{0:T(512)(128)(4,1)} %get-tuple-element.10) | copy-start | bytes 52
  47.2 50.9 %all-to-all-start.1 = ((bf16[4,256,1280]{1,2,0:T(8,128)(2,1)}), bf16[4,256,1280]{1,2,0:T(8,128)(2,1)S(1)}, u32[]{:S(2)}, u32[]{:S(2)}) async-start(bf16[4,256,1280]{1,2,0:T(8,128)(2,1)} %broadcast_in_dim.53), calls=%async_computation.1 | async-start | bytes 5242880 | tf_op jit(solution)/shard_map/all_to_all | solution.py:130
  51.9 11.8 %copy-start.9 = (s32[16]{0:T(128)S(1)}, s32[16]{0:T(128)}, u32[]{:S(2)}) copy-start(s32[16]{0:T(128)} %get-tuple-element.14) | copy-start | bytes 196
  66.0 4.2 %slice-start = ((s8[6291456]{0:T(1024)(128)(4,1)}), s8[4194304]{0:T(1024)(128)(4,1)S(1)}, s32[]{:S(2)}) async-start(s8[6291456]{0:T(1024)(128)(4,1)} %bitcast.83), calls=%async_computation.2 | async-start | bytes 8388608
  66.1 4.2 %slice-start.1 = ((s8[6291456]{0:T(1024)(128)(4,1)}), s8[2097152]{0:T(1024)(128)(4,1)S(1)}, s32[]{:S(2)}) async-start(s8[6291456]{0:T(1024)(128)(4,1)} %bitcast.83), calls=%async_computation.3 | async-start | bytes 4194304
  71.1 27.1 %copy-start.13 = (f32[2,128]{1,0:T(2,128)S(1)}, f32[2,128]{1,0:T(2,128)}, u32[]{:S(2)}) copy-start(f32[2,128]{1,0:T(2,128)} %param.16) | copy-start | bytes 3076
  71.1 3.0 %collective-permute-start.7 = (bf16[16,640]{1,0:T(8,128)(2,1)S(1)}, bf16[16,640]{1,0:T(8,128)(2,1)S(1)}, u32[]{:S(2)}, u32[]{:S(2)}) collective-permute-start(bf16[16,640]{1,0:T(8,128)(2,1)S(1)} %bitcast.97), channel_id=1, source_target_pairs={{0,1},{1,0},{2,3},{3,2},{4,5},{5,4},{6,7},{7,6},{8,9},{9,8},{10,11... | collective-permute-start | bytes 61448 | tf_op jit(solution)/shard_map/ppermute | solution.py:106
  74.8 4.4 %collective-permute-start.8 = (bf16[32,640]{1,0:T(8,128)(2,1)S(1)}, bf16[32,640]{1,0:T(8,128)(2,1)S(1)}, u32[]{:S(2)}, u32[]{:S(2)}) collective-permute-start(bf16[32,640]{1,0:T(8,128)(2,1)S(1)} %get-tuple-element.46), channel_id=1, source_target_pairs={{0,2},{1,3},{2,4},{3,5},{4,6},{5,7},{6,0},{7,1},{8,10},{9,11},{10,... | collective-permute-start | bytes 122888 | tf_op jit(solution)/shard_map/ppermute | solution.py:106
  74.8 7.9 %collective-permute-start.10 = (bf16[32,640]{1,0:T(8,128)(2,1)S(1)}, bf16[32,640]{1,0:T(8,128)(2,1)S(1)}, u32[]{:S(2)}, u32[]{:S(2)}) collective-permute-start(bf16[32,640]{1,0:T(8,128)(2,1)S(1)} %get-tuple-element.46), channel_id=1, source_target_pairs={{0,6},{1,7},{2,0},{3,1},{4,2},{5,3},{6,4},{7,5},{8,14},{9,15},{10,... | collective-permute-start | bytes 122888 | tf_op jit(solution)/shard_map/ppermute | solution.py:106
  77.4 4.7 %collective-permute-start.9 = (bf16[32,640]{1,0:T(8,128)(2,1)S(1)}, bf16[32,640]{1,0:T(8,128)(2,1)S(1)}, u32[]{:S(2)}, u32[]{:S(2)}) collective-permute-start(bf16[32,640]{1,0:T(8,128)(2,1)S(1)} %get-tuple-element.46), channel_id=1, source_target_pairs={{0,4},{1,5},{2,6},{3,7},{4,0},{5,1},{6,2},{7,3},{8,12},{9,13},{10,... | collective-permute-start | bytes 122888 | tf_op jit(solution)/shard_map/ppermute | solution.py:106
  83.3 11.0 %collective-permute-start.12 = (bf16[128,640]{1,0:T(8,128)(2,1)S(1)}, bf16[128,640]{1,0:T(8,128)(2,1)S(1)}, u32[]{:S(2)}, u32[]{:S(2)}) collective-permute-start(bf16[128,640]{1,0:T(8,128)(2,1)S(1)} %get-tuple-element.34), channel_id=1, source_target_pairs={{0,16},{1,17},{2,18},{3,19},{4,20},{5,21},{6,22},{7,23},{8,24},{9,... | collective-permute-start | bytes 491528 | tf_op jit(solution)/shard_map/ppermute | solution.py:106
  84.9 8.8 %collective-permute-start.11 = (bf16[128,640]{1,0:T(8,128)(2,1)S(1)}, bf16[128,640]{1,0:T(8,128)(2,1)S(1)}, u32[]{:S(2)}, u32[]{:S(2)}) collective-permute-start(bf16[128,640]{1,0:T(8,128)(2,1)S(1)} %get-tuple-element.34), channel_id=1, source_target_pairs={{0,8},{1,9},{2,10},{3,11},{4,12},{5,13},{6,14},{7,15},{8,16},{9,17... | collective-permute-start | bytes 491528 | tf_op jit(solution)/shard_map/ppermute | solution.py:106
  88.1 7.0 %collective-permute-start.13 = (bf16[128,640]{1,0:T(8,128)(2,1)S(1)}, bf16[128,640]{1,0:T(8,128)(2,1)S(1)}, u32[]{:S(2)}, u32[]{:S(2)}) collective-permute-start(bf16[128,640]{1,0:T(8,128)(2,1)S(1)} %get-tuple-element.34), channel_id=1, source_target_pairs={{0,24},{1,25},{2,26},{3,27},{4,28},{5,29},{6,30},{7,31},{8,0},{9,1... | collective-permute-start | bytes 491528 | tf_op jit(solution)/shard_map/ppermute | solution.py:106
  101.1 5.7 %copy-start.8 = (f32[256]{0:T(256)S(1)}, f32[256]{0:T(256)}, u32[]{:S(2)}) copy-start(f32[256]{0:T(256)} %copy-done.7) | copy-start | bytes 3076
  106.2 2.7 %copy-start.3 = (f32[256,64]{0,1:T(8,128)S(1)}, f32[256,64]{0,1:T(8,128)}, u32[]{:S(2)}) copy-start(f32[256,64]{0,1:T(8,128)} %get-tuple-element.55) | copy-start | bytes 196612
  106.3 3.8 %copy-start = (bf16[2,2048,128]{2,1,0:T(8,128)(2,1)S(1)}, bf16[2,2048,128]{2,1,0:T(8,128)(2,1)}, u32[]{:S(2)}) copy-start(bf16[2,2048,128]{2,1,0:T(8,128)(2,1)} %maximum_select_fusion) | copy-start | bytes 3145732
  107.5 3.7 %copy-start.4 = (bf16[2,256,128]{2,1,0:T(8,128)(2,1)}, bf16[2,256,128]{2,1,0:T(8,128)(2,1)S(1)}, u32[]{:S(2)}) copy-start(bf16[2,256,128]{2,1,0:T(8,128)(2,1)S(1)} %pad_maximum_fusion.2) | copy-start | bytes 393220
  107.5 2.4 %collective-permute-start.15 = (bf16[2,256,128]{2,1,0:T(8,128)(2,1)S(1)}, bf16[2,256,128]{2,1,0:T(8,128)(2,1)S(1)}, u32[]{:S(2)}, u32[]{:S(2)}) collective-permute-start(bf16[2,256,128]{2,1,0:T(8,128)(2,1)S(1)} %pad_maximum_fusion.2), channel_id=1, source_target_pairs={{0,1},{1,0},{2,3},{3,2},{4,5},{5,4},{6,7},{7,6},{8,9},{9,8},{10,11... | collective-permute-start | bytes 393224 | tf_op jit(solution)/shard_map/ppermute | solution.py:14

commit v14 on v12

--- a/solution.py
+++ b/solution.py
@@ -98,7 +98,7 @@
 
 def tree_gather(value):
     buffer = value
-    for stride, count in ((1, 2), (2, 4), (8, 4)):
+    for level, stride, count in (("c", 1, 2), ("y", 2, 4), ("z", 8, 4)):
       parts = [buffer]
       for shift in range(1, count):
           pairs = []
@@ -107,8 +107,19 @@
               target = i + (((digit + shift) % count) - digit) * stride
               pairs.append((i, target))
           parts.append(lax.ppermute(buffer, "tok", pairs))
-      buffer = jnp.concatenate(parts, axis=0)
-    return buffer
+      if level != "z":
+          buffer = jnp.concatenate(parts, axis=0)
+    return parts
+
+
+def pick(parts, rows):
+    block = parts[0].shape[0]
+    out = None
+    for k, part in enumerate(parts):
+        onehot = (rows[:, None] == k * block + jnp.arange(block, dtype=jnp.int32)[None, :]).astype(part.dtype)
+        piece = jnp.dot(onehot, part, preferred_element_type=jnp.float32)
+        out = piece if out is None else out + piece
+    return out.astype(parts[0].dtype)
 
 
 def tree_row(place, source, rows):
@@ -154,16 +165,16 @@
     sent = jnp.concatenate([dec_q.astype(jnp.bfloat16), dec_kv.astype(jnp.bfloat16), ids, pad], axis=1)
     got = tree_gather(sent)
     rows = tree_row(tok_place, owner_slots // dec_count, dec_count) + owner_slots % dec_count
-    chosen = jnp.take(got, rows, axis=0)
+    chosen = pick(got, rows)
     dec_query = chosen[:, :q_width]
     dec_keyval = chosen[:, q_width:q_width + 2 * kv_width].reshape(dec_count, 2, kv_width)
     served, new_pool = serve_owner(dec_query, dec_keyval, dec_lengths, dec_pool)
     back = tree_gather(served)
-    got_ids = got[:, q_width + 2 * kv_width:used].astype(jnp.int32)
+    got_ids = jnp.concatenate([part[:, q_width + 2 * kv_width:used] for part in got], axis=0).astype(jnp.int32)
     requests = got_ids[:, 0] * dec_count + got_ids[:, 1]
     wanted = tok_place * dec_count + jnp.arange(dec_count, dtype=jnp.int32)
     where = jnp.argmax(requests[None, :] == wanted[:, None], axis=1)
-    dec_attn = jnp.take(back, where, axis=0)
+    dec_attn = pick(back, where.astype(jnp.int32))
     all_query, all_keyval = pre_q, pre_kv
     return dec_attn, new_pool, all_query, all_keyval
 

time: 123 us -> 120 us (0.976)
  local copies, waits for them, and re-layouts: 32.4 us -> 22.7 us
  matrix products: 16.6 us -> 21.3 us
  starting transfers between devices: 30.6 us -> 33.9 us
    unnamed x68 -> x69, local copies, waits for them, and re-layouts: 16 us -> 9.18 us
    dot_general x0 -> x8, matrix products: none -> 4.7 us  [pick(): piece = jnp.dot(onehot, part, preferred_element_type=jnp.float32)]
    gather x2 -> x0, local copies, waits for them, and re-layouts: 3.74 us -> none  [the longest x1 1.97 us: body_inner(): chosen = jnp.take(got, rows, axis=0)]
    concatenate x4 -> x3, local copies, waits for them, and re-layouts: 3.64 us -> 0.03 us  [tree_gather(): buffer = jnp.concatenate(parts, axis=0)]
    ppermute x14, starting transfers between devices: 18.6 us -> 21 us  [tree_gather(): parts.append(lax.ppermute(buffer, 'tok', pairs))]
    slice x0 -> x8, local copies, waits for them, and re-layouts: none -> 2.41 us  [body_inner(): part[:, q_width + 2 * kv_width:used]]
    add x0 -> x4, other arithmetic: none -> 2.15 us  [the longest x3 1.63 us: pick(): k * block + jnp.arange(block, dtype=jnp.int32)[None, :]]
    another operation x2, local copies, waits for them, and re-layouts: 1.37 us -> 2.67 us  [body_inner(): jnp.stack([owner_slots // dec_count, owner_slots % dec_count], axis=1)]
  transfers between devices with their start and end apart: 18 -> 18, of which waited for: 6 -> 9; matrix products, arithmetic and copies ran while one was open for 37% -> 33% of each run, Pallas kernels for 0% -> 0%
where the time goes in v14:
time: 120 us; the launch traced here: 119 us
  starting transfers between devices  33.9 us (28%)
  local copies, waits for them, and re-layouts  22.7 us (19%)
  matrix products  21.3 us (18%)
  waiting for transfers between devices  15.9 us (13%)
  other arithmetic  14.5 us (12%)
  Pallas kernels  9.2 us (8%)
  between operations  1.9 us (2%)
    ppermute x14, starting transfers between devices, tree_gather(): parts.append(lax.ppermute(buffer, 'tok', pairs))  21 us
    ppermute x14, waiting for transfers between devices, tree_gather(): parts.append(lax.ppermute(buffer, 'tok', pairs))  15.9 us
    pallas_call x1, Pallas kernels, attend(): pl.pallas_call(attend_kernel, grid=(width // HD,), in_specs=[pl.BlockSpec...  9.2 us
    unnamed x69, local copies, waits for them, and re-layouts  9.18 us
    dot_general x1, matrix products, block_project(): query = jnp.dot(cols, w_query, preferred_element_type=jnp.float32) + b_query  5.12 us
    all_to_all x1, starting transfers between devices, swap_columns(): blocks = lax.all_to_all(tiled, 'kv', 0, 0, tiled=False)  4.96 us
    dot_general x8, matrix products, pick(): piece = jnp.dot(onehot, part, preferred_element_type=jnp.float32)  4.7 us
    all_to_all x1, starting transfers between devices, block_project(): blocks = lax.all_to_all(tiled, 'kv', 0, 0, tiled=False)  4.52 us
  transfers between devices with their start and end apart: 18, of which 9 were waited for; matrix products, arithmetic and copies ran while one was open for 33% of the time, Pallas kernels for 0%

profile of v14, /device:TPU:1, one launch (start us, length us, event | category | flops | bytes accessed | tf_op | source)
XLA Modules:
  0.0 119.4 jit_solution(9816067114722530235)
XLA Ops:
  0.7 6.4 %copy.122 = bf16[2,12288,128]{2,1,0:T(8,128)(2,1)} copy(bf16[2,12288,128]{2,1,0:T(8,128)(2,1)} %param.17) | data formatting | bytes 12582912
  7.1 0.7 broadcast_in_dim.20
  7.8 5.0 %all-to-all-start = ((bf16[4,16,1280]{2,1,0:T(8,128)(2,1)}), bf16[4,16,1280]{2,1,0:T(8,128)(2,1)}, u32[]{:S(2)}, u32[]{:S(2)}) async-start(bf16[4,16,1280]{2,1,0:T(8,128)(2,1)} %broadcast_in_dim.20), calls=%async_computation | async-start | bytes 327680 | tf_op jit(solution)/shard_map/all_to_all | solution.py:135
  12.8 1.0 collective-permute-start.14
  13.8 0.6 dynamic_slice.3
  14.4 1.3 %or_select_fusion.kpos_ref = s32[1,2560]{1,0:T(1,128)} fusion(s32[]{:T(128)} %bitcast.17), kind=kLoop, calls=%fused_computation.68 | loop fusion | flops 20480 | bytes 10244 | tf_op jit(solution)/shard_map/jit(_where)/select_n | solution.py:216
  16.3 0.9 multiply_cosine_fusion.1
  17.7 0.5 compare_select_fusion.1
  18.2 0.5 multiply_add_fusion
  18.7 0.6 convert_bitcast_fusion.1
  19.6 0.6 iota_add_fusion.3
  20.1 1.3 %copy.55 = bf16[256,1280]{0,1:T(8,128)(2,1)S(1)} copy(bf16[256,1280]{1,0:T(8,128)(2,1)} %param.12) | data formatting | bytes 1310720 | tf_op args[1]
  21.5 1.3 %copy.57 = bf16[16,1]{1,0:T(8,128)(2,1)} copy(bf16[16,1]{0,1:T(2,128)(2,1)} %get-tuple-element.45) | data formatting | bytes 64 | tf_op jit(solution)/shard_map/stack | solution.py:162
  22.8 1.3 %copy.58 = bf16[16,1]{1,0:T(8,128)(2,1)} copy(bf16[16,1]{0,1:T(2,128)(2,1)} %get-tuple-element.44) | data formatting | bytes 64 | tf_op jit(solution)/shard_map/stack | solution.py:162
  24.1 0.5 iota_add_fusion.2
  24.7 1.0 copy.81
  25.6 1.6 %broadcast_in_dim.19 = bf16[4,256,1280]{1,2,0:T(8,128)(2,1)} broadcast(bf16[256,1280]{0,1:T(8,128)(2,1)S(1)} %copy.55), dimensions={1,2} | broadcast | bytes 3276800 | tf_op jit(solution)/shard_map/broadcast_in_dim | solution.py:142
  27.3 0.5 fusion.25
  27.8 3.8 %fusion.20 = bf16[16,640]{1,0:T(8,128)(2,1)S(1)} fusion(bf16[16,5120]{1,0:T(8,128)(2,1)S(1)} %bitcast.97, bf16[5120,640]{1,0:T(8,128)(2,1)} %param.13, f32[640]{0:T(1024)S(1)} %copy-done.5), kind=kOutput, calls=%fused_computation.28 | convolution fusion | flops 104878080 | bytes 6740480 | tf_op jit(solution)/shard_map/dot_general | solution.py:159
  31.8 1.2 collective-permute-done
  33.0 1.3 %collective-permute-start.1 = (bf16[32,1024]{1,0:T(8,128)(2,1)S(1)}, bf16[32,1024]{1,0:T(8,128)(2,1)S(1)}, u32[]{:S(2)}, u32[]{:S(2)}) collective-permute-start(bf16[32,1024]{1,0:T(8,128)(2,1)S(1)} %pad_maximum_fusion.3), channel_id=1, source_target_pairs={{0,2},{1,3},{2,4},{3,5},{4,6},{5,7},{6,0},{7,1},{8,10},{9,11},{10,... | collective-permute-start | bytes 196616 | tf_op jit(solution)/shard_map/ppermute | solution.py:109
  34.3 2.6 %collective-permute-start.2 = (bf16[32,1024]{1,0:T(8,128)(2,1)S(1)}, bf16[32,1024]{1,0:T(8,128)(2,1)S(1)}, u32[]{:S(2)}, u32[]{:S(2)}) collective-permute-start(bf16[32,1024]{1,0:T(8,128)(2,1)S(1)} %pad_maximum_fusion.3), channel_id=1, source_target_pairs={{0,4},{1,5},{2,6},{3,7},{4,0},{5,1},{6,2},{7,3},{8,12},{9,13},{10,... | collective-permute-start | bytes 196616 | tf_op jit(solution)/shard_map/ppermute | solution.py:109
  36.9 1.1 collective-permute-start.3
  38.0 2.3 %collective-permute-done.2 = bf16[32,1024]{1,0:T(8,128)(2,1)S(1)} collective-permute-done((bf16[32,1024]{1,0:T(8,128)(2,1)S(1)}, bf16[32,1024]{1,0:T(8,128)(2,1)S(1)}, u32[]{:S(2)}, u32[]{:S(2)}) %collective-permute-start.2) | collective-permute-done | bytes 65568 | tf_op jit(solution)/shard_map/ppermute | solution.py:109
  40.3 1.7 %collective-permute-start.4 = (bf16[128,1024]{1,0:T(8,128)(2,1)S(1)}, bf16[128,1024]{1,0:T(8,128)(2,1)S(1)}, u32[]{:S(2)}, u32[]{:S(2)}) collective-permute-start(bf16[128,1024]{1,0:T(8,128)(2,1)S(1)} %constant_dynamic-update-slice_fusion), channel_id=1, source_target_pairs={{0,8},{1,9},{2,10},{3,11},{4,12},{5,13},{6,14},{7,15},{8,16},{9,17... | collective-permute-start | bytes 786440 | tf_op jit(solution)/shard_map/ppermute | solution.py:109
  42.0 0.5 iota_add_fusion.1
  42.6 0.7 iota_add_fusion.qpos_ref
  43.2 3.3 %collective-permute-start.5 = (bf16[128,1024]{1,0:T(8,128)(2,1)S(1)}, bf16[128,1024]{1,0:T(8,128)(2,1)}, u32[]{:S(2)}, u32[]{:S(2)}) collective-permute-start(bf16[128,1024]{1,0:T(8,128)(2,1)S(1)} %constant_dynamic-update-slice_fusion), channel_id=1, source_target_pairs={{0,16},{1,17},{2,18},{3,19},{4,20},{5,21},{6,22},{7,23},{8,24},{9,... | collective-permute-start | bytes 786440 | tf_op jit(solution)/shard_map/ppermute | solution.py:109
  46.5 0.5 iota_add_fusion.4
  47.0 4.5 %all-to-all-start.1 = ((bf16[4,256,1280]{1,2,0:T(8,128)(2,1)}), bf16[4,256,1280]{1,2,0:T(8,128)(2,1)S(1)}, u32[]{:S(2)}, u32[]{:S(2)}) async-start(bf16[4,256,1280]{1,2,0:T(8,128)(2,1)} %broadcast_in_dim.19), calls=%async_computation.1 | async-start | bytes 5242880 | tf_op jit(solution)/shard_map/all_to_all | solution.py:144
  51.6 0.7 collective-permute-start.6
  52.3 0.6 copy.59
  53.1 2.9 %collective-permute-done.5 = bf16[128,1024]{1,0:T(8,128)(2,1)} collective-permute-done((bf16[128,1024]{1,0:T(8,128)(2,1)S(1)}, bf16[128,1024]{1,0:T(8,128)(2,1)}, u32[]{:S(2)}, u32[]{:S(2)}) %collective-permute-start.5) | collective-permute-done | bytes 262176 | tf_op jit(solution)/shard_map/ppermute | solution.py:109
  56.0 1.2 fusion.70
  57.2 1.2 fusion.68
  58.4 0.8 fusion.17
  59.3 0.8 fusion.81
  60.2 2.4 %scatter_fusion = bf16[2,12288,128]{2,1,0:T(8,128)(2,1)} fusion(bf16[2,12288,128]{2,1,0:T(8,128)(2,1)} %copy.122, s32[16]{0:T(128)} %get-tuple-element.13, bf16[16,2,128]{2,0,1:T(8,128)(2,1)S(1)} %maximum_bitcast_fusion), kind=kCustom, calls=%fused_computation | custom fusion | bytes 24640 | tf_op jit(solution)/shard_map/scatter | solution.py:90
  62.7 3.4 %fusion.105 = (f32[16,5]{0,1:T(8,128)S(1)}, f32[16,5,12288]{2,0,1:T(8,128)S(1)}) fusion(bf16[2,12288,128]{2,1,0:T(8,128)(2,1)} %scatter_fusion, bf16[16,5,64]{2,0,1:T(8,128)(2,1)S(1)} %get-tuple-element.24, bf16[16,5,64]{2,0,1:T(8,128)(2,1)S(1)} %get-tuple-element.23, pred[16,12288]{1,0:T(8,128)(4,1)S(1)} %fusion.37), kind=kOutput, calls=%fused_computation.183 | convolution fusion | flops 254648240 | bytes 7295296 | tf_op jit(solution)/shard_map/ngd,md->ngm/dot_general | solution.py:66
  66.1 0.8 fusion.1
  66.9 0.9 fusion.34
  67.9 0.8 slice.98
  68.8 0.8 slice.99
  69.7 3.2 %collective-permute-start.7 = (bf16[16,640]{1,0:T(8,128)(2,1)S(1)}, bf16[16,640]{1,0:T(8,128)(2,1)S(1)}, u32[]{:S(2)}, u32[]{:S(2)}) collective-permute-start(bf16[16,640]{1,0:T(8,128)(2,1)S(1)} %bitcast.103), channel_id=1, source_target_pairs={{0,1},{1,0},{2,3},{3,2},{4,5},{5,4},{6,7},{7,6},{8,9},{9,8},{10,11... | collective-permute-start | bytes 61448 | tf_op jit(solution)/shard_map/ppermute | solution.py:109
  72.9 0.8 collective-permute-done.7
  74.2 0.7 iota_reduce_fusion
  74.9 3.0 %collective-permute-start.9 = (bf16[32,640]{1,0:T(8,128)(2,1)S(1)}, bf16[32,640]{1,0:T(8,128)(2,1)S(1)}, u32[]{:S(2)}, u32[]{:S(2)}) collective-permute-start(bf16[32,640]{1,0:T(8,128)(2,1)S(1)} %get-tuple-element.27), channel_id=1, source_target_pairs={{0,4},{1,5},{2,6},{3,7},{4,0},{5,1},{6,2},{7,3},{8,12},{9,13},{10,... | collective-permute-start | bytes 122888 | tf_op jit(solution)/shard_map/ppermute | solution.py:109
  77.9 0.5 collective-permute-start.10
  78.4 1.5 %collective-permute-done.9 = bf16[32,640]{1,0:T(8,128)(2,1)S(1)} collective-permute-done((bf16[32,640]{1,0:T(8,128)(2,1)S(1)}, bf16[32,640]{1,0:T(8,128)(2,1)S(1)}, u32[]{:S(2)}, u32[]{:S(2)}) %collective-permute-start.9) | collective-permute-done | bytes 40992 | tf_op jit(solution)/shard_map/ppermute | solution.py:109
  79.9 1.1 collective-permute-done.10
  81.3 2.8 %maximum_select_fusion = bf16[2,2048,128]{2,1,0:T(8,128)(2,1)} fusion(bf16[2,1024,128]{2,1,0:T(8,128)(2,1)} %collective-permute-done.14, bf16[2,1024,128]{2,1,0:T(8,128)(2,1)} %param.20, pred[]{:T(512)S(6)} %eq.139), kind=kLoop, calls=%fused_computation.35 | loop fusion | flops 4718592 | bytes 2097153 | tf_op jit(solution)/shard_map/jit(_where)/select_n | solution.py:202
  84.1 2.8 %collective-permute-start.12 = (bf16[128,640]{1,0:T(8,128)(2,1)S(1)}, bf16[128,640]{1,0:T(8,128)(2,1)S(1)}, u32[]{:S(2)}, u32[]{:S(2)}) collective-permute-start(bf16[128,640]{1,0:T(8,128)(2,1)S(1)} %constant_dynamic-update-slice_fusion.7), channel_id=1, source_target_pairs={{0,16},{1,17},{2,18},{3,19},{4,20},{5,21},{6,22},{7,23},{8,24},{9,... | collective-permute-start | bytes 491528 | tf_op jit(solution)/shard_map/ppermute | solution.py:109
  87.1 4.5 %collective-permute-done.12 = bf16[128,640]{1,0:T(8,128)(2,1)S(1)} collective-permute-done((bf16[128,640]{1,0:T(8,128)(2,1)S(1)}, bf16[128,640]{1,0:T(8,128)(2,1)S(1)}, u32[]{:S(2)}, u32[]{:S(2)}) %collective-permute-start.12) | collective-permute-done | bytes 163872 | tf_op jit(solution)/shard_map/ppermute | solution.py:109
  91.8 1.5 %collective-permute-done.13 = bf16[128,640]{1,0:T(8,128)(2,1)S(1)} collective-permute-done((bf16[128,640]{1,0:T(8,128)(2,1)S(1)}, bf16[128,640]{1,0:T(8,128)(2,1)S(1)}, u32[]{:S(2)}, u32[]{:S(2)}) %collective-permute-start.13) | collective-permute-done | bytes 163872 | tf_op jit(solution)/shard_map/ppermute | solution.py:109
  93.5 0.8 fusion.21
  94.4 2.9 %fusion.12 = f32[256,256]{0,1:T(8,128)S(1)} fusion(bf16[256,5120]{0,1:T(8,128)(2,1)S(1)} %bitcast.91, bf16[640,8,2,128]{3,2,1,0:T(2,128)(2,1)} %bitcast.93, f32[256]{0:T(256)S(1)} %bitcast.107), kind=kOutput, calls=%fused_computation.19 | convolution fusion | flops 671154176 | bytes 5506048 | tf_op jit(solution)/shard_map/dot_general | solution.py:147
  97.3 0.6 fusion.101
  98.0 5.1 %convolution_add_fusion = f32[256,640]{1,0:T(8,128)S(1)} fusion(bf16[256,5120]{0,1:T(8,128)(2,1)S(1)} %bitcast.92, bf16[5120,640]{1,0:T(8,128)(2,1)} %param.13, f32[640]{0:T(1024)S(1)} %copy-done.6), kind=kOutput, calls=%fused_computation.18 | convolution fusion | flops 1677885440 | bytes 9832960 | tf_op jit(solution)/shard_map/dot_general | solution.py:146
  103.1 1.0 copy.78
  104.4 0.6 fusion.50
  105.1 2.5 %collective-permute-start.15 = (bf16[2,256,128]{2,1,0:T(8,128)(2,1)S(1)}, bf16[2,256,128]{2,1,0:T(8,128)(2,1)S(1)}, u32[]{:S(2)}, u32[]{:S(2)}) collective-permute-start(bf16[2,256,128]{2,1,0:T(8,128)(2,1)S(1)} %pad_maximum_fusion.2), channel_id=1, source_target_pairs={{0,1},{1,0},{2,3},{3,2},{4,5},{5,4},{6,7},{7,6},{8,9},{9,8},{10,11... | collective-permute-start | bytes 393224 | tf_op jit(solution)/shard_map/ppermute | solution.py:14
  107.9 0.9 copy.73.q_ref
  109.0 1.2 fusion.40
  110.2 9.2 %shard_map.138 = bf16[256,640]{1,0:T(8,128)(2,1)} custom-call(bf16[256,640]{1,0:T(8,128)(2,1)} %copy.73.q_ref, bf16[2560,128]{1,0:T(8,128)(2,1)} %get-tuple-element.16.k_ref, bf16[2560,128]{1,0:T(8,128)(2,1)} %get-tuple-element.15.v_ref, s32[256,1]{1,0:T(8,128)} %iota_add_fusion.qpos_ref, s32[1,2560]{1,0:T(1,128)} %or_select_fusion.kpos_ref), custom_call_target="tpu_custom_call" | custom-call | tf_op jit(solution)/shard_map/pallas_call | solution.py:47
  (122 shorter events, 3.8 us)
Async XLA Ops:
  0.6 6.5 %copy-start.4 = (bf16[16,1280]{1,0:T(8,128)(2,1)S(1)}, bf16[16,1280]{1,0:T(8,128)(2,1)}, u32[]{:S(2)}) copy-start(bf16[16,1280]{1,0:T(8,128)(2,1)} %param.11) | copy-start | bytes 122884
  0.6 13.1 %copy-start.25 = (s32[16]{0:T(128)S(1)}, s32[16]{0:T(128)}, u32[]{:S(2)}) copy-start(s32[16]{0:T(128)} %param.21) | copy-start | bytes 196
  0.7 15.7 %copy-start.22 = (s32[16]{0:T(128)S(1)}, s32[16]{0:T(128)}, u32[]{:S(2)}) copy-start(s32[16]{0:T(128)} %param.19) | copy-start | bytes 196
  0.7 17.6 %copy-start.23 = (s32[16]{0:T(128)S(1)}, s32[16]{0:T(128)}, u32[]{:S(2)}) copy-start(s32[16]{0:T(128)} %param.18) | copy-start | bytes 196
  7.1 20.2 %copy-start.1 = (bf16[5120,2,128]{2,1,0:T(2,128)(2,1)S(1)}, bf16[5120,2,128]{2,1,0:T(2,128)(2,1)}, u32[]{:S(2)}) copy-start(bf16[5120,2,128]{2,1,0:T(2,128)(2,1)} %param.14) | copy-start | bytes 7864324
  7.8 16.9 %all-to-all-start = ((bf16[4,16,1280]{2,1,0:T(8,128)(2,1)}), bf16[4,16,1280]{2,1,0:T(8,128)(2,1)}, u32[]{:S(2)}, u32[]{:S(2)}) async-start(bf16[4,16,1280]{2,1,0:T(8,128)(2,1)} %broadcast_in_dim.20), calls=%async_computation | async-start | bytes 327680 | tf_op jit(solution)/shard_map/all_to_all | solution.py:135
  12.8 68.6 %collective-permute-start.14 = (bf16[2,1024,128]{2,1,0:T(8,128)(2,1)}, bf16[2,1024,128]{2,1,0:T(8,128)(2,1)}, u32[]{:S(2)}, u32[]{:S(2)}) collective-permute-start(bf16[2,1024,128]{2,1,0:T(8,128)(2,1)} %param.20), channel_id=1, source_target_pairs={{0,1},{1,0},{2,3},{3,2},{4,5},{5,4},{6,7},{7,6},{8,9},{9,8},{10,11... | collective-permute-start | bytes 1572872 | tf_op jit(solution)/shard_map/ppermute | solution.py:14
  13.7 3.7 %copy-start.10 = (f32[64]{0:T(128)}, f32[64]{0:T(128)S(1)}, u32[]{:S(2)}) copy-start(f32[64]{0:T(128)S(1)} %negate_power_fusion) | copy-start | bytes 772
  16.3 1.1 copy-start.12
  16.3 1.1 copy-start.19
  24.7 2.6 %copy-start.20 = (f32[2,128]{1,0:T(2,128)S(1)}, f32[2,128]{1,0:T(2,128)}, u32[]{:S(2)}) copy-start(f32[2,128]{1,0:T(2,128)} %param.16) | copy-start | bytes 3076
  24.7 3.1 %copy-start.5 = (f32[640]{0:T(1024)S(1)}, f32[640]{0:T(1024)}, u32[]{:S(2)}) copy-start(f32[640]{0:T(1024)} %param.15) | copy-start | bytes 7684
  27.8 3.9 %copy-start.7 = (bf16[16,1]{1,0:T(8,128)(2,1)S(1)}, bf16[16,1]{1,0:T(8,128)(2,1)}, u32[]{:S(2)}) copy-start(bf16[16,1]{1,0:T(8,128)(2,1)} %copy.57) | copy-start | bytes 100
  27.8 3.9 %copy-start.8 = (bf16[16,1]{1,0:T(8,128)(2,1)S(1)}, bf16[16,1]{1,0:T(8,128)(2,1)}, u32[]{:S(2)}) copy-start(bf16[16,1]{1,0:T(8,128)(2,1)} %copy.58) | copy-start | bytes 100
  31.6 21.3 %copy-start.9 = (s32[16]{0:T(128)S(1)}, s32[16]{0:T(128)}, u32[]{:S(2)}) copy-start(s32[16]{0:T(128)} %get-tuple-element.10) | copy-start | bytes 196
  31.6 21.3 %copy-start.14 = (s32[128]{0:T(128)S(1)}, s32[128]{0:T(128)}, u32[]{:S(2)}) copy-start(s32[128]{0:T(128)} %iota_add_fusion.3) | copy-start | bytes 1540
  31.7 1.2 %collective-permute-start = (bf16[16,1024]{1,0:T(8,128)(2,1)S(1)}, bf16[16,1024]{1,0:T(8,128)(2,1)S(1)}, u32[]{:S(2)}, u32[]{:S(2)}) collective-permute-start(bf16[16,1024]{1,0:T(8,128)(2,1)S(1)} %concatenate.78), channel_id=1, source_target_pairs={{0,1},{1,0},{2,3},{3,2},{4,5},{5,4},{6,7},{7,6},{8,9},{9,8},{10,11... | collective-permute-start | bytes 98312 | tf_op jit(solution)/shard_map/ppermute | solution.py:109
  33.0 5.0 %collective-permute-start.1 = (bf16[32,1024]{1,0:T(8,128)(2,1)S(1)}, bf16[32,1024]{1,0:T(8,128)(2,1)S(1)}, u32[]{:S(2)}, u32[]{:S(2)}) collective-permute-start(bf16[32,1024]{1,0:T(8,128)(2,1)S(1)} %pad_maximum_fusion.3), channel_id=1, source_target_pairs={{0,2},{1,3},{2,4},{3,5},{4,6},{5,7},{6,0},{7,1},{8,10},{9,11},{10,... | collective-permute-start | bytes 196616 | tf_op jit(solution)/shard_map/ppermute | solution.py:109
  34.3 6.0 %collective-permute-start.2 = (bf16[32,1024]{1,0:T(8,128)(2,1)S(1)}, bf16[32,1024]{1,0:T(8,128)(2,1)S(1)}, u32[]{:S(2)}, u32[]{:S(2)}) collective-permute-start(bf16[32,1024]{1,0:T(8,128)(2,1)S(1)} %pad_maximum_fusion.3), channel_id=1, source_target_pairs={{0,4},{1,5},{2,6},{3,7},{4,0},{5,1},{6,2},{7,3},{8,12},{9,13},{10,... | collective-permute-start | bytes 196616 | tf_op jit(solution)/shard_map/ppermute | solution.py:109
  36.9 3.4 %collective-permute-start.3 = (bf16[32,1024]{1,0:T(8,128)(2,1)S(1)}, bf16[32,1024]{1,0:T(8,128)(2,1)S(1)}, u32[]{:S(2)}, u32[]{:S(2)}) collective-permute-start(bf16[32,1024]{1,0:T(8,128)(2,1)S(1)} %pad_maximum_fusion.3), channel_id=1, source_target_pairs={{0,6},{1,7},{2,0},{3,1},{4,2},{5,3},{6,4},{7,5},{8,14},{9,15},{10,... | collective-permute-start | bytes 196616 | tf_op jit(solution)/shard_map/ppermute | solution.py:109
  40.3 12.6 %collective-permute-start.4 = (bf16[128,1024]{1,0:T(8,128)(2,1)S(1)}, bf16[128,1024]{1,0:T(8,128)(2,1)S(1)}, u32[]{:S(2)}, u32[]{:S(2)}) collective-permute-start(bf16[128,1024]{1,0:T(8,128)(2,1)S(1)} %constant_dynamic-update-slice_fusion), channel_id=1, source_target_pairs={{0,8},{1,9},{2,10},{3,11},{4,12},{5,13},{6,14},{7,15},{8,16},{9,17... | collective-permute-start | bytes 786440 | tf_op jit(solution)/shard_map/ppermute | solution.py:109
  43.2 12.8 %collective-permute-start.5 = (bf16[128,1024]{1,0:T(8,128)(2,1)S(1)}, bf16[128,1024]{1,0:T(8,128)(2,1)}, u32[]{:S(2)}, u32[]{:S(2)}) collective-permute-start(bf16[128,1024]{1,0:T(8,128)(2,1)S(1)} %constant_dynamic-update-slice_fusion), channel_id=1, source_target_pairs={{0,16},{1,17},{2,18},{3,19},{4,20},{5,21},{6,22},{7,23},{8,24},{9,... | collective-permute-start | bytes 786440 | tf_op jit(solution)/shard_map/ppermute | solution.py:109
  47.0 47.3 %all-to-all-start.1 = ((bf16[4,256,1280]{1,2,0:T(8,128)(2,1)}), bf16[4,256,1280]{1,2,0:T(8,128)(2,1)S(1)}, u32[]{:S(2)}, u32[]{:S(2)}) async-start(bf16[4,256,1280]{1,2,0:T(8,128)(2,1)} %broadcast_in_dim.19), calls=%async_computation.1 | async-start | bytes 5242880 | tf_op jit(solution)/shard_map/all_to_all | solution.py:144
  51.6 5.7 %collective-permute-start.6 = (bf16[128,1024]{1,0:T(8,128)(2,1)S(1)}, bf16[128,1024]{1,0:T(8,128)(2,1)}, u32[]{:S(2)}, u32[]{:S(2)}) collective-permute-start(bf16[128,1024]{1,0:T(8,128)(2,1)S(1)} %constant_dynamic-update-slice_fusion), channel_id=1, source_target_pairs={{0,24},{1,25},{2,26},{3,27},{4,28},{5,29},{6,30},{7,31},{8,0},{9,1... | collective-permute-start | bytes 786440 | tf_op jit(solution)/shard_map/ppermute | solution.py:109
  62.7 4.2 %slice-start = ((s8[6291456]{0:T(1024)(128)(4,1)}), s8[4194304]{0:T(1024)(128)(4,1)S(1)}, s32[]{:S(2)}) async-start(s8[6291456]{0:T(1024)(128)(4,1)} %bitcast.89), calls=%async_computation.2 | async-start | bytes 8388608
  62.7 4.2 %slice-start.1 = ((s8[6291456]{0:T(1024)(128)(4,1)}), s8[2097152]{0:T(1024)(128)(4,1)S(1)}, s32[]{:S(2)}) async-start(s8[6291456]{0:T(1024)(128)(4,1)} %bitcast.89), calls=%async_computation.3 | async-start | bytes 4194304
  66.9 6.0 %copy-start.18 = (bf16[128,2]{0,1:T(2,128)(2,1)S(1)}, bf16[128,2]{0,1:T(2,128)(2,1)}, u32[]{:S(2)}) copy-start(bf16[128,2]{0,1:T(2,128)(2,1)} %copy.59) | copy-start | bytes 1540
  66.9 7.3 %copy-start.24 = (s32[16]{0:T(128)S(1)}, s32[16]{0:T(128)}, u32[]{:S(2)}) copy-start(s32[16]{0:T(128)} %iota_add_fusion.4) | copy-start | bytes 196
  66.9 20.0 %copy-start.15 = (s32[128]{0:T(128)S(1)}, s32[128]{0:T(128)}, u32[]{:S(2)}) copy-start(s32[128]{0:T(128)} %iota_add_fusion.3) | copy-start | bytes 1540
  66.9 24.7 %copy-start.16 = (s32[128]{0:T(128)S(1)}, s32[128]{0:T(128)}, u32[]{:S(2)}) copy-start(s32[128]{0:T(128)} %iota_add_fusion.2) | copy-start | bytes 1540
  67.8 25.5 %copy-start.17 = (s32[128]{0:T(128)S(1)}, s32[128]{0:T(128)}, u32[]{:S(2)}) copy-start(s32[128]{0:T(128)} %iota_add_fusion.1) | copy-start | bytes 1540
  67.8 26.5 %copy-start.21 = (f32[2,128]{1,0:T(2,128)S(1)}, f32[2,128]{1,0:T(2,128)}, u32[]{:S(2)}) copy-start(f32[2,128]{1,0:T(2,128)} %param.16) | copy-start | bytes 3076
  69.7 4.1 %collective-permute-start.7 = (bf16[16,640]{1,0:T(8,128)(2,1)S(1)}, bf16[16,640]{1,0:T(8,128)(2,1)S(1)}, u32[]{:S(2)}, u32[]{:S(2)}) collective-permute-start(bf16[16,640]{1,0:T(8,128)(2,1)S(1)} %bitcast.103), channel_id=1, source_target_pairs={{0,1},{1,0},{2,3},{3,2},{4,5},{5,4},{6,7},{7,6},{8,9},{9,8},{10,11... | collective-permute-start | bytes 61448 | tf_op jit(solution)/shard_map/ppermute | solution.py:109
  73.7 4.7 %collective-permute-start.8 = (bf16[32,640]{1,0:T(8,128)(2,1)S(1)}, bf16[32,640]{1,0:T(8,128)(2,1)S(1)}, u32[]{:S(2)}, u32[]{:S(2)}) collective-permute-start(bf16[32,640]{1,0:T(8,128)(2,1)S(1)} %get-tuple-element.27), channel_id=1, source_target_pairs={{0,2},{1,3},{2,4},{3,5},{4,6},{5,7},{6,0},{7,1},{8,10},{9,11},{10,... | collective-permute-start | bytes 122888 | tf_op jit(solution)/shard_map/ppermute | solution.py:109
  74.9 5.0 %collective-permute-start.9 = (bf16[32,640]{1,0:T(8,128)(2,1)S(1)}, bf16[32,640]{1,0:T(8,128)(2,1)S(1)}, u32[]{:S(2)}, u32[]{:S(2)}) collective-permute-start(bf16[32,640]{1,0:T(8,128)(2,1)S(1)} %get-tuple-element.27), channel_id=1, source_target_pairs={{0,4},{1,5},{2,6},{3,7},{4,0},{5,1},{6,2},{7,3},{8,12},{9,13},{10,... | collective-permute-start | bytes 122888 | tf_op jit(solution)/shard_map/ppermute | solution.py:109
  77.9 3.1 %collective-permute-start.10 = (bf16[32,640]{1,0:T(8,128)(2,1)S(1)}, bf16[32,640]{1,0:T(8,128)(2,1)S(1)}, u32[]{:S(2)}, u32[]{:S(2)}) collective-permute-start(bf16[32,640]{1,0:T(8,128)(2,1)S(1)} %get-tuple-element.27), channel_id=1, source_target_pairs={{0,6},{1,7},{2,0},{3,1},{4,2},{5,3},{6,4},{7,5},{8,14},{9,15},{10,... | collective-permute-start | bytes 122888 | tf_op jit(solution)/shard_map/ppermute | solution.py:109
  81.0 5.9 %collective-permute-start.11 = (bf16[128,640]{1,0:T(8,128)(2,1)S(1)}, bf16[128,640]{1,0:T(8,128)(2,1)S(1)}, u32[]{:S(2)}, u32[]{:S(2)}) collective-permute-start(bf16[128,640]{1,0:T(8,128)(2,1)S(1)} %constant_dynamic-update-slice_fusion.7), channel_id=1, source_target_pairs={{0,8},{1,9},{2,10},{3,11},{4,12},{5,13},{6,14},{7,15},{8,16},{9,17... | collective-permute-start | bytes 491528 | tf_op jit(solution)/shard_map/ppermute | solution.py:109
  84.1 7.5 %collective-permute-start.12 = (bf16[128,640]{1,0:T(8,128)(2,1)S(1)}, bf16[128,640]{1,0:T(8,128)(2,1)S(1)}, u32[]{:S(2)}, u32[]{:S(2)}) collective-permute-start(bf16[128,640]{1,0:T(8,128)(2,1)S(1)} %constant_dynamic-update-slice_fusion.7), channel_id=1, source_target_pairs={{0,16},{1,17},{2,18},{3,19},{4,20},{5,21},{6,22},{7,23},{8,24},{9,... | collective-permute-start | bytes 491528 | tf_op jit(solution)/shard_map/ppermute | solution.py:109
  86.9 6.4 %collective-permute-start.13 = (bf16[128,640]{1,0:T(8,128)(2,1)S(1)}, bf16[128,640]{1,0:T(8,128)(2,1)S(1)}, u32[]{:S(2)}, u32[]{:S(2)}) collective-permute-start(bf16[128,640]{1,0:T(8,128)(2,1)S(1)} %constant_dynamic-update-slice_fusion.7), channel_id=1, source_target_pairs={{0,24},{1,25},{2,26},{3,27},{4,28},{5,29},{6,30},{7,31},{8,0},{9,1... | collective-permute-start | bytes 491528 | tf_op jit(solution)/shard_map/ppermute | solution.py:109
  94.4 3.6 %copy-start.6 = (f32[640]{0:T(1024)S(1)}, f32[640]{0:T(1024)}, u32[]{:S(2)}) copy-start(f32[640]{0:T(1024)} %param.15) | copy-start | bytes 7684
  97.9 6.4 %copy-start.11 = (f32[64]{0:T(128)S(1)}, f32[64]{0:T(128)}, u32[]{:S(2)}) copy-start(f32[64]{0:T(128)} %copy-done.10) | copy-start | bytes 772
  98.0 6.4 %copy-start.13 = (f32[256]{0:T(256)S(1)}, f32[256]{0:T(256)}, u32[]{:S(2)}) copy-start(f32[256]{0:T(256)} %copy-done.12) | copy-start | bytes 3076
  98.0 9.8 %copy-start.2 = (f32[256,64]{0,1:T(8,128)S(1)}, f32[256,64]{0,1:T(8,128)}, u32[]{:S(2)}) copy-start(f32[256,64]{0,1:T(8,128)} %get-tuple-element.36) | copy-start | bytes 196612
  103.1 5.9 %copy-start = (bf16[2,2048,128]{2,1,0:T(8,128)(2,1)S(1)}, bf16[2,2048,128]{2,1,0:T(8,128)(2,1)}, u32[]{:S(2)}) copy-start(bf16[2,2048,128]{2,1,0:T(8,128)(2,1)} %maximum_select_fusion) | copy-start | bytes 3145732
  105.0 5.1 %copy-start.3 = (bf16[2,256,128]{2,1,0:T(8,128)(2,1)}, bf16[2,256,128]{2,1,0:T(8,128)(2,1)S(1)}, u32[]{:S(2)}) copy-start(bf16[2,256,128]{2,1,0:T(8,128)(2,1)S(1)} %pad_maximum_fusion.2) | copy-start | bytes 393220
  105.1 3.8 %collective-permute-start.15 = (bf16[2,256,128]{2,1,0:T(8,128)(2,1)S(1)}, bf16[2,256,128]{2,1,0:T(8,128)(2,1)S(1)}, u32[]{:S(2)}, u32[]{:S(2)}) collective-permute-start(bf16[2,256,128]{2,1,0:T(8,128)(2,1)S(1)} %pad_maximum_fusion.2), channel_id=1, source_target_pairs={{0,1},{1,0},{2,3},{3,2},{4,5},{5,4},{6,7},{7,6},{8,9},{9,8},{10,11... | collective-permute-start | bytes 393224 | tf_op jit(solution)/shard_map/ppermute | solution.py:14
